TPU v7x, 512 devices: a whole 4x4x16 slice. The times are simulated.
512 devices in a mesh: rows: 128 (over z, y, core), dp: 4 (over x).
Axes of the slice: x: 4, y: 4, z: 16, core: 2. Of those that a mesh axis runs over, the one named last changes fastest.
Arguments:
- tokens: bfloat16 [262144, 512], P(('rows', 'dp')), may hold values from -24 to 24
- out_grad: bfloat16 [262144, 512], P(('rows', 'dp')), may hold values from -24 to 24
- seq_lengths: int32 [512, 4], P(('rows', 'dp')), may hold values from 1 to 256, 512 in all within a row
- owners: int32 [262144, 1], P(('rows', 'dp')), may hold values from 0 to 127; in each aligned block of 512 rows (0 to 511, 512 to 1023, ...) at most 16 rows name the same one
- slots: int32 [262144], P(('rows', 'dp')), may hold values from 0 to 127
- w_in: bfloat16 [512, 1024], replicated, may hold values from -0.25 to 0.25
- w_out: bfloat16 [512, 256], replicated, may hold values from -0.375 to 0.375
- emb_rows: float32 [16384, 512], P('rows'), may hold values from -0.6 to 0.6
- emb_mom: float32 [16384, 512], P('rows'), may hold values from -0.6 to 0.6
- emb_var: float32 [16384], P('rows'), may hold values from 0.01 to 0.1
Outputs:
- new_rows: float32 [16384, 512], P('rows')
- new_mom: float32 [16384, 512], P('rows')
- new_var: float32 [16384], P('rows')
- w_in_grad: float32 [512, 1024], P('rows')
- w_out_grad: float32 [512, 256], P('rows')
Inputs may be any that keep to these rules, and one draw needn't show every extreme that they name: `seq_lengths`: each row sums to 512; its largest entry is exactly 256. `owners`: among the 512 tokens of one device at most 16 name the same owner; some device reaches 16.
All inputs are finite; a program needn't handle non-finite values.
Results may differ from a plain program's by a relative error of at most 0.015.
Values may be sent and summed in bfloat16 or wider, within the bound.
No kernel may reach another device: no remote copies, remote signals or barrier semaphores. Data moves between devices by JAX's collectives and lax.ppermute only.
A program may use at most 64 MiB of HBM per device.

v0:
```python
import jax
import jax.numpy as jnp
from jax import lax
from jax.sharding import PartitionSpec as P

HEADS = 4
HEAD_DIM = 64
HW = 256
MAXLEN = 256


norm_eps = 1e-06
beta_one = 0.9
beta_two = 0.99
learn_rate = 0.05
adam_eps = 1e-08
bias_one = 1.0 - 0.9**10
bias_two = 1.0 - 0.99**10


def layer_norm(values):
    average = jnp.mean(values, axis=-1, keepdims=True)
    centered = values - average
    spread = jnp.mean(centered * centered, axis=-1, keepdims=True)
    return centered * lax.rsqrt(spread + norm_eps)


def allowed_mask(lengths, tok_count):
    ends = jnp.cumsum(lengths)
    position = jnp.arange(tok_count, dtype=jnp.int32)
    segment = jnp.sum((position[:, None] >= ends[None, :]).astype(jnp.int32), axis=1)
    same = segment[:, None] == segment[None, :]
    causal = position[None, :] <= position[:, None]
    return (same & causal).astype(jnp.float32)


def core(pre, allowed):
    tok_count = pre.shape[0]
    proj = jax.nn.silu(pre).astype(jnp.bfloat16)
    upart, vpart, qpart, kpart = jnp.split(proj, 4, axis=1)
    queries = qpart.reshape(tok_count, HEADS, HEAD_DIM)
    keys_part = kpart.reshape(tok_count, HEADS, HEAD_DIM)
    values_part = vpart.reshape(tok_count, HEADS, HEAD_DIM)
    scores = jnp.einsum(
        "thd,shd->hts", queries, keys_part, preferred_element_type=jnp.float32
    ) * HEAD_DIM ** (-0.5)
    weights = (jax.nn.silu(scores) * allowed[None] / MAXLEN).astype(jnp.bfloat16)
    attn = jnp.einsum(
        "hts,shd->thd", weights, values_part, preferred_element_type=jnp.float32
    ).reshape(tok_count, HW)
    return (layer_norm(attn) * upart.astype(jnp.float32)).astype(jnp.bfloat16)


def row_adam(rows_now, mom_now, var_now, grad, counts):
    touched = counts > 0.5
    mom_next = beta_one * mom_now + (1.0 - beta_one) * grad
    var_next = beta_two * var_now + (1.0 - beta_two) * jnp.mean(grad * grad, axis=1)
    advance = mom_next / bias_one / (jnp.sqrt(var_next / bias_two)[:, None] + adam_eps)
    rows_next = rows_now - learn_rate * advance
    return (
        jnp.where(touched[:, None], rows_next, rows_now),
        jnp.where(touched[:, None], mom_next, mom_now),
        jnp.where(touched, var_next, var_now),
    )


def local(tokens, out_grad, seq_lengths, owners, slots, w_in, w_out, emb_rows, emb_mom, emb_var):
    tok_count = tokens.shape[0]
    width = tokens.shape[1]
    allowed = allowed_mask(seq_lengths[0], tok_count)
    normed_exact, norm_back = jax.vjp(layer_norm, tokens.astype(jnp.float32))
    normed = normed_exact.astype(jnp.bfloat16)
    pre = jnp.dot(normed, w_in, preferred_element_type=jnp.float32)
    y_out, core_back = jax.vjp(lambda inner: core(inner, allowed), pre)
    y_grad = jnp.dot(out_grad, w_out, preferred_element_type=jnp.float32).astype(jnp.bfloat16)
    pre_grad_b = core_back(y_grad)[0].astype(jnp.bfloat16)
    normed_grad = lax.dot_general(
        pre_grad_b, w_in, (((1,), (1,)), ((), ())), preferred_element_type=jnp.float32
    )
    emb_grad = (norm_back(normed_grad)[0] + out_grad.astype(jnp.float32)).astype(jnp.bfloat16)
    contract = (((0,), (0,)), ((), ()))
    in_cols = w_in.shape[1]
    owner_count = lax.axis_size("rows")
    weight_share = lax.psum_scatter(
        jnp.concatenate(
            [
                lax.dot_general(normed, pre_grad_b, contract, preferred_element_type=jnp.float32),
                lax.dot_general(out_grad, y_out, contract, preferred_element_type=jnp.float32),
            ],
            axis=1,
        ),
        "rows",
        scatter_dimension=0,
        tiled=True,
    )
    weight_share = lax.psum(weight_share, "dp")
    w_in_grad = weight_share[:, :in_cols]
    w_out_grad = weight_share[:, in_cols:]
    capacity = max(2, 4 * tok_count // owner_count)
    buffer_rows = owner_count * capacity
    owner_of = owners[:, 0]
    position = jnp.arange(tok_count, dtype=jnp.int32)
    earlier = jnp.sum(
        ((owner_of[:, None] == owner_of[None, :]) & (position[None, :] < position[:, None])).astype(
            jnp.int32
        ),
        axis=1,
    )
    position_to = owner_of * capacity + earlier
    chosen = position_to[None, :] == jnp.arange(buffer_rows, dtype=jnp.int32)[:, None]
    outgoing = jnp.dot(
        chosen.astype(jnp.bfloat16), emb_grad, preferred_element_type=jnp.float32
    ).astype(jnp.bfloat16)
    outgoing = outgoing.reshape(owner_count, capacity, width)
    out_slots = (jnp.sum(jnp.where(chosen, slots[None, :] + 1, 0), axis=1) - 1).reshape(
        owner_count, capacity
    )
    arrived, arrived_slots = (
        lax.all_to_all(outgoing, "rows", split_axis=0, concat_axis=0, tiled=True),
        lax.all_to_all(out_slots, "rows", split_axis=0, concat_axis=0, tiled=True),
    )
    received = arrived.reshape(buffer_rows, width)
    got_slots = arrived_slots.reshape(buffer_rows)
    slot_count = emb_rows.shape[0]
    matches = got_slots[None, :] == jnp.arange(slot_count, dtype=jnp.int32)[:, None]
    grad_part = jnp.dot(matches.astype(jnp.bfloat16), received, preferred_element_type=jnp.float32)
    count_part = jnp.sum(matches.astype(jnp.float32), axis=1)
    grad_all, count_all = lax.psum((grad_part, count_part), "dp")
    new_rows, new_mom, new_var = row_adam(emb_rows, emb_mom, emb_var, grad_all, count_all)
    return (new_rows, new_mom, new_var, w_in_grad, w_out_grad)


def solution(mesh):
    in_specs = (
        P(("rows", "dp"), None),
        P(("rows", "dp"), None),
        P(("rows", "dp"), None),
        P(("rows", "dp"), None),
        P(("rows", "dp")),
        P(),
        P(),
        P("rows", None),
        P("rows", None),
        P("rows"),
    )
    out_specs = (P("rows", None), P("rows", None), P("rows"), P("rows", None), P("rows", None))
    return jax.shard_map(local, mesh=mesh, in_specs=in_specs, out_specs=out_specs, check_vma=False)
```

profile of v0, /device:TPU:6, one launch (start us, length us, event | category | flops | bytes accessed | tf_op | source)
XLA Modules:
  0.0 541.9 jit_solution(1255831491882362884)
XLA Ops:
  7.2 1.1 convert_reduce_fusion.2
  8.2 0.7 multiply_add_fusion.3
  9.0 0.5 select_reduce_fusion
  9.5 0.7 sub.39
  10.2 20.1 %all-to-all-start = ((s32[128,1,16]{2,1,0:T(1,128)}), s32[128,1,16]{2,1,0:T(1,128)S(1)}, u32[]{:S(2)}, u32[]{:S(2)}) async-start(s32[128,1,16]{2,1,0:T(1,128)} %bitcast.1), calls=%async_computation | async-start | bytes 131072 | tf_op jit(solution)/shard_map/all_to_all | solution.py:120
  30.3 0.8 reduce-window.8
  31.1 0.1 convert_reduce_fusion.3
  31.2 1.2 fusion.21
  32.4 1.3 fusion.20
  33.7 0.2 copy.56
  33.9 0.1 convert_reduce_fusion
  34.1 0.2 fusion.14
  34.2 2.3 multiply_convert_fusion.1
  36.5 1.0 copy-done.4
  37.5 0.1 fusion.41
  37.6 0.1 copy.58
  37.7 0.1 copy.59
  37.9 0.1 copy.57
  38.0 4.8 multiply_convert_fusion
  42.8 1.3 copy-done.1
  44.2 0.8 fusion.42
  45.0 0.2 copy.60
  45.2 0.1 fusion.24
  45.3 1.4 multiply_reduce_fusion
  46.7 1.9 fusion.40
  48.6 0.8 broadcast_add_fusion
  49.5 1.1 copy.62
  50.6 2.9 fusion.45
  53.5 4.2 fusion.2
  57.7 1.5 fusion.44
  59.2 1.2 fusion.43
  60.4 1.0 copy.66
  61.4 0.1 copy.63
  61.6 1.1 copy.64
  62.6 0.8 copy.65
  63.5 2.5 fusion.6
  66.0 0.8 fusion.16
  66.8 0.2 copy-done.3
  67.0 0.3 fusion.27
  67.3 0.1 copy-done.14
  67.4 2.8 fusion.4
  70.2 16.7 %all-to-all-start.1 = ((bf16[128,16,512]{2,1,0:T(8,128)(2,1)}), bf16[128,16,512]{2,1,0:T(8,128)(2,1)}, u32[]{:S(2)}, u32[]{:S(2)}) async-start(bf16[128,16,512]{2,1,0:T(8,128)(2,1)} %bitcast.53), calls=%async_computation.1 | async-start | bytes 4194304 | tf_op jit(solution)/shard_map/all_to_all | solution.py:119
  86.9 0.0 all-reduce.7.cloned.1.call-start
  86.9 1.5 convolution_bitcast_fusion
  88.4 1.9 fusion.28
  90.4 1.7 pad_maximum_fusion
  92.1 0.0 all-reduce.7.cloned.1.call-update
  92.2 0.0 all-reduce.5.cloned.1.call-start
  92.2 1.3 dynamic-slice
  94.2 0.5 broadcast.185
  94.7 0.8 reduce.6
  95.5 0.1 eq.64
  95.6 0.2 convert_reduce_fusion.1
  95.8 95.0 %all-to-all-done.1 = bf16[128,16,512]{2,1,0:T(8,128)(2,1)} async-done(((bf16[128,16,512]{2,1,0:T(8,128)(2,1)}), bf16[128,16,512]{2,1,0:T(8,128)(2,1)}, u32[]{:S(2)}, u32[]{:S(2)}) %all-to-all-start.1) | async-done | bytes 2097184 | tf_op jit(solution)/shard_map/all_to_all | solution.py:119
  190.7 2.7 fusion.17
  193.5 281.2 %all-reduce.7.cloned.1.call-done = f32[512,1280]{1,0:T(8,128)} async-done(((f32[512,1280]{1,0:T(8,128)}), f32[512,1280]{1,0:T(8,128)}) %all-reduce.7.cloned.1.call-update) | async-done | bytes 2621456
  474.7 0.8 constant_dynamic-slice_fusion
  475.5 14.0 %all-reduce.1 = (f32[128]{0:T(128)S(1)}, f32[4,1280]{1,0:T(4,128)S(1)}) all-reduce(f32[128]{0:T(128)S(1)} %convert_reduce_fusion.1, f32[4,1280]{1,0:T(4,128)S(1)} %constant_dynamic-slice_fusion), channel_id=1, replica_groups=mesh['rows'=128,'dp'=4] {'dp'}, use_global_device_ids=true, to_apply=%region_3.4 | all-reduce | flops 5248 | bytes 41984 | tf_op jit(solution)/shard_map/psum | solution.py:128
  489.5 0.6 slice.8
  490.1 0.6 slice.9
  490.7 40.9 %all-reduce.5.cloned.1.call-done = f32[128,512]{1,0:T(8,128)} async-done(((f32[128,512]{1,0:T(8,128)}), f32[128,512]{1,0:T(8,128)}) %all-reduce.5.cloned.1.call-update) | async-done | bytes 262160 | tf_op jit(solution)/shard_map/psum | solution.py:128
  531.6 1.1 multiply_reduce_fusion.1
  532.7 0.5 fusion.39
  533.2 1.9 fusion.35
  (43 shorter events, 0.2 us)
Async XLA Ops:
  7.2 27.1 %copy-start = (bf16[512,1024]{1,0:T(8,128)(2,1)S(1)}, bf16[512,1024]{1,0:T(8,128)(2,1)}, u32[]{:S(2)}) copy-start(bf16[512,1024]{1,0:T(8,128)(2,1)} %param.15) | copy-start | bytes 3145732
  7.2 26.5 %copy-start.13 = (bf16[512,512]{1,0:T(8,128)(2,1)S(1)}, bf16[512,512]{1,0:T(8,128)(2,1)}, u32[]{:S(2)}) copy-start(bf16[512,512]{1,0:T(8,128)(2,1)} %param.10) | copy-start | bytes 1572868
  10.2 60.0 %all-to-all-start = ((s32[128,1,16]{2,1,0:T(1,128)}), s32[128,1,16]{2,1,0:T(1,128)S(1)}, u32[]{:S(2)}, u32[]{:S(2)}) async-start(s32[128,1,16]{2,1,0:T(1,128)} %bitcast.1), calls=%async_computation | async-start | bytes 131072 | tf_op jit(solution)/shard_map/all_to_all | solution.py:120
  36.5 1.0 copy-start.4
  37.9 5.0 copy-start.5
  38.0 4.8 copy-start.7
  42.8 1.3 copy-start.1
  44.2 1.1 copy-start.2
  48.6 4.9 copy-start.8
  50.6 2.9 copy-start.10
  50.6 2.9 copy-start.12
  53.5 4.2 copy-start.6
  59.2 2.2 copy-start.9
  60.4 2.3 copy-start.11
  66.0 1.0 copy-start.3
  66.0 1.4 copy-start.14
  70.2 120.5 %all-to-all-start.1 = ((bf16[128,16,512]{2,1,0:T(8,128)(2,1)}), bf16[128,16,512]{2,1,0:T(8,128)(2,1)}, u32[]{:S(2)}, u32[]{:S(2)}) async-start(bf16[128,16,512]{2,1,0:T(8,128)(2,1)} %bitcast.53), calls=%async_computation.1 | async-start | bytes 4194304 | tf_op jit(solution)/shard_map/all_to_all | solution.py:119
  86.9 387.8 %all-reduce.7.cloned.1.call-start = ((), (), s32[]{:S(2)}) async-start(), calls=%async_computation.3 | async-start | bytes 5242880
  92.1 440.5 %copy-start.17 = (f32[128]{0:T(128)S(1)}, f32[128]{0:T(128)}, u32[]{:S(2)}) copy-start(f32[128]{0:T(128)} %param.19) | copy-start | bytes 1540
  92.1 441.1 %copy-start.15 = (f32[128,512]{1,0:T(8,128)S(1)}, f32[128,512]{1,0:T(8,128)}, u32[]{:S(2)}) copy-start(f32[128,512]{1,0:T(8,128)} %param.18) | copy-start | bytes 786436
  92.1 441.1 %copy-start.16 = (f32[128,512]{1,0:T(8,128)S(1)}, f32[128,512]{1,0:T(8,128)}, u32[]{:S(2)}) copy-start(f32[128,512]{1,0:T(8,128)} %param.17) | copy-start | bytes 786436
  92.2 439.5 %all-reduce.5.cloned.1.call-start = ((), (), s32[]{:S(2)}) async-start(), calls=%async_computation.2 | async-start | bytes 524288 | tf_op jit(solution)/shard_map/psum | solution.py:128
Sparse Core Ops, SparseCore 0:
  92.2 382.4 all-reduce.6
  477.6 53.9 all-reduce.4
where the time goes:
time: 544 us; the launch traced here: 542 us
  waiting for transfers between devices  417 us (77%)
  starting transfers between devices  36.9 us (7%)
  matrix products  28.7 us (5%)
  other arithmetic  17.9 us (3%)
  between operations  15 us (3%)
  blocking collectives  14 us (3%)
  local copies, waits for them, and re-layouts  12.4 us (2%)
    unnamed x3, waiting for transfers between devices  281 us
    all_to_all x1, waiting for transfers between devices, local(): lax.all_to_all(outgoing, 'rows', split_axis=0, concat_axis=0, tiled=True)  95 us
    psum x1, waiting for transfers between devices, local(): grad_all, count_all = lax.psum((grad_part, count_part), 'dp')  40.9 us
    all_to_all x1, starting transfers between devices, local(): lax.all_to_all(out_slots, 'rows', split_axis=0, concat_axis=0, tiled=True)  20.1 us
    all_to_all x1, starting transfers between devices, local(): lax.all_to_all(outgoing, 'rows', split_axis=0, concat_axis=0, tiled=True)  16.7 us
    psum x1, blocking collectives, local(): grad_all, count_all = lax.psum((grad_part, count_part), 'dp')  14 us
  transfers between devices with their start and end apart: 4, of which 3 were waited for; matrix products, arithmetic and copies ran while one was open for 9% of the time, Pallas kernels for 0%

commit v1 on v0

--- a/solution.py
+++ b/solution.py
@@ -1,7 +1,9 @@
+import functools
+
 import jax
 import jax.numpy as jnp
 from jax import lax
-from jax.sharding import PartitionSpec as P
+from jax.sharding import Mesh, PartitionSpec as P
 
 HEADS = 4
 HEAD_DIM = 64
@@ -64,7 +66,23 @@
     )
 
 
-def local(tokens, out_grad, seq_lengths, owners, slots, w_in, w_out, emb_rows, emb_mom, emb_var):
+ROW_AXES = ("z", "y", "core")
+ALL_AXES = ("z", "y", "core", "x")
+
+
+def reduce_weights(partial, sizes):
+    width = partial.shape[1]
+    blocks = partial.reshape(tuple(sizes[a] for a in ROW_AXES) + (-1, width))
+    for i, ax in enumerate(ROW_AXES):
+        moved = jnp.moveaxis(blocks, i, 0)
+        rest = moved.shape[1:]
+        flat = moved.reshape(moved.shape[0], -1, 128)
+        flat = lax.psum_scatter(flat, ax, scatter_dimension=0, tiled=True)
+        blocks = jnp.moveaxis(flat.reshape((1,) + rest), 0, i)
+    return lax.psum(blocks.reshape(-1, width), "x")
+
+
+def local(sizes, tokens, out_grad, seq_lengths, owners, slots, w_in, w_out, emb_rows, emb_mom, emb_var):
     tok_count = tokens.shape[0]
     width = tokens.shape[1]
     allowed = allowed_mask(seq_lengths[0], tok_count)
@@ -80,8 +98,10 @@
     emb_grad = (norm_back(normed_grad)[0] + out_grad.astype(jnp.float32)).astype(jnp.bfloat16)
     contract = (((0,), (0,)), ((), ()))
     in_cols = w_in.shape[1]
-    owner_count = lax.axis_size("rows")
-    weight_share = lax.psum_scatter(
+    owner_count = 1
+    for a in ROW_AXES:
+        owner_count *= sizes[a]
+    weight_share = reduce_weights(
         jnp.concatenate(
             [
                 lax.dot_general(normed, pre_grad_b, contract, preferred_element_type=jnp.float32),
@@ -89,11 +109,8 @@
             ],
             axis=1,
         ),
-        "rows",
-        scatter_dimension=0,
-        tiled=True,
+        sizes,
     )
-    weight_share = lax.psum(weight_share, "dp")
     w_in_grad = weight_share[:, :in_cols]
     w_out_grad = weight_share[:, in_cols:]
     capacity = max(2, 4 * tok_count // owner_count)
@@ -115,33 +132,35 @@
     out_slots = (jnp.sum(jnp.where(chosen, slots[None, :] + 1, 0), axis=1) - 1).reshape(
         owner_count, capacity
     )
-    arrived, arrived_slots = (
-        lax.all_to_all(outgoing, "rows", split_axis=0, concat_axis=0, tiled=True),
-        lax.all_to_all(out_slots, "rows", split_axis=0, concat_axis=0, tiled=True),
+    slot_row = jnp.zeros((owner_count, 1, width), jnp.bfloat16)
+    slot_row = slot_row.at[:, 0, :capacity].set(out_slots.astype(jnp.bfloat16))
+    arrived = lax.all_to_all(
+        jnp.concatenate([outgoing, slot_row], axis=1), ROW_AXES, 0, 0, tiled=True
     )
-    received = arrived.reshape(buffer_rows, width)
-    got_slots = arrived_slots.reshape(buffer_rows)
+    received = arrived[:, :capacity, :].reshape(buffer_rows, width)
+    got_slots = arrived[:, capacity, :capacity].astype(jnp.int32).reshape(buffer_rows)
     slot_count = emb_rows.shape[0]
     matches = got_slots[None, :] == jnp.arange(slot_count, dtype=jnp.int32)[:, None]
     grad_part = jnp.dot(matches.astype(jnp.bfloat16), received, preferred_element_type=jnp.float32)
     count_part = jnp.sum(matches.astype(jnp.float32), axis=1)
-    grad_all, count_all = lax.psum((grad_part, count_part), "dp")
+    grad_all, count_all = lax.psum((grad_part, count_part), "x")
     new_rows, new_mom, new_var = row_adam(emb_rows, emb_mom, emb_var, grad_all, count_all)
     return (new_rows, new_mom, new_var, w_in_grad, w_out_grad)
 
 
 def solution(mesh):
-    in_specs = (
-        P(("rows", "dp"), None),
-        P(("rows", "dp"), None),
-        P(("rows", "dp"), None),
-        P(("rows", "dp"), None),
-        P(("rows", "dp")),
-        P(),
-        P(),
-        P("rows", None),
-        P("rows", None),
-        P("rows"),
+    n_rows, n_dp = mesh.shape["rows"], mesh.shape["dp"]
+    sizes = {"core": 2, "y": 4}
+    sizes["z"] = n_rows // (sizes["core"] * sizes["y"])
+    sizes["x"] = n_dp
+    fine = Mesh(
+        mesh.devices.reshape(sizes["z"], sizes["y"], sizes["core"], sizes["x"]), ALL_AXES
     )
-    out_specs = (P("rows", None), P("rows", None), P("rows"), P("rows", None), P("rows", None))
-    return jax.shard_map(local, mesh=mesh, in_specs=in_specs, out_specs=out_specs, check_vma=False)
+    tok = P(ALL_AXES, None)
+    own = P(ROW_AXES, None)
+    in_specs = (tok, tok, tok, tok, P(ALL_AXES), P(), P(), own, own, P(ROW_AXES))
+    out_specs = (own, own, P(ROW_AXES), own, own)
+    return jax.shard_map(
+        functools.partial(local, sizes), mesh=fine, in_specs=in_specs, out_specs=out_specs,
+        check_vma=False,
+    )

time: 544 us -> 366 us (0.67)
  waiting for transfers between devices: 417 us -> 250 us
  starting transfers between devices: 36.9 us -> 20.6 us
  local copies, waits for them, and re-layouts: 12.4 us -> 18.7 us
    unnamed x3 -> x5, waiting for transfers between devices: 281 us -> 20.4 us
    reduce_scatter x0 -> x2, waiting for transfers between devices: none -> 189 us  [reduce_weights(): flat = lax.psum_scatter(flat, ax, scatter_dimension=0, tiled=True)]
    all_to_all x2 -> x1, waiting for transfers between devices: 95 us -> 0.01 us  [local(): lax.all_to_all(jnp.concatenate([outgoing, slot_row], axis=1), ROW_AXES, 0...]
    all_to_all x2 -> x1, starting transfers between devices: 36.8 us -> 20.4 us  [local(): lax.all_to_all(jnp.concatenate([outgoing, slot_row], axis=1), ROW_AXES, 0...]
  transfers between devices with their start and end apart: 4 -> 5, of which waited for: 3 -> 4; matrix products, arithmetic and copies ran while one was open for 9% -> 3% of each run, Pallas kernels for 0% -> 0%
where the time goes in v1:
time: 366 us; the launch traced here: 364 us
  waiting for transfers between devices  250 us (68%)
  matrix products  26.2 us (7%)
  starting transfers between devices  20.6 us (6%)
  local copies, waits for them, and re-layouts  18.7 us (5%)
  other arithmetic  18 us (5%)
  between operations  15.5 us (4%)
  blocking collectives  14.4 us (4%)
    reduce_scatter x2, waiting for transfers between devices, reduce_weights(): flat = lax.psum_scatter(flat, ax, scatter_dimension=0, tiled=True)  189 us
    psum x1, waiting for transfers between devices, local(): grad_all, count_all = lax.psum((grad_part, count_part), 'x')  41.4 us
    unnamed x5, waiting for transfers between devices  20.4 us
    all_to_all x1, starting transfers between devices, local(): lax.all_to_all(jnp.concatenate([outgoing, slot_row], axis=1), ROW_AXES, 0...  20.4 us
    psum x1, blocking collectives, local(): grad_all, count_all = lax.psum((grad_part, count_part), 'x')  14.4 us
    dot_general x3, matrix products, core(): jnp.einsum('thd,shd->hts', queries, keys_part, preferred_element_type=jnp...  7.41 us
  transfers between devices with their start and end apart: 5, of which 4 were waited for; matrix products, arithmetic and copies ran while one was open for 3% of the time, Pallas kernels for 0%

profile of v1, /device:TPU:6, one launch (start us, length us, event | category | flops | bytes accessed | tf_op | source)
XLA Modules:
  0.0 363.8 jit_solution(11338276143965527013)
XLA Ops:
  8.0 0.9 reduce-window.8
  8.9 0.1 convert_reduce_fusion.3
  9.0 1.2 fusion.23
  10.2 1.2 fusion.22
  11.4 1.3 copy.69
  12.7 0.1 convert_reduce_fusion
  12.8 0.2 fusion.16
  13.0 2.3 multiply_convert_fusion.1
  15.3 0.9 fusion.44
  16.1 0.1 copy.71
  16.3 1.1 copy.72
  17.4 0.8 copy.70
  18.2 4.8 %multiply_convert_fusion = (bf16[4,512,512]{2,1,0:T(8,128)(2,1)S(1)}, f32[4,512,512]{2,1,0:T(8,128)}) fusion(f32[512,512]{1,0:T(8,128)} %fusion.23, bf16[512,4,64]{0,2,1:T(8,128)(2,1)S(1)} %bitcast.56, bf16[512,4,64]{0,2,1:T(8,128)(2,1)S(1)} %bitcast.58), kind=kOutput, calls=%fused_computation.7 | convolution fusion | flops 142606336 | bytes 7864320 | tf_op jit(solution)/shard_map/jvp(thd,shd->hts)/dot_general | solution.py:46
  23.0 1.3 copy-done.1
  24.3 0.8 fusion.45
  25.1 0.2 copy.73
  25.3 0.1 fusion.26
  25.4 1.4 multiply_reduce_fusion
  26.8 2.0 fusion.43
  28.8 0.1 broadcast_add_fusion
  29.0 0.9 copy.75
  29.8 2.2 fusion.48
  32.1 4.2 %fusion.3 = bf16[4,512,512]{2,1,0:T(8,128)(2,1)S(1)} fusion(f32[4,512,512]{2,1,0:T(8,128)} %get-tuple-element.34, f32[512,512]{1,0:T(8,128)S(1)} %copy-done.11, bf16[4,64,512]{2,1,0:T(8,128)(2,1)S(1)} %bitcast.64, bf16[512,4,64]{0,2,1:T(8,128)(2,1)S(1)} %bitcast.61), kind=kOutput, calls=%fused_computation.5 | convolution fusion | flops 148897792 | bytes 7864320 | tf_op jit(solution)/shard_map/transpose(jvp(hts,shd->thd))/dot_general | solution.py:50
  36.3 1.5 fusion.47
  37.8 1.2 fusion.46
  39.0 1.0 copy.79
  40.0 0.1 copy.76
  40.1 1.1 copy.77
  41.2 1.1 copy.78
  42.3 2.4 fusion.8
  44.8 0.8 fusion.18
  45.5 0.2 copy-done.3
  45.7 1.0 copy-done.10
  46.7 0.3 fusion.29
  47.0 0.2 convert_reduce_fusion.2
  47.3 0.5 select_reduce_fusion
  47.8 0.1 convert_element_type.136
  47.9 2.6 fusion.6
  50.5 2.0 fusion.5
  52.5 20.4 %all-to-all-start = ((bf16[128,17,512]{2,1,0:T(8,128)(2,1)}), bf16[128,17,512]{2,1,0:T(8,128)(2,1)}, u32[]{:S(2)}, u32[]{:S(2)}) async-start(bf16[128,17,512]{2,1,0:T(8,128)(2,1)} %fusion.5), calls=%async_computation | async-start | bytes 6291456 | tf_op jit(solution)/shard_map/all_to_all | solution.py:137
  73.0 0.0 reduce-scatter.7.cloned.1.call-start
  73.0 1.5 convolution_bitcast_fusion
  74.5 1.9 fusion.30
  76.4 1.8 pad_maximum_fusion
  78.2 3.6 reshape_reshape.3
  81.9 0.0 reduce-scatter.9.cloned.1.call-start
  81.9 155.0 %reduce-scatter.7.cloned.1.call-done = f32[1,320,128]{2,1,0:T(8,128)} async-done(((f32[16,320,128]{2,1,0:T(8,128)}), f32[1,320,128]{2,1,0:T(8,128)}) %reduce-scatter.7.cloned.1.call-update) | async-done | bytes 163856 | tf_op jit(solution)/shard_map/reduce_scatter | solution.py:80
  236.9 0.0 reduce-scatter.11.cloned.1.call-start
  237.0 33.5 %reduce-scatter.9.cloned.1.call-done = f32[1,80,128]{2,1,0:T(8,128)} async-done(((f32[4,80,128]{2,1,0:T(8,128)}), f32[1,80,128]{2,1,0:T(8,128)}) %reduce-scatter.9.cloned.1.call-update) | async-done | bytes 40976 | tf_op jit(solution)/shard_map/reduce_scatter | solution.py:80
  270.5 0.0 all-reduce.5.cloned.1.call-start
  270.6 20.4 %reduce-scatter.11.cloned.1.call-done = f32[1,40,128]{2,1,0:T(8,128)} async-done(((f32[2,40,128]{2,1,0:T(8,128)}), f32[1,40,128]{2,1,0:T(8,128)}) %reduce-scatter.11.cloned.1.call-update) | async-done | bytes 20496
  290.9 0.7 reshape_transpose_reshape.7
  291.7 1.2 fusion.39
  292.8 0.1 reshape.241
  292.9 1.8 slice.40
  294.8 1.2 fusion.19
  296.0 0.2 convert_reduce_fusion.1
  296.2 14.4 %all-reduce.2 = (f32[128]{0:T(128)S(1)}, f32[4,1280]{1,0:T(4,128)S(1)}) all-reduce(f32[128]{0:T(128)S(1)} %convert_reduce_fusion.1, f32[4,1280]{1,0:T(4,128)S(1)} %reshape_transpose_reshape.7), channel_id=1, replica_groups=mesh['z'=16,'y'=4,'core'=2,'x'=4] {'x'}, use_global_device_ids=true, to_apply=%region_13.14 | all-reduce | flops 5248 | bytes 41984 | tf_op jit(solution)/shard_map/psum | solution.py:146
  310.5 0.6 slice.41
  311.1 0.6 slice.42
  311.7 41.4 %all-reduce.5.cloned.1.call-done = f32[128,512]{1,0:T(8,128)} async-done(((f32[128,512]{1,0:T(8,128)}), f32[128,512]{1,0:T(8,128)}) %all-reduce.5.cloned.1.call-update) | async-done | bytes 262160 | tf_op jit(solution)/shard_map/psum | solution.py:146
  353.2 1.1 multiply_reduce_fusion.1
  354.2 0.5 fusion.42
  354.8 1.9 fusion.37
  (48 shorter events, 0.2 us)
Async XLA Ops:
  8.0 5.0 %copy-start = (bf16[512,1024]{1,0:T(8,128)(2,1)S(1)}, bf16[512,1024]{1,0:T(8,128)(2,1)}, u32[]{:S(2)}) copy-start(bf16[512,1024]{1,0:T(8,128)(2,1)} %param.17) | copy-start | bytes 3145732
  15.3 3.0 copy-start.4
  17.4 5.6 %copy-start.5 = (bf16[512,256]{0,1:T(8,128)(2,1)}, bf16[512,256]{0,1:T(8,128)(2,1)S(1)}, u32[]{:S(2)}) copy-start(bf16[512,256]{0,1:T(8,128)(2,1)S(1)} %copy.72) | copy-start | bytes 786436
  18.2 6.1 %copy-start.7 = (bf16[512,256]{0,1:T(8,128)(2,1)S(1)}, bf16[512,256]{0,1:T(8,128)(2,1)}, u32[]{:S(2)}) copy-start(bf16[512,256]{0,1:T(8,128)(2,1)} %copy.70) | copy-start | bytes 786436
  23.0 1.3 copy-start.1
  23.0 2.4 copy-start.2
  26.8 5.2 %copy-start.8 = (bf16[512,256]{0,1:T(8,128)(2,1)S(1)}, bf16[512,256]{0,1:T(8,128)(2,1)}, u32[]{:S(2)}) copy-start(bf16[512,256]{0,1:T(8,128)(2,1)} %copy.70) | copy-start | bytes 786436
  29.8 2.3 copy-start.9
  29.8 2.3 copy-start.11
  32.1 4.2 %copy-start.6 = (bf16[512,256]{0,1:T(8,128)(2,1)S(1)}, bf16[512,256]{0,1:T(8,128)(2,1)}, u32[]{:S(2)}) copy-start(bf16[512,256]{0,1:T(8,128)(2,1)} %copy-done.5) | copy-start | bytes 786436
  44.7 1.0 copy-start.3
  44.7 2.2 copy-start.15
  44.7 2.5 copy-start.16
  44.8 3.1 copy-start.12
  45.7 1.0 copy-start.10
  52.5 239.1 %all-to-all-start = ((bf16[128,17,512]{2,1,0:T(8,128)(2,1)}), bf16[128,17,512]{2,1,0:T(8,128)(2,1)}, u32[]{:S(2)}, u32[]{:S(2)}) async-start(bf16[128,17,512]{2,1,0:T(8,128)(2,1)} %fusion.5), calls=%async_computation | async-start | bytes 6291456 | tf_op jit(solution)/shard_map/all_to_all | solution.py:137
  73.0 163.9 %reduce-scatter.7.cloned.1.call-start = ((), (), s32[]{:S(2)}) async-start(), calls=%async_computation.5 | async-start | bytes 2785280 | tf_op jit(solution)/shard_map/reduce_scatter | solution.py:80
  81.9 188.6 %reduce-scatter.9.cloned.1.call-start = ((), (), s32[]{:S(2)}) async-start(), calls=%async_computation.6 | async-start | bytes 204800 | tf_op jit(solution)/shard_map/reduce_scatter | solution.py:80
  236.9 54.0 %reduce-scatter.11.cloned.1.call-start = ((), (), s32[]{:S(2)}) async-start(), calls=%async_computation.7 | async-start | bytes 61440
  270.5 82.7 %all-reduce.5.cloned.1.call-start = ((), (), s32[]{:S(2)}) async-start(), calls=%async_computation.4 | async-start | bytes 524288 | tf_op jit(solution)/shard_map/psum | solution.py:146
  292.9 61.3 %copy-start.17 = (f32[128]{0:T(128)S(1)}, f32[128]{0:T(128)}, u32[]{:S(2)}) copy-start(f32[128]{0:T(128)} %param.21) | copy-start | bytes 1540
  292.9 61.8 %copy-start.13 = (f32[128,512]{1,0:T(8,128)S(1)}, f32[128,512]{1,0:T(8,128)}, u32[]{:S(2)}) copy-start(f32[128,512]{1,0:T(8,128)} %param.20) | copy-start | bytes 786436
  292.9 61.8 %copy-start.14 = (f32[128,512]{1,0:T(8,128)S(1)}, f32[128,512]{1,0:T(8,128)}, u32[]{:S(2)}) copy-start(f32[128,512]{1,0:T(8,128)} %param.19) | copy-start | bytes 786436
Sparse Core Ops, SparseCore 0:
  82.0 154.8 reduce-scatter.6
  239.9 30.5 reduce-scatter.8
  273.2 17.6 reduce-scatter.10
Sparse Core Ops, SparseCore 1:
  296.1 57.1 all-reduce.4

commit v2 on v1

--- a/solution.py
+++ b/solution.py
@@ -70,16 +70,46 @@
 ALL_AXES = ("z", "y", "core", "x")
 
 
+def shifted(value, axis, size, step):
+    return lax.ppermute(value, axis, [(i, (i + step) % size) for i in range(size)])
+
+
+def scatter_sum(blocks, axis, size, dim):
+    me = lax.axis_index(axis)
+    total = lax.dynamic_index_in_dim(blocks, me, dim, keepdims=False)
+    for step in range(1, size):
+        piece = lax.dynamic_index_in_dim(blocks, (me + step) % size, dim, keepdims=False)
+        total = total + shifted(piece, axis, size, step)
+    return total
+
+
+def gather_rows(row, axis, size):
+    me = lax.axis_index(axis)
+    pieces = [row]
+    for step in range(1, size):
+        pieces.append(shifted(row, axis, size, step))
+    stacked = jnp.stack(pieces)
+    order = (me - jnp.arange(size)) % size
+    return jnp.zeros_like(stacked).at[order].set(stacked)
+
+
 def reduce_weights(partial, sizes):
     width = partial.shape[1]
-    blocks = partial.reshape(tuple(sizes[a] for a in ROW_AXES) + (-1, width))
-    for i, ax in enumerate(ROW_AXES):
-        moved = jnp.moveaxis(blocks, i, 0)
-        rest = moved.shape[1:]
-        flat = moved.reshape(moved.shape[0], -1, 128)
-        flat = lax.psum_scatter(flat, ax, scatter_dimension=0, tiled=True)
-        blocks = jnp.moveaxis(flat.reshape((1,) + rest), 0, i)
-    return lax.psum(blocks.reshape(-1, width), "x")
+    per_owner = partial.shape[0] // (sizes["z"] * sizes["y"] * sizes["core"])
+    blocks = partial.reshape(sizes["z"], sizes["y"], sizes["core"], per_owner, width)
+    blocks = scatter_sum(blocks, "core", sizes["core"], 2)
+    blocks = blocks.reshape(sizes["z"], sizes["y"], sizes["x"], per_owner // sizes["x"], width)
+    blocks = scatter_sum(blocks, "x", sizes["x"], 2)
+    blocks = scatter_sum(blocks, "y", sizes["y"], 1)
+    blocks = scatter_sum(blocks, "z", sizes["z"], 0)
+    return gather_rows(blocks, "x", sizes["x"]).reshape(per_owner, width)
+
+
+def sum_over(value, axis, size):
+    total = value
+    for step in range(1, size):
+        total = total + shifted(value, axis, size, step)
+    return total
 
 
 def local(sizes, tokens, out_grad, seq_lengths, owners, slots, w_in, w_out, emb_rows, emb_mom, emb_var):
@@ -143,7 +173,12 @@
     matches = got_slots[None, :] == jnp.arange(slot_count, dtype=jnp.int32)[:, None]
     grad_part = jnp.dot(matches.astype(jnp.bfloat16), received, preferred_element_type=jnp.float32)
     count_part = jnp.sum(matches.astype(jnp.float32), axis=1)
-    grad_all, count_all = lax.psum((grad_part, count_part), "x")
+    both = sum_over(
+        jnp.concatenate([grad_part, jnp.broadcast_to(count_part[:, None], (slot_count, 128))], axis=1),
+        "x",
+        sizes["x"],
+    )
+    grad_all, count_all = both[:, :width], both[:, width]
     new_rows, new_mom, new_var = row_adam(emb_rows, emb_mom, emb_var, grad_all, count_all)
     return (new_rows, new_mom, new_var, w_in_grad, w_out_grad)
 

time: 366 us -> 294 us (0.80)
  waiting for transfers between devices: 250 us -> 83.9 us
  starting transfers between devices: 20.6 us -> 139 us
  blocking collectives: 14.4 us -> 0 us
  between operations: 15.5 us -> 1.72 us
    reduce_scatter x2 -> x0, waiting for transfers between devices: 189 us -> none  [reduce_weights(): flat = lax.psum_scatter(flat, ax, scatter_dimension=0, tiled=True)]
    ppermute x0 -> x28, starting transfers between devices: none -> 119 us  [shifted(): lax.ppermute(value, axis, [(i, (i + step) % size) for i in range(size)])]
    all_to_all x1, waiting for transfers between devices: 0.01 us -> 60.7 us  [local(): lax.all_to_all(jnp.concatenate([outgoing, slot_row], axis=1), ROW_AXES, 0...]
    psum x1 -> x0, waiting for transfers between devices: 41.4 us -> none  [local(): grad_all, count_all = lax.psum((grad_part, count_part), 'x')]
    ppermute x0 -> x28, waiting for transfers between devices: none -> 23.2 us  [shifted(): lax.ppermute(value, axis, [(i, (i + step) % size) for i in range(size)])]
    unnamed x5 -> x0, waiting for transfers between devices: 20.4 us -> none
    psum x1 -> x0, blocking collectives: 14.4 us -> none  [local(): grad_all, count_all = lax.psum((grad_part, count_part), 'x')]
    another operation x2 -> x0, local copies, waits for them, and re-layouts: 4.37 us -> none  [the longest x1 3.63 us: reduce_weights(): flat = moved.reshape(moved.shape[0], -1, 128)]
  transfers between devices with their start and end apart: 5 -> 29, of which waited for: 4 -> 9; matrix products, arithmetic and copies ran while one was open for 3% -> 8% of each run, Pallas kernels for 0% -> 0%
where the time goes in v2:
time: 294 us; the launch traced here: 291 us
  starting transfers between devices  139 us (47%)
  waiting for transfers between devices  83.9 us (29%)
  matrix products  24.8 us (8%)
  local copies, waits for them, and re-layouts  20.9 us (7%)
  other arithmetic  20.5 us (7%)
    ppermute x28, starting transfers between devices, shifted(): lax.ppermute(value, axis, [(i, (i + step) % size) for i in range(size)])  119 us
    all_to_all x1, waiting for transfers between devices, local(): lax.all_to_all(jnp.concatenate([outgoing, slot_row], axis=1), ROW_AXES, 0...  60.7 us
    ppermute x28, waiting for transfers between devices, shifted(): lax.ppermute(value, axis, [(i, (i + step) % size) for i in range(size)])  23.2 us
    all_to_all x1, starting transfers between devices, local(): lax.all_to_all(jnp.concatenate([outgoing, slot_row], axis=1), ROW_AXES, 0...  20.4 us
    dot_general x3, matrix products, core(): jnp.einsum('hts,shd->thd', weights, values_part, preferred_element_type=j...  7.52 us
    dot_general x3, matrix products, core(): jnp.einsum('thd,shd->hts', queries, keys_part, preferred_element_type=jnp...  6.16 us
  transfers between devices with their start and end apart: 29, of which 9 were waited for; matrix products, arithmetic and copies ran while one was open for 8% of the time, Pallas kernels for 0%

profile of v2, /device:TPU:6, one launch (start us, length us, event | category | flops | bytes accessed | tf_op | source)
XLA Modules:
  0.0 291.2 jit_solution(6084936698408695383)
XLA Ops:
  1.9 1.2 fusion.22
  3.6 2.3 multiply_convert_fusion.1
  5.9 1.1 copy-done.4
  8.0 1.2 copy.57
  9.2 3.5 %multiply_convert_fusion = (bf16[4,512,512]{2,1,0:T(8,128)(2,1)S(1)}, f32[4,512,512]{2,1,0:T(8,128)}) fusion(f32[512,512]{1,0:T(8,128)S(1)} %fusion.23, bf16[512,4,64]{0,2,1:T(8,128)(2,1)S(1)} %bitcast.118, bf16[512,4,64]{0,2,1:T(8,128)(2,1)S(1)} %bitcast.120), kind=kOutput, calls=%fused_computation.8 | convolution fusion | flops 142606336 | bytes 7864320 | tf_op jit(solution)/shard_map/jvp(thd,shd->hts)/dot_general | solution.py:46
  12.7 1.3 copy-done.1
  15.1 1.4 multiply_reduce_fusion
  16.6 1.9 fusion.75
  19.3 1.1 copy.62
  20.5 2.2 fusion.80
  22.7 4.6 %fusion.3 = bf16[4,512,512]{2,1,0:T(8,128)(2,1)S(1)} fusion(f32[4,512,512]{2,1,0:T(8,128)} %get-tuple-element.53, f32[512,512]{1,0:T(8,128)S(1)} %copy-done.11, bf16[4,64,512]{2,1,0:T(8,128)(2,1)} %bitcast.126, bf16[512,4,64]{0,2,1:T(8,128)(2,1)} %bitcast.123), kind=kOutput, calls=%fused_computation.6 | convolution fusion | flops 148897792 | bytes 7864320 | tf_op jit(solution)/shard_map/transpose(jvp(hts,shd->thd))/dot_general | solution.py:50
  27.3 1.5 fusion.79
  28.7 1.2 fusion.78
  31.1 1.1 copy.64
  33.0 2.5 fusion.8
  38.7 2.8 fusion.6
  41.5 2.0 fusion.5
  43.5 20.4 %all-to-all-start = ((bf16[128,17,512]{2,1,0:T(8,128)(2,1)}), bf16[128,17,512]{2,1,0:T(8,128)(2,1)}, u32[]{:S(2)}, u32[]{:S(2)}) async-start(bf16[128,17,512]{2,1,0:T(8,128)(2,1)} %fusion.5), calls=%async_computation | async-start | bytes 6291456 | tf_op jit(solution)/shard_map/all_to_all | solution.py:167
  64.0 1.5 convolution_bitcast_fusion
  65.4 1.9 fusion.30
  67.4 1.7 pad_maximum_fusion
  69.1 3.9 %reshape.307 = f32[16,4,2,4,1280]{4,3,2,1,0:T(4,128)} reshape(f32[512,1280]{1,0:T(8,128)} %pad_maximum_fusion) | data formatting | bytes 5242880 | tf_op jit(solution)/shard_map/reshape | solution.py:99
  73.0 1.4 dynamic-slice_bitcast_fusion
  74.4 1.9 collective-permute-start.3
  76.4 3.1 %collective-permute-done.3 = f32[16,4,4,1280]{3,2,1,0:T(4,128)} collective-permute-done((f32[16,4,4,1280]{3,2,1,0:T(4,128)S(1)}, f32[16,4,4,1280]{3,2,1,0:T(4,128)}, u32[]{:S(2)}, u32[]{:S(2)}) %collective-permute-start.3) | collective-permute-done | bytes 1310752 | tf_op jit(solution)/shard_map/ppermute | solution.py:74
  79.5 2.1 bitcast_add_fusion
  81.5 1.7 constant_dynamic-slice_fusion.18
  83.2 2.4 collective-permute-start.4
  85.6 4.3 %collective-permute-start.5 = (f32[16,4,1,1280]{3,2,1,0:T(1,128)S(1)}, f32[16,4,1,1280]{3,2,1,0:T(1,128)}, u32[]{:S(2)}, u32[]{:S(2)}) collective-permute-start(f32[16,4,1,1280]{3,2,1,0:T(1,128)S(1)} %get-tuple-element.21), channel_id=1, source_target_pairs={{0,2},{1,3},{2,0},{3,1},{4,6},{5,7},{6,4},{7,5},{8,10},{9,11},{10,... | collective-permute-start | bytes 983048 | tf_op jit(solution)/shard_map/ppermute | solution.py:74
  90.0 1.9 collective-permute-start.6
  91.9 3.9 %collective-permute-done.4 = f32[16,4,1,1280]{3,2,1,0:T(1,128)S(1)} collective-permute-done((f32[16,4,1,1280]{3,2,1,0:T(1,128)}, f32[16,4,1,1280]{3,2,1,0:T(1,128)S(1)}, u32[]{:S(2)}, u32[]{:S(2)}) %collective-permute-start.4) | collective-permute-done | bytes 327712 | tf_op jit(solution)/shard_map/ppermute | solution.py:74
  95.9 3.9 %collective-permute-done.5 = f32[16,4,1,1280]{3,2,1,0:T(1,128)} collective-permute-done((f32[16,4,1,1280]{3,2,1,0:T(1,128)S(1)}, f32[16,4,1,1280]{3,2,1,0:T(1,128)}, u32[]{:S(2)}, u32[]{:S(2)}) %collective-permute-start.5) | collective-permute-done | bytes 327712 | tf_op jit(solution)/shard_map/ppermute | solution.py:74
  99.8 5.9 %collective-permute-done.6 = f32[16,4,1,1280]{3,2,1,0:T(1,128)} collective-permute-done((f32[16,4,1,1280]{3,2,1,0:T(1,128)S(1)}, f32[16,4,1,1280]{3,2,1,0:T(1,128)}, u32[]{:S(2)}, u32[]{:S(2)}) %collective-permute-start.6) | collective-permute-done | bytes 327712 | tf_op jit(solution)/shard_map/ppermute | solution.py:74
  105.6 1.7 add_add_fusion.3
  107.4 3.0 %collective-permute-start.7 = (f32[16,1,1280]{2,1,0:T(1,128)S(1)}, f32[16,1,1280]{2,1,0:T(1,128)S(1)}, u32[]{:S(2)}, u32[]{:S(2)}) collective-permute-start(f32[16,1,1280]{2,1,0:T(1,128)S(1)} %get-tuple-element.28), channel_id=1, source_target_pairs={{0,8},{8,16},{16,24},{24,0},{1,9},{9,17},{17,25},{25,1},{2,10},{10... | collective-permute-start | bytes 245768 | tf_op jit(solution)/shard_map/ppermute | solution.py:74
  110.4 4.6 %collective-permute-start.8 = (f32[16,1,1280]{2,1,0:T(1,128)S(1)}, f32[16,1,1280]{2,1,0:T(1,128)S(1)}, u32[]{:S(2)}, u32[]{:S(2)}) collective-permute-start(f32[16,1,1280]{2,1,0:T(1,128)S(1)} %get-tuple-element.30), channel_id=1, source_target_pairs={{0,16},{8,24},{16,0},{24,8},{1,17},{9,25},{17,1},{25,9},{2,18},{10... | collective-permute-start | bytes 245768 | tf_op jit(solution)/shard_map/ppermute | solution.py:74
  115.0 3.4 %collective-permute-start.9 = (f32[16,1,1280]{2,1,0:T(1,128)S(1)}, f32[16,1,1280]{2,1,0:T(1,128)S(1)}, u32[]{:S(2)}, u32[]{:S(2)}) collective-permute-start(f32[16,1,1280]{2,1,0:T(1,128)S(1)} %get-tuple-element.29), channel_id=1, source_target_pairs={{0,24},{8,0},{16,8},{24,16},{1,25},{9,1},{17,9},{25,17},{2,26},{10... | collective-permute-start | bytes 245768 | tf_op jit(solution)/shard_map/ppermute | solution.py:74
  119.1 2.5 collective-permute-done.9
  121.8 3.2 %collective-permute-start.10 = (f32[1,1280]{1,0:T(1,128)S(1)}, f32[1,1280]{1,0:T(1,128)S(1)}, u32[]{:S(2)}, u32[]{:S(2)}) collective-permute-start(f32[1,1280]{1,0:T(1,128)S(1)} %get-tuple-element.31), channel_id=1, source_target_pairs={{0,32},{32,64},{64,96},{96,128},{128,160},{160,192},{192,224},{224... | collective-permute-start | bytes 15368 | tf_op jit(solution)/shard_map/ppermute | solution.py:74
  125.0 4.5 %collective-permute-start.11 = (f32[1,1280]{1,0:T(1,128)S(1)}, f32[1,1280]{1,0:T(1,128)S(1)}, u32[]{:S(2)}, u32[]{:S(2)}) collective-permute-start(f32[1,1280]{1,0:T(1,128)S(1)} %get-tuple-element.45), channel_id=1, source_target_pairs={{0,64},{32,96},{64,128},{96,160},{128,192},{160,224},{192,256},{22... | collective-permute-start | bytes 15368 | tf_op jit(solution)/shard_map/ppermute | solution.py:74
  129.5 6.9 %collective-permute-start.12 = (f32[1,1280]{1,0:T(1,128)S(1)}, f32[1,1280]{1,0:T(1,128)S(1)}, u32[]{:S(2)}, u32[]{:S(2)}) collective-permute-start(f32[1,1280]{1,0:T(1,128)S(1)} %get-tuple-element.44), channel_id=1, source_target_pairs={{0,96},{32,128},{64,160},{96,192},{128,224},{160,256},{192,288},{2... | collective-permute-start | bytes 15368 | tf_op jit(solution)/shard_map/ppermute | solution.py:74
  136.4 5.3 %collective-permute-start.13 = (f32[1,1280]{1,0:T(1,128)S(1)}, f32[1,1280]{1,0:T(1,128)S(1)}, u32[]{:S(2)}, u32[]{:S(2)}) collective-permute-start(f32[1,1280]{1,0:T(1,128)S(1)} %get-tuple-element.43), channel_id=1, source_target_pairs={{0,128},{32,160},{64,192},{96,224},{128,256},{160,288},{192,320},{... | collective-permute-start | bytes 15368 | tf_op jit(solution)/shard_map/ppermute | solution.py:74
  141.8 3.8 %collective-permute-start.14 = (f32[1,1280]{1,0:T(1,128)S(1)}, f32[1,1280]{1,0:T(1,128)S(1)}, u32[]{:S(2)}, u32[]{:S(2)}) collective-permute-start(f32[1,1280]{1,0:T(1,128)S(1)} %get-tuple-element.42), channel_id=1, source_target_pairs={{0,160},{32,192},{64,224},{96,256},{128,288},{160,320},{192,352},{... | collective-permute-start | bytes 15368 | tf_op jit(solution)/shard_map/ppermute | solution.py:74
  145.6 60.7 %all-to-all-done = bf16[128,17,512]{2,1,0:T(8,128)(2,1)} async-done(((bf16[128,17,512]{2,1,0:T(8,128)(2,1)}), bf16[128,17,512]{2,1,0:T(8,128)(2,1)}, u32[]{:S(2)}, u32[]{:S(2)}) %all-to-all-start) | async-done | bytes 2228256 | tf_op jit(solution)/shard_map/all_to_all | solution.py:167
  206.2 1.2 fusion.41
  207.5 1.8 slice.48
  209.8 4.4 %collective-permute-start.15 = (f32[1,1280]{1,0:T(1,128)S(1)}, f32[1,1280]{1,0:T(1,128)S(1)}, u32[]{:S(2)}, u32[]{:S(2)}) collective-permute-start(f32[1,1280]{1,0:T(1,128)S(1)} %get-tuple-element.41), channel_id=1, source_target_pairs={{0,192},{32,224},{64,256},{96,288},{128,320},{160,352},{192,384},{... | collective-permute-start | bytes 15368 | tf_op jit(solution)/shard_map/ppermute | solution.py:74
  214.2 10.5 %collective-permute-start.16 = (f32[1,1280]{1,0:T(1,128)S(1)}, f32[1,1280]{1,0:T(1,128)S(1)}, u32[]{:S(2)}, u32[]{:S(2)}) collective-permute-start(f32[1,1280]{1,0:T(1,128)S(1)} %get-tuple-element.40), channel_id=1, source_target_pairs={{0,224},{32,256},{64,288},{96,320},{128,352},{160,384},{192,416},{... | collective-permute-start | bytes 15368 | tf_op jit(solution)/shard_map/ppermute | solution.py:74
  224.7 5.0 %collective-permute-start.17 = (f32[1,1280]{1,0:T(1,128)S(1)}, f32[1,1280]{1,0:T(1,128)S(1)}, u32[]{:S(2)}, u32[]{:S(2)}) collective-permute-start(f32[1,1280]{1,0:T(1,128)S(1)} %get-tuple-element.39), channel_id=1, source_target_pairs={{0,256},{32,288},{64,320},{96,352},{128,384},{160,416},{192,448},{... | collective-permute-start | bytes 15368 | tf_op jit(solution)/shard_map/ppermute | solution.py:74
  229.7 9.5 %collective-permute-start.18 = (f32[1,1280]{1,0:T(1,128)S(1)}, f32[1,1280]{1,0:T(1,128)S(1)}, u32[]{:S(2)}, u32[]{:S(2)}) collective-permute-start(f32[1,1280]{1,0:T(1,128)S(1)} %get-tuple-element.38), channel_id=1, source_target_pairs={{0,288},{32,320},{64,352},{96,384},{128,416},{160,448},{192,480},{... | collective-permute-start | bytes 15368 | tf_op jit(solution)/shard_map/ppermute | solution.py:74
  239.2 5.2 %collective-permute-start.19 = (f32[1,1280]{1,0:T(1,128)S(1)}, f32[1,1280]{1,0:T(1,128)S(1)}, u32[]{:S(2)}, u32[]{:S(2)}) collective-permute-start(f32[1,1280]{1,0:T(1,128)S(1)} %get-tuple-element.37), channel_id=1, source_target_pairs={{0,320},{32,352},{64,384},{96,416},{128,448},{160,480},{192,0},{22... | collective-permute-start | bytes 15368 | tf_op jit(solution)/shard_map/ppermute | solution.py:74
  244.6 4.0 %collective-permute-start.20 = (f32[1,1280]{1,0:T(1,128)S(1)}, f32[1,1280]{1,0:T(1,128)S(1)}, u32[]{:S(2)}, u32[]{:S(2)}) collective-permute-start(f32[1,1280]{1,0:T(1,128)S(1)} %get-tuple-element.36), channel_id=1, source_target_pairs={{0,352},{32,384},{64,416},{96,448},{128,480},{160,0},{192,32},{224... | collective-permute-start | bytes 15368 | tf_op jit(solution)/shard_map/ppermute | solution.py:74
  248.7 6.9 %collective-permute-start.21 = (f32[1,1280]{1,0:T(1,128)S(1)}, f32[1,1280]{1,0:T(1,128)S(1)}, u32[]{:S(2)}, u32[]{:S(2)}) collective-permute-start(f32[1,1280]{1,0:T(1,128)S(1)} %get-tuple-element.35), channel_id=1, source_target_pairs={{0,384},{32,416},{64,448},{96,480},{128,0},{160,32},{192,64},{224,... | collective-permute-start | bytes 15368 | tf_op jit(solution)/shard_map/ppermute | solution.py:74
  255.5 4.4 %collective-permute-start.22 = (f32[1,1280]{1,0:T(1,128)S(1)}, f32[1,1280]{1,0:T(1,128)S(1)}, u32[]{:S(2)}, u32[]{:S(2)}) collective-permute-start(f32[1,1280]{1,0:T(1,128)S(1)} %get-tuple-element.34), channel_id=1, source_target_pairs={{0,416},{32,448},{64,480},{96,0},{128,32},{160,64},{192,96},{224,1... | collective-permute-start | bytes 15368 | tf_op jit(solution)/shard_map/ppermute | solution.py:74
  259.9 1.9 collective-permute-start.23
  261.9 2.9 %collective-permute-start.24 = (f32[1,1280]{1,0:T(1,128)S(1)}, f32[1,1280]{1,0:T(1,128)S(1)}, u32[]{:S(2)}, u32[]{:S(2)}) collective-permute-start(f32[1,1280]{1,0:T(1,128)S(1)} %get-tuple-element.32), channel_id=1, source_target_pairs={{0,480},{32,0},{64,32},{96,64},{128,96},{160,128},{192,160},{224,1... | collective-permute-start | bytes 15368 | tf_op jit(solution)/shard_map/ppermute | solution.py:74
  264.9 2.4 collective-permute-start
  267.4 4.3 %collective-permute-start.1 = (f32[128,640]{1,0:T(8,128)S(1)}, f32[128,640]{1,0:T(8,128)S(1)}, u32[]{:S(2)}, u32[]{:S(2)}) collective-permute-start(f32[128,640]{1,0:T(8,128)S(1)} %pad_maximum_fusion.1), channel_id=1, source_target_pairs={{0,2},{1,3},{2,0},{3,1},{4,6},{5,7},{6,4},{7,5},{8,10},{9,11},{10,... | collective-permute-start | bytes 983048 | tf_op jit(solution)/shard_map/ppermute | solution.py:74
  271.7 1.9 collective-permute-start.2
  273.7 5.1 %collective-permute-start.25 = (f32[1,1280]{1,0:T(1,128)S(1)}, f32[1,1280]{1,0:T(1,128)S(1)}, u32[]{:S(2)}, u32[]{:S(2)}) collective-permute-start(f32[1,1280]{1,0:T(1,128)S(1)} %add_add_fusion.5), channel_id=1, source_target_pairs={{0,1},{1,2},{2,3},{3,0},{4,5},{5,6},{6,7},{7,4},{8,9},{9,10},{10,1... | collective-permute-start | bytes 15368 | tf_op jit(solution)/shard_map/ppermute | solution.py:74
  278.8 1.9 collective-permute-start.26
  280.8 3.3 %collective-permute-start.27 = (f32[1,1280]{1,0:T(1,128)S(1)}, f32[1,1280]{1,0:T(1,128)S(1)}, u32[]{:S(2)}, u32[]{:S(2)}) collective-permute-start(f32[1,1280]{1,0:T(1,128)S(1)} %add_add_fusion.5), channel_id=1, source_target_pairs={{0,3},{1,0},{2,1},{3,2},{4,7},{5,4},{6,5},{7,6},{8,11},{9,8},{10,9... | collective-permute-start | bytes 15368 | tf_op jit(solution)/shard_map/ppermute | solution.py:74
  284.1 1.7 collective-permute-done.26
  285.9 1.7 collective-permute-done.27
  (105 shorter events, 15.1 us)
Async XLA Ops:
  0.6 2.9 %copy-start = (bf16[512,1024]{1,0:T(8,128)(2,1)S(1)}, bf16[512,1024]{1,0:T(8,128)(2,1)}, u32[]{:S(2)}) copy-start(bf16[512,1024]{1,0:T(8,128)(2,1)} %param.17) | copy-start | bytes 3145732
  0.6 2.4 copy-start.12
  5.8 1.1 copy-start.4
  8.0 4.7 %copy-start.5 = (bf16[512,256]{0,1:T(8,128)(2,1)}, bf16[512,256]{0,1:T(8,128)(2,1)S(1)}, u32[]{:S(2)}) copy-start(bf16[512,256]{0,1:T(8,128)(2,1)S(1)} %copy.59) | copy-start | bytes 786436
  9.2 3.5 %copy-start.7 = (bf16[512,256]{0,1:T(8,128)(2,1)}, bf16[512,256]{0,1:T(8,128)(2,1)S(1)}, u32[]{:S(2)}) copy-start(bf16[512,256]{0,1:T(8,128)(2,1)S(1)} %copy.57) | copy-start | bytes 786436
  12.7 1.3 copy-start.1
  14.0 1.1 copy-start.2
  20.4 2.2 copy-start.8
  20.4 2.2 copy-start.11
  22.7 4.6 %copy-start.6 = (bf16[512,256]{0,1:T(8,128)(2,1)S(1)}, bf16[512,256]{0,1:T(8,128)(2,1)}, u32[]{:S(2)}) copy-start(bf16[512,256]{0,1:T(8,128)(2,1)} %copy-done.5) | copy-start | bytes 786436
  29.9 2.2 copy-start.9
  35.5 1.0 copy-start.3
  35.5 2.3 copy-start.16
  35.5 2.5 copy-start.17
  35.5 3.2 %copy-start.13 = (bf16[512,512]{0,1:T(8,128)(2,1)S(1)}, bf16[512,512]{0,1:T(8,128)(2,1)}, u32[]{:S(2)}) copy-start(bf16[512,512]{0,1:T(8,128)(2,1)} %copy.66) | copy-start | bytes 1572868
  36.5 1.0 copy-start.10
  43.5 162.7 %all-to-all-start = ((bf16[128,17,512]{2,1,0:T(8,128)(2,1)}), bf16[128,17,512]{2,1,0:T(8,128)(2,1)}, u32[]{:S(2)}, u32[]{:S(2)}) async-start(bf16[128,17,512]{2,1,0:T(8,128)(2,1)} %fusion.5), calls=%async_computation | async-start | bytes 6291456 | tf_op jit(solution)/shard_map/all_to_all | solution.py:167
  74.4 5.1 %collective-permute-start.3 = (f32[16,4,4,1280]{3,2,1,0:T(4,128)S(1)}, f32[16,4,4,1280]{3,2,1,0:T(4,128)}, u32[]{:S(2)}, u32[]{:S(2)}) collective-permute-start(f32[16,4,4,1280]{3,2,1,0:T(4,128)S(1)} %dynamic-slice_bitcast_fusion), channel_id=1, source_target_pairs={{0,4},{4,0},{1,5},{5,1},{2,6},{6,2},{3,7},{7,3},{8,12},{12,8},{9,1... | collective-permute-start | bytes 3932168 | tf_op jit(solution)/shard_map/ppermute | solution.py:74
  83.2 12.6 %collective-permute-start.4 = (f32[16,4,1,1280]{3,2,1,0:T(1,128)}, f32[16,4,1,1280]{3,2,1,0:T(1,128)S(1)}, u32[]{:S(2)}, u32[]{:S(2)}) collective-permute-start(f32[16,4,1,1280]{3,2,1,0:T(1,128)} %get-tuple-element.19), channel_id=1, source_target_pairs={{0,1},{1,2},{2,3},{3,0},{4,5},{5,6},{6,7},{7,4},{8,9},{9,10},{10,1... | collective-permute-start | bytes 983048 | tf_op jit(solution)/shard_map/ppermute | solution.py:74
  85.6 14.1 %collective-permute-start.5 = (f32[16,4,1,1280]{3,2,1,0:T(1,128)S(1)}, f32[16,4,1,1280]{3,2,1,0:T(1,128)}, u32[]{:S(2)}, u32[]{:S(2)}) collective-permute-start(f32[16,4,1,1280]{3,2,1,0:T(1,128)S(1)} %get-tuple-element.21), channel_id=1, source_target_pairs={{0,2},{1,3},{2,0},{3,1},{4,6},{5,7},{6,4},{7,5},{8,10},{9,11},{10,... | collective-permute-start | bytes 983048 | tf_op jit(solution)/shard_map/ppermute | solution.py:74
  90.0 15.7 %collective-permute-start.6 = (f32[16,4,1,1280]{3,2,1,0:T(1,128)S(1)}, f32[16,4,1,1280]{3,2,1,0:T(1,128)}, u32[]{:S(2)}, u32[]{:S(2)}) collective-permute-start(f32[16,4,1,1280]{3,2,1,0:T(1,128)S(1)} %get-tuple-element.20), channel_id=1, source_target_pairs={{0,3},{1,0},{2,1},{3,2},{4,7},{5,4},{6,5},{7,6},{8,11},{9,8},{10,9... | collective-permute-start | bytes 983048 | tf_op jit(solution)/shard_map/ppermute | solution.py:74
  107.4 11.2 %collective-permute-start.7 = (f32[16,1,1280]{2,1,0:T(1,128)S(1)}, f32[16,1,1280]{2,1,0:T(1,128)S(1)}, u32[]{:S(2)}, u32[]{:S(2)}) collective-permute-start(f32[16,1,1280]{2,1,0:T(1,128)S(1)} %get-tuple-element.28), channel_id=1, source_target_pairs={{0,8},{8,16},{16,24},{24,0},{1,9},{9,17},{17,25},{25,1},{2,10},{10... | collective-permute-start | bytes 245768 | tf_op jit(solution)/shard_map/ppermute | solution.py:74
  110.4 8.6 %collective-permute-start.8 = (f32[16,1,1280]{2,1,0:T(1,128)S(1)}, f32[16,1,1280]{2,1,0:T(1,128)S(1)}, u32[]{:S(2)}, u32[]{:S(2)}) collective-permute-start(f32[16,1,1280]{2,1,0:T(1,128)S(1)} %get-tuple-element.30), channel_id=1, source_target_pairs={{0,16},{8,24},{16,0},{24,8},{1,17},{9,25},{17,1},{25,9},{2,18},{10... | collective-permute-start | bytes 245768 | tf_op jit(solution)/shard_map/ppermute | solution.py:74
  115.0 6.5 %collective-permute-start.9 = (f32[16,1,1280]{2,1,0:T(1,128)S(1)}, f32[16,1,1280]{2,1,0:T(1,128)S(1)}, u32[]{:S(2)}, u32[]{:S(2)}) collective-permute-start(f32[16,1,1280]{2,1,0:T(1,128)S(1)} %get-tuple-element.29), channel_id=1, source_target_pairs={{0,24},{8,0},{16,8},{24,16},{1,25},{9,1},{17,9},{25,17},{2,26},{10... | collective-permute-start | bytes 245768 | tf_op jit(solution)/shard_map/ppermute | solution.py:74
  121.8 87.9 %collective-permute-start.10 = (f32[1,1280]{1,0:T(1,128)S(1)}, f32[1,1280]{1,0:T(1,128)S(1)}, u32[]{:S(2)}, u32[]{:S(2)}) collective-permute-start(f32[1,1280]{1,0:T(1,128)S(1)} %get-tuple-element.31), channel_id=1, source_target_pairs={{0,32},{32,64},{64,96},{96,128},{128,160},{160,192},{192,224},{224... | collective-permute-start | bytes 15368 | tf_op jit(solution)/shard_map/ppermute | solution.py:74
  125.0 89.1 %collective-permute-start.11 = (f32[1,1280]{1,0:T(1,128)S(1)}, f32[1,1280]{1,0:T(1,128)S(1)}, u32[]{:S(2)}, u32[]{:S(2)}) collective-permute-start(f32[1,1280]{1,0:T(1,128)S(1)} %get-tuple-element.45), channel_id=1, source_target_pairs={{0,64},{32,96},{64,128},{96,160},{128,192},{160,224},{192,256},{22... | collective-permute-start | bytes 15368 | tf_op jit(solution)/shard_map/ppermute | solution.py:74
  129.5 95.2 %collective-permute-start.12 = (f32[1,1280]{1,0:T(1,128)S(1)}, f32[1,1280]{1,0:T(1,128)S(1)}, u32[]{:S(2)}, u32[]{:S(2)}) collective-permute-start(f32[1,1280]{1,0:T(1,128)S(1)} %get-tuple-element.44), channel_id=1, source_target_pairs={{0,96},{32,128},{64,160},{96,192},{128,224},{160,256},{192,288},{2... | collective-permute-start | bytes 15368 | tf_op jit(solution)/shard_map/ppermute | solution.py:74
  136.4 93.2 %collective-permute-start.13 = (f32[1,1280]{1,0:T(1,128)S(1)}, f32[1,1280]{1,0:T(1,128)S(1)}, u32[]{:S(2)}, u32[]{:S(2)}) collective-permute-start(f32[1,1280]{1,0:T(1,128)S(1)} %get-tuple-element.43), channel_id=1, source_target_pairs={{0,128},{32,160},{64,192},{96,224},{128,256},{160,288},{192,320},{... | collective-permute-start | bytes 15368 | tf_op jit(solution)/shard_map/ppermute | solution.py:74
  141.8 97.4 %collective-permute-start.14 = (f32[1,1280]{1,0:T(1,128)S(1)}, f32[1,1280]{1,0:T(1,128)S(1)}, u32[]{:S(2)}, u32[]{:S(2)}) collective-permute-start(f32[1,1280]{1,0:T(1,128)S(1)} %get-tuple-element.42), channel_id=1, source_target_pairs={{0,160},{32,192},{64,224},{96,256},{128,288},{160,320},{192,352},{... | collective-permute-start | bytes 15368 | tf_op jit(solution)/shard_map/ppermute | solution.py:74
  209.3 80.5 %copy-start.18 = (f32[128]{0:T(128)S(1)}, f32[128]{0:T(128)}, u32[]{:S(2)}) copy-start(f32[128]{0:T(128)} %param.21) | copy-start | bytes 1540
  209.3 81.0 %copy-start.14 = (f32[128,512]{1,0:T(8,128)S(1)}, f32[128,512]{1,0:T(8,128)}, u32[]{:S(2)}) copy-start(f32[128,512]{1,0:T(8,128)} %param.20) | copy-start | bytes 786436
  209.3 81.0 %copy-start.15 = (f32[128,512]{1,0:T(8,128)S(1)}, f32[128,512]{1,0:T(8,128)}, u32[]{:S(2)}) copy-start(f32[128,512]{1,0:T(8,128)} %param.19) | copy-start | bytes 786436
  209.8 34.8 %collective-permute-start.15 = (f32[1,1280]{1,0:T(1,128)S(1)}, f32[1,1280]{1,0:T(1,128)S(1)}, u32[]{:S(2)}, u32[]{:S(2)}) collective-permute-start(f32[1,1280]{1,0:T(1,128)S(1)} %get-tuple-element.41), channel_id=1, source_target_pairs={{0,192},{32,224},{64,256},{96,288},{128,320},{160,352},{192,384},{... | collective-permute-start | bytes 15368 | tf_op jit(solution)/shard_map/ppermute | solution.py:74
  214.2 34.5 %collective-permute-start.16 = (f32[1,1280]{1,0:T(1,128)S(1)}, f32[1,1280]{1,0:T(1,128)S(1)}, u32[]{:S(2)}, u32[]{:S(2)}) collective-permute-start(f32[1,1280]{1,0:T(1,128)S(1)} %get-tuple-element.40), channel_id=1, source_target_pairs={{0,224},{32,256},{64,288},{96,320},{128,352},{160,384},{192,416},{... | collective-permute-start | bytes 15368 | tf_op jit(solution)/shard_map/ppermute | solution.py:74
  224.7 30.8 %collective-permute-start.17 = (f32[1,1280]{1,0:T(1,128)S(1)}, f32[1,1280]{1,0:T(1,128)S(1)}, u32[]{:S(2)}, u32[]{:S(2)}) collective-permute-start(f32[1,1280]{1,0:T(1,128)S(1)} %get-tuple-element.39), channel_id=1, source_target_pairs={{0,256},{32,288},{64,320},{96,352},{128,384},{160,416},{192,448},{... | collective-permute-start | bytes 15368 | tf_op jit(solution)/shard_map/ppermute | solution.py:74
  229.7 30.3 %collective-permute-start.18 = (f32[1,1280]{1,0:T(1,128)S(1)}, f32[1,1280]{1,0:T(1,128)S(1)}, u32[]{:S(2)}, u32[]{:S(2)}) collective-permute-start(f32[1,1280]{1,0:T(1,128)S(1)} %get-tuple-element.38), channel_id=1, source_target_pairs={{0,288},{32,320},{64,352},{96,384},{128,416},{160,448},{192,480},{... | collective-permute-start | bytes 15368 | tf_op jit(solution)/shard_map/ppermute | solution.py:74
  239.2 22.6 %collective-permute-start.19 = (f32[1,1280]{1,0:T(1,128)S(1)}, f32[1,1280]{1,0:T(1,128)S(1)}, u32[]{:S(2)}, u32[]{:S(2)}) collective-permute-start(f32[1,1280]{1,0:T(1,128)S(1)} %get-tuple-element.37), channel_id=1, source_target_pairs={{0,320},{32,352},{64,384},{96,416},{128,448},{160,480},{192,0},{22... | collective-permute-start | bytes 15368 | tf_op jit(solution)/shard_map/ppermute | solution.py:74
  244.6 20.3 %collective-permute-start.20 = (f32[1,1280]{1,0:T(1,128)S(1)}, f32[1,1280]{1,0:T(1,128)S(1)}, u32[]{:S(2)}, u32[]{:S(2)}) collective-permute-start(f32[1,1280]{1,0:T(1,128)S(1)} %get-tuple-element.36), channel_id=1, source_target_pairs={{0,352},{32,384},{64,416},{96,448},{128,480},{160,0},{192,32},{224... | collective-permute-start | bytes 15368 | tf_op jit(solution)/shard_map/ppermute | solution.py:74
  248.7 18.7 %collective-permute-start.21 = (f32[1,1280]{1,0:T(1,128)S(1)}, f32[1,1280]{1,0:T(1,128)S(1)}, u32[]{:S(2)}, u32[]{:S(2)}) collective-permute-start(f32[1,1280]{1,0:T(1,128)S(1)} %get-tuple-element.35), channel_id=1, source_target_pairs={{0,384},{32,416},{64,448},{96,480},{128,0},{160,32},{192,64},{224,... | collective-permute-start | bytes 15368 | tf_op jit(solution)/shard_map/ppermute | solution.py:74
  255.5 16.2 %collective-permute-start.22 = (f32[1,1280]{1,0:T(1,128)S(1)}, f32[1,1280]{1,0:T(1,128)S(1)}, u32[]{:S(2)}, u32[]{:S(2)}) collective-permute-start(f32[1,1280]{1,0:T(1,128)S(1)} %get-tuple-element.34), channel_id=1, source_target_pairs={{0,416},{32,448},{64,480},{96,0},{128,32},{160,64},{192,96},{224,1... | collective-permute-start | bytes 15368 | tf_op jit(solution)/shard_map/ppermute | solution.py:74
  259.9 13.7 %collective-permute-start.23 = (f32[1,1280]{1,0:T(1,128)S(1)}, f32[1,1280]{1,0:T(1,128)S(1)}, u32[]{:S(2)}, u32[]{:S(2)}) collective-permute-start(f32[1,1280]{1,0:T(1,128)S(1)} %get-tuple-element.33), channel_id=1, source_target_pairs={{0,448},{32,480},{64,0},{96,32},{128,64},{160,96},{192,128},{224,1... | collective-permute-start | bytes 15368 | tf_op jit(solution)/shard_map/ppermute | solution.py:74
  261.9 11.8 %collective-permute-start.24 = (f32[1,1280]{1,0:T(1,128)S(1)}, f32[1,1280]{1,0:T(1,128)S(1)}, u32[]{:S(2)}, u32[]{:S(2)}) collective-permute-start(f32[1,1280]{1,0:T(1,128)S(1)} %get-tuple-element.32), channel_id=1, source_target_pairs={{0,480},{32,0},{64,32},{96,64},{128,96},{160,128},{192,160},{224,1... | collective-permute-start | bytes 15368 | tf_op jit(solution)/shard_map/ppermute | solution.py:74
  264.9 24.5 %collective-permute-start = (f32[128,640]{1,0:T(8,128)S(1)}, f32[128,640]{1,0:T(8,128)S(1)}, u32[]{:S(2)}, u32[]{:S(2)}) collective-permute-start(f32[128,640]{1,0:T(8,128)S(1)} %pad_maximum_fusion.1), channel_id=1, source_target_pairs={{0,1},{1,2},{2,3},{3,0},{4,5},{5,6},{6,7},{7,4},{8,9},{9,10},{10,1... | collective-permute-start | bytes 983048 | tf_op jit(solution)/shard_map/ppermute | solution.py:74
  267.4 22.1 %collective-permute-start.1 = (f32[128,640]{1,0:T(8,128)S(1)}, f32[128,640]{1,0:T(8,128)S(1)}, u32[]{:S(2)}, u32[]{:S(2)}) collective-permute-start(f32[128,640]{1,0:T(8,128)S(1)} %pad_maximum_fusion.1), channel_id=1, source_target_pairs={{0,2},{1,3},{2,0},{3,1},{4,6},{5,7},{6,4},{7,5},{8,10},{9,11},{10,... | collective-permute-start | bytes 983048 | tf_op jit(solution)/shard_map/ppermute | solution.py:74
  271.7 17.7 %collective-permute-start.2 = (f32[128,640]{1,0:T(8,128)S(1)}, f32[128,640]{1,0:T(8,128)S(1)}, u32[]{:S(2)}, u32[]{:S(2)}) collective-permute-start(f32[128,640]{1,0:T(8,128)S(1)} %pad_maximum_fusion.1), channel_id=1, source_target_pairs={{0,3},{1,0},{2,1},{3,2},{4,7},{5,4},{6,5},{7,6},{8,11},{9,8},{10,9... | collective-permute-start | bytes 983048 | tf_op jit(solution)/shard_map/ppermute | solution.py:74
  273.7 7.1 %collective-permute-start.25 = (f32[1,1280]{1,0:T(1,128)S(1)}, f32[1,1280]{1,0:T(1,128)S(1)}, u32[]{:S(2)}, u32[]{:S(2)}) collective-permute-start(f32[1,1280]{1,0:T(1,128)S(1)} %add_add_fusion.5), channel_id=1, source_target_pairs={{0,1},{1,2},{2,3},{3,0},{4,5},{5,6},{6,7},{7,4},{8,9},{9,10},{10,1... | collective-permute-start | bytes 15368 | tf_op jit(solution)/shard_map/ppermute | solution.py:74
  278.8 7.0 %collective-permute-start.26 = (f32[1,1280]{1,0:T(1,128)S(1)}, f32[1,1280]{1,0:T(1,128)S(1)}, u32[]{:S(2)}, u32[]{:S(2)}) collective-permute-start(f32[1,1280]{1,0:T(1,128)S(1)} %add_add_fusion.5), channel_id=1, source_target_pairs={{0,2},{1,3},{2,0},{3,1},{4,6},{5,7},{6,4},{7,5},{8,10},{9,11},{10,... | collective-permute-start | bytes 15368 | tf_op jit(solution)/shard_map/ppermute | solution.py:74
  280.8 6.7 %collective-permute-start.27 = (f32[1,1280]{1,0:T(1,128)S(1)}, f32[1,1280]{1,0:T(1,128)S(1)}, u32[]{:S(2)}, u32[]{:S(2)}) collective-permute-start(f32[1,1280]{1,0:T(1,128)S(1)} %add_add_fusion.5), channel_id=1, source_target_pairs={{0,3},{1,0},{2,1},{3,2},{4,7},{5,4},{6,5},{7,6},{8,11},{9,8},{10,9... | collective-permute-start | bytes 15368 | tf_op jit(solution)/shard_map/ppermute | solution.py:74

commit v3 on v2

--- a/solution.py
+++ b/solution.py
@@ -70,45 +70,50 @@
 ALL_AXES = ("z", "y", "core", "x")
 
 
-def shifted(value, axis, size, step):
-    return lax.ppermute(value, axis, [(i, (i + step) % size) for i in range(size)])
-
-
-def scatter_sum(blocks, axis, size, dim):
-    me = lax.axis_index(axis)
+def moved(value, axis, pairs):
+    return lax.ppermute(value, axis, pairs)
+
+
+def scatter_sum(blocks, axis, me, pairs_of, size, dim):
     total = lax.dynamic_index_in_dim(blocks, me, dim, keepdims=False)
     for step in range(1, size):
         piece = lax.dynamic_index_in_dim(blocks, (me + step) % size, dim, keepdims=False)
-        total = total + shifted(piece, axis, size, step)
+        total = total + moved(piece, axis, pairs_of(step))
     return total
 
 
-def gather_rows(row, axis, size):
-    me = lax.axis_index(axis)
-    pieces = [row]
-    for step in range(1, size):
-        pieces.append(shifted(row, axis, size, step))
-    stacked = jnp.stack(pieces)
-    order = (me - jnp.arange(size)) % size
-    return jnp.zeros_like(stacked).at[order].set(stacked)
+def ring(total, size, group=1):
+    span = size * group
+
+    def pairs_of(step):
+        return [
+            (i, (i // span) * span + (i % group) + ((i % span) // group + step) % size * group)
+            for i in range(total)
+        ]
+
+    return pairs_of
 
 
 def reduce_weights(partial, sizes):
     width = partial.shape[1]
-    per_owner = partial.shape[0] // (sizes["z"] * sizes["y"] * sizes["core"])
-    blocks = partial.reshape(sizes["z"], sizes["y"], sizes["core"], per_owner, width)
-    blocks = scatter_sum(blocks, "core", sizes["core"], 2)
-    blocks = blocks.reshape(sizes["z"], sizes["y"], sizes["x"], per_owner // sizes["x"], width)
-    blocks = scatter_sum(blocks, "x", sizes["x"], 2)
-    blocks = scatter_sum(blocks, "y", sizes["y"], 1)
-    blocks = scatter_sum(blocks, "z", sizes["z"], 0)
-    return gather_rows(blocks, "x", sizes["x"]).reshape(per_owner, width)
+    n_z, n_y, n_c, n_x = sizes["z"], sizes["y"], sizes["core"], sizes["x"]
+    per_owner = partial.shape[0] // (n_z * n_y * n_c)
+    blocks = partial.reshape(n_z, n_y, n_c, per_owner, width)
+    blocks = scatter_sum(blocks, "core", lax.axis_index("core"), ring(n_c, n_c), n_c, 2)
+    blocks = scatter_sum(blocks, "y", lax.axis_index("y"), ring(n_y, n_y), n_y, 1)
+    z_lo = 4 if n_z % 4 == 0 else 1
+    z_hi = n_z // z_lo
+    z_me = lax.axis_index("z")
+    blocks = blocks.reshape(z_hi, z_lo, per_owner, width)
+    blocks = scatter_sum(blocks, "z", z_me % z_lo, ring(n_z, z_lo), z_lo, 1)
+    blocks = scatter_sum(blocks, "z", z_me // z_lo, ring(n_z, z_hi, z_lo), z_hi, 0)
+    return sum_over(blocks, "x", n_x)
 
 
 def sum_over(value, axis, size):
     total = value
     for step in range(1, size):
-        total = total + shifted(value, axis, size, step)
+        total = total + moved(value, axis, ring(size, size)(step))
     return total
 
 
@@ -141,8 +146,6 @@
         ),
         sizes,
     )
-    w_in_grad = weight_share[:, :in_cols]
-    w_out_grad = weight_share[:, in_cols:]
     capacity = max(2, 4 * tok_count // owner_count)
     buffer_rows = owner_count * capacity
     owner_of = owners[:, 0]
@@ -167,6 +170,9 @@
     arrived = lax.all_to_all(
         jnp.concatenate([outgoing, slot_row], axis=1), ROW_AXES, 0, 0, tiled=True
     )
+    arrived, weight_share = lax.optimization_barrier((arrived, weight_share))
+    w_in_grad = weight_share[:, :in_cols]
+    w_out_grad = weight_share[:, in_cols:]
     received = arrived[:, :capacity, :].reshape(buffer_rows, width)
     got_slots = arrived[:, capacity, :capacity].astype(jnp.int32).reshape(buffer_rows)
     slot_count = emb_rows.shape[0]

time: 294 us -> 269 us (0.915)
  starting transfers between devices: 139 us -> 80.6 us
  waiting for transfers between devices: 83.9 us -> 118 us
    ppermute x28 -> x16, waiting for transfers between devices: 23.2 us -> 118 us  [moved(): return lax.ppermute(value, axis, pairs)]
    all_to_all x1, waiting for transfers between devices: 60.7 us -> 0.01 us  [local(): lax.all_to_all(jnp.concatenate([outgoing, slot_row], axis=1), ROW_AXES, 0...]
    ppermute x28 -> x16, starting transfers between devices: 119 us -> 60.2 us  [moved(): return lax.ppermute(value, axis, pairs)]
    dynamic_slice x0 -> x1, local copies, waits for them, and re-layouts: none -> 2.97 us  [scatter_sum(): total = lax.dynamic_index_in_dim(blocks, me, dim, keepdims=False)]
  transfers between devices with their start and end apart: 29 -> 17, of which waited for: 9 -> 13; matrix products, arithmetic and copies ran while one was open for 8% -> 7% of each run, Pallas kernels for 0% -> 0%
where the time goes in v3:
time: 269 us; the launch traced here: 267 us
  waiting for transfers between devices  118 us (44%)
  starting transfers between devices  80.6 us (30%)
  matrix products  24.8 us (9%)
  local copies, waits for them, and re-layouts  22.4 us (8%)
  other arithmetic  19.7 us (7%)
    ppermute x16, waiting for transfers between devices, moved(): return lax.ppermute(value, axis, pairs)  118 us
    ppermute x16, starting transfers between devices, moved(): return lax.ppermute(value, axis, pairs)  60.2 us
    all_to_all x1, starting transfers between devices, local(): lax.all_to_all(jnp.concatenate([outgoing, slot_row], axis=1), ROW_AXES, 0...  20.4 us
    dot_general x3, matrix products, core(): jnp.einsum('hts,shd->thd', weights, values_part, preferred_element_type=j...  7.51 us
    dot_general x3, matrix products, core(): jnp.einsum('thd,shd->hts', queries, keys_part, preferred_element_type=jnp...  6.16 us
    unnamed x41, local copies, waits for them, and re-layouts  5.61 us
  transfers between devices with their start and end apart: 17, of which 13 were waited for; matrix products, arithmetic and copies ran while one was open for 7% of the time, Pallas kernels for 0%

profile of v3, /device:TPU:6, one launch (start us, length us, event | category | flops | bytes accessed | tf_op | source)
XLA Modules:
  0.0 267.2 jit_solution(3354664067562602821)
XLA Ops:
  0.7 0.9 reduce-window.8
  1.9 1.2 fusion.23
  3.6 2.3 multiply_convert_fusion.1
  5.8 1.0 copy-done.4
  7.9 1.2 copy.75
  9.1 3.5 %multiply_convert_fusion = (bf16[4,512,512]{2,1,0:T(8,128)(2,1)S(1)}, f32[4,512,512]{2,1,0:T(8,128)}) fusion(f32[512,512]{1,0:T(8,128)S(1)} %fusion.24, bf16[512,4,64]{0,2,1:T(8,128)(2,1)S(1)} %bitcast.100, bf16[512,4,64]{0,2,1:T(8,128)(2,1)S(1)} %bitcast.102), kind=kOutput, calls=%fused_computation.7 | convolution fusion | flops 142606336 | bytes 7864320 | tf_op jit(solution)/shard_map/jvp(thd,shd->hts)/dot_general | solution.py:46
  12.7 1.3 copy-done.1
  14.0 0.8 fusion.52
  15.1 1.4 multiply_reduce_fusion
  16.5 1.9 fusion.50
  18.4 0.8 broadcast_add_fusion
  19.3 1.1 copy.80
  20.4 2.2 fusion.55
  22.6 4.6 %fusion.3 = bf16[4,512,512]{2,1,0:T(8,128)(2,1)S(1)} fusion(f32[4,512,512]{2,1,0:T(8,128)} %get-tuple-element.47, f32[512,512]{1,0:T(8,128)S(1)} %copy-done.11, bf16[4,64,512]{2,1,0:T(8,128)(2,1)} %bitcast.108, bf16[512,4,64]{0,2,1:T(8,128)(2,1)} %bitcast.105), kind=kOutput, calls=%fused_computation.5 | convolution fusion | flops 148897792 | bytes 7864320 | tf_op jit(solution)/shard_map/transpose(jvp(hts,shd->thd))/dot_general | solution.py:50
  27.2 1.5 fusion.54
  28.7 1.2 fusion.53
  29.9 1.0 copy.84
  31.0 1.1 copy.82
  32.1 0.8 copy.83
  32.9 2.5 fusion.8
  36.5 1.0 copy-done.10
  38.6 2.8 %fusion.6 = bf16[2048,512]{1,0:T(8,128)(2,1)S(1)} fusion(s32[512]{0:T(512)S(1)} %get-tuple-element.54, bf16[512,512]{0,1:T(8,128)(2,1)S(1)} %copy-done.13, f32[512]{0:T(512)S(1)} %negate_multiply_fusion, bf16[512,512]{0,1:T(8,128)(2,1)S(1)} %copy.74, f32[512,512]{0,1:T(8,128)} %copy-done.10, f32[512]{0:T(512)S(1)} %multiply_multiply_fusion, ...), kind=kOutput, calls=%fused_computation.13 | convolution fusion | flops 1078460416 | bytes 4204544 | tf_op jit(solution)/shard_map/dot_general | solution.py:161
  41.5 2.0 fusion.5
  43.5 20.4 %all-to-all-start = ((bf16[128,17,512]{2,1,0:T(8,128)(2,1)}), bf16[128,17,512]{2,1,0:T(8,128)(2,1)}, u32[]{:S(2)}, u32[]{:S(2)}) async-start(bf16[128,17,512]{2,1,0:T(8,128)(2,1)} %fusion.5), calls=%async_computation | async-start | bytes 6291456 | tf_op jit(solution)/shard_map/all_to_all | solution.py:170
  63.9 1.5 convolution_bitcast_fusion
  65.4 1.9 fusion.31
  67.3 1.7 pad_maximum_fusion
  69.1 3.9 %reshape.248 = f32[16,4,2,4,1280]{4,3,2,1,0:T(4,128)} reshape(f32[512,1280]{1,0:T(8,128)} %pad_maximum_fusion) | data formatting | bytes 5242880 | tf_op jit(solution)/shard_map/reshape | solution.py:101
  73.0 3.0 %constant_dynamic-slice_fusion.1 = (f32[16,4,1,4,1280]{4,3,2,1,0:T(4,128)}, f32[16,4,1,4,1280]{4,3,2,1,0:T(4,128)S(1)}) fusion(f32[16,4,2,4,1280]{4,3,2,1,0:T(4,128)} %reshape.248, s32[]{:T(128)S(6)} %select_n.113, s32[]{:T(128)S(6)} %select_n.115), kind=kLoop, calls=%fused_computation.103 | loop fusion | bytes 5242888 | tf_op jit(solution)/shard_map/jit(dynamic_index_in_dim)/dynamic_slice | solution.py:78
  76.0 0.8 copy.99
  76.7 1.9 collective-permute-start
  78.7 3.1 %collective-permute-done = f32[16,4,4,1280]{3,0,2,1:T(8,128)} collective-permute-done((f32[16,4,4,1280]{3,0,2,1:T(8,128)S(1)}, f32[16,4,4,1280]{3,0,2,1:T(8,128)}, u32[]{:S(2)}, u32[]{:S(2)}) %collective-permute-start) | collective-permute-done | bytes 1310752 | tf_op jit(solution)/shard_map/ppermute | solution.py:74
  81.8 2.5 fusion.15
  84.3 0.8 dynamic-slice_bitcast_fusion.2
  85.1 3.0 %collective-permute-start.1 = (f32[16,4,1280]{2,0,1:T(8,128)}, f32[16,4,1280]{2,0,1:T(8,128)S(1)}, u32[]{:S(2)}, u32[]{:S(2)}) collective-permute-start(f32[16,4,1280]{2,0,1:T(8,128)} %get-tuple-element.25), channel_id=1, source_target_pairs={{0,8},{8,16},{16,24},{24,0},{1,9},{9,17},{17,25},{25,1},{2,10},{10... | collective-permute-start | bytes 983048 | tf_op jit(solution)/shard_map/ppermute | solution.py:74
  88.1 4.6 %collective-permute-start.2 = (f32[16,4,1280]{2,0,1:T(8,128)S(1)}, f32[16,4,1280]{2,0,1:T(8,128)}, u32[]{:S(2)}, u32[]{:S(2)}) collective-permute-start(f32[16,4,1280]{2,0,1:T(8,128)S(1)} %get-tuple-element.27), channel_id=1, source_target_pairs={{0,16},{8,24},{16,0},{24,8},{1,17},{9,25},{17,1},{25,9},{2,18},{10... | collective-permute-start | bytes 983048 | tf_op jit(solution)/shard_map/ppermute | solution.py:74
  92.7 3.4 %collective-permute-start.3 = (f32[16,4,1280]{2,0,1:T(8,128)S(1)}, f32[16,4,1280]{2,0,1:T(8,128)}, u32[]{:S(2)}, u32[]{:S(2)}) collective-permute-start(f32[16,4,1280]{2,0,1:T(8,128)S(1)} %get-tuple-element.26), channel_id=1, source_target_pairs={{0,24},{8,0},{16,8},{24,16},{1,25},{9,1},{17,9},{25,17},{2,26},{10... | collective-permute-start | bytes 983048 | tf_op jit(solution)/shard_map/ppermute | solution.py:74
  96.1 3.8 %collective-permute-done.1 = f32[16,4,1280]{2,0,1:T(8,128)S(1)} collective-permute-done((f32[16,4,1280]{2,0,1:T(8,128)}, f32[16,4,1280]{2,0,1:T(8,128)S(1)}, u32[]{:S(2)}, u32[]{:S(2)}) %collective-permute-start.1) | collective-permute-done | bytes 327712 | tf_op jit(solution)/shard_map/ppermute | solution.py:74
  99.9 10.9 %collective-permute-done.2 = f32[16,4,1280]{2,0,1:T(8,128)} collective-permute-done((f32[16,4,1280]{2,0,1:T(8,128)S(1)}, f32[16,4,1280]{2,0,1:T(8,128)}, u32[]{:S(2)}, u32[]{:S(2)}) %collective-permute-start.2) | collective-permute-done | bytes 327712 | tf_op jit(solution)/shard_map/ppermute | solution.py:74
  110.8 0.9 collective-permute-done.3
  111.7 1.1 fusion.36
  113.1 3.4 %collective-permute-start.4 = (f32[4,4,1280]{2,1,0:T(4,128)S(1)}, f32[4,4,1280]{2,1,0:T(4,128)S(1)}, u32[]{:S(2)}, u32[]{:S(2)}) collective-permute-start(f32[4,4,1280]{2,1,0:T(4,128)S(1)} %get-tuple-element.34), channel_id=1, source_target_pairs={{0,32},{32,64},{64,96},{96,0},{128,160},{160,192},{192,224},{224,1... | collective-permute-start | bytes 245768 | tf_op jit(solution)/shard_map/ppermute | solution.py:74
  116.5 4.8 %collective-permute-start.5 = (f32[4,4,1280]{2,1,0:T(4,128)S(1)}, f32[4,4,1280]{2,1,0:T(4,128)S(1)}, u32[]{:S(2)}, u32[]{:S(2)}) collective-permute-start(f32[4,4,1280]{2,1,0:T(4,128)S(1)} %get-tuple-element.36), channel_id=1, source_target_pairs={{0,64},{32,96},{64,0},{96,32},{128,192},{160,224},{192,128},{224,1... | collective-permute-start | bytes 245768 | tf_op jit(solution)/shard_map/ppermute | solution.py:74
  121.3 2.6 collective-permute-start.6
  123.9 78.2 %collective-permute-done.4 = f32[4,4,1280]{2,1,0:T(4,128)S(1)} collective-permute-done((f32[4,4,1280]{2,1,0:T(4,128)S(1)}, f32[4,4,1280]{2,1,0:T(4,128)S(1)}, u32[]{:S(2)}, u32[]{:S(2)}) %collective-permute-start.4) | collective-permute-done | bytes 81952 | tf_op jit(solution)/shard_map/ppermute | solution.py:74
  202.2 4.1 %collective-permute-done.5 = f32[4,4,1280]{2,1,0:T(4,128)S(1)} collective-permute-done((f32[4,4,1280]{2,1,0:T(4,128)S(1)}, f32[4,4,1280]{2,1,0:T(4,128)S(1)}, u32[]{:S(2)}, u32[]{:S(2)}) %collective-permute-start.5) | collective-permute-done | bytes 81952 | tf_op jit(solution)/shard_map/ppermute | solution.py:74
  206.4 7.5 %collective-permute-start.7 = (f32[4,1280]{1,0:T(4,128)S(1)}, f32[4,1280]{1,0:T(4,128)S(1)}, u32[]{:S(2)}, u32[]{:S(2)}) collective-permute-start(f32[4,1280]{1,0:T(4,128)S(1)} %get-tuple-element.37), channel_id=1, source_target_pairs={{0,128},{32,160},{64,192},{96,224},{128,256},{160,288},{192,320},{... | collective-permute-start | bytes 61448 | tf_op jit(solution)/shard_map/ppermute | solution.py:74
  213.8 5.2 %collective-permute-start.8 = (f32[4,1280]{1,0:T(4,128)S(1)}, f32[4,1280]{1,0:T(4,128)S(1)}, u32[]{:S(2)}, u32[]{:S(2)}) collective-permute-start(f32[4,1280]{1,0:T(4,128)S(1)} %get-tuple-element.39), channel_id=1, source_target_pairs={{0,256},{32,288},{64,320},{96,352},{128,384},{160,416},{192,448},{... | collective-permute-start | bytes 61448 | tf_op jit(solution)/shard_map/ppermute | solution.py:74
  219.0 7.6 %collective-permute-start.9 = (f32[4,1280]{1,0:T(4,128)S(1)}, f32[4,1280]{1,0:T(4,128)S(1)}, u32[]{:S(2)}, u32[]{:S(2)}) collective-permute-start(f32[4,1280]{1,0:T(4,128)S(1)} %get-tuple-element.38), channel_id=1, source_target_pairs={{0,384},{32,416},{64,448},{96,480},{128,0},{160,32},{192,64},{224,... | collective-permute-start | bytes 61448 | tf_op jit(solution)/shard_map/ppermute | solution.py:74
  226.7 1.6 collective-permute-done.8
  228.6 2.4 collective-permute-start.10
  231.0 4.3 %collective-permute-start.11 = (f32[4,1280]{1,0:T(4,128)S(1)}, f32[4,1280]{1,0:T(4,128)S(1)}, u32[]{:S(2)}, u32[]{:S(2)}) collective-permute-start(f32[4,1280]{1,0:T(4,128)S(1)} %fusion.46), channel_id=1, source_target_pairs={{0,2},{1,3},{2,0},{3,1},{4,6},{5,7},{6,4},{7,5},{8,10},{9,11},{10,... | collective-permute-start | bytes 61448 | tf_op jit(solution)/shard_map/ppermute | solution.py:74
  235.4 1.9 collective-permute-start.12
  237.3 0.9 collective-permute-done.11
  238.2 4.0 %collective-permute-done.12 = f32[4,1280]{1,0:T(4,128)S(1)} collective-permute-done((f32[4,1280]{1,0:T(4,128)S(1)}, f32[4,1280]{1,0:T(4,128)S(1)}, u32[]{:S(2)}, u32[]{:S(2)}) %collective-permute-start.12) | collective-permute-done | bytes 20512 | tf_op jit(solution)/shard_map/ppermute | solution.py:74
  242.3 1.8 slice.42
  244.1 1.2 convert_reduce_fusion.3
  246.1 2.5 collective-permute-start.13
  248.6 2.2 collective-permute-start.14
  250.8 3.1 %collective-permute-start.15 = (f32[128,640]{1,0:T(8,128)S(1)}, f32[128,640]{1,0:T(8,128)S(1)}, u32[]{:S(2)}, u32[]{:S(2)}) collective-permute-start(f32[128,640]{1,0:T(8,128)S(1)} %pad_maximum_fusion.1), channel_id=1, source_target_pairs={{0,3},{1,0},{2,1},{3,2},{4,7},{5,4},{6,5},{7,6},{8,11},{9,8},{10,9... | collective-permute-start | bytes 983048 | tf_op jit(solution)/shard_map/ppermute | solution.py:74
  255.1 3.1 %collective-permute-done.13 = f32[128,640]{1,0:T(8,128)S(1)} collective-permute-done((f32[128,640]{1,0:T(8,128)S(1)}, f32[128,640]{1,0:T(8,128)S(1)}, u32[]{:S(2)}, u32[]{:S(2)}) %collective-permute-start.13) | collective-permute-done | bytes 327712 | tf_op jit(solution)/shard_map/ppermute | solution.py:74
  258.2 3.9 %collective-permute-done.14 = f32[128,640]{1,0:T(8,128)S(1)} collective-permute-done((f32[128,640]{1,0:T(8,128)S(1)}, f32[128,640]{1,0:T(8,128)S(1)}, u32[]{:S(2)}, u32[]{:S(2)}) %collective-permute-start.14) | collective-permute-done | bytes 327712 | tf_op jit(solution)/shard_map/ppermute | solution.py:74
  262.1 3.3 %collective-permute-done.15 = f32[128,640]{1,0:T(8,128)S(1)} collective-permute-done((f32[128,640]{1,0:T(8,128)S(1)}, f32[128,640]{1,0:T(8,128)S(1)}, u32[]{:S(2)}, u32[]{:S(2)}) %collective-permute-start.15) | collective-permute-done | bytes 327712 | tf_op jit(solution)/shard_map/ppermute | solution.py:74
  266.2 0.9 fusion.40
  (82 shorter events, 8.0 us)
Async XLA Ops:
  0.6 2.9 %copy-start = (bf16[512,1024]{1,0:T(8,128)(2,1)S(1)}, bf16[512,1024]{1,0:T(8,128)(2,1)}, u32[]{:S(2)}) copy-start(bf16[512,1024]{1,0:T(8,128)(2,1)} %param.17) | copy-start | bytes 3145732
  0.6 2.4 copy-start.12
  5.8 1.0 copy-start.4
  7.9 4.7 %copy-start.5 = (bf16[512,256]{0,1:T(8,128)(2,1)}, bf16[512,256]{0,1:T(8,128)(2,1)S(1)}, u32[]{:S(2)}) copy-start(bf16[512,256]{0,1:T(8,128)(2,1)S(1)} %copy.77) | copy-start | bytes 786436
  9.1 3.5 %copy-start.7 = (bf16[512,256]{0,1:T(8,128)(2,1)}, bf16[512,256]{0,1:T(8,128)(2,1)S(1)}, u32[]{:S(2)}) copy-start(bf16[512,256]{0,1:T(8,128)(2,1)S(1)} %copy.75) | copy-start | bytes 786436
  12.6 1.3 copy-start.1
  14.0 1.1 copy-start.2
  20.4 2.2 copy-start.8
  20.4 2.2 copy-start.11
  22.6 4.6 %copy-start.6 = (bf16[512,256]{0,1:T(8,128)(2,1)S(1)}, bf16[512,256]{0,1:T(8,128)(2,1)}, u32[]{:S(2)}) copy-start(bf16[512,256]{0,1:T(8,128)(2,1)} %copy-done.5) | copy-start | bytes 786436
  29.9 2.2 copy-start.9
  35.4 1.0 copy-start.3
  35.5 2.3 copy-start.16
  35.5 2.5 copy-start.17
  35.5 3.1 %copy-start.13 = (bf16[512,512]{0,1:T(8,128)(2,1)S(1)}, bf16[512,512]{0,1:T(8,128)(2,1)}, u32[]{:S(2)}) copy-start(bf16[512,512]{0,1:T(8,128)(2,1)} %copy.84) | copy-start | bytes 1572868
  36.4 1.0 copy-start.10
  43.5 198.8 %all-to-all-start = ((bf16[128,17,512]{2,1,0:T(8,128)(2,1)}), bf16[128,17,512]{2,1,0:T(8,128)(2,1)}, u32[]{:S(2)}, u32[]{:S(2)}) async-start(bf16[128,17,512]{2,1,0:T(8,128)(2,1)} %fusion.5), calls=%async_computation | async-start | bytes 6291456 | tf_op jit(solution)/shard_map/all_to_all | solution.py:170
  76.7 5.1 %collective-permute-start = (f32[16,4,4,1280]{3,0,2,1:T(8,128)S(1)}, f32[16,4,4,1280]{3,0,2,1:T(8,128)}, u32[]{:S(2)}, u32[]{:S(2)}) collective-permute-start(f32[16,4,4,1280]{3,0,2,1:T(8,128)S(1)} %bitcast.97), channel_id=1, source_target_pairs={{0,4},{4,0},{1,5},{5,1},{2,6},{6,2},{3,7},{7,3},{8,12},{12,8},{9,1... | collective-permute-start | bytes 3932168 | tf_op jit(solution)/shard_map/ppermute | solution.py:74
  85.1 14.8 %collective-permute-start.1 = (f32[16,4,1280]{2,0,1:T(8,128)}, f32[16,4,1280]{2,0,1:T(8,128)S(1)}, u32[]{:S(2)}, u32[]{:S(2)}) collective-permute-start(f32[16,4,1280]{2,0,1:T(8,128)} %get-tuple-element.25), channel_id=1, source_target_pairs={{0,8},{8,16},{16,24},{24,0},{1,9},{9,17},{17,25},{25,1},{2,10},{10... | collective-permute-start | bytes 983048 | tf_op jit(solution)/shard_map/ppermute | solution.py:74
  88.1 22.7 %collective-permute-start.2 = (f32[16,4,1280]{2,0,1:T(8,128)S(1)}, f32[16,4,1280]{2,0,1:T(8,128)}, u32[]{:S(2)}, u32[]{:S(2)}) collective-permute-start(f32[16,4,1280]{2,0,1:T(8,128)S(1)} %get-tuple-element.27), channel_id=1, source_target_pairs={{0,16},{8,24},{16,0},{24,8},{1,17},{9,25},{17,1},{25,9},{2,18},{10... | collective-permute-start | bytes 983048 | tf_op jit(solution)/shard_map/ppermute | solution.py:74
  92.7 19.0 %collective-permute-start.3 = (f32[16,4,1280]{2,0,1:T(8,128)S(1)}, f32[16,4,1280]{2,0,1:T(8,128)}, u32[]{:S(2)}, u32[]{:S(2)}) collective-permute-start(f32[16,4,1280]{2,0,1:T(8,128)S(1)} %get-tuple-element.26), channel_id=1, source_target_pairs={{0,24},{8,0},{16,8},{24,16},{1,25},{9,1},{17,9},{25,17},{2,26},{10... | collective-permute-start | bytes 983048 | tf_op jit(solution)/shard_map/ppermute | solution.py:74
  113.1 89.1 %collective-permute-start.4 = (f32[4,4,1280]{2,1,0:T(4,128)S(1)}, f32[4,4,1280]{2,1,0:T(4,128)S(1)}, u32[]{:S(2)}, u32[]{:S(2)}) collective-permute-start(f32[4,4,1280]{2,1,0:T(4,128)S(1)} %get-tuple-element.34), channel_id=1, source_target_pairs={{0,32},{32,64},{64,96},{96,0},{128,160},{160,192},{192,224},{224,1... | collective-permute-start | bytes 245768 | tf_op jit(solution)/shard_map/ppermute | solution.py:74
  116.5 89.8 %collective-permute-start.5 = (f32[4,4,1280]{2,1,0:T(4,128)S(1)}, f32[4,4,1280]{2,1,0:T(4,128)S(1)}, u32[]{:S(2)}, u32[]{:S(2)}) collective-permute-start(f32[4,4,1280]{2,1,0:T(4,128)S(1)} %get-tuple-element.36), channel_id=1, source_target_pairs={{0,64},{32,96},{64,0},{96,32},{128,192},{160,224},{192,128},{224,1... | collective-permute-start | bytes 245768 | tf_op jit(solution)/shard_map/ppermute | solution.py:74
  121.3 85.0 %collective-permute-start.6 = (f32[4,4,1280]{2,1,0:T(4,128)S(1)}, f32[4,4,1280]{2,1,0:T(4,128)S(1)}, u32[]{:S(2)}, u32[]{:S(2)}) collective-permute-start(f32[4,4,1280]{2,1,0:T(4,128)S(1)} %get-tuple-element.35), channel_id=1, source_target_pairs={{0,96},{32,0},{64,32},{96,64},{128,224},{160,128},{192,160},{224,1... | collective-permute-start | bytes 245768 | tf_op jit(solution)/shard_map/ppermute | solution.py:74
  206.4 20.3 %collective-permute-start.7 = (f32[4,1280]{1,0:T(4,128)S(1)}, f32[4,1280]{1,0:T(4,128)S(1)}, u32[]{:S(2)}, u32[]{:S(2)}) collective-permute-start(f32[4,1280]{1,0:T(4,128)S(1)} %get-tuple-element.37), channel_id=1, source_target_pairs={{0,128},{32,160},{64,192},{96,224},{128,256},{160,288},{192,320},{... | collective-permute-start | bytes 61448 | tf_op jit(solution)/shard_map/ppermute | solution.py:74
  213.8 14.4 %collective-permute-start.8 = (f32[4,1280]{1,0:T(4,128)S(1)}, f32[4,1280]{1,0:T(4,128)S(1)}, u32[]{:S(2)}, u32[]{:S(2)}) collective-permute-start(f32[4,1280]{1,0:T(4,128)S(1)} %get-tuple-element.39), channel_id=1, source_target_pairs={{0,256},{32,288},{64,320},{96,352},{128,384},{160,416},{192,448},{... | collective-permute-start | bytes 61448 | tf_op jit(solution)/shard_map/ppermute | solution.py:74
  219.0 9.6 %collective-permute-start.9 = (f32[4,1280]{1,0:T(4,128)S(1)}, f32[4,1280]{1,0:T(4,128)S(1)}, u32[]{:S(2)}, u32[]{:S(2)}) collective-permute-start(f32[4,1280]{1,0:T(4,128)S(1)} %get-tuple-element.38), channel_id=1, source_target_pairs={{0,384},{32,416},{64,448},{96,480},{128,0},{160,32},{192,64},{224,... | collective-permute-start | bytes 61448 | tf_op jit(solution)/shard_map/ppermute | solution.py:74
  228.6 8.7 %collective-permute-start.10 = (f32[4,1280]{1,0:T(4,128)S(1)}, f32[4,1280]{1,0:T(4,128)S(1)}, u32[]{:S(2)}, u32[]{:S(2)}) collective-permute-start(f32[4,1280]{1,0:T(4,128)S(1)} %fusion.46), channel_id=1, source_target_pairs={{0,1},{1,2},{2,3},{3,0},{4,5},{5,6},{6,7},{7,4},{8,9},{9,10},{10,1... | collective-permute-start | bytes 61448 | tf_op jit(solution)/shard_map/ppermute | solution.py:74
  231.0 7.2 %collective-permute-start.11 = (f32[4,1280]{1,0:T(4,128)S(1)}, f32[4,1280]{1,0:T(4,128)S(1)}, u32[]{:S(2)}, u32[]{:S(2)}) collective-permute-start(f32[4,1280]{1,0:T(4,128)S(1)} %fusion.46), channel_id=1, source_target_pairs={{0,2},{1,3},{2,0},{3,1},{4,6},{5,7},{6,4},{7,5},{8,10},{9,11},{10,... | collective-permute-start | bytes 61448 | tf_op jit(solution)/shard_map/ppermute | solution.py:74
  235.4 6.9 %collective-permute-start.12 = (f32[4,1280]{1,0:T(4,128)S(1)}, f32[4,1280]{1,0:T(4,128)S(1)}, u32[]{:S(2)}, u32[]{:S(2)}) collective-permute-start(f32[4,1280]{1,0:T(4,128)S(1)} %fusion.46), channel_id=1, source_target_pairs={{0,3},{1,0},{2,1},{3,2},{4,7},{5,4},{6,5},{7,6},{8,11},{9,8},{10,9... | collective-permute-start | bytes 61448 | tf_op jit(solution)/shard_map/ppermute | solution.py:74
  245.5 20.2 %copy-start.18 = (f32[128]{0:T(128)S(1)}, f32[128]{0:T(128)}, u32[]{:S(2)}) copy-start(f32[128]{0:T(128)} %param.21) | copy-start | bytes 1540
  245.5 20.7 %copy-start.14 = (f32[128,512]{1,0:T(8,128)S(1)}, f32[128,512]{1,0:T(8,128)}, u32[]{:S(2)}) copy-start(f32[128,512]{1,0:T(8,128)} %param.20) | copy-start | bytes 786436
  245.5 20.7 %copy-start.15 = (f32[128,512]{1,0:T(8,128)S(1)}, f32[128,512]{1,0:T(8,128)}, u32[]{:S(2)}) copy-start(f32[128,512]{1,0:T(8,128)} %param.19) | copy-start | bytes 786436
  246.1 12.1 %collective-permute-start.13 = (f32[128,640]{1,0:T(8,128)S(1)}, f32[128,640]{1,0:T(8,128)S(1)}, u32[]{:S(2)}, u32[]{:S(2)}) collective-permute-start(f32[128,640]{1,0:T(8,128)S(1)} %pad_maximum_fusion.1), channel_id=1, source_target_pairs={{0,1},{1,2},{2,3},{3,0},{4,5},{5,6},{6,7},{7,4},{8,9},{9,10},{10,1... | collective-permute-start | bytes 983048 | tf_op jit(solution)/shard_map/ppermute | solution.py:74
  248.6 13.5 %collective-permute-start.14 = (f32[128,640]{1,0:T(8,128)S(1)}, f32[128,640]{1,0:T(8,128)S(1)}, u32[]{:S(2)}, u32[]{:S(2)}) collective-permute-start(f32[128,640]{1,0:T(8,128)S(1)} %pad_maximum_fusion.1), channel_id=1, source_target_pairs={{0,2},{1,3},{2,0},{3,1},{4,6},{5,7},{6,4},{7,5},{8,10},{9,11},{10,... | collective-permute-start | bytes 983048 | tf_op jit(solution)/shard_map/ppermute | solution.py:74
  250.8 14.6 %collective-permute-start.15 = (f32[128,640]{1,0:T(8,128)S(1)}, f32[128,640]{1,0:T(8,128)S(1)}, u32[]{:S(2)}, u32[]{:S(2)}) collective-permute-start(f32[128,640]{1,0:T(8,128)S(1)} %pad_maximum_fusion.1), channel_id=1, source_target_pairs={{0,3},{1,0},{2,1},{3,2},{4,7},{5,4},{6,5},{7,6},{8,11},{9,8},{10,9... | collective-permute-start | bytes 983048 | tf_op jit(solution)/shard_map/ppermute | solution.py:74

commit v4 on v1

--- a/solution.py
+++ b/solution.py
@@ -70,16 +70,36 @@
 ALL_AXES = ("z", "y", "core", "x")
 
 
+def halve_sum(blocks, axis, size, dim):
+    me = lax.axis_index(axis)
+    lead = blocks.shape[:dim]
+    bits = size.bit_length() - 1
+    blocks = blocks.reshape(lead + (2,) * bits + blocks.shape[dim + 1 :])
+    for bit in range(bits):
+        at = dim + bits - 1 - bit
+        mine = (me >> bit) & 1
+        keep = lax.dynamic_index_in_dim(blocks, mine, at, keepdims=True)
+        send = lax.dynamic_index_in_dim(blocks, 1 - mine, at, keepdims=True)
+        pairs = [(i, i ^ (1 << bit)) for i in range(size)]
+        blocks = keep + lax.ppermute(send, axis, pairs)
+    return blocks.reshape(lead + blocks.shape[dim + bits :])
+
+
+def double_sum(value, axis, size):
+    for bit in range(size.bit_length() - 1):
+        value = value + lax.ppermute(value, axis, [(i, i ^ (1 << bit)) for i in range(size)])
+    return value
+
+
 def reduce_weights(partial, sizes):
     width = partial.shape[1]
-    blocks = partial.reshape(tuple(sizes[a] for a in ROW_AXES) + (-1, width))
-    for i, ax in enumerate(ROW_AXES):
-        moved = jnp.moveaxis(blocks, i, 0)
-        rest = moved.shape[1:]
-        flat = moved.reshape(moved.shape[0], -1, 128)
-        flat = lax.psum_scatter(flat, ax, scatter_dimension=0, tiled=True)
-        blocks = jnp.moveaxis(flat.reshape((1,) + rest), 0, i)
-    return lax.psum(blocks.reshape(-1, width), "x")
+    n_z, n_y, n_c = sizes["z"], sizes["y"], sizes["core"]
+    per_owner = partial.shape[0] // (n_z * n_y * n_c)
+    blocks = partial.reshape(n_z, n_y, n_c, per_owner, width)
+    blocks = halve_sum(blocks, "core", n_c, 2)
+    blocks = halve_sum(blocks, "y", n_y, 1)
+    blocks = halve_sum(blocks, "z", n_z, 0)
+    return blocks.reshape(per_owner, width)
 
 
 def local(sizes, tokens, out_grad, seq_lengths, owners, slots, w_in, w_out, emb_rows, emb_mom, emb_var):
@@ -111,8 +131,6 @@
         ),
         sizes,
     )
-    w_in_grad = weight_share[:, :in_cols]
-    w_out_grad = weight_share[:, in_cols:]
     capacity = max(2, 4 * tok_count // owner_count)
     buffer_rows = owner_count * capacity
     owner_of = owners[:, 0]
@@ -137,13 +155,31 @@
     arrived = lax.all_to_all(
         jnp.concatenate([outgoing, slot_row], axis=1), ROW_AXES, 0, 0, tiled=True
     )
+    arrived, weight_share = lax.optimization_barrier((arrived, weight_share))
     received = arrived[:, :capacity, :].reshape(buffer_rows, width)
     got_slots = arrived[:, capacity, :capacity].astype(jnp.int32).reshape(buffer_rows)
     slot_count = emb_rows.shape[0]
     matches = got_slots[None, :] == jnp.arange(slot_count, dtype=jnp.int32)[:, None]
     grad_part = jnp.dot(matches.astype(jnp.bfloat16), received, preferred_element_type=jnp.float32)
     count_part = jnp.sum(matches.astype(jnp.float32), axis=1)
-    grad_all, count_all = lax.psum((grad_part, count_part), "x")
+    lanes = width + 128
+    both = double_sum(
+        jnp.concatenate(
+            [
+                jnp.concatenate(
+                    [grad_part, jnp.broadcast_to(count_part[:, None], (slot_count, 128))], axis=1
+                ),
+                weight_share.reshape(-1, lanes),
+            ],
+            axis=0,
+        ),
+        "x",
+        sizes["x"],
+    )
+    grad_all, count_all = both[:slot_count, :width], both[:slot_count, width]
+    weight_share = both[slot_count:].reshape(weight_share.shape)
+    w_in_grad = weight_share[:, :in_cols]
+    w_out_grad = weight_share[:, in_cols:]
     new_rows, new_mom, new_var = row_adam(emb_rows, emb_mom, emb_var, grad_all, count_all)
     return (new_rows, new_mom, new_var, w_in_grad, w_out_grad)
 

time: 366 us -> 265 us (0.72)
  waiting for transfers between devices: 250 us -> 138 us
  starting transfers between devices: 20.6 us -> 61.1 us
  blocking collectives: 14.4 us -> 0 us
  between operations: 15.5 us -> 1.21 us
    reduce_scatter x2 -> x0, waiting for transfers between devices: 189 us -> none  [reduce_weights(): flat = lax.psum_scatter(flat, ax, scatter_dimension=0, tiled=True)]
    ppermute x0 -> x9, waiting for transfers between devices: none -> 138 us  [the longest x7 123 us: halve_sum(): blocks = keep + lax.ppermute(send, axis, pairs)]
    psum x1 -> x0, waiting for transfers between devices: 41.4 us -> none  [local(): grad_all, count_all = lax.psum((grad_part, count_part), 'x')]
    ppermute x0 -> x9, starting transfers between devices: none -> 40.7 us  [the longest x7 35.2 us: halve_sum(): blocks = keep + lax.ppermute(send, axis, pairs)]
    unnamed x5 -> x0, waiting for transfers between devices: 20.4 us -> none
    psum x1 -> x0, blocking collectives: 14.4 us -> none  [local(): grad_all, count_all = lax.psum((grad_part, count_part), 'x')]
    another operation x2 -> x0, local copies, waits for them, and re-layouts: 4.37 us -> none  [the longest x1 3.63 us: reduce_weights(): flat = moved.reshape(moved.shape[0], -1, 128)]
    reshape x0 -> x3, local copies, waits for them, and re-layouts: none -> 3.97 us  [the longest x1 3.95 us: reduce_weights(): blocks = partial.reshape(n_z, n_y, n_c, per_owner, width)]
  transfers between devices with their start and end apart: 5 -> 10, of which waited for: 4 -> 9; matrix products, arithmetic and copies ran while one was open for 3% -> 5% of each run, Pallas kernels for 0% -> 0%
where the time goes in v4:
time: 265 us; the launch traced here: 264 us
  waiting for transfers between devices  138 us (52%)
  starting transfers between devices  61.1 us (23%)
  matrix products  24.8 us (9%)
  other arithmetic  19.5 us (7%)
  local copies, waits for them, and re-layouts  19.2 us (7%)
    ppermute x7, waiting for transfers between devices, halve_sum(): blocks = keep + lax.ppermute(send, axis, pairs)  123 us
    ppermute x7, starting transfers between devices, halve_sum(): blocks = keep + lax.ppermute(send, axis, pairs)  35.2 us
    all_to_all x1, starting transfers between devices, local(): lax.all_to_all(jnp.concatenate([outgoing, slot_row], axis=1), ROW_AXES, 0...  20.4 us
    ppermute x2, waiting for transfers between devices, double_sum(): lax.ppermute(value, axis, [(i, i ^ 1 << bit) for i in range(size)])  15 us
    dot_general x3, matrix products, core(): jnp.einsum('hts,shd->thd', weights, values_part, preferred_element_type=j...  7.52 us
    dot_general x3, matrix products, core(): jnp.einsum('thd,shd->hts', queries, keys_part, preferred_element_type=jnp...  6.15 us
    ppermute x2, starting transfers between devices, double_sum(): lax.ppermute(value, axis, [(i, i ^ 1 << bit) for i in range(size)])  5.48 us
  transfers between devices with their start and end apart: 10, of which 9 were waited for; matrix products, arithmetic and copies ran while one was open for 5% of the time, Pallas kernels for 0%

profile of v4, /device:TPU:6, one launch (start us, length us, event | category | flops | bytes accessed | tf_op | source)
XLA Modules:
  0.0 264.2 jit_solution(6124821462022835547)
XLA Ops:
  0.7 0.9 reduce-window.8
  1.9 1.2 fusion.22
  3.1 0.2 copy.56
  3.6 2.3 multiply_convert_fusion.1
  5.9 1.1 copy-done.4
  6.9 0.8 fusion.45
  8.0 1.2 copy.57
  9.2 3.5 %multiply_convert_fusion = (bf16[4,512,512]{2,1,0:T(8,128)(2,1)S(1)}, f32[4,512,512]{2,1,0:T(8,128)}) fusion(f32[512,512]{1,0:T(8,128)S(1)} %fusion.23, bf16[512,4,64]{0,2,1:T(8,128)(2,1)S(1)} %bitcast.61, bf16[512,4,64]{0,2,1:T(8,128)(2,1)S(1)} %bitcast.63), kind=kOutput, calls=%fused_computation.7 | convolution fusion | flops 142606336 | bytes 7864320 | tf_op jit(solution)/shard_map/jvp(thd,shd->hts)/dot_general | solution.py:46
  12.7 1.3 copy-done.1
  14.0 0.8 fusion.46
  14.8 0.2 copy.60
  15.1 1.4 multiply_reduce_fusion
  16.5 1.9 fusion.44
  18.5 0.8 broadcast_add_fusion
  19.3 1.1 copy.62
  20.4 2.2 fusion.49
  22.7 4.6 %fusion.3 = bf16[4,512,512]{2,1,0:T(8,128)(2,1)S(1)} fusion(f32[4,512,512]{2,1,0:T(8,128)} %get-tuple-element.36, f32[512,512]{1,0:T(8,128)S(1)} %copy-done.11, bf16[4,64,512]{2,1,0:T(8,128)(2,1)} %bitcast.69, bf16[512,4,64]{0,2,1:T(8,128)(2,1)} %bitcast.66), kind=kOutput, calls=%fused_computation.5 | convolution fusion | flops 148897792 | bytes 7864320 | tf_op jit(solution)/shard_map/transpose(jvp(hts,shd->thd))/dot_general | solution.py:50
  27.3 1.5 fusion.48
  28.7 1.2 fusion.47
  29.9 1.0 copy.66
  31.0 1.1 copy.64
  32.1 0.8 copy.65
  33.0 2.5 fusion.8
  35.5 0.8 fusion.18
  36.3 0.2 copy-done.3
  36.5 1.0 copy-done.10
  37.5 0.3 fusion.29
  37.7 0.2 convert_reduce_fusion.2
  38.0 0.5 select_reduce_fusion
  38.7 2.8 %fusion.6 = bf16[2048,512]{1,0:T(8,128)(2,1)S(1)} fusion(s32[512]{0:T(512)S(1)} %get-tuple-element.43, bf16[512,512]{0,1:T(8,128)(2,1)S(1)} %copy-done.13, f32[512]{0:T(512)S(1)} %negate_multiply_fusion, bf16[512,512]{0,1:T(8,128)(2,1)S(1)} %copy.56, f32[512,512]{0,1:T(8,128)} %copy-done.10, f32[512]{0:T(512)S(1)} %multiply_multiply_fusion, ...), kind=kOutput, calls=%fused_computation.13 | convolution fusion | flops 1078460416 | bytes 4204544 | tf_op jit(solution)/shard_map/dot_general | solution.py:146
  41.5 2.0 fusion.5
  43.5 20.4 %all-to-all-start = ((bf16[128,17,512]{2,1,0:T(8,128)(2,1)}), bf16[128,17,512]{2,1,0:T(8,128)(2,1)}, u32[]{:S(2)}, u32[]{:S(2)}) async-start(bf16[128,17,512]{2,1,0:T(8,128)(2,1)} %fusion.5), calls=%async_computation | async-start | bytes 6291456 | tf_op jit(solution)/shard_map/all_to_all | solution.py:155
  63.9 1.5 convolution_bitcast_fusion
  65.4 1.9 fusion.30
  67.4 1.8 pad_maximum_fusion
  69.1 3.9 %reshape.254 = f32[16,4,2,4,1280]{4,3,2,1,0:T(4,128)} reshape(f32[512,1280]{1,0:T(8,128)} %pad_maximum_fusion) | data formatting | bytes 5242880 | tf_op jit(solution)/shard_map/reshape | solution.py:98
  73.1 1.4 constant_dynamic-slice_fusion.6
  74.5 1.9 collective-permute-start
  76.4 3.1 %collective-permute-done = f32[16,4,1,4,1280]{4,3,2,1,0:T(4,128)} collective-permute-done((f32[16,4,1,4,1280]{4,3,2,1,0:T(4,128)S(1)}, f32[16,4,1,4,1280]{4,3,2,1,0:T(4,128)}, u32[]{:S(2)}, u32[]{:S(2)}) %collective-permute-start) | collective-permute-done | bytes 1310752 | tf_op jit(solution)/shard_map/ppermute | solution.py:84
  79.5 2.1 dynamic-slice_add_fusion
  81.7 3.0 %collective-permute-start.1 = (f32[16,2,1,4,1280]{4,3,2,1,0:T(4,128)S(1)}, f32[16,2,1,4,1280]{4,3,2,1,0:T(4,128)}, u32[]{:S(2)}, u32[]{:S(2)}) collective-permute-start(f32[16,2,1,4,1280]{4,3,2,1,0:T(4,128)S(1)} %constant_dynamic-slice_fusion.5), channel_id=1, source_target_pairs={{0,8},{8,0},{16,24},{24,16},{1,9},{9,1},{17,25},{25,17},{2,10},{10... | collective-permute-start | bytes 1966088 | tf_op jit(solution)/shard_map/ppermute | solution.py:84
  84.6 20.6 %collective-permute-done.1 = f32[16,2,1,4,1280]{4,3,2,1,0:T(4,128)} collective-permute-done((f32[16,2,1,4,1280]{4,3,2,1,0:T(4,128)S(1)}, f32[16,2,1,4,1280]{4,3,2,1,0:T(4,128)}, u32[]{:S(2)}, u32[]{:S(2)}) %collective-permute-start.1) | collective-permute-done | bytes 655392 | tf_op jit(solution)/shard_map/ppermute | solution.py:84
  105.2 1.3 dynamic-slice_add_fusion.1
  106.5 4.0 %collective-permute-start.2 = (f32[16,1,1,4,1280]{4,3,2,1,0:T(4,128)S(1)}, f32[16,1,1,4,1280]{4,3,2,1,0:T(4,128)S(1)}, u32[]{:S(2)}, u32[]{:S(2)}) collective-permute-start(f32[16,1,1,4,1280]{4,3,2,1,0:T(4,128)S(1)} %constant_dynamic-slice_fusion.4), channel_id=1, source_target_pairs={{0,16},{8,24},{16,0},{24,8},{1,17},{9,25},{17,1},{25,9},{2,18},{10... | collective-permute-start | bytes 983048 | tf_op jit(solution)/shard_map/ppermute | solution.py:84
  110.5 10.8 %collective-permute-done.2 = f32[16,1,1,4,1280]{4,3,2,1,0:T(4,128)S(1)} collective-permute-done((f32[16,1,1,4,1280]{4,3,2,1,0:T(4,128)S(1)}, f32[16,1,1,4,1280]{4,3,2,1,0:T(4,128)S(1)}, u32[]{:S(2)}, u32[]{:S(2)}) %collective-permute-start.2) | collective-permute-done | bytes 327712 | tf_op jit(solution)/shard_map/ppermute | solution.py:84
  121.4 3.2 %collective-permute-start.3 = (f32[2,2,2,1,4,1280]{5,4,3,2,1,0:T(4,128)S(1)}, f32[2,2,2,1,4,1280]{5,4,3,2,1,0:T(4,128)S(1)}, u32[]{:S(2)}, u32[]{:S(2)}) collective-permute-start(f32[2,2,2,1,4,1280]{5,4,3,2,1,0:T(4,128)S(1)} %constant_dynamic-slice_fusion.3), channel_id=1, source_target_pairs={{0,32},{32,0},{64,96},{96,64},{128,160},{160,128},{192,224},{224,1... | collective-permute-start | bytes 491528 | tf_op jit(solution)/shard_map/ppermute | solution.py:84
  124.7 78.7 %collective-permute-done.3 = f32[2,2,2,1,4,1280]{5,4,3,2,1,0:T(4,128)S(1)} collective-permute-done((f32[2,2,2,1,4,1280]{5,4,3,2,1,0:T(4,128)S(1)}, f32[2,2,2,1,4,1280]{5,4,3,2,1,0:T(4,128)S(1)}, u32[]{:S(2)}, u32[]{:S(2)}) %collective-permute-start.3) | collective-permute-done | bytes 163872 | tf_op jit(solution)/shard_map/ppermute | solution.py:84
  203.4 3.7 %collective-permute-start.4 = (f32[2,2,1,1,4,1280]{5,4,3,2,1,0:T(4,128)S(1)}, f32[2,2,1,1,4,1280]{5,4,3,2,1,0:T(4,128)S(1)}, u32[]{:S(2)}, u32[]{:S(2)}) collective-permute-start(f32[2,2,1,1,4,1280]{5,4,3,2,1,0:T(4,128)S(1)} %constant_dynamic-slice_fusion.2), channel_id=1, source_target_pairs={{0,64},{32,96},{64,0},{96,32},{128,192},{160,224},{192,128},{224,1... | collective-permute-start | bytes 245768 | tf_op jit(solution)/shard_map/ppermute | solution.py:84
  207.1 4.6 %collective-permute-done.4 = f32[2,2,1,1,4,1280]{5,4,3,2,1,0:T(4,128)S(1)} collective-permute-done((f32[2,2,1,1,4,1280]{5,4,3,2,1,0:T(4,128)S(1)}, f32[2,2,1,1,4,1280]{5,4,3,2,1,0:T(4,128)S(1)}, u32[]{:S(2)}, u32[]{:S(2)}) %collective-permute-start.4) | collective-permute-done | bytes 81952 | tf_op jit(solution)/shard_map/ppermute | solution.py:84
  211.8 7.5 %collective-permute-start.5 = (f32[2,1,1,1,4,1280]{5,4,3,2,1,0:T(4,128)S(1)}, f32[2,1,1,1,4,1280]{5,4,3,2,1,0:T(4,128)S(1)}, u32[]{:S(2)}, u32[]{:S(2)}) collective-permute-start(f32[2,1,1,1,4,1280]{5,4,3,2,1,0:T(4,128)S(1)} %constant_dynamic-slice_fusion.1), channel_id=1, source_target_pairs={{0,128},{32,160},{64,192},{96,224},{128,0},{160,32},{192,64},{224,... | collective-permute-start | bytes 122888 | tf_op jit(solution)/shard_map/ppermute | solution.py:84
  219.3 3.1 %collective-permute-done.5 = f32[2,1,1,1,4,1280]{5,4,3,2,1,0:T(4,128)S(1)} collective-permute-done((f32[2,1,1,1,4,1280]{5,4,3,2,1,0:T(4,128)S(1)}, f32[2,1,1,1,4,1280]{5,4,3,2,1,0:T(4,128)S(1)}, u32[]{:S(2)}, u32[]{:S(2)}) %collective-permute-start.5) | collective-permute-done | bytes 40992 | tf_op jit(solution)/shard_map/ppermute | solution.py:84
  222.5 11.9 %collective-permute-start.6 = (f32[1,1,1,1,4,1280]{5,4,3,2,1,0:T(4,128)S(1)}, f32[1,1,1,1,4,1280]{5,4,3,2,1,0:T(4,128)S(1)}, u32[]{:S(2)}, u32[]{:S(2)}) collective-permute-start(f32[1,1,1,1,4,1280]{5,4,3,2,1,0:T(4,128)S(1)} %constant_dynamic-slice_fusion), channel_id=1, source_target_pairs={{0,256},{32,288},{64,320},{96,352},{128,384},{160,416},{192,448},{... | collective-permute-start | bytes 61448 | tf_op jit(solution)/shard_map/ppermute | solution.py:84
  234.4 2.5 collective-permute-done.6
  236.9 1.8 slice.45
  238.7 1.2 convert_reduce_fusion.3
  240.1 0.4 fusion.19
  240.8 2.7 %collective-permute-start.7 = (f32[136,640]{1,0:T(8,128)S(1)}, f32[136,640]{1,0:T(8,128)S(1)}, u32[]{:S(2)}, u32[]{:S(2)}) collective-permute-start(f32[136,640]{1,0:T(8,128)S(1)} %pad_maximum_fusion.1), channel_id=1, source_target_pairs={{0,1},{1,0},{2,3},{3,2},{4,5},{5,4},{6,7},{7,6},{8,9},{9,8},{10,11... | collective-permute-start | bytes 1044488 | tf_op jit(solution)/shard_map/ppermute | solution.py:90
  243.5 7.0 %collective-permute-done.7 = f32[136,640]{1,0:T(8,128)S(1)} collective-permute-done((f32[136,640]{1,0:T(8,128)S(1)}, f32[136,640]{1,0:T(8,128)S(1)}, u32[]{:S(2)}, u32[]{:S(2)}) %collective-permute-start.7) | collective-permute-done | bytes 348192 | tf_op jit(solution)/shard_map/ppermute | solution.py:90
  250.6 2.7 %collective-permute-start.8 = (f32[136,640]{1,0:T(8,128)S(1)}, f32[136,640]{1,0:T(8,128)S(1)}, u32[]{:S(2)}, u32[]{:S(2)}) collective-permute-start(f32[136,640]{1,0:T(8,128)S(1)} %fusion.43), channel_id=1, source_target_pairs={{0,2},{1,3},{2,0},{3,1},{4,6},{5,7},{6,4},{7,5},{8,10},{9,11},{10,... | collective-permute-start | bytes 1044488 | tf_op jit(solution)/shard_map/ppermute | solution.py:90
  253.3 7.9 %collective-permute-done.8 = f32[136,640]{1,0:T(8,128)S(1)} collective-permute-done((f32[136,640]{1,0:T(8,128)S(1)}, f32[136,640]{1,0:T(8,128)S(1)}, u32[]{:S(2)}, u32[]{:S(2)}) %collective-permute-start.8) | collective-permute-done | bytes 348192 | tf_op jit(solution)/shard_map/ppermute | solution.py:90
  261.6 0.6 slice.54
  262.2 0.6 slice.55
  262.8 0.5 fusion.42
  263.3 0.9 fusion.37
  (75 shorter events, 2.3 us)
Async XLA Ops:
  0.6 3.0 %copy-start = (bf16[512,1024]{1,0:T(8,128)(2,1)S(1)}, bf16[512,1024]{1,0:T(8,128)(2,1)}, u32[]{:S(2)}) copy-start(bf16[512,1024]{1,0:T(8,128)(2,1)} %param.17) | copy-start | bytes 3145732
  0.6 2.4 copy-start.12
  5.9 1.1 copy-start.4
  8.0 4.7 %copy-start.5 = (bf16[512,256]{0,1:T(8,128)(2,1)}, bf16[512,256]{0,1:T(8,128)(2,1)S(1)}, u32[]{:S(2)}) copy-start(bf16[512,256]{0,1:T(8,128)(2,1)S(1)} %copy.59) | copy-start | bytes 786436
  9.2 3.5 %copy-start.7 = (bf16[512,256]{0,1:T(8,128)(2,1)}, bf16[512,256]{0,1:T(8,128)(2,1)S(1)}, u32[]{:S(2)}) copy-start(bf16[512,256]{0,1:T(8,128)(2,1)S(1)} %copy.57) | copy-start | bytes 786436
  12.7 1.3 copy-start.1
  14.0 1.1 copy-start.2
  20.4 2.2 copy-start.8
  20.4 2.2 copy-start.11
  22.6 4.6 %copy-start.6 = (bf16[512,256]{0,1:T(8,128)(2,1)S(1)}, bf16[512,256]{0,1:T(8,128)(2,1)}, u32[]{:S(2)}) copy-start(bf16[512,256]{0,1:T(8,128)(2,1)} %copy-done.5) | copy-start | bytes 786436
  29.9 2.2 copy-start.9
  35.5 1.0 copy-start.3
  35.5 2.2 copy-start.16
  35.5 2.5 copy-start.17
  35.5 3.1 %copy-start.13 = (bf16[512,512]{0,1:T(8,128)(2,1)S(1)}, bf16[512,512]{0,1:T(8,128)(2,1)}, u32[]{:S(2)}) copy-start(bf16[512,512]{0,1:T(8,128)(2,1)} %copy.66) | copy-start | bytes 1572868
  36.5 1.0 copy-start.10
  43.5 193.4 %all-to-all-start = ((bf16[128,17,512]{2,1,0:T(8,128)(2,1)}), bf16[128,17,512]{2,1,0:T(8,128)(2,1)}, u32[]{:S(2)}, u32[]{:S(2)}) async-start(bf16[128,17,512]{2,1,0:T(8,128)(2,1)} %fusion.5), calls=%async_computation | async-start | bytes 6291456 | tf_op jit(solution)/shard_map/all_to_all | solution.py:155
  74.5 5.1 %collective-permute-start = (f32[16,4,1,4,1280]{4,3,2,1,0:T(4,128)S(1)}, f32[16,4,1,4,1280]{4,3,2,1,0:T(4,128)}, u32[]{:S(2)}, u32[]{:S(2)}) collective-permute-start(f32[16,4,1,4,1280]{4,3,2,1,0:T(4,128)S(1)} %constant_dynamic-slice_fusion.6), channel_id=1, source_target_pairs={{0,4},{4,0},{1,5},{5,1},{2,6},{6,2},{3,7},{7,3},{8,12},{12,8},{9,1... | collective-permute-start | bytes 3932168 | tf_op jit(solution)/shard_map/ppermute | solution.py:84
  81.7 23.6 %collective-permute-start.1 = (f32[16,2,1,4,1280]{4,3,2,1,0:T(4,128)S(1)}, f32[16,2,1,4,1280]{4,3,2,1,0:T(4,128)}, u32[]{:S(2)}, u32[]{:S(2)}) collective-permute-start(f32[16,2,1,4,1280]{4,3,2,1,0:T(4,128)S(1)} %constant_dynamic-slice_fusion.5), channel_id=1, source_target_pairs={{0,8},{8,0},{16,24},{24,16},{1,9},{9,1},{17,25},{25,17},{2,10},{10... | collective-permute-start | bytes 1966088 | tf_op jit(solution)/shard_map/ppermute | solution.py:84
  106.5 14.8 %collective-permute-start.2 = (f32[16,1,1,4,1280]{4,3,2,1,0:T(4,128)S(1)}, f32[16,1,1,4,1280]{4,3,2,1,0:T(4,128)S(1)}, u32[]{:S(2)}, u32[]{:S(2)}) collective-permute-start(f32[16,1,1,4,1280]{4,3,2,1,0:T(4,128)S(1)} %constant_dynamic-slice_fusion.4), channel_id=1, source_target_pairs={{0,16},{8,24},{16,0},{24,8},{1,17},{9,25},{17,1},{25,9},{2,18},{10... | collective-permute-start | bytes 983048 | tf_op jit(solution)/shard_map/ppermute | solution.py:84
  121.4 81.9 %collective-permute-start.3 = (f32[2,2,2,1,4,1280]{5,4,3,2,1,0:T(4,128)S(1)}, f32[2,2,2,1,4,1280]{5,4,3,2,1,0:T(4,128)S(1)}, u32[]{:S(2)}, u32[]{:S(2)}) collective-permute-start(f32[2,2,2,1,4,1280]{5,4,3,2,1,0:T(4,128)S(1)} %constant_dynamic-slice_fusion.3), channel_id=1, source_target_pairs={{0,32},{32,0},{64,96},{96,64},{128,160},{160,128},{192,224},{224,1... | collective-permute-start | bytes 491528 | tf_op jit(solution)/shard_map/ppermute | solution.py:84
  203.4 8.3 %collective-permute-start.4 = (f32[2,2,1,1,4,1280]{5,4,3,2,1,0:T(4,128)S(1)}, f32[2,2,1,1,4,1280]{5,4,3,2,1,0:T(4,128)S(1)}, u32[]{:S(2)}, u32[]{:S(2)}) collective-permute-start(f32[2,2,1,1,4,1280]{5,4,3,2,1,0:T(4,128)S(1)} %constant_dynamic-slice_fusion.2), channel_id=1, source_target_pairs={{0,64},{32,96},{64,0},{96,32},{128,192},{160,224},{192,128},{224,1... | collective-permute-start | bytes 245768 | tf_op jit(solution)/shard_map/ppermute | solution.py:84
  211.8 10.7 %collective-permute-start.5 = (f32[2,1,1,1,4,1280]{5,4,3,2,1,0:T(4,128)S(1)}, f32[2,1,1,1,4,1280]{5,4,3,2,1,0:T(4,128)S(1)}, u32[]{:S(2)}, u32[]{:S(2)}) collective-permute-start(f32[2,1,1,1,4,1280]{5,4,3,2,1,0:T(4,128)S(1)} %constant_dynamic-slice_fusion.1), channel_id=1, source_target_pairs={{0,128},{32,160},{64,192},{96,224},{128,0},{160,32},{192,64},{224,... | collective-permute-start | bytes 122888 | tf_op jit(solution)/shard_map/ppermute | solution.py:84
  222.5 14.4 %collective-permute-start.6 = (f32[1,1,1,1,4,1280]{5,4,3,2,1,0:T(4,128)S(1)}, f32[1,1,1,1,4,1280]{5,4,3,2,1,0:T(4,128)S(1)}, u32[]{:S(2)}, u32[]{:S(2)}) collective-permute-start(f32[1,1,1,1,4,1280]{5,4,3,2,1,0:T(4,128)S(1)} %constant_dynamic-slice_fusion), channel_id=1, source_target_pairs={{0,256},{32,288},{64,320},{96,352},{128,384},{160,416},{192,448},{... | collective-permute-start | bytes 61448 | tf_op jit(solution)/shard_map/ppermute | solution.py:84
  240.6 22.2 %copy-start.18 = (f32[128]{0:T(128)S(1)}, f32[128]{0:T(128)}, u32[]{:S(2)}) copy-start(f32[128]{0:T(128)} %param.21) | copy-start | bytes 1540
  240.6 22.7 %copy-start.14 = (f32[128,512]{1,0:T(8,128)S(1)}, f32[128,512]{1,0:T(8,128)}, u32[]{:S(2)}) copy-start(f32[128,512]{1,0:T(8,128)} %param.20) | copy-start | bytes 786436
  240.6 22.7 %copy-start.15 = (f32[128,512]{1,0:T(8,128)S(1)}, f32[128,512]{1,0:T(8,128)}, u32[]{:S(2)}) copy-start(f32[128,512]{1,0:T(8,128)} %param.19) | copy-start | bytes 786436
  240.8 9.8 %collective-permute-start.7 = (f32[136,640]{1,0:T(8,128)S(1)}, f32[136,640]{1,0:T(8,128)S(1)}, u32[]{:S(2)}, u32[]{:S(2)}) collective-permute-start(f32[136,640]{1,0:T(8,128)S(1)} %pad_maximum_fusion.1), channel_id=1, source_target_pairs={{0,1},{1,0},{2,3},{3,2},{4,5},{5,4},{6,7},{7,6},{8,9},{9,8},{10,11... | collective-permute-start | bytes 1044488 | tf_op jit(solution)/shard_map/ppermute | solution.py:90
  250.6 10.7 %collective-permute-start.8 = (f32[136,640]{1,0:T(8,128)S(1)}, f32[136,640]{1,0:T(8,128)S(1)}, u32[]{:S(2)}, u32[]{:S(2)}) collective-permute-start(f32[136,640]{1,0:T(8,128)S(1)} %fusion.43), channel_id=1, source_target_pairs={{0,2},{1,3},{2,0},{3,1},{4,6},{5,7},{6,4},{7,5},{8,10},{9,11},{10,... | collective-permute-start | bytes 1044488 | tf_op jit(solution)/shard_map/ppermute | solution.py:90

commit v5 on v4

--- a/solution.py
+++ b/solution.py
@@ -131,6 +131,7 @@
         ),
         sizes,
     )
+    emb_grad, weight_share = lax.optimization_barrier((emb_grad, weight_share))
     capacity = max(2, 4 * tok_count // owner_count)
     buffer_rows = owner_count * capacity
     owner_of = owners[:, 0]
@@ -155,7 +156,6 @@
     arrived = lax.all_to_all(
         jnp.concatenate([outgoing, slot_row], axis=1), ROW_AXES, 0, 0, tiled=True
     )
-    arrived, weight_share = lax.optimization_barrier((arrived, weight_share))
     received = arrived[:, :capacity, :].reshape(buffer_rows, width)
     got_slots = arrived[:, capacity, :capacity].astype(jnp.int32).reshape(buffer_rows)
     slot_count = emb_rows.shape[0]

time: 265 us -> 325 us (1.23); the launches traced: 264 us -> 320 us
  waiting for transfers between devices: 138 us -> 187 us
  starting transfers between devices: 61.1 us -> 68 us
    all_to_all x1, waiting for transfers between devices: 0.01 us -> 142 us  [local(): lax.all_to_all(jnp.concatenate([outgoing, slot_row], axis=1), ROW_AXES, 0...]
    ppermute x7, waiting for transfers between devices: 123 us -> 30.6 us  [halve_sum(): blocks = keep + lax.ppermute(send, axis, pairs)]
    ppermute x7, starting transfers between devices: 35.2 us -> 44.4 us  [halve_sum(): blocks = keep + lax.ppermute(send, axis, pairs)]
  transfers between devices with their start and end apart: 10 -> 10, of which waited for: 9 -> 10; matrix products, arithmetic and copies ran while one was open for 5% -> 1% of each run, Pallas kernels for 0% -> 0%
where the time goes in v5:
time: 325 us; the launch traced here: 320 us
  waiting for transfers between devices  187 us (58%)
  starting transfers between devices  68 us (21%)
  matrix products  24.7 us (8%)
  other arithmetic  20.9 us (6%)
  local copies, waits for them, and re-layouts  18.3 us (6%)
    all_to_all x1, waiting for transfers between devices, local(): lax.all_to_all(jnp.concatenate([outgoing, slot_row], axis=1), ROW_AXES, 0...  142 us
    ppermute x7, starting transfers between devices, halve_sum(): blocks = keep + lax.ppermute(send, axis, pairs)  44.4 us
    ppermute x7, waiting for transfers between devices, halve_sum(): blocks = keep + lax.ppermute(send, axis, pairs)  30.6 us
    all_to_all x1, starting transfers between devices, local(): lax.all_to_all(jnp.concatenate([outgoing, slot_row], axis=1), ROW_AXES, 0...  17.3 us
    ppermute x2, waiting for transfers between devices, double_sum(): lax.ppermute(value, axis, [(i, i ^ 1 << bit) for i in range(size)])  14.6 us
    dot_general x3, matrix products, core(): jnp.einsum('hts,shd->thd', weights, values_part, preferred_element_type=j...  7.64 us
    dot_general x3, matrix products, core(): jnp.einsum('thd,shd->hts', queries, keys_part, preferred_element_type=jnp...  7.46 us
  transfers between devices with their start and end apart: 10, of which 10 were waited for; matrix products, arithmetic and copies ran while one was open for 1% of the time, Pallas kernels for 0%

profile of v5, /device:TPU:6, one launch (start us, length us, event | category | flops | bytes accessed | tf_op | source)
XLA Modules:
  0.0 320.0 jit_solution(13970627620168776108)
XLA Ops:
  0.7 0.9 reduce-window.8
  1.7 1.2 fusion.23
  2.9 1.2 fusion.22
  4.1 0.2 copy.56
  4.6 2.3 multiply_convert_fusion.1
  6.9 1.1 copy-done.4
  8.5 4.8 %multiply_convert_fusion = (bf16[4,512,512]{2,1,0:T(8,128)(2,1)S(1)}, f32[4,512,512]{2,1,0:T(8,128)}) fusion(f32[512,512]{1,0:T(8,128)} %fusion.23, bf16[512,4,64]{0,2,1:T(8,128)(2,1)S(1)} %bitcast.62, bf16[512,4,64]{0,2,1:T(8,128)(2,1)S(1)} %bitcast.64), kind=kOutput, calls=%fused_computation.7 | convolution fusion | flops 142606336 | bytes 7864320 | tf_op jit(solution)/shard_map/jvp(thd,shd->hts)/dot_general | solution.py:46
  13.3 1.3 copy-done.1
  14.6 0.8 fusion.46
  15.7 1.4 multiply_reduce_fusion
  17.1 1.9 fusion.44
  19.1 0.8 broadcast_add_fusion
  19.9 1.1 copy.62
  21.0 2.9 fusion.49
  23.9 4.0 %fusion.3 = bf16[4,512,512]{2,1,0:T(8,128)(2,1)S(1)} fusion(f32[4,512,512]{2,1,0:T(8,128)} %get-tuple-element.36, f32[512,512]{1,0:T(8,128)S(1)} %copy-done.10, bf16[4,64,512]{2,1,0:T(8,128)(2,1)S(1)} %bitcast.72, bf16[512,4,64]{0,2,1:T(8,128)(2,1)} %bitcast.67), kind=kOutput, calls=%fused_computation.5 | convolution fusion | flops 148897792 | bytes 7864320 | tf_op jit(solution)/shard_map/transpose(jvp(hts,shd->thd))/dot_general | solution.py:50
  27.9 1.5 fusion.48
  29.4 1.2 fusion.47
  30.6 1.5 convolution_bitcast_fusion
  32.1 1.1 copy.63
  33.4 1.1 copy.65
  34.4 2.4 fusion.8
  36.9 1.0 copy-done.3
  37.9 0.7 fusion.29
  38.6 1.7 pad_maximum_fusion
  40.3 3.9 %reshape.253 = f32[16,4,2,4,1280]{4,3,2,1,0:T(4,128)} reshape(f32[512,1280]{1,0:T(8,128)} %pad_maximum_fusion) | data formatting | bytes 5242880 | tf_op jit(solution)/shard_map/reshape | solution.py:98
  44.2 1.4 constant_dynamic-slice_fusion.6
  45.7 1.9 collective-permute-start
  47.6 3.1 collective-permute-done
  50.7 2.1 dynamic-slice_add_fusion
  52.8 0.9 constant_dynamic-slice_fusion.5
  53.7 3.7 %collective-permute-start.1 = (f32[16,2,1,4,1280]{4,3,2,1,0:T(4,128)}, f32[16,2,1,4,1280]{4,3,2,1,0:T(4,128)}, u32[]{:S(2)}, u32[]{:S(2)}) collective-permute-start(f32[16,2,1,4,1280]{4,3,2,1,0:T(4,128)} %constant_dynamic-slice_fusion.5), channel_id=1, source_target_pairs={{0,8},{8,0},{16,24},{24,16},{1,9},{9,1},{17,25},{25,17},{2,10},{10... | collective-permute-start | bytes 1966088 | tf_op jit(solution)/shard_map/ppermute | solution.py:84
  57.4 1.0 copy.66
  58.4 2.0 fusion.18
  60.4 12.2 %collective-permute-done.1 = f32[16,2,1,4,1280]{4,3,2,1,0:T(4,128)} collective-permute-done((f32[16,2,1,4,1280]{4,3,2,1,0:T(4,128)}, f32[16,2,1,4,1280]{4,3,2,1,0:T(4,128)}, u32[]{:S(2)}, u32[]{:S(2)}) %collective-permute-start.1) | collective-permute-done | bytes 655392 | tf_op jit(solution)/shard_map/ppermute | solution.py:84
  72.6 1.3 dynamic-slice_add_fusion.1
  73.9 5.3 %collective-permute-start.2 = (f32[16,1,1,4,1280]{4,3,2,1,0:T(4,128)S(1)}, f32[16,1,1,4,1280]{4,3,2,1,0:T(4,128)S(1)}, u32[]{:S(2)}, u32[]{:S(2)}) collective-permute-start(f32[16,1,1,4,1280]{4,3,2,1,0:T(4,128)S(1)} %constant_dynamic-slice_fusion.4), channel_id=1, source_target_pairs={{0,16},{8,24},{16,0},{24,8},{1,17},{9,25},{17,1},{25,9},{2,18},{10... | collective-permute-start | bytes 983048 | tf_op jit(solution)/shard_map/ppermute | solution.py:84
  79.2 0.3 fusion.28
  79.5 6.9 %collective-permute-done.2 = f32[16,1,1,4,1280]{4,3,2,1,0:T(4,128)S(1)} collective-permute-done((f32[16,1,1,4,1280]{4,3,2,1,0:T(4,128)S(1)}, f32[16,1,1,4,1280]{4,3,2,1,0:T(4,128)S(1)}, u32[]{:S(2)}, u32[]{:S(2)}) %collective-permute-start.2) | collective-permute-done | bytes 327712 | tf_op jit(solution)/shard_map/ppermute | solution.py:84
  86.5 3.8 %collective-permute-start.3 = (f32[2,2,2,1,4,1280]{5,4,3,2,1,0:T(4,128)S(1)}, f32[2,2,2,1,4,1280]{5,4,3,2,1,0:T(4,128)S(1)}, u32[]{:S(2)}, u32[]{:S(2)}) collective-permute-start(f32[2,2,2,1,4,1280]{5,4,3,2,1,0:T(4,128)S(1)} %constant_dynamic-slice_fusion.3), channel_id=1, source_target_pairs={{0,32},{32,0},{64,96},{96,64},{128,160},{160,128},{192,224},{224,1... | collective-permute-start | bytes 491528 | tf_op jit(solution)/shard_map/ppermute | solution.py:84
  90.4 0.4 add_convert_fusion
  90.8 0.2 convert_reduce_fusion.2
  91.0 2.7 collective-permute-done.3
  93.8 5.2 %collective-permute-start.4 = (f32[2,2,1,1,4,1280]{5,4,3,2,1,0:T(4,128)S(1)}, f32[2,2,1,1,4,1280]{5,4,3,2,1,0:T(4,128)S(1)}, u32[]{:S(2)}, u32[]{:S(2)}) collective-permute-start(f32[2,2,1,1,4,1280]{5,4,3,2,1,0:T(4,128)S(1)} %constant_dynamic-slice_fusion.2), channel_id=1, source_target_pairs={{0,64},{32,96},{64,0},{96,32},{128,192},{160,224},{192,128},{224,1... | collective-permute-start | bytes 245768 | tf_op jit(solution)/shard_map/ppermute | solution.py:84
  99.0 2.4 collective-permute-done.4
  101.5 9.1 %collective-permute-start.5 = (f32[2,1,1,1,4,1280]{5,4,3,2,1,0:T(4,128)S(1)}, f32[2,1,1,1,4,1280]{5,4,3,2,1,0:T(4,128)S(1)}, u32[]{:S(2)}, u32[]{:S(2)}) collective-permute-start(f32[2,1,1,1,4,1280]{5,4,3,2,1,0:T(4,128)S(1)} %constant_dynamic-slice_fusion.1), channel_id=1, source_target_pairs={{0,128},{32,160},{64,192},{96,224},{128,0},{160,32},{192,64},{224,... | collective-permute-start | bytes 122888 | tf_op jit(solution)/shard_map/ppermute | solution.py:84
  110.6 0.5 select_reduce_fusion
  111.1 1.6 collective-permute-done.5
  112.7 15.4 %collective-permute-start.6 = (f32[1,1,1,1,4,1280]{5,4,3,2,1,0:T(4,128)S(1)}, f32[1,1,1,1,4,1280]{5,4,3,2,1,0:T(4,128)S(1)}, u32[]{:S(2)}, u32[]{:S(2)}) collective-permute-start(f32[1,1,1,1,4,1280]{5,4,3,2,1,0:T(4,128)S(1)} %constant_dynamic-slice_fusion), channel_id=1, source_target_pairs={{0,256},{32,288},{64,320},{96,352},{128,384},{160,416},{192,448},{... | collective-permute-start | bytes 61448 | tf_op jit(solution)/shard_map/ppermute | solution.py:84
  128.3 1.6 collective-permute-done.6
  129.9 1.3 fusion.6
  131.2 2.0 fusion.5
  133.2 17.3 %all-to-all-start = ((bf16[128,17,512]{2,1,0:T(8,128)(2,1)}), bf16[128,17,512]{2,1,0:T(8,128)(2,1)}, u32[]{:S(2)}, u32[]{:S(2)}) async-start(bf16[128,17,512]{2,1,0:T(8,128)(2,1)} %fusion.5), calls=%async_computation | async-start | bytes 6291456 | tf_op jit(solution)/shard_map/all_to_all | solution.py:156
  150.6 141.8 %all-to-all-done = bf16[128,17,512]{2,1,0:T(8,128)(2,1)} async-done(((bf16[128,17,512]{2,1,0:T(8,128)(2,1)}), bf16[128,17,512]{2,1,0:T(8,128)(2,1)}, u32[]{:S(2)}, u32[]{:S(2)}) %all-to-all-start) | async-done | bytes 2228256 | tf_op jit(solution)/shard_map/all_to_all | solution.py:156
  292.3 1.2 fusion.38
  293.8 1.8 slice.52
  295.6 0.4 fusion.19
  296.2 2.9 collective-permute-start.7
  299.1 7.3 %collective-permute-done.7 = f32[136,640]{1,0:T(8,128)S(1)} collective-permute-done((f32[136,640]{1,0:T(8,128)S(1)}, f32[136,640]{1,0:T(8,128)S(1)}, u32[]{:S(2)}, u32[]{:S(2)}) %collective-permute-start.7) | collective-permute-done | bytes 348192 | tf_op jit(solution)/shard_map/ppermute | solution.py:90
  306.4 3.3 %collective-permute-start.8 = (f32[136,640]{1,0:T(8,128)S(1)}, f32[136,640]{1,0:T(8,128)S(1)}, u32[]{:S(2)}, u32[]{:S(2)}) collective-permute-start(f32[136,640]{1,0:T(8,128)S(1)} %fusion.43), channel_id=1, source_target_pairs={{0,2},{1,3},{2,0},{3,1},{4,6},{5,7},{6,4},{7,5},{8,10},{9,11},{10,... | collective-permute-start | bytes 1044488 | tf_op jit(solution)/shard_map/ppermute | solution.py:90
  309.7 7.4 %collective-permute-done.8 = f32[136,640]{1,0:T(8,128)S(1)} collective-permute-done((f32[136,640]{1,0:T(8,128)S(1)}, f32[136,640]{1,0:T(8,128)S(1)}, u32[]{:S(2)}, u32[]{:S(2)}) %collective-permute-start.8) | collective-permute-done | bytes 348192 | tf_op jit(solution)/shard_map/ppermute | solution.py:90
  317.4 0.6 slice.56
  318.0 0.6 slice.57
  318.6 0.5 fusion.42
  319.1 0.9 fusion.36
  (72 shorter events, 2.5 us)
Async XLA Ops:
  0.6 4.0 %copy-start = (bf16[512,1024]{1,0:T(8,128)(2,1)S(1)}, bf16[512,1024]{1,0:T(8,128)(2,1)}, u32[]{:S(2)}) copy-start(bf16[512,1024]{1,0:T(8,128)(2,1)} %param.17) | copy-start | bytes 3145732
  0.6 3.4 %copy-start.11 = (bf16[512,512]{1,0:T(8,128)(2,1)S(1)}, bf16[512,512]{1,0:T(8,128)(2,1)}, u32[]{:S(2)}) copy-start(bf16[512,512]{1,0:T(8,128)(2,1)} %param.12) | copy-start | bytes 1572868
  6.9 1.1 copy-start.4
  8.3 5.0 %copy-start.6 = (bf16[512,256]{0,1:T(8,128)(2,1)}, bf16[512,256]{0,1:T(8,128)(2,1)S(1)}, u32[]{:S(2)}) copy-start(bf16[512,256]{0,1:T(8,128)(2,1)S(1)} %copy.59) | copy-start | bytes 786436
  8.5 4.8 %copy-start.8 = (bf16[512,256]{0,1:T(8,128)(2,1)}, bf16[512,256]{0,1:T(8,128)(2,1)S(1)}, u32[]{:S(2)}) copy-start(bf16[512,256]{0,1:T(8,128)(2,1)S(1)} %copy.57) | copy-start | bytes 786436
  13.3 1.3 copy-start.1
  14.6 1.1 copy-start.2
  21.0 2.9 copy-start.10
  23.9 4.0 %copy-start.7 = (bf16[512,256]{0,1:T(8,128)(2,1)S(1)}, bf16[512,256]{0,1:T(8,128)(2,1)}, u32[]{:S(2)}) copy-start(bf16[512,256]{0,1:T(8,128)(2,1)} %copy-done.6) | copy-start | bytes 786436
  30.6 2.6 copy-start.9
  36.9 1.0 copy-start.3
  45.7 5.1 %collective-permute-start = (f32[16,4,1,4,1280]{4,3,2,1,0:T(4,128)S(1)}, f32[16,4,1,4,1280]{4,3,2,1,0:T(4,128)}, u32[]{:S(2)}, u32[]{:S(2)}) collective-permute-start(f32[16,4,1,4,1280]{4,3,2,1,0:T(4,128)S(1)} %constant_dynamic-slice_fusion.6), channel_id=1, source_target_pairs={{0,4},{4,0},{1,5},{5,1},{2,6},{6,2},{3,7},{7,3},{8,12},{12,8},{9,1... | collective-permute-start | bytes 3932168 | tf_op jit(solution)/shard_map/ppermute | solution.py:84
  53.7 19.0 %collective-permute-start.1 = (f32[16,2,1,4,1280]{4,3,2,1,0:T(4,128)}, f32[16,2,1,4,1280]{4,3,2,1,0:T(4,128)}, u32[]{:S(2)}, u32[]{:S(2)}) collective-permute-start(f32[16,2,1,4,1280]{4,3,2,1,0:T(4,128)} %constant_dynamic-slice_fusion.5), channel_id=1, source_target_pairs={{0,8},{8,0},{16,24},{24,16},{1,9},{9,1},{17,25},{25,17},{2,10},{10... | collective-permute-start | bytes 1966088 | tf_op jit(solution)/shard_map/ppermute | solution.py:84
  73.9 16.5 %copy-start.5 = (bf16[512,512]{0,1:T(8,128)(2,1)S(1)}, bf16[512,512]{0,1:T(8,128)(2,1)}, u32[]{:S(2)}) copy-start(bf16[512,512]{0,1:T(8,128)(2,1)} %copy.66) | copy-start | bytes 1572868
  73.9 12.5 %collective-permute-start.2 = (f32[16,1,1,4,1280]{4,3,2,1,0:T(4,128)S(1)}, f32[16,1,1,4,1280]{4,3,2,1,0:T(4,128)S(1)}, u32[]{:S(2)}, u32[]{:S(2)}) collective-permute-start(f32[16,1,1,4,1280]{4,3,2,1,0:T(4,128)S(1)} %constant_dynamic-slice_fusion.4), channel_id=1, source_target_pairs={{0,16},{8,24},{16,0},{24,8},{1,17},{9,25},{17,1},{25,9},{2,18},{10... | collective-permute-start | bytes 983048 | tf_op jit(solution)/shard_map/ppermute | solution.py:84
  79.5 11.2 %copy-start.14 = (s32[512,1]{0,1:T(1,128)S(1)}, s32[512,1]{0,1:T(1,128)}, u32[]{:S(2)}) copy-start(s32[512,1]{0,1:T(1,128)} %param.15) | copy-start | bytes 6148
  79.5 19.5 %copy-start.15 = (s32[512]{0:T(512)S(1)}, s32[512]{0:T(512)}, u32[]{:S(2)}) copy-start(s32[512]{0:T(512)} %param.16) | copy-start | bytes 6148
  86.5 7.2 %collective-permute-start.3 = (f32[2,2,2,1,4,1280]{5,4,3,2,1,0:T(4,128)S(1)}, f32[2,2,2,1,4,1280]{5,4,3,2,1,0:T(4,128)S(1)}, u32[]{:S(2)}, u32[]{:S(2)}) collective-permute-start(f32[2,2,2,1,4,1280]{5,4,3,2,1,0:T(4,128)S(1)} %constant_dynamic-slice_fusion.3), channel_id=1, source_target_pairs={{0,32},{32,0},{64,96},{96,64},{128,160},{160,128},{192,224},{224,1... | collective-permute-start | bytes 491528 | tf_op jit(solution)/shard_map/ppermute | solution.py:84
  93.8 7.6 %collective-permute-start.4 = (f32[2,2,1,1,4,1280]{5,4,3,2,1,0:T(4,128)S(1)}, f32[2,2,1,1,4,1280]{5,4,3,2,1,0:T(4,128)S(1)}, u32[]{:S(2)}, u32[]{:S(2)}) collective-permute-start(f32[2,2,1,1,4,1280]{5,4,3,2,1,0:T(4,128)S(1)} %constant_dynamic-slice_fusion.2), channel_id=1, source_target_pairs={{0,64},{32,96},{64,0},{96,32},{128,192},{160,224},{192,128},{224,1... | collective-permute-start | bytes 245768 | tf_op jit(solution)/shard_map/ppermute | solution.py:84
  101.5 11.2 %collective-permute-start.5 = (f32[2,1,1,1,4,1280]{5,4,3,2,1,0:T(4,128)S(1)}, f32[2,1,1,1,4,1280]{5,4,3,2,1,0:T(4,128)S(1)}, u32[]{:S(2)}, u32[]{:S(2)}) collective-permute-start(f32[2,1,1,1,4,1280]{5,4,3,2,1,0:T(4,128)S(1)} %constant_dynamic-slice_fusion.1), channel_id=1, source_target_pairs={{0,128},{32,160},{64,192},{96,224},{128,0},{160,32},{192,64},{224,... | collective-permute-start | bytes 122888 | tf_op jit(solution)/shard_map/ppermute | solution.py:84
  112.7 17.2 %collective-permute-start.6 = (f32[1,1,1,1,4,1280]{5,4,3,2,1,0:T(4,128)S(1)}, f32[1,1,1,1,4,1280]{5,4,3,2,1,0:T(4,128)S(1)}, u32[]{:S(2)}, u32[]{:S(2)}) collective-permute-start(f32[1,1,1,1,4,1280]{5,4,3,2,1,0:T(4,128)S(1)} %constant_dynamic-slice_fusion), channel_id=1, source_target_pairs={{0,256},{32,288},{64,320},{96,352},{128,384},{160,416},{192,448},{... | collective-permute-start | bytes 61448 | tf_op jit(solution)/shard_map/ppermute | solution.py:84
  133.2 159.1 %all-to-all-start = ((bf16[128,17,512]{2,1,0:T(8,128)(2,1)}), bf16[128,17,512]{2,1,0:T(8,128)(2,1)}, u32[]{:S(2)}, u32[]{:S(2)}) async-start(bf16[128,17,512]{2,1,0:T(8,128)(2,1)} %fusion.5), calls=%async_computation | async-start | bytes 6291456 | tf_op jit(solution)/shard_map/all_to_all | solution.py:156
  296.0 22.6 %copy-start.16 = (f32[128]{0:T(128)S(1)}, f32[128]{0:T(128)}, u32[]{:S(2)}) copy-start(f32[128]{0:T(128)} %param.21) | copy-start | bytes 1540
  296.0 23.1 %copy-start.12 = (f32[128,512]{1,0:T(8,128)S(1)}, f32[128,512]{1,0:T(8,128)}, u32[]{:S(2)}) copy-start(f32[128,512]{1,0:T(8,128)} %param.20) | copy-start | bytes 786436
  296.0 23.1 %copy-start.13 = (f32[128,512]{1,0:T(8,128)S(1)}, f32[128,512]{1,0:T(8,128)}, u32[]{:S(2)}) copy-start(f32[128,512]{1,0:T(8,128)} %param.19) | copy-start | bytes 786436
  296.2 10.2 %collective-permute-start.7 = (f32[136,640]{1,0:T(8,128)S(1)}, f32[136,640]{1,0:T(8,128)S(1)}, u32[]{:S(2)}, u32[]{:S(2)}) collective-permute-start(f32[136,640]{1,0:T(8,128)S(1)} %pad_maximum_fusion.1), channel_id=1, source_target_pairs={{0,1},{1,0},{2,3},{3,2},{4,5},{5,4},{6,7},{7,6},{8,9},{9,8},{10,11... | collective-permute-start | bytes 1044488 | tf_op jit(solution)/shard_map/ppermute | solution.py:90
  306.4 10.7 %collective-permute-start.8 = (f32[136,640]{1,0:T(8,128)S(1)}, f32[136,640]{1,0:T(8,128)S(1)}, u32[]{:S(2)}, u32[]{:S(2)}) collective-permute-start(f32[136,640]{1,0:T(8,128)S(1)} %fusion.43), channel_id=1, source_target_pairs={{0,2},{1,3},{2,0},{3,1},{4,6},{5,7},{6,4},{7,5},{8,10},{9,11},{10,... | collective-permute-start | bytes 1044488 | tf_op jit(solution)/shard_map/ppermute | solution.py:90

commit v6 on v4

--- a/solution.py
+++ b/solution.py
@@ -150,14 +150,19 @@
     out_slots = (jnp.sum(jnp.where(chosen, slots[None, :] + 1, 0), axis=1) - 1).reshape(
         owner_count, capacity
     )
-    slot_row = jnp.zeros((owner_count, 1, width), jnp.bfloat16)
+    block_rows = capacity * width // 128
+    slot_row = jnp.zeros((owner_count, 1, 128), jnp.bfloat16)
     slot_row = slot_row.at[:, 0, :capacity].set(out_slots.astype(jnp.bfloat16))
     arrived = lax.all_to_all(
-        jnp.concatenate([outgoing, slot_row], axis=1), ROW_AXES, 0, 0, tiled=True
+        jnp.concatenate([outgoing.reshape(owner_count, block_rows, 128), slot_row], axis=1),
+        ROW_AXES,
+        0,
+        0,
+        tiled=True,
     )
     arrived, weight_share = lax.optimization_barrier((arrived, weight_share))
-    received = arrived[:, :capacity, :].reshape(buffer_rows, width)
-    got_slots = arrived[:, capacity, :capacity].astype(jnp.int32).reshape(buffer_rows)
+    received = arrived[:, :block_rows, :].reshape(buffer_rows, width)
+    got_slots = arrived[:, block_rows, :capacity].astype(jnp.int32).reshape(buffer_rows)
     slot_count = emb_rows.shape[0]
     matches = got_slots[None, :] == jnp.arange(slot_count, dtype=jnp.int32)[:, None]
     grad_part = jnp.dot(matches.astype(jnp.bfloat16), received, preferred_element_type=jnp.float32)

time: 265 us -> 241 us (0.909)
  waiting for transfers between devices: 138 us -> 104 us
  local copies, waits for them, and re-layouts: 19.2 us -> 26.9 us
    ppermute x7, waiting for transfers between devices: 123 us -> 89.4 us  [halve_sum(): blocks = keep + lax.ppermute(send, axis, pairs)]
    another operation x0 -> x1, local copies, waits for them, and re-layouts: none -> 4.35 us  [local(): outgoing.reshape(owner_count, block_rows, 128)]
    reshape x0 -> x1, local copies, waits for them, and re-layouts: none -> 3.1 us  [local(): received = arrived[:, :block_rows, :].reshape(buffer_rows, width)]
  transfers between devices with their start and end apart: 10 -> 10, of which waited for: 9 -> 9; matrix products, arithmetic and copies ran while one was open for 5% -> 6% of each run, Pallas kernels for 0% -> 0%
where the time goes in v6:
time: 241 us; the launch traced here: 239 us
  waiting for transfers between devices  104 us (43%)
  starting transfers between devices  61.6 us (26%)
  local copies, waits for them, and re-layouts  26.9 us (11%)
  matrix products  24.9 us (10%)
  other arithmetic  21 us (9%)
    ppermute x7, waiting for transfers between devices, halve_sum(): blocks = keep + lax.ppermute(send, axis, pairs)  89.4 us
    ppermute x7, starting transfers between devices, halve_sum(): blocks = keep + lax.ppermute(send, axis, pairs)  35.2 us
    all_to_all x1, starting transfers between devices, local(): lax.all_to_all(jnp.concatenate([outgoing.reshape(owner_count, block_rows,...  20.4 us
    ppermute x2, waiting for transfers between devices, double_sum(): lax.ppermute(value, axis, [(i, i ^ 1 << bit) for i in range(size)])  14.2 us
    dot_general x3, matrix products, core(): jnp.einsum('hts,shd->thd', weights, values_part, preferred_element_type=j...  7.52 us
    dot_general x3, matrix products, core(): jnp.einsum('thd,shd->hts', queries, keys_part, preferred_element_type=jnp...  6.16 us
    ppermute x2, starting transfers between devices, double_sum(): lax.ppermute(value, axis, [(i, i ^ 1 << bit) for i in range(size)])  6.05 us
  transfers between devices with their start and end apart: 10, of which 9 were waited for; matrix products, arithmetic and copies ran while one was open for 6% of the time, Pallas kernels for 0%

profile of v6, /device:TPU:6, one launch (start us, length us, event | category | flops | bytes accessed | tf_op | source)
XLA Modules:
  0.0 239.2 jit_solution(16380954643658042098)
XLA Ops:
  0.7 0.9 reduce-window.8
  1.9 1.3 fusion.22
  3.1 0.2 copy.56
  3.7 2.3 multiply_convert_fusion.1
  6.0 1.0 copy-done.4
  7.0 0.8 fusion.45
  8.0 1.2 copy.57
  9.2 3.5 %multiply_convert_fusion = (bf16[4,512,512]{2,1,0:T(8,128)(2,1)S(1)}, f32[4,512,512]{2,1,0:T(8,128)}) fusion(f32[512,512]{1,0:T(8,128)S(1)} %fusion.23, bf16[512,4,64]{0,2,1:T(8,128)(2,1)S(1)} %bitcast.57, bf16[512,4,64]{0,2,1:T(8,128)(2,1)S(1)} %bitcast.59), kind=kOutput, calls=%fused_computation.7 | convolution fusion | flops 142606336 | bytes 7864320 | tf_op jit(solution)/shard_map/jvp(thd,shd->hts)/dot_general | solution.py:46
  12.7 1.3 copy-done.1
  14.1 0.8 fusion.46
  14.8 0.2 copy.60
  15.1 1.4 multiply_reduce_fusion
  16.6 1.9 fusion.44
  18.5 0.8 broadcast_add_fusion
  19.4 1.1 copy.62
  20.5 2.2 fusion.49
  22.7 4.6 %fusion.3 = bf16[4,512,512]{2,1,0:T(8,128)(2,1)S(1)} fusion(f32[4,512,512]{2,1,0:T(8,128)} %get-tuple-element.36, f32[512,512]{1,0:T(8,128)S(1)} %copy-done.10, bf16[4,64,512]{2,1,0:T(8,128)(2,1)} %bitcast.65, bf16[512,4,64]{0,2,1:T(8,128)(2,1)} %bitcast.62), kind=kOutput, calls=%fused_computation.5 | convolution fusion | flops 148897792 | bytes 7864320 | tf_op jit(solution)/shard_map/transpose(jvp(hts,shd->thd))/dot_general | solution.py:50
  27.3 1.5 fusion.48
  28.8 1.2 fusion.47
  30.0 1.0 copy.66
  31.1 1.1 copy.64
  32.2 0.8 copy.65
  33.0 2.5 %fusion.8 = bf16[512,1024]{1,0:T(8,128)(2,1)S(1)} fusion(f32[512,1024]{1,0:T(8,128)} %get-tuple-element.34, bf16[512,256]{1,0:T(8,128)(2,1)} %copy.65, bf16[512,256]{1,0:T(8,128)(2,1)S(1)} %copy.64, bf16[512,256]{1,0:T(8,128)(2,1)S(1)} %copy.63, bf16[512,256]{1,0:T(8,128)(2,1)} %get-tuple-element.23), kind=kLoop, calls=%fused_computation.18 | loop fusion | flops 9437184 | bytes 4194304 | tf_op jit(solution)/shard_map/convert_element_type | solution.py:114
  35.6 0.8 fusion.18
  36.5 0.3 fusion.29
  36.8 0.2 convert_reduce_fusion.2
  37.1 2.9 %fusion.5 = bf16[2048,512]{1,0:T(8,128)(2,1)} fusion(s32[512]{0:T(512)S(1)} %get-tuple-element.43, bf16[512,512]{0,1:T(8,128)(2,1)S(1)} %copy-done.12, f32[512]{0:T(512)S(1)} %negate_multiply_fusion, bf16[512,512]{0,1:T(8,128)(2,1)S(1)} %copy.56, f32[512,512]{0,1:T(8,128)S(1)} %get-tuple-element.42, f32[512]{0:T(512)S(1)} %multiply_multiply_fusion, ...), kind=kOutput, calls=%fused_computation.12 | convolution fusion | flops 1078460416 | bytes 4204544 | tf_op jit(solution)/shard_map/dot_general | solution.py:146
  40.0 4.3 %reshape_reshape.9 = bf16[128,64,128]{2,1,0:T(8,128)(2,1)} reshape(bf16[2048,512]{1,0:T(8,128)(2,1)} %fusion.5) | data formatting | bytes 4194304 | tf_op jit(solution)/shard_map/reshape;reshape | solution.py:157
  44.4 0.5 select_reduce_fusion
  45.0 3.4 %fusion.6 = bf16[128,65,128]{2,1,0:T(8,128)(2,1)} fusion(bf16[128,1,16]{2,1,0:T(2,128)(2,1)S(1)} %convert_element_type.136, bf16[128,64,128]{2,1,0:T(8,128)(2,1)} %reshape_reshape.9), kind=kLoop, calls=%fused_computation.16 | loop fusion | flops 6389760 | bytes 4231168 | tf_op jit(solution)/shard_map/concatenate | solution.py:157
  48.4 20.4 %all-to-all-start = ((bf16[128,65,128]{2,1,0:T(8,128)(2,1)}), bf16[128,65,128]{2,1,0:T(8,128)(2,1)}, u32[]{:S(2)}, u32[]{:S(2)}) async-start(bf16[128,65,128]{2,1,0:T(8,128)(2,1)} %fusion.6), calls=%async_computation | async-start | bytes 4718592 | tf_op jit(solution)/shard_map/all_to_all | solution.py:156
  68.8 1.5 convolution_bitcast_fusion
  70.3 1.9 fusion.30
  72.2 1.7 pad_maximum_fusion
  74.0 3.9 %reshape.250 = f32[16,4,2,4,1280]{4,3,2,1,0:T(4,128)} reshape(f32[512,1280]{1,0:T(8,128)} %pad_maximum_fusion) | data formatting | bytes 5242880 | tf_op jit(solution)/shard_map/reshape | solution.py:98
  77.9 1.4 constant_dynamic-slice_fusion.6
  79.3 1.9 collective-permute-start
  81.2 3.1 %collective-permute-done = f32[16,4,1,4,1280]{4,3,2,1,0:T(4,128)} collective-permute-done((f32[16,4,1,4,1280]{4,3,2,1,0:T(4,128)S(1)}, f32[16,4,1,4,1280]{4,3,2,1,0:T(4,128)}, u32[]{:S(2)}, u32[]{:S(2)}) %collective-permute-start) | collective-permute-done | bytes 1310752 | tf_op jit(solution)/shard_map/ppermute | solution.py:84
  84.3 2.1 dynamic-slice_add_fusion
  86.5 3.0 %collective-permute-start.1 = (f32[16,2,1,4,1280]{4,3,2,1,0:T(4,128)S(1)}, f32[16,2,1,4,1280]{4,3,2,1,0:T(4,128)}, u32[]{:S(2)}, u32[]{:S(2)}) collective-permute-start(f32[16,2,1,4,1280]{4,3,2,1,0:T(4,128)S(1)} %constant_dynamic-slice_fusion.5), channel_id=1, source_target_pairs={{0,8},{8,0},{16,24},{24,16},{1,9},{9,1},{17,25},{25,17},{2,10},{10... | collective-permute-start | bytes 1966088 | tf_op jit(solution)/shard_map/ppermute | solution.py:84
  89.5 19.7 %collective-permute-done.1 = f32[16,2,1,4,1280]{4,3,2,1,0:T(4,128)} collective-permute-done((f32[16,2,1,4,1280]{4,3,2,1,0:T(4,128)S(1)}, f32[16,2,1,4,1280]{4,3,2,1,0:T(4,128)}, u32[]{:S(2)}, u32[]{:S(2)}) %collective-permute-start.1) | collective-permute-done | bytes 655392 | tf_op jit(solution)/shard_map/ppermute | solution.py:84
  109.1 1.3 dynamic-slice_add_fusion.1
  110.4 4.3 %collective-permute-start.2 = (f32[16,1,1,4,1280]{4,3,2,1,0:T(4,128)S(1)}, f32[16,1,1,4,1280]{4,3,2,1,0:T(4,128)S(1)}, u32[]{:S(2)}, u32[]{:S(2)}) collective-permute-start(f32[16,1,1,4,1280]{4,3,2,1,0:T(4,128)S(1)} %constant_dynamic-slice_fusion.4), channel_id=1, source_target_pairs={{0,16},{8,24},{16,0},{24,8},{1,17},{9,25},{17,1},{25,9},{2,18},{10... | collective-permute-start | bytes 983048 | tf_op jit(solution)/shard_map/ppermute | solution.py:84
  114.7 10.8 %collective-permute-done.2 = f32[16,1,1,4,1280]{4,3,2,1,0:T(4,128)S(1)} collective-permute-done((f32[16,1,1,4,1280]{4,3,2,1,0:T(4,128)S(1)}, f32[16,1,1,4,1280]{4,3,2,1,0:T(4,128)S(1)}, u32[]{:S(2)}, u32[]{:S(2)}) %collective-permute-start.2) | collective-permute-done | bytes 327712 | tf_op jit(solution)/shard_map/ppermute | solution.py:84
  125.6 2.9 %collective-permute-start.3 = (f32[2,2,2,1,4,1280]{5,4,3,2,1,0:T(4,128)S(1)}, f32[2,2,2,1,4,1280]{5,4,3,2,1,0:T(4,128)S(1)}, u32[]{:S(2)}, u32[]{:S(2)}) collective-permute-start(f32[2,2,2,1,4,1280]{5,4,3,2,1,0:T(4,128)S(1)} %constant_dynamic-slice_fusion.3), channel_id=1, source_target_pairs={{0,32},{32,0},{64,96},{96,64},{128,160},{160,128},{192,224},{224,1... | collective-permute-start | bytes 491528 | tf_op jit(solution)/shard_map/ppermute | solution.py:84
  128.6 45.8 %collective-permute-done.3 = f32[2,2,2,1,4,1280]{5,4,3,2,1,0:T(4,128)S(1)} collective-permute-done((f32[2,2,2,1,4,1280]{5,4,3,2,1,0:T(4,128)S(1)}, f32[2,2,2,1,4,1280]{5,4,3,2,1,0:T(4,128)S(1)}, u32[]{:S(2)}, u32[]{:S(2)}) %collective-permute-start.3) | collective-permute-done | bytes 163872 | tf_op jit(solution)/shard_map/ppermute | solution.py:84
  174.4 3.7 %collective-permute-start.4 = (f32[2,2,1,1,4,1280]{5,4,3,2,1,0:T(4,128)S(1)}, f32[2,2,1,1,4,1280]{5,4,3,2,1,0:T(4,128)S(1)}, u32[]{:S(2)}, u32[]{:S(2)}) collective-permute-start(f32[2,2,1,1,4,1280]{5,4,3,2,1,0:T(4,128)S(1)} %constant_dynamic-slice_fusion.2), channel_id=1, source_target_pairs={{0,64},{32,96},{64,0},{96,32},{128,192},{160,224},{192,128},{224,1... | collective-permute-start | bytes 245768 | tf_op jit(solution)/shard_map/ppermute | solution.py:84
  178.2 4.7 %collective-permute-done.4 = f32[2,2,1,1,4,1280]{5,4,3,2,1,0:T(4,128)S(1)} collective-permute-done((f32[2,2,1,1,4,1280]{5,4,3,2,1,0:T(4,128)S(1)}, f32[2,2,1,1,4,1280]{5,4,3,2,1,0:T(4,128)S(1)}, u32[]{:S(2)}, u32[]{:S(2)}) %collective-permute-start.4) | collective-permute-done | bytes 81952 | tf_op jit(solution)/shard_map/ppermute | solution.py:84
  182.9 7.4 %collective-permute-start.5 = (f32[2,1,1,1,4,1280]{5,4,3,2,1,0:T(4,128)S(1)}, f32[2,1,1,1,4,1280]{5,4,3,2,1,0:T(4,128)S(1)}, u32[]{:S(2)}, u32[]{:S(2)}) collective-permute-start(f32[2,1,1,1,4,1280]{5,4,3,2,1,0:T(4,128)S(1)} %constant_dynamic-slice_fusion.1), channel_id=1, source_target_pairs={{0,128},{32,160},{64,192},{96,224},{128,0},{160,32},{192,64},{224,... | collective-permute-start | bytes 122888 | tf_op jit(solution)/shard_map/ppermute | solution.py:84
  190.4 2.8 %collective-permute-done.5 = f32[2,1,1,1,4,1280]{5,4,3,2,1,0:T(4,128)S(1)} collective-permute-done((f32[2,1,1,1,4,1280]{5,4,3,2,1,0:T(4,128)S(1)}, f32[2,1,1,1,4,1280]{5,4,3,2,1,0:T(4,128)S(1)}, u32[]{:S(2)}, u32[]{:S(2)}) %collective-permute-start.5) | collective-permute-done | bytes 40992 | tf_op jit(solution)/shard_map/ppermute | solution.py:84
  193.2 11.9 %collective-permute-start.6 = (f32[1,1,1,1,4,1280]{5,4,3,2,1,0:T(4,128)S(1)}, f32[1,1,1,1,4,1280]{5,4,3,2,1,0:T(4,128)S(1)}, u32[]{:S(2)}, u32[]{:S(2)}) collective-permute-start(f32[1,1,1,1,4,1280]{5,4,3,2,1,0:T(4,128)S(1)} %constant_dynamic-slice_fusion), channel_id=1, source_target_pairs={{0,256},{32,288},{64,320},{96,352},{128,384},{160,416},{192,448},{... | collective-permute-start | bytes 61448 | tf_op jit(solution)/shard_map/ppermute | solution.py:84
  205.1 2.5 %collective-permute-done.6 = f32[1,1,1,1,4,1280]{5,4,3,2,1,0:T(4,128)S(1)} collective-permute-done((f32[1,1,1,1,4,1280]{5,4,3,2,1,0:T(4,128)S(1)}, f32[1,1,1,1,4,1280]{5,4,3,2,1,0:T(4,128)S(1)}, u32[]{:S(2)}, u32[]{:S(2)}) %collective-permute-start.6) | collective-permute-done | bytes 20512 | tf_op jit(solution)/shard_map/ppermute | solution.py:84
  207.6 3.1 %slice.45 = bf16[128,64,128]{2,1,0:T(8,128)(2,1)} slice(bf16[128,65,128]{2,1,0:T(8,128)(2,1)} %all-to-all-done), slice={[0:128], [0:64], [0:128]} | slice | bytes 4194304 | tf_op jit(solution)/shard_map/slice | solution.py:164
  210.7 1.2 convert_reduce_fusion.3
  211.9 3.1 %reshape.252 = bf16[2048,512]{1,0:T(8,128)(2,1)S(1)} reshape(bf16[128,64,128]{2,1,0:T(8,128)(2,1)} %slice.45) | data formatting | bytes 4194304 | tf_op jit(solution)/shard_map/reshape | solution.py:164
  215.3 0.4 fusion.19
  215.9 2.7 %collective-permute-start.7 = (f32[136,640]{1,0:T(8,128)S(1)}, f32[136,640]{1,0:T(8,128)S(1)}, u32[]{:S(2)}, u32[]{:S(2)}) collective-permute-start(f32[136,640]{1,0:T(8,128)S(1)} %pad_maximum_fusion.1), channel_id=1, source_target_pairs={{0,1},{1,0},{2,3},{3,2},{4,5},{5,4},{6,7},{7,6},{8,9},{9,8},{10,11... | collective-permute-start | bytes 1044488 | tf_op jit(solution)/shard_map/ppermute | solution.py:90
  218.7 6.9 %collective-permute-done.7 = f32[136,640]{1,0:T(8,128)S(1)} collective-permute-done((f32[136,640]{1,0:T(8,128)S(1)}, f32[136,640]{1,0:T(8,128)S(1)}, u32[]{:S(2)}, u32[]{:S(2)}) %collective-permute-start.7) | collective-permute-done | bytes 348192 | tf_op jit(solution)/shard_map/ppermute | solution.py:90
  225.6 3.3 %collective-permute-start.8 = (f32[136,640]{1,0:T(8,128)S(1)}, f32[136,640]{1,0:T(8,128)S(1)}, u32[]{:S(2)}, u32[]{:S(2)}) collective-permute-start(f32[136,640]{1,0:T(8,128)S(1)} %fusion.43), channel_id=1, source_target_pairs={{0,2},{1,3},{2,0},{3,1},{4,6},{5,7},{6,4},{7,5},{8,10},{9,11},{10,... | collective-permute-start | bytes 1044488 | tf_op jit(solution)/shard_map/ppermute | solution.py:90
  228.9 7.4 %collective-permute-done.8 = f32[136,640]{1,0:T(8,128)S(1)} collective-permute-done((f32[136,640]{1,0:T(8,128)S(1)}, f32[136,640]{1,0:T(8,128)S(1)}, u32[]{:S(2)}, u32[]{:S(2)}) %collective-permute-start.8) | collective-permute-done | bytes 348192 | tf_op jit(solution)/shard_map/ppermute | solution.py:90
  236.6 0.6 slice.54
  237.2 0.6 slice.55
  237.8 0.5 fusion.42
  238.3 0.9 fusion.37
  (75 shorter events, 2.5 us)
Async XLA Ops:
  0.6 3.0 %copy-start = (bf16[512,1024]{1,0:T(8,128)(2,1)S(1)}, bf16[512,1024]{1,0:T(8,128)(2,1)}, u32[]{:S(2)}) copy-start(bf16[512,1024]{1,0:T(8,128)(2,1)} %param.17) | copy-start | bytes 3145732
  0.6 2.5 %copy-start.11 = (bf16[512,512]{1,0:T(8,128)(2,1)S(1)}, bf16[512,512]{1,0:T(8,128)(2,1)}, u32[]{:S(2)}) copy-start(bf16[512,512]{1,0:T(8,128)(2,1)} %param.12) | copy-start | bytes 1572868
  6.0 1.0 copy-start.4
  8.0 4.7 %copy-start.5 = (bf16[512,256]{0,1:T(8,128)(2,1)}, bf16[512,256]{0,1:T(8,128)(2,1)S(1)}, u32[]{:S(2)}) copy-start(bf16[512,256]{0,1:T(8,128)(2,1)S(1)} %copy.59) | copy-start | bytes 786436
  9.2 3.5 %copy-start.7 = (bf16[512,256]{0,1:T(8,128)(2,1)}, bf16[512,256]{0,1:T(8,128)(2,1)S(1)}, u32[]{:S(2)}) copy-start(bf16[512,256]{0,1:T(8,128)(2,1)S(1)} %copy.57) | copy-start | bytes 786436
  12.7 1.3 copy-start.1
  14.1 1.1 copy-start.2
  20.5 2.2 copy-start.8
  20.5 2.2 copy-start.10
  22.7 4.6 %copy-start.6 = (bf16[512,256]{0,1:T(8,128)(2,1)S(1)}, bf16[512,256]{0,1:T(8,128)(2,1)}, u32[]{:S(2)}) copy-start(bf16[512,256]{0,1:T(8,128)(2,1)} %copy-done.5) | copy-start | bytes 786436
  29.9 2.3 copy-start.9
  35.5 1.0 copy-start.3
  35.6 1.3 copy-start.15
  35.6 1.5 copy-start.16
  35.6 1.5 copy-start.12
  48.4 159.2 %all-to-all-start = ((bf16[128,65,128]{2,1,0:T(8,128)(2,1)}), bf16[128,65,128]{2,1,0:T(8,128)(2,1)}, u32[]{:S(2)}, u32[]{:S(2)}) async-start(bf16[128,65,128]{2,1,0:T(8,128)(2,1)} %fusion.6), calls=%async_computation | async-start | bytes 4718592 | tf_op jit(solution)/shard_map/all_to_all | solution.py:156
  79.3 5.1 %collective-permute-start = (f32[16,4,1,4,1280]{4,3,2,1,0:T(4,128)S(1)}, f32[16,4,1,4,1280]{4,3,2,1,0:T(4,128)}, u32[]{:S(2)}, u32[]{:S(2)}) collective-permute-start(f32[16,4,1,4,1280]{4,3,2,1,0:T(4,128)S(1)} %constant_dynamic-slice_fusion.6), channel_id=1, source_target_pairs={{0,4},{4,0},{1,5},{5,1},{2,6},{6,2},{3,7},{7,3},{8,12},{12,8},{9,1... | collective-permute-start | bytes 3932168 | tf_op jit(solution)/shard_map/ppermute | solution.py:84
  86.5 22.6 %collective-permute-start.1 = (f32[16,2,1,4,1280]{4,3,2,1,0:T(4,128)S(1)}, f32[16,2,1,4,1280]{4,3,2,1,0:T(4,128)}, u32[]{:S(2)}, u32[]{:S(2)}) collective-permute-start(f32[16,2,1,4,1280]{4,3,2,1,0:T(4,128)S(1)} %constant_dynamic-slice_fusion.5), channel_id=1, source_target_pairs={{0,8},{8,0},{16,24},{24,16},{1,9},{9,1},{17,25},{25,17},{2,10},{10... | collective-permute-start | bytes 1966088 | tf_op jit(solution)/shard_map/ppermute | solution.py:84
  110.4 15.1 %collective-permute-start.2 = (f32[16,1,1,4,1280]{4,3,2,1,0:T(4,128)S(1)}, f32[16,1,1,4,1280]{4,3,2,1,0:T(4,128)S(1)}, u32[]{:S(2)}, u32[]{:S(2)}) collective-permute-start(f32[16,1,1,4,1280]{4,3,2,1,0:T(4,128)S(1)} %constant_dynamic-slice_fusion.4), channel_id=1, source_target_pairs={{0,16},{8,24},{16,0},{24,8},{1,17},{9,25},{17,1},{25,9},{2,18},{10... | collective-permute-start | bytes 983048 | tf_op jit(solution)/shard_map/ppermute | solution.py:84
  125.6 48.7 %collective-permute-start.3 = (f32[2,2,2,1,4,1280]{5,4,3,2,1,0:T(4,128)S(1)}, f32[2,2,2,1,4,1280]{5,4,3,2,1,0:T(4,128)S(1)}, u32[]{:S(2)}, u32[]{:S(2)}) collective-permute-start(f32[2,2,2,1,4,1280]{5,4,3,2,1,0:T(4,128)S(1)} %constant_dynamic-slice_fusion.3), channel_id=1, source_target_pairs={{0,32},{32,0},{64,96},{96,64},{128,160},{160,128},{192,224},{224,1... | collective-permute-start | bytes 491528 | tf_op jit(solution)/shard_map/ppermute | solution.py:84
  174.4 8.4 %collective-permute-start.4 = (f32[2,2,1,1,4,1280]{5,4,3,2,1,0:T(4,128)S(1)}, f32[2,2,1,1,4,1280]{5,4,3,2,1,0:T(4,128)S(1)}, u32[]{:S(2)}, u32[]{:S(2)}) collective-permute-start(f32[2,2,1,1,4,1280]{5,4,3,2,1,0:T(4,128)S(1)} %constant_dynamic-slice_fusion.2), channel_id=1, source_target_pairs={{0,64},{32,96},{64,0},{96,32},{128,192},{160,224},{192,128},{224,1... | collective-permute-start | bytes 245768 | tf_op jit(solution)/shard_map/ppermute | solution.py:84
  182.9 10.2 %collective-permute-start.5 = (f32[2,1,1,1,4,1280]{5,4,3,2,1,0:T(4,128)S(1)}, f32[2,1,1,1,4,1280]{5,4,3,2,1,0:T(4,128)S(1)}, u32[]{:S(2)}, u32[]{:S(2)}) collective-permute-start(f32[2,1,1,1,4,1280]{5,4,3,2,1,0:T(4,128)S(1)} %constant_dynamic-slice_fusion.1), channel_id=1, source_target_pairs={{0,128},{32,160},{64,192},{96,224},{128,0},{160,32},{192,64},{224,... | collective-permute-start | bytes 122888 | tf_op jit(solution)/shard_map/ppermute | solution.py:84
  193.2 14.4 %collective-permute-start.6 = (f32[1,1,1,1,4,1280]{5,4,3,2,1,0:T(4,128)S(1)}, f32[1,1,1,1,4,1280]{5,4,3,2,1,0:T(4,128)S(1)}, u32[]{:S(2)}, u32[]{:S(2)}) collective-permute-start(f32[1,1,1,1,4,1280]{5,4,3,2,1,0:T(4,128)S(1)} %constant_dynamic-slice_fusion), channel_id=1, source_target_pairs={{0,256},{32,288},{64,320},{96,352},{128,384},{160,416},{192,448},{... | collective-permute-start | bytes 61448 | tf_op jit(solution)/shard_map/ppermute | solution.py:84
  215.8 22.0 %copy-start.17 = (f32[128]{0:T(128)S(1)}, f32[128]{0:T(128)}, u32[]{:S(2)}) copy-start(f32[128]{0:T(128)} %param.21) | copy-start | bytes 1540
  215.8 22.5 %copy-start.13 = (f32[128,512]{1,0:T(8,128)S(1)}, f32[128,512]{1,0:T(8,128)}, u32[]{:S(2)}) copy-start(f32[128,512]{1,0:T(8,128)} %param.20) | copy-start | bytes 786436
  215.8 22.5 %copy-start.14 = (f32[128,512]{1,0:T(8,128)S(1)}, f32[128,512]{1,0:T(8,128)}, u32[]{:S(2)}) copy-start(f32[128,512]{1,0:T(8,128)} %param.19) | copy-start | bytes 786436
  215.9 9.6 %collective-permute-start.7 = (f32[136,640]{1,0:T(8,128)S(1)}, f32[136,640]{1,0:T(8,128)S(1)}, u32[]{:S(2)}, u32[]{:S(2)}) collective-permute-start(f32[136,640]{1,0:T(8,128)S(1)} %pad_maximum_fusion.1), channel_id=1, source_target_pairs={{0,1},{1,0},{2,3},{3,2},{4,5},{5,4},{6,7},{7,6},{8,9},{9,8},{10,11... | collective-permute-start | bytes 1044488 | tf_op jit(solution)/shard_map/ppermute | solution.py:90
  225.6 10.7 %collective-permute-start.8 = (f32[136,640]{1,0:T(8,128)S(1)}, f32[136,640]{1,0:T(8,128)S(1)}, u32[]{:S(2)}, u32[]{:S(2)}) collective-permute-start(f32[136,640]{1,0:T(8,128)S(1)} %fusion.43), channel_id=1, source_target_pairs={{0,2},{1,3},{2,0},{3,1},{4,6},{5,7},{6,4},{7,5},{8,10},{9,11},{10,... | collective-permute-start | bytes 1044488 | tf_op jit(solution)/shard_map/ppermute | solution.py:90

commit v7 on v6

--- a/solution.py
+++ b/solution.py
@@ -143,10 +143,20 @@
     )
     position_to = owner_of * capacity + earlier
     chosen = position_to[None, :] == jnp.arange(buffer_rows, dtype=jnp.int32)[:, None]
-    outgoing = jnp.dot(
-        chosen.astype(jnp.bfloat16), emb_grad, preferred_element_type=jnp.float32
-    ).astype(jnp.bfloat16)
-    outgoing = outgoing.reshape(owner_count, capacity, width)
+    lane_blocks = width // 128
+    outgoing = jnp.stack(
+        [
+            jnp.dot(
+                chosen.astype(jnp.bfloat16),
+                emb_grad[:, j * 128 : (j + 1) * 128],
+                preferred_element_type=jnp.float32,
+            )
+            .astype(jnp.bfloat16)
+            .reshape(owner_count, capacity, 128)
+            for j in range(lane_blocks)
+        ],
+        axis=1,
+    )
     out_slots = (jnp.sum(jnp.where(chosen, slots[None, :] + 1, 0), axis=1) - 1).reshape(
         owner_count, capacity
     )
@@ -161,11 +171,21 @@
         tiled=True,
     )
     arrived, weight_share = lax.optimization_barrier((arrived, weight_share))
-    received = arrived[:, :block_rows, :].reshape(buffer_rows, width)
+    received = arrived[:, :block_rows, :].reshape(owner_count, lane_blocks, capacity, 128)
     got_slots = arrived[:, block_rows, :capacity].astype(jnp.int32).reshape(buffer_rows)
     slot_count = emb_rows.shape[0]
     matches = got_slots[None, :] == jnp.arange(slot_count, dtype=jnp.int32)[:, None]
-    grad_part = jnp.dot(matches.astype(jnp.bfloat16), received, preferred_element_type=jnp.float32)
+    grad_part = jnp.concatenate(
+        [
+            jnp.dot(
+                matches.astype(jnp.bfloat16),
+                received[:, j].reshape(buffer_rows, 128),
+                preferred_element_type=jnp.float32,
+            )
+            for j in range(lane_blocks)
+        ],
+        axis=1,
+    )
     count_part = jnp.sum(matches.astype(jnp.float32), axis=1)
     lanes = width + 128
     both = double_sum(

time: 241 us -> 242 us (level)
  matrix products: 24.9 us -> 29.9 us
    dot_general x2 -> x8, matrix products: 3.38 us -> 8.21 us  [the longest x4 5.61 us: local(): jnp.dot(chosen.astype(jnp.bfloat16), emb_grad[:, j * 128:(j + 1) * 128],...]
    another operation x1 -> x0, local copies, waits for them, and re-layouts: 4.35 us -> none  [local(): outgoing.reshape(owner_count, block_rows, 128)]
    reshape x1 -> x0, local copies, waits for them, and re-layouts: 3.1 us -> none  [local(): received = arrived[:, :block_rows, :].reshape(buffer_rows, width)]
    unnamed x38 -> x35, local copies, waits for them, and re-layouts: 3.83 us -> 5.95 us
where the time goes in v7:
time: 242 us; the launch traced here: 241 us
  waiting for transfers between devices  103 us (43%)
  starting transfers between devices  61 us (25%)
  matrix products  29.9 us (12%)
  local copies, waits for them, and re-layouts  26.2 us (11%)
  other arithmetic  19.1 us (8%)
    ppermute x7, waiting for transfers between devices, halve_sum(): blocks = keep + lax.ppermute(send, axis, pairs)  90.4 us
    ppermute x7, starting transfers between devices, halve_sum(): blocks = keep + lax.ppermute(send, axis, pairs)  34.2 us
    all_to_all x1, starting transfers between devices, local(): lax.all_to_all(jnp.concatenate([outgoing.reshape(owner_count, block_rows,...  20.6 us
    ppermute x2, waiting for transfers between devices, double_sum(): lax.ppermute(value, axis, [(i, i ^ 1 << bit) for i in range(size)])  13 us
    dot_general x3, matrix products, core(): jnp.einsum('hts,shd->thd', weights, values_part, preferred_element_type=j...  7.65 us
    ppermute x2, starting transfers between devices, double_sum(): lax.ppermute(value, axis, [(i, i ^ 1 << bit) for i in range(size)])  6.21 us
    dot_general x3, matrix products, core(): jnp.einsum('thd,shd->hts', queries, keys_part, preferred_element_type=jnp...  6.14 us
    unnamed x35, local copies, waits for them, and re-layouts  5.95 us
  transfers between devices with their start and end apart: 10, of which 9 were waited for; matrix products, arithmetic and copies ran while one was open for 6% of the time, Pallas kernels for 0%

profile of v7, /device:TPU:6, one launch (start us, length us, event | category | flops | bytes accessed | tf_op | source)
XLA Modules:
  0.0 240.8 jit_solution(8045183289048549085)
XLA Ops:
  0.7 0.9 reduce-window.8
  1.9 1.3 fusion.30
  3.7 2.3 multiply_convert_fusion.1
  6.0 1.0 copy-done.4
  7.0 0.8 fusion.59
  8.0 1.2 copy.95
  9.2 3.5 %multiply_convert_fusion = (bf16[4,512,512]{2,1,0:T(8,128)(2,1)S(1)}, f32[4,512,512]{2,1,0:T(8,128)}) fusion(f32[512,512]{1,0:T(8,128)S(1)} %fusion.31, bf16[512,4,64]{0,2,1:T(8,128)(2,1)S(1)} %bitcast.83, bf16[512,4,64]{0,2,1:T(8,128)(2,1)S(1)} %bitcast.85), kind=kOutput, calls=%fused_computation.7 | convolution fusion | flops 142606336 | bytes 7864320 | tf_op jit(solution)/shard_map/jvp(thd,shd->hts)/dot_general | solution.py:46
  12.7 1.3 copy-done.1
  14.1 0.8 fusion.60
  15.1 1.4 multiply_reduce_fusion
  16.6 1.9 fusion.57
  18.5 0.8 broadcast_add_fusion
  19.4 1.1 copy.100
  20.5 2.9 %fusion.63 = bf16[4,64,512]{2,1,0:T(8,128)(2,1)} fusion(bf16[4,64,512]{2,1,0:T(8,128)(2,1)S(1)} %bitcast.90, bf16[4,512,512]{2,1,0:T(8,128)(2,1)} %copy-done.1), kind=kOutput, calls=%fused_computation.135 | convolution fusion | flops 134217728 | bytes 2621440 | tf_op jit(solution)/shard_map/transpose(jvp(hts,shd->thd))/dot_general | solution.py:50
  23.3 4.0 %fusion.3 = bf16[4,512,512]{2,1,0:T(8,128)(2,1)S(1)} fusion(f32[4,512,512]{2,1,0:T(8,128)} %get-tuple-element.62, f32[512,512]{1,0:T(8,128)S(1)} %copy-done.8, bf16[4,64,512]{2,1,0:T(8,128)(2,1)S(1)} %bitcast.91, bf16[512,4,64]{0,2,1:T(8,128)(2,1)} %bitcast.88), kind=kOutput, calls=%fused_computation.5 | convolution fusion | flops 148897792 | bytes 7864320 | tf_op jit(solution)/shard_map/transpose(jvp(hts,shd->thd))/dot_general | solution.py:50
  27.4 1.5 fusion.62
  28.8 1.2 fusion.61
  30.2 1.1 copy.101
  31.3 1.8 copy.102
  33.1 1.8 copy.103
  34.9 2.6 %fusion.14 = bf16[512,1024]{1,0:T(8,128)(2,1)S(1)} fusion(f32[512,1024]{1,0:T(8,128)} %get-tuple-element.60, bf16[512,256]{1,0:T(8,128)(2,1)} %copy.103, bf16[512,256]{1,0:T(8,128)(2,1)} %copy.102, bf16[512,256]{1,0:T(8,128)(2,1)S(1)} %copy.101, bf16[512,256]{1,0:T(8,128)(2,1)} %get-tuple-element.49), kind=kLoop, calls=%fused_computation.24 | loop fusion | flops 9437184 | bytes 4194304 | tf_op jit(solution)/shard_map/convert_element_type | solution.py:114
  37.5 0.8 fusion.27
  39.5 0.8 fusion.8
  40.2 1.6 fusion.9
  41.8 1.6 fusion.10
  43.5 1.6 fusion.11
  45.1 0.5 select_reduce_fusion
  45.7 1.6 pad_maximum_fusion.1
  47.3 1.8 fusion.12
  49.1 20.6 %all-to-all-start = ((bf16[128,65,128]{2,1,0:T(8,128)(2,1)}), bf16[128,65,128]{2,1,0:T(8,128)(2,1)}, u32[]{:S(2)}, u32[]{:S(2)}) async-start(bf16[128,65,128]{2,1,0:T(8,128)(2,1)} %fusion.12), calls=%async_computation | async-start | bytes 4718592 | tf_op jit(solution)/shard_map/all_to_all | solution.py:166
  69.7 1.5 convolution_bitcast_fusion
  71.2 1.9 fusion.40
  73.1 1.7 pad_maximum_fusion
  74.9 3.9 %reshape.254 = f32[16,4,2,4,1280]{4,3,2,1,0:T(4,128)} reshape(f32[512,1280]{1,0:T(8,128)} %pad_maximum_fusion) | data formatting | bytes 5242880 | tf_op jit(solution)/shard_map/reshape | solution.py:98
  78.8 2.5 %constant_dynamic-slice_fusion.7 = f32[16,4,1,4,1280]{4,3,2,1,0:T(4,128)} fusion(f32[16,4,2,4,1280]{4,3,2,1,0:T(4,128)} %reshape.254, s32[]{:T(128)S(6)} %select_n.66), kind=kLoop, calls=%fused_computation.111 | loop fusion | bytes 2621444 | tf_op jit(solution)/shard_map/jit(dynamic_index_in_dim)/dynamic_slice | solution.py:82
  81.3 1.9 collective-permute-start
  83.2 3.2 %collective-permute-done = f32[16,4,1,4,1280]{4,3,2,1,0:T(4,128)S(1)} collective-permute-done((f32[16,4,1,4,1280]{4,3,2,1,0:T(4,128)}, f32[16,4,1,4,1280]{4,3,2,1,0:T(4,128)S(1)}, u32[]{:S(2)}, u32[]{:S(2)}) %collective-permute-start) | collective-permute-done | bytes 1310752 | tf_op jit(solution)/shard_map/ppermute | solution.py:84
  86.4 1.7 dynamic-slice_add_fusion
  88.2 2.8 %collective-permute-start.1 = (f32[16,2,1,4,1280]{4,3,0,2,1:T(4,128)S(1)}, f32[16,2,1,4,1280]{4,3,0,2,1:T(4,128)S(1)}, u32[]{:S(2)}, u32[]{:S(2)}) collective-permute-start(f32[16,2,1,4,1280]{4,3,0,2,1:T(4,128)S(1)} %copy.128), channel_id=1, source_target_pairs={{0,8},{8,0},{16,24},{24,16},{1,9},{9,1},{17,25},{25,17},{2,10},{10... | collective-permute-start | bytes 1966088 | tf_op jit(solution)/shard_map/ppermute | solution.py:84
  91.0 19.7 %collective-permute-done.1 = f32[16,2,1,4,1280]{4,3,0,2,1:T(4,128)S(1)} collective-permute-done((f32[16,2,1,4,1280]{4,3,0,2,1:T(4,128)S(1)}, f32[16,2,1,4,1280]{4,3,0,2,1:T(4,128)S(1)}, u32[]{:S(2)}, u32[]{:S(2)}) %collective-permute-start.1) | collective-permute-done | bytes 655392 | tf_op jit(solution)/shard_map/ppermute | solution.py:84
  110.9 4.0 %collective-permute-start.2 = (f32[16,1,1,4,1280]{4,3,0,2,1:T(4,128)S(1)}, f32[16,1,1,4,1280]{4,3,0,2,1:T(4,128)S(1)}, u32[]{:S(2)}, u32[]{:S(2)}) collective-permute-start(f32[16,1,1,4,1280]{4,3,0,2,1:T(4,128)S(1)} %constant_dynamic-slice_fusion.4), channel_id=1, source_target_pairs={{0,16},{8,24},{16,0},{24,8},{1,17},{9,25},{17,1},{25,9},{2,18},{10... | collective-permute-start | bytes 983048 | tf_op jit(solution)/shard_map/ppermute | solution.py:84
  114.9 11.3 %collective-permute-done.2 = f32[16,1,1,4,1280]{4,3,0,2,1:T(4,128)S(1)} collective-permute-done((f32[16,1,1,4,1280]{4,3,0,2,1:T(4,128)S(1)}, f32[16,1,1,4,1280]{4,3,0,2,1:T(4,128)S(1)}, u32[]{:S(2)}, u32[]{:S(2)}) %collective-permute-start.2) | collective-permute-done | bytes 327712 | tf_op jit(solution)/shard_map/ppermute | solution.py:84
  126.3 2.5 %collective-permute-start.3 = (f32[2,2,2,1,4,1280]{5,4,3,2,1,0:T(4,128)S(1)}, f32[2,2,2,1,4,1280]{5,4,3,2,1,0:T(4,128)S(1)}, u32[]{:S(2)}, u32[]{:S(2)}) collective-permute-start(f32[2,2,2,1,4,1280]{5,4,3,2,1,0:T(4,128)S(1)} %constant_dynamic-slice_fusion.3), channel_id=1, source_target_pairs={{0,32},{32,0},{64,96},{96,64},{128,160},{160,128},{192,224},{224,1... | collective-permute-start | bytes 491528 | tf_op jit(solution)/shard_map/ppermute | solution.py:84
  128.9 46.2 %collective-permute-done.3 = f32[2,2,2,1,4,1280]{5,4,3,2,1,0:T(4,128)S(1)} collective-permute-done((f32[2,2,2,1,4,1280]{5,4,3,2,1,0:T(4,128)S(1)}, f32[2,2,2,1,4,1280]{5,4,3,2,1,0:T(4,128)S(1)}, u32[]{:S(2)}, u32[]{:S(2)}) %collective-permute-start.3) | collective-permute-done | bytes 163872 | tf_op jit(solution)/shard_map/ppermute | solution.py:84
  175.2 3.7 %collective-permute-start.4 = (f32[2,2,1,1,4,1280]{5,4,3,2,1,0:T(4,128)S(1)}, f32[2,2,1,1,4,1280]{5,4,3,2,1,0:T(4,128)S(1)}, u32[]{:S(2)}, u32[]{:S(2)}) collective-permute-start(f32[2,2,1,1,4,1280]{5,4,3,2,1,0:T(4,128)S(1)} %constant_dynamic-slice_fusion.2), channel_id=1, source_target_pairs={{0,64},{32,96},{64,0},{96,32},{128,192},{160,224},{192,128},{224,1... | collective-permute-start | bytes 245768 | tf_op jit(solution)/shard_map/ppermute | solution.py:84
  178.8 4.7 %collective-permute-done.4 = f32[2,2,1,1,4,1280]{5,4,3,2,1,0:T(4,128)S(1)} collective-permute-done((f32[2,2,1,1,4,1280]{5,4,3,2,1,0:T(4,128)S(1)}, f32[2,2,1,1,4,1280]{5,4,3,2,1,0:T(4,128)S(1)}, u32[]{:S(2)}, u32[]{:S(2)}) %collective-permute-start.4) | collective-permute-done | bytes 81952 | tf_op jit(solution)/shard_map/ppermute | solution.py:84
  183.6 7.4 %collective-permute-start.5 = (f32[2,1,1,1,4,1280]{5,4,3,2,1,0:T(4,128)S(1)}, f32[2,1,1,1,4,1280]{5,4,3,2,1,0:T(4,128)S(1)}, u32[]{:S(2)}, u32[]{:S(2)}) collective-permute-start(f32[2,1,1,1,4,1280]{5,4,3,2,1,0:T(4,128)S(1)} %constant_dynamic-slice_fusion.1), channel_id=1, source_target_pairs={{0,128},{32,160},{64,192},{96,224},{128,0},{160,32},{192,64},{224,... | collective-permute-start | bytes 122888 | tf_op jit(solution)/shard_map/ppermute | solution.py:84
  191.1 2.8 %collective-permute-done.5 = f32[2,1,1,1,4,1280]{5,4,3,2,1,0:T(4,128)S(1)} collective-permute-done((f32[2,1,1,1,4,1280]{5,4,3,2,1,0:T(4,128)S(1)}, f32[2,1,1,1,4,1280]{5,4,3,2,1,0:T(4,128)S(1)}, u32[]{:S(2)}, u32[]{:S(2)}) %collective-permute-start.5) | collective-permute-done | bytes 40992 | tf_op jit(solution)/shard_map/ppermute | solution.py:84
  193.9 11.9 %collective-permute-start.6 = (f32[1,1,1,1,4,1280]{5,4,3,2,1,0:T(4,128)S(1)}, f32[1,1,1,1,4,1280]{5,4,3,2,1,0:T(4,128)S(1)}, u32[]{:S(2)}, u32[]{:S(2)}) collective-permute-start(f32[1,1,1,1,4,1280]{5,4,3,2,1,0:T(4,128)S(1)} %constant_dynamic-slice_fusion), channel_id=1, source_target_pairs={{0,256},{32,288},{64,320},{96,352},{128,384},{160,416},{192,448},{... | collective-permute-start | bytes 61448 | tf_op jit(solution)/shard_map/ppermute | solution.py:84
  205.8 2.5 %collective-permute-done.6 = f32[1,1,1,1,4,1280]{5,4,3,2,1,0:T(4,128)S(1)} collective-permute-done((f32[1,1,1,1,4,1280]{5,4,3,2,1,0:T(4,128)S(1)}, f32[1,1,1,1,4,1280]{5,4,3,2,1,0:T(4,128)S(1)}, u32[]{:S(2)}, u32[]{:S(2)}) %collective-permute-start.6) | collective-permute-done | bytes 20512 | tf_op jit(solution)/shard_map/ppermute | solution.py:84
  208.3 1.8 slice.73
  210.1 1.2 convert_reduce_fusion.3
  211.2 1.2 fusion.58
  212.7 1.4 convolution_dynamic-update-slice_fusion.3
  215.8 2.9 %collective-permute-start.7 = (f32[136,640]{1,0:T(8,128)S(1)}, f32[136,640]{1,0:T(8,128)S(1)}, u32[]{:S(2)}, u32[]{:S(2)}) collective-permute-start(f32[136,640]{1,0:T(8,128)S(1)} %copy.114), channel_id=1, source_target_pairs={{0,1},{1,0},{2,3},{3,2},{4,5},{5,4},{6,7},{7,6},{8,9},{9,8},{10,11... | collective-permute-start | bytes 1044488 | tf_op jit(solution)/shard_map/ppermute | solution.py:90
  218.6 6.8 %collective-permute-done.7 = f32[136,640]{1,0:T(8,128)S(1)} collective-permute-done((f32[136,640]{1,0:T(8,128)S(1)}, f32[136,640]{1,0:T(8,128)S(1)}, u32[]{:S(2)}, u32[]{:S(2)}) %collective-permute-start.7) | collective-permute-done | bytes 348192 | tf_op jit(solution)/shard_map/ppermute | solution.py:90
  226.0 3.3 %collective-permute-start.8 = (f32[136,640]{1,0:T(8,128)S(1)}, f32[136,640]{1,0:T(8,128)S(1)}, u32[]{:S(2)}, u32[]{:S(2)}) collective-permute-start(f32[136,640]{1,0:T(8,128)S(1)} %copy.116), channel_id=1, source_target_pairs={{0,2},{1,3},{2,0},{3,1},{4,6},{5,7},{6,4},{7,5},{8,10},{9,11},{10,... | collective-permute-start | bytes 1044488 | tf_op jit(solution)/shard_map/ppermute | solution.py:90
  229.5 1.1 copy.119
  230.6 6.1 %collective-permute-done.8 = f32[136,640]{1,0:T(8,128)S(1)} collective-permute-done((f32[136,640]{1,0:T(8,128)S(1)}, f32[136,640]{1,0:T(8,128)S(1)}, u32[]{:S(2)}, u32[]{:S(2)}) %collective-permute-start.8) | collective-permute-done | bytes 348192 | tf_op jit(solution)/shard_map/ppermute | solution.py:90
  237.3 0.6 slice.94
  237.9 0.6 slice.95
  238.5 0.5 fusion.55
  239.1 0.8 copy.123
  239.9 0.8 copy.124
  (85 shorter events, 6.6 us)
Async XLA Ops:
  0.6 3.0 %copy-start = (bf16[512,1024]{1,0:T(8,128)(2,1)S(1)}, bf16[512,1024]{1,0:T(8,128)(2,1)}, u32[]{:S(2)}) copy-start(bf16[512,1024]{1,0:T(8,128)(2,1)} %param.17) | copy-start | bytes 3145732
  0.6 2.5 %copy-start.9 = (bf16[512,512]{1,0:T(8,128)(2,1)S(1)}, bf16[512,512]{1,0:T(8,128)(2,1)}, u32[]{:S(2)}) copy-start(bf16[512,512]{1,0:T(8,128)(2,1)} %param.12) | copy-start | bytes 1572868
  6.0 1.0 copy-start.4
  8.0 4.7 %copy-start.5 = (bf16[512,256]{0,1:T(8,128)(2,1)}, bf16[512,256]{0,1:T(8,128)(2,1)S(1)}, u32[]{:S(2)}) copy-start(bf16[512,256]{0,1:T(8,128)(2,1)S(1)} %copy.97) | copy-start | bytes 786436
  9.2 3.5 %copy-start.7 = (bf16[512,256]{0,1:T(8,128)(2,1)}, bf16[512,256]{0,1:T(8,128)(2,1)S(1)}, u32[]{:S(2)}) copy-start(bf16[512,256]{0,1:T(8,128)(2,1)S(1)} %copy.95) | copy-start | bytes 786436
  12.7 1.3 copy-start.1
  14.1 1.1 copy-start.2
  20.5 2.9 %copy-start.8 = (f32[512,512]{1,0:T(8,128)S(1)}, f32[512,512]{1,0:T(8,128)}, u32[]{:S(2)}) copy-start(f32[512,512]{1,0:T(8,128)} %fusion.30) | copy-start | bytes 3145732
  23.3 4.0 %copy-start.6 = (bf16[512,256]{0,1:T(8,128)(2,1)S(1)}, bf16[512,256]{0,1:T(8,128)(2,1)}, u32[]{:S(2)}) copy-start(bf16[512,256]{0,1:T(8,128)(2,1)} %copy-done.5) | copy-start | bytes 786436
  37.5 1.0 copy-start.3
  37.5 1.3 copy-start.11
  38.5 0.9 copy-start.12
  49.1 159.2 %all-to-all-start = ((bf16[128,65,128]{2,1,0:T(8,128)(2,1)}), bf16[128,65,128]{2,1,0:T(8,128)(2,1)}, u32[]{:S(2)}, u32[]{:S(2)}) async-start(bf16[128,65,128]{2,1,0:T(8,128)(2,1)} %fusion.12), calls=%async_computation | async-start | bytes 4718592 | tf_op jit(solution)/shard_map/all_to_all | solution.py:166
  81.3 5.1 %collective-permute-start = (f32[16,4,1,4,1280]{4,3,2,1,0:T(4,128)}, f32[16,4,1,4,1280]{4,3,2,1,0:T(4,128)S(1)}, u32[]{:S(2)}, u32[]{:S(2)}) collective-permute-start(f32[16,4,1,4,1280]{4,3,2,1,0:T(4,128)} %constant_dynamic-slice_fusion.7), channel_id=1, source_target_pairs={{0,4},{4,0},{1,5},{5,1},{2,6},{6,2},{3,7},{7,3},{8,12},{12,8},{9,1... | collective-permute-start | bytes 3932168 | tf_op jit(solution)/shard_map/ppermute | solution.py:84
  88.2 22.4 %collective-permute-start.1 = (f32[16,2,1,4,1280]{4,3,0,2,1:T(4,128)S(1)}, f32[16,2,1,4,1280]{4,3,0,2,1:T(4,128)S(1)}, u32[]{:S(2)}, u32[]{:S(2)}) collective-permute-start(f32[16,2,1,4,1280]{4,3,0,2,1:T(4,128)S(1)} %copy.128), channel_id=1, source_target_pairs={{0,8},{8,0},{16,24},{24,16},{1,9},{9,1},{17,25},{25,17},{2,10},{10... | collective-permute-start | bytes 1966088 | tf_op jit(solution)/shard_map/ppermute | solution.py:84
  110.9 15.3 %collective-permute-start.2 = (f32[16,1,1,4,1280]{4,3,0,2,1:T(4,128)S(1)}, f32[16,1,1,4,1280]{4,3,0,2,1:T(4,128)S(1)}, u32[]{:S(2)}, u32[]{:S(2)}) collective-permute-start(f32[16,1,1,4,1280]{4,3,0,2,1:T(4,128)S(1)} %constant_dynamic-slice_fusion.4), channel_id=1, source_target_pairs={{0,16},{8,24},{16,0},{24,8},{1,17},{9,25},{17,1},{25,9},{2,18},{10... | collective-permute-start | bytes 983048 | tf_op jit(solution)/shard_map/ppermute | solution.py:84
  126.3 48.8 %collective-permute-start.3 = (f32[2,2,2,1,4,1280]{5,4,3,2,1,0:T(4,128)S(1)}, f32[2,2,2,1,4,1280]{5,4,3,2,1,0:T(4,128)S(1)}, u32[]{:S(2)}, u32[]{:S(2)}) collective-permute-start(f32[2,2,2,1,4,1280]{5,4,3,2,1,0:T(4,128)S(1)} %constant_dynamic-slice_fusion.3), channel_id=1, source_target_pairs={{0,32},{32,0},{64,96},{96,64},{128,160},{160,128},{192,224},{224,1... | collective-permute-start | bytes 491528 | tf_op jit(solution)/shard_map/ppermute | solution.py:84
  175.2 8.4 %collective-permute-start.4 = (f32[2,2,1,1,4,1280]{5,4,3,2,1,0:T(4,128)S(1)}, f32[2,2,1,1,4,1280]{5,4,3,2,1,0:T(4,128)S(1)}, u32[]{:S(2)}, u32[]{:S(2)}) collective-permute-start(f32[2,2,1,1,4,1280]{5,4,3,2,1,0:T(4,128)S(1)} %constant_dynamic-slice_fusion.2), channel_id=1, source_target_pairs={{0,64},{32,96},{64,0},{96,32},{128,192},{160,224},{192,128},{224,1... | collective-permute-start | bytes 245768 | tf_op jit(solution)/shard_map/ppermute | solution.py:84
  183.6 10.2 %collective-permute-start.5 = (f32[2,1,1,1,4,1280]{5,4,3,2,1,0:T(4,128)S(1)}, f32[2,1,1,1,4,1280]{5,4,3,2,1,0:T(4,128)S(1)}, u32[]{:S(2)}, u32[]{:S(2)}) collective-permute-start(f32[2,1,1,1,4,1280]{5,4,3,2,1,0:T(4,128)S(1)} %constant_dynamic-slice_fusion.1), channel_id=1, source_target_pairs={{0,128},{32,160},{64,192},{96,224},{128,0},{160,32},{192,64},{224,... | collective-permute-start | bytes 122888 | tf_op jit(solution)/shard_map/ppermute | solution.py:84
  193.9 14.4 %collective-permute-start.6 = (f32[1,1,1,1,4,1280]{5,4,3,2,1,0:T(4,128)S(1)}, f32[1,1,1,1,4,1280]{5,4,3,2,1,0:T(4,128)S(1)}, u32[]{:S(2)}, u32[]{:S(2)}) collective-permute-start(f32[1,1,1,1,4,1280]{5,4,3,2,1,0:T(4,128)S(1)} %constant_dynamic-slice_fusion), channel_id=1, source_target_pairs={{0,256},{32,288},{64,320},{96,352},{128,384},{160,416},{192,448},{... | collective-permute-start | bytes 61448 | tf_op jit(solution)/shard_map/ppermute | solution.py:84
  215.8 13.6 %copy-start.10 = (f32[128,512]{1,0:T(8,128)S(1)}, f32[128,512]{1,0:T(8,128)}, u32[]{:S(2)}) copy-start(f32[128,512]{1,0:T(8,128)} %param.20) | copy-start | bytes 786436
  215.8 9.7 %collective-permute-start.7 = (f32[136,640]{1,0:T(8,128)S(1)}, f32[136,640]{1,0:T(8,128)S(1)}, u32[]{:S(2)}, u32[]{:S(2)}) collective-permute-start(f32[136,640]{1,0:T(8,128)S(1)} %copy.114), channel_id=1, source_target_pairs={{0,1},{1,0},{2,3},{3,2},{4,5},{5,4},{6,7},{7,6},{8,9},{9,8},{10,11... | collective-permute-start | bytes 1044488 | tf_op jit(solution)/shard_map/ppermute | solution.py:90
  226.0 10.7 %collective-permute-start.8 = (f32[136,640]{1,0:T(8,128)S(1)}, f32[136,640]{1,0:T(8,128)S(1)}, u32[]{:S(2)}, u32[]{:S(2)}) collective-permute-start(f32[136,640]{1,0:T(8,128)S(1)} %copy.116), channel_id=1, source_target_pairs={{0,2},{1,3},{2,0},{3,1},{4,6},{5,7},{6,4},{7,5},{8,10},{9,11},{10,... | collective-permute-start | bytes 1044488 | tf_op jit(solution)/shard_map/ppermute | solution.py:90
  230.6 7.9 %copy-start.13 = (f32[128]{0:T(128)S(1)}, f32[128]{0:T(128)}, u32[]{:S(2)}) copy-start(f32[128]{0:T(128)} %param.21) | copy-start | bytes 1540

commit v8 on v6

--- a/solution.py
+++ b/solution.py
@@ -93,13 +93,17 @@
 
 def reduce_weights(partial, sizes):
     width = partial.shape[1]
-    n_z, n_y, n_c = sizes["z"], sizes["y"], sizes["core"]
+    n_z, n_y, n_c, n_x = sizes["z"], sizes["y"], sizes["core"], sizes["x"]
     per_owner = partial.shape[0] // (n_z * n_y * n_c)
     blocks = partial.reshape(n_z, n_y, n_c, per_owner, width)
     blocks = halve_sum(blocks, "core", n_c, 2)
-    blocks = halve_sum(blocks, "y", n_y, 1)
-    blocks = halve_sum(blocks, "z", n_z, 0)
-    return blocks.reshape(per_owner, width)
+    blocks = blocks.reshape(n_z, n_y, n_x, per_owner // n_x, width)
+    blocks = halve_sum(blocks, "x", n_x, 2)
+    piece = lax.psum_scatter(blocks.reshape(n_z, -1, 128), "z", scatter_dimension=0, tiled=True)
+    piece = lax.psum_scatter(piece.reshape(n_y, -1, 128), "y", scatter_dimension=0, tiled=True)
+    piece = piece.reshape(per_owner // n_x, width)
+    mine = lax.axis_index("x") * (per_owner // n_x)
+    return lax.dynamic_update_slice_in_dim(jnp.zeros((per_owner, width), piece.dtype), piece, mine, 0)
 
 
 def local(sizes, tokens, out_grad, seq_lengths, owners, slots, w_in, w_out, emb_rows, emb_mom, emb_var):

time: 241 us -> 276 us (1.15)
  waiting for transfers between devices: 104 us -> 149 us
  starting transfers between devices: 61.6 us -> 34.6 us
  between operations: 1.22 us -> 14.5 us
  local copies, waits for them, and re-layouts: 26.9 us -> 31.2 us
    unnamed x0 -> x3, waiting for transfers between devices: none -> 78.5 us
    ppermute x7 -> x3, waiting for transfers between devices: 89.4 us -> 28.2 us  [halve_sum(): blocks = keep + lax.ppermute(send, axis, pairs)]
    reduce_scatter x0 -> x1, waiting for transfers between devices: none -> 27.9 us  [reduce_weights(): lax.psum_scatter(piece.reshape(n_y, -1, 128), 'y', scatter_dimension=0, t...]
    ppermute x7 -> x3, starting transfers between devices: 35.2 us -> 7.96 us  [halve_sum(): blocks = keep + lax.ppermute(send, axis, pairs)]
  transfers between devices with their start and end apart: 10 -> 8, of which waited for: 9 -> 7; matrix products, arithmetic and copies ran while one was open for 6% -> 7% of each run, Pallas kernels for 0% -> 0%
where the time goes in v8:
time: 276 us; the launch traced here: 274 us
  waiting for transfers between devices  149 us (54%)
  starting transfers between devices  34.6 us (13%)
  local copies, waits for them, and re-layouts  31.2 us (11%)
  matrix products  24.9 us (9%)
  other arithmetic  20.5 us (7%)
  between operations  14.5 us (5%)
    unnamed x3, waiting for transfers between devices  78.5 us
    ppermute x3, waiting for transfers between devices, halve_sum(): blocks = keep + lax.ppermute(send, axis, pairs)  28.2 us
    reduce_scatter x1, waiting for transfers between devices, reduce_weights(): lax.psum_scatter(piece.reshape(n_y, -1, 128), 'y', scatter_dimension=0, t...  27.9 us
    all_to_all x1, starting transfers between devices, local(): lax.all_to_all(jnp.concatenate([outgoing.reshape(owner_count, block_rows,...  20.4 us
    ppermute x2, waiting for transfers between devices, double_sum(): lax.ppermute(value, axis, [(i, i ^ 1 << bit) for i in range(size)])  14.2 us
    ppermute x3, starting transfers between devices, halve_sum(): blocks = keep + lax.ppermute(send, axis, pairs)  7.96 us
    dot_general x3, matrix products, core(): jnp.einsum('hts,shd->thd', weights, values_part, preferred_element_type=j...  7.51 us
    dot_general x3, matrix products, core(): jnp.einsum('thd,shd->hts', queries, keys_part, preferred_element_type=jnp...  6.15 us
  transfers between devices with their start and end apart: 8, of which 7 were waited for; matrix products, arithmetic and copies ran while one was open for 7% of the time, Pallas kernels for 0%

profile of v8, /device:TPU:6, one launch (start us, length us, event | category | flops | bytes accessed | tf_op | source)
XLA Modules:
  0.0 274.4 jit_solution(5257861984766775932)
XLA Ops:
  7.2 0.9 reduce-window.8
  8.4 1.3 fusion.22
  9.7 0.2 copy.75
  10.0 0.2 fusion.16
  10.2 2.3 multiply_convert_fusion.1
  12.5 1.0 copy-done.4
  13.5 0.8 fusion.45
  14.6 1.2 copy.76
  15.8 3.5 %multiply_convert_fusion = (bf16[4,512,512]{2,1,0:T(8,128)(2,1)S(1)}, f32[4,512,512]{2,1,0:T(8,128)}) fusion(f32[512,512]{1,0:T(8,128)S(1)} %fusion.23, bf16[512,4,64]{0,2,1:T(8,128)(2,1)S(1)} %bitcast.59, bf16[512,4,64]{0,2,1:T(8,128)(2,1)S(1)} %bitcast.61), kind=kOutput, calls=%fused_computation.7 | convolution fusion | flops 142606336 | bytes 7864320 | tf_op jit(solution)/shard_map/jvp(thd,shd->hts)/dot_general | solution.py:46
  19.3 1.3 copy-done.1
  20.6 0.8 fusion.46
  21.4 0.2 copy.79
  21.7 1.4 multiply_reduce_fusion
  23.1 1.9 fusion.44
  25.1 0.8 broadcast_add_fusion
  25.9 1.1 copy.81
  27.0 2.2 fusion.49
  29.2 4.6 %fusion.3 = bf16[4,512,512]{2,1,0:T(8,128)(2,1)S(1)} fusion(f32[4,512,512]{2,1,0:T(8,128)} %get-tuple-element.36, f32[512,512]{1,0:T(8,128)S(1)} %copy-done.10, bf16[4,64,512]{2,1,0:T(8,128)(2,1)} %bitcast.67, bf16[512,4,64]{0,2,1:T(8,128)(2,1)} %bitcast.64), kind=kOutput, calls=%fused_computation.5 | convolution fusion | flops 148897792 | bytes 7864320 | tf_op jit(solution)/shard_map/transpose(jvp(hts,shd->thd))/dot_general | solution.py:50
  33.8 1.5 fusion.48
  35.3 1.2 fusion.47
  36.5 1.0 copy.85
  37.6 1.1 copy.83
  38.7 0.8 copy.84
  39.6 2.5 fusion.8
  42.1 0.8 fusion.18
  43.1 0.3 fusion.29
  43.4 0.2 convert_reduce_fusion.2
  43.6 2.9 %fusion.5 = bf16[2048,512]{1,0:T(8,128)(2,1)} fusion(s32[512]{0:T(512)S(1)} %get-tuple-element.43, bf16[512,512]{0,1:T(8,128)(2,1)S(1)} %copy-done.12, f32[512]{0:T(512)S(1)} %negate_multiply_fusion, bf16[512,512]{0,1:T(8,128)(2,1)S(1)} %copy.75, f32[512,512]{0,1:T(8,128)S(1)} %get-tuple-element.42, f32[512]{0:T(512)S(1)} %multiply_multiply_fusion, ...), kind=kOutput, calls=%fused_computation.12 | convolution fusion | flops 1078460416 | bytes 4204544 | tf_op jit(solution)/shard_map/dot_general | solution.py:150
  46.6 4.3 %reshape_reshape.6 = bf16[128,64,128]{2,1,0:T(8,128)(2,1)} reshape(bf16[2048,512]{1,0:T(8,128)(2,1)} %fusion.5) | data formatting | bytes 4194304 | tf_op jit(solution)/shard_map/reshape;reshape | solution.py:161
  50.9 0.5 select_reduce_fusion
  51.6 3.4 %fusion.6 = bf16[128,65,128]{2,1,0:T(8,128)(2,1)} fusion(bf16[128,1,16]{2,1,0:T(2,128)(2,1)S(1)} %convert_element_type.136, bf16[128,64,128]{2,1,0:T(8,128)(2,1)} %reshape_reshape.6), kind=kLoop, calls=%fused_computation.16 | loop fusion | flops 6389760 | bytes 4231168 | tf_op jit(solution)/shard_map/concatenate | solution.py:161
  54.9 20.4 %all-to-all-start = ((bf16[128,65,128]{2,1,0:T(8,128)(2,1)}), bf16[128,65,128]{2,1,0:T(8,128)(2,1)}, u32[]{:S(2)}, u32[]{:S(2)}) async-start(bf16[128,65,128]{2,1,0:T(8,128)(2,1)} %fusion.6), calls=%async_computation | async-start | bytes 4718592 | tf_op jit(solution)/shard_map/all_to_all | solution.py:160
  75.4 1.5 convolution_bitcast_fusion
  76.9 1.9 fusion.30
  78.8 1.7 pad_maximum_fusion
  80.5 3.9 %reshape.253 = f32[16,4,2,4,1280]{4,3,2,1,0:T(4,128)} reshape(f32[512,1280]{1,0:T(8,128)} %pad_maximum_fusion) | data formatting | bytes 5242880 | tf_op jit(solution)/shard_map/reshape | solution.py:98
  84.5 2.5 constant_dynamic-slice_fusion.2
  86.9 1.9 collective-permute-start
  88.9 3.2 %collective-permute-done = f32[16,4,1,4,1280]{4,3,2,1,0:T(4,128)S(1)} collective-permute-done((f32[16,4,1,4,1280]{4,3,2,1,0:T(4,128)}, f32[16,4,1,4,1280]{4,3,2,1,0:T(4,128)S(1)}, u32[]{:S(2)}, u32[]{:S(2)}) %collective-permute-start) | collective-permute-done | bytes 1310752 | tf_op jit(solution)/shard_map/ppermute | solution.py:84
  92.1 1.7 dynamic-slice_add_fusion
  93.7 0.3 copy.92
  94.1 2.7 collective-permute-start.1
  96.9 16.0 %collective-permute-done.1 = f32[16,4,2,1,1,1280]{5,1,0,4,3,2:T(4,128)} collective-permute-done((f32[16,4,2,1,1,1280]{5,1,0,4,3,2:T(4,128)S(1)}, f32[16,4,2,1,1,1280]{5,1,0,4,3,2:T(4,128)}, u32[]{:S(2)}, u32[]{:S(2)}) %collective-permute-start.1) | collective-permute-done | bytes 655392 | tf_op jit(solution)/shard_map/ppermute | solution.py:84
  112.9 1.3 dynamic-slice_add_fusion.1
  114.2 3.3 %collective-permute-start.2 = (f32[16,4,1,1,1,1280]{5,1,0,4,3,2:T(4,128)S(1)}, f32[16,4,1,1,1,1280]{5,1,0,4,3,2:T(4,128)S(1)}, u32[]{:S(2)}, u32[]{:S(2)}) collective-permute-start(f32[16,4,1,1,1,1280]{5,1,0,4,3,2:T(4,128)S(1)} %constant_dynamic-slice_fusion), channel_id=1, source_target_pairs={{0,2},{1,3},{2,0},{3,1},{4,6},{5,7},{6,4},{7,5},{8,10},{9,11},{10,... | collective-permute-start | bytes 983048 | tf_op jit(solution)/shard_map/ppermute | solution.py:84
  117.5 9.0 %collective-permute-done.2 = f32[16,4,1,1,1,1280]{5,1,0,4,3,2:T(4,128)S(1)} collective-permute-done((f32[16,4,1,1,1,1280]{5,1,0,4,3,2:T(4,128)S(1)}, f32[16,4,1,1,1,1280]{5,1,0,4,3,2:T(4,128)S(1)}, u32[]{:S(2)}, u32[]{:S(2)}) %collective-permute-start.2) | collective-permute-done | bytes 327712 | tf_op jit(solution)/shard_map/ppermute | solution.py:84
  126.6 0.8 reshape_reshape.7
  127.5 78.4 %reduce-scatter.7.cloned.1.call-done = f32[1,40,128]{2,1,0:T(8,128)} async-done(((f32[16,40,128]{2,1,0:T(8,128)}), f32[1,40,128]{2,1,0:T(8,128)}) %reduce-scatter.7.cloned.1.call-update) | async-done | bytes 20496
  206.0 1.3 reshape.254
  207.3 27.9 %reduce-scatter.5.cloned.1.call-done = f32[1,10,128]{2,1,0:T(8,128)} async-done(((f32[4,10,128]{2,1,0:T(8,128)}), f32[1,10,128]{2,1,0:T(8,128)}) %reduce-scatter.5.cloned.1.call-update) | async-done | bytes 5136 | tf_op jit(solution)/shard_map/reduce_scatter | solution.py:103
  235.2 0.7 copy.96
  236.0 3.1 %slice.45 = bf16[128,64,128]{2,1,0:T(8,128)(2,1)} slice(bf16[128,65,128]{2,1,0:T(8,128)(2,1)} %all-to-all-done), slice={[0:128], [0:64], [0:128]} | slice | bytes 4194304 | tf_op jit(solution)/shard_map/slice | solution.py:168
  239.1 1.2 convert_reduce_fusion.3
  240.3 3.1 %reshape.256 = bf16[2048,512]{1,0:T(8,128)(2,1)S(1)} reshape(bf16[128,64,128]{2,1,0:T(8,128)(2,1)} %slice.45) | data formatting | bytes 4194304 | tf_op jit(solution)/shard_map/reshape | solution.py:168
  243.5 0.2 convert_reduce_fusion.1
  243.7 0.5 fusion.19
  244.3 2.8 %collective-permute-start.3 = (f32[136,640]{1,0:T(8,128)S(1)}, f32[136,640]{1,0:T(8,128)S(1)}, u32[]{:S(2)}, u32[]{:S(2)}) collective-permute-start(f32[136,640]{1,0:T(8,128)S(1)} %pad_maximum_fusion.1), channel_id=1, source_target_pairs={{0,1},{1,0},{2,3},{3,2},{4,5},{5,4},{6,7},{7,6},{8,9},{9,8},{10,11... | collective-permute-start | bytes 1044488 | tf_op jit(solution)/shard_map/ppermute | solution.py:90
  247.1 6.8 %collective-permute-done.3 = f32[136,640]{1,0:T(8,128)S(1)} collective-permute-done((f32[136,640]{1,0:T(8,128)S(1)}, f32[136,640]{1,0:T(8,128)S(1)}, u32[]{:S(2)}, u32[]{:S(2)}) %collective-permute-start.3) | collective-permute-done | bytes 348192 | tf_op jit(solution)/shard_map/ppermute | solution.py:90
  254.0 3.3 %collective-permute-start.4 = (f32[136,640]{1,0:T(8,128)S(1)}, f32[136,640]{1,0:T(8,128)S(1)}, u32[]{:S(2)}, u32[]{:S(2)}) collective-permute-start(f32[136,640]{1,0:T(8,128)S(1)} %fusion.43), channel_id=1, source_target_pairs={{0,2},{1,3},{2,0},{3,1},{4,6},{5,7},{6,4},{7,5},{8,10},{9,11},{10,... | collective-permute-start | bytes 1044488 | tf_op jit(solution)/shard_map/ppermute | solution.py:90
  257.3 7.3 %collective-permute-done.4 = f32[136,640]{1,0:T(8,128)S(1)} collective-permute-done((f32[136,640]{1,0:T(8,128)S(1)}, f32[136,640]{1,0:T(8,128)S(1)}, u32[]{:S(2)}, u32[]{:S(2)}) %collective-permute-start.4) | collective-permute-done | bytes 348192 | tf_op jit(solution)/shard_map/ppermute | solution.py:90
  264.9 0.6 slice.54
  265.6 0.6 slice.55
  266.2 0.5 fusion.42
  266.7 0.9 fusion.37
  (71 shorter events, 2.2 us)
Async XLA Ops:
  7.2 3.0 %copy-start = (bf16[512,1024]{1,0:T(8,128)(2,1)S(1)}, bf16[512,1024]{1,0:T(8,128)(2,1)}, u32[]{:S(2)}) copy-start(bf16[512,1024]{1,0:T(8,128)(2,1)} %param.17) | copy-start | bytes 3145732
  7.2 2.5 copy-start.11
  12.5 1.0 copy-start.4
  14.5 4.7 %copy-start.5 = (bf16[512,256]{0,1:T(8,128)(2,1)}, bf16[512,256]{0,1:T(8,128)(2,1)S(1)}, u32[]{:S(2)}) copy-start(bf16[512,256]{0,1:T(8,128)(2,1)S(1)} %copy.78) | copy-start | bytes 786436
  15.7 3.5 %copy-start.7 = (bf16[512,256]{0,1:T(8,128)(2,1)}, bf16[512,256]{0,1:T(8,128)(2,1)S(1)}, u32[]{:S(2)}) copy-start(bf16[512,256]{0,1:T(8,128)(2,1)S(1)} %copy.76) | copy-start | bytes 786436
  19.3 1.3 copy-start.1
  20.6 1.1 copy-start.2
  27.0 2.2 copy-start.8
  27.0 2.2 copy-start.10
  29.2 4.6 %copy-start.6 = (bf16[512,256]{0,1:T(8,128)(2,1)S(1)}, bf16[512,256]{0,1:T(8,128)(2,1)}, u32[]{:S(2)}) copy-start(bf16[512,256]{0,1:T(8,128)(2,1)} %copy-done.5) | copy-start | bytes 786436
  36.5 2.3 copy-start.9
  42.1 1.0 copy-start.3
  42.1 1.3 copy-start.15
  42.1 1.5 copy-start.16
  42.1 1.5 copy-start.12
  54.9 181.1 %all-to-all-start = ((bf16[128,65,128]{2,1,0:T(8,128)(2,1)}), bf16[128,65,128]{2,1,0:T(8,128)(2,1)}, u32[]{:S(2)}, u32[]{:S(2)}) async-start(bf16[128,65,128]{2,1,0:T(8,128)(2,1)} %fusion.6), calls=%async_computation | async-start | bytes 4718592 | tf_op jit(solution)/shard_map/all_to_all | solution.py:160
  75.3 130.6 %reduce-scatter.7.cloned.1.call-start = ((), (), s32[]{:S(2)}) async-start(), calls=%async_computation.4 | async-start | bytes 348160
  86.9 5.1 %collective-permute-start = (f32[16,4,1,4,1280]{4,3,2,1,0:T(4,128)}, f32[16,4,1,4,1280]{4,3,2,1,0:T(4,128)S(1)}, u32[]{:S(2)}, u32[]{:S(2)}) collective-permute-start(f32[16,4,1,4,1280]{4,3,2,1,0:T(4,128)} %constant_dynamic-slice_fusion.2), channel_id=1, source_target_pairs={{0,4},{4,0},{1,5},{5,1},{2,6},{6,2},{3,7},{7,3},{8,12},{12,8},{9,1... | collective-permute-start | bytes 3932168 | tf_op jit(solution)/shard_map/ppermute | solution.py:84
  94.1 18.8 %collective-permute-start.1 = (f32[16,4,2,1,1,1280]{5,1,0,4,3,2:T(4,128)S(1)}, f32[16,4,2,1,1,1280]{5,1,0,4,3,2:T(4,128)}, u32[]{:S(2)}, u32[]{:S(2)}) collective-permute-start(f32[16,4,2,1,1,1280]{5,1,0,4,3,2:T(4,128)S(1)} %constant_dynamic-slice_fusion.1), channel_id=1, source_target_pairs={{0,1},{1,0},{2,3},{3,2},{4,5},{5,4},{6,7},{7,6},{8,9},{9,8},{10,11... | collective-permute-start | bytes 1966088 | tf_op jit(solution)/shard_map/ppermute | solution.py:84
  114.2 12.3 %collective-permute-start.2 = (f32[16,4,1,1,1,1280]{5,1,0,4,3,2:T(4,128)S(1)}, f32[16,4,1,1,1,1280]{5,1,0,4,3,2:T(4,128)S(1)}, u32[]{:S(2)}, u32[]{:S(2)}) collective-permute-start(f32[16,4,1,1,1,1280]{5,1,0,4,3,2:T(4,128)S(1)} %constant_dynamic-slice_fusion), channel_id=1, source_target_pairs={{0,2},{1,3},{2,0},{3,1},{4,6},{5,7},{6,4},{7,5},{8,10},{9,11},{10,... | collective-permute-start | bytes 983048 | tf_op jit(solution)/shard_map/ppermute | solution.py:84
  127.5 107.7 %reduce-scatter.5.cloned.1.call-start = ((), (), s32[]{:S(2)}) async-start(), calls=%async_computation.3 | async-start | bytes 40960 | tf_op jit(solution)/shard_map/reduce_scatter | solution.py:103
  244.1 22.0 %copy-start.17 = (f32[128]{0:T(128)S(1)}, f32[128]{0:T(128)}, u32[]{:S(2)}) copy-start(f32[128]{0:T(128)} %param.21) | copy-start | bytes 1540
  244.2 22.5 %copy-start.13 = (f32[128,512]{1,0:T(8,128)S(1)}, f32[128,512]{1,0:T(8,128)}, u32[]{:S(2)}) copy-start(f32[128,512]{1,0:T(8,128)} %param.20) | copy-start | bytes 786436
  244.2 22.5 %copy-start.14 = (f32[128,512]{1,0:T(8,128)S(1)}, f32[128,512]{1,0:T(8,128)}, u32[]{:S(2)}) copy-start(f32[128,512]{1,0:T(8,128)} %param.19) | copy-start | bytes 786436
  244.3 9.6 %collective-permute-start.3 = (f32[136,640]{1,0:T(8,128)S(1)}, f32[136,640]{1,0:T(8,128)S(1)}, u32[]{:S(2)}, u32[]{:S(2)}) collective-permute-start(f32[136,640]{1,0:T(8,128)S(1)} %pad_maximum_fusion.1), channel_id=1, source_target_pairs={{0,1},{1,0},{2,3},{3,2},{4,5},{5,4},{6,7},{7,6},{8,9},{9,8},{10,11... | collective-permute-start | bytes 1044488 | tf_op jit(solution)/shard_map/ppermute | solution.py:90
  254.0 10.7 %collective-permute-start.4 = (f32[136,640]{1,0:T(8,128)S(1)}, f32[136,640]{1,0:T(8,128)S(1)}, u32[]{:S(2)}, u32[]{:S(2)}) collective-permute-start(f32[136,640]{1,0:T(8,128)S(1)} %fusion.43), channel_id=1, source_target_pairs={{0,2},{1,3},{2,0},{3,1},{4,6},{5,7},{6,4},{7,5},{8,10},{9,11},{10,... | collective-permute-start | bytes 1044488 | tf_op jit(solution)/shard_map/ppermute | solution.py:90
Sparse Core Ops, SparseCore 0:
  127.6 78.3 reduce-scatter.6
  209.5 25.5 reduce-scatter.4

commit v9 on v8

--- a/solution.py
+++ b/solution.py
@@ -99,9 +99,8 @@
     blocks = halve_sum(blocks, "core", n_c, 2)
     blocks = blocks.reshape(n_z, n_y, n_x, per_owner // n_x, width)
     blocks = halve_sum(blocks, "x", n_x, 2)
-    piece = lax.psum_scatter(blocks.reshape(n_z, -1, 128), "z", scatter_dimension=0, tiled=True)
-    piece = lax.psum_scatter(piece.reshape(n_y, -1, 128), "y", scatter_dimension=0, tiled=True)
-    piece = piece.reshape(per_owner // n_x, width)
+    blocks = halve_sum(blocks, "y", n_y, 1)
+    piece = halve_sum(blocks, "z", n_z, 0)
     mine = lax.axis_index("x") * (per_owner // n_x)
     return lax.dynamic_update_slice_in_dim(jnp.zeros((per_owner, width), piece.dtype), piece, mine, 0)
 

time: 276 us -> 241 us (0.87)
  waiting for transfers between devices: 149 us -> 86.1 us
  starting transfers between devices: 34.6 us -> 70.5 us
  between operations: 14.5 us -> 1.26 us
  other arithmetic: 20.5 us -> 24.5 us
    unnamed x3 -> x0, waiting for transfers between devices: 78.5 us -> none
    ppermute x3 -> x9, waiting for transfers between devices: 28.2 us -> 71 us  [halve_sum(): blocks = keep + lax.ppermute(send, axis, pairs)]
    ppermute x3 -> x9, starting transfers between devices: 7.96 us -> 45.1 us  [halve_sum(): blocks = keep + lax.ppermute(send, axis, pairs)]
    reduce_scatter x1 -> x0, waiting for transfers between devices: 27.9 us -> none  [reduce_weights(): lax.psum_scatter(piece.reshape(n_y, -1, 128), 'y', scatter_dimension=0, t...]
    add x3 -> x8, other arithmetic: 3 us -> 10 us  [halve_sum(): blocks = keep + lax.ppermute(send, axis, pairs)]
    dynamic_slice x3 -> x9, local copies, waits for them, and re-layouts: 2.58 us -> 6.86 us  [halve_sum(): send = lax.dynamic_index_in_dim(blocks, 1 - mine, at, keepdims=True)]
    another operation x1, local copies, waits for them, and re-layouts: 0.34 us -> 3.11 us  [halve_sum(): blocks = blocks.reshape(lead + (2,) * bits + blocks.shape[dim + 1:])]
    unnamed x39 -> x44, local copies, waits for them, and re-layouts: 4.54 us -> 6.12 us
  transfers between devices with their start and end apart: 8 -> 12, of which waited for: 7 -> 10; matrix products, arithmetic and copies ran while one was open for 7% -> 13% of each run, Pallas kernels for 0% -> 0%
where the time goes in v9:
time: 241 us; the launch traced here: 240 us
  waiting for transfers between devices  86.1 us (36%)
  starting transfers between devices  70.5 us (29%)
  local copies, waits for them, and re-layouts  33.8 us (14%)
  other arithmetic  24.5 us (10%)
  matrix products  23.4 us (10%)
    ppermute x9, waiting for transfers between devices, halve_sum(): blocks = keep + lax.ppermute(send, axis, pairs)  71 us
    ppermute x9, starting transfers between devices, halve_sum(): blocks = keep + lax.ppermute(send, axis, pairs)  45.1 us
    all_to_all x1, starting transfers between devices, local(): lax.all_to_all(jnp.concatenate([outgoing.reshape(owner_count, block_rows,...  20.1 us
    ppermute x2, waiting for transfers between devices, double_sum(): lax.ppermute(value, axis, [(i, i ^ 1 << bit) for i in range(size)])  15.1 us
    add x8, other arithmetic, halve_sum(): blocks = keep + lax.ppermute(send, axis, pairs)  10 us
    dot_general x3, matrix products, core(): jnp.einsum('hts,shd->thd', weights, values_part, preferred_element_type=j...  6.92 us
    dynamic_slice x9, local copies, waits for them, and re-layouts, halve_sum(): send = lax.dynamic_index_in_dim(blocks, 1 - mine, at, keepdims=True)  6.86 us
    unnamed x44, local copies, waits for them, and re-layouts  6.12 us
  transfers between devices with their start and end apart: 12, of which 10 were waited for; matrix products, arithmetic and copies ran while one was open for 13% of the time, Pallas kernels for 0%

profile of v9, /device:TPU:6, one launch (start us, length us, event | category | flops | bytes accessed | tf_op | source)
XLA Modules:
  0.0 239.6 jit_solution(14060374945632238886)
XLA Ops:
  0.7 0.9 reduce-window.8
  1.9 1.3 fusion.22
  3.7 2.3 multiply_convert_fusion.1
  6.0 1.0 copy-done.4
  6.9 0.8 fusion.45
  8.0 1.2 copy.57
  9.2 3.5 %multiply_convert_fusion = (bf16[4,512,512]{2,1,0:T(8,128)(2,1)S(1)}, f32[4,512,512]{2,1,0:T(8,128)}) fusion(f32[512,512]{1,0:T(8,128)S(1)} %fusion.23, bf16[512,4,64]{0,2,1:T(8,128)(2,1)S(1)} %bitcast.55, bf16[512,4,64]{0,2,1:T(8,128)(2,1)S(1)} %bitcast.57), kind=kOutput, calls=%fused_computation.7 | convolution fusion | flops 142606336 | bytes 7864320 | tf_op jit(solution)/shard_map/jvp(thd,shd->hts)/dot_general | solution.py:46
  12.7 1.3 copy-done.1
  14.0 0.8 fusion.46
  15.1 1.5 multiply_reduce_fusion
  16.6 1.3 convolution_bitcast_fusion
  18.0 1.0 fusion.44
  19.2 2.1 fusion.49
  21.4 4.0 %fusion.3 = bf16[4,512,512]{2,1,0:T(8,128)(2,1)S(1)} fusion(f32[4,512,512]{2,1,0:T(8,128)} %get-tuple-element.36, f32[512,512]{1,0:T(8,128)S(1)} %copy-done.13, bf16[4,64,512]{2,1,0:T(8,128)(2,1)S(1)} %bitcast.63, bf16[512,4,64]{0,2,1:T(8,128)(2,1)S(1)} %bitcast.60), kind=kOutput, calls=%fused_computation.5 | convolution fusion | flops 148897792 | bytes 7864320 | tf_op jit(solution)/shard_map/transpose(jvp(hts,shd->thd))/dot_general | solution.py:50
  25.5 0.8 fusion.48
  26.8 0.8 copy.64
  27.7 0.8 copy.65
  28.5 2.6 %fusion.8 = bf16[512,1024]{1,0:T(8,128)(2,1)S(1)} fusion(f32[512,1024]{1,0:T(8,128)} %get-tuple-element.34, bf16[512,256]{1,0:T(8,128)(2,1)} %copy.65, bf16[512,256]{1,0:T(8,128)(2,1)} %copy.64, bf16[512,256]{1,0:T(8,128)(2,1)S(1)} %copy.63, bf16[512,256]{1,0:T(8,128)(2,1)} %get-tuple-element.23), kind=kLoop, calls=%fused_computation.18 | loop fusion | flops 9437184 | bytes 4194304 | tf_op jit(solution)/shard_map/convert_element_type | solution.py:117
  31.1 0.7 fusion.30
  32.1 1.7 pad_maximum_fusion
  33.9 3.9 %reshape.250 = f32[16,4,2,4,1280]{4,3,2,1,0:T(4,128)} reshape(f32[512,1280]{1,0:T(8,128)} %pad_maximum_fusion) | data formatting | bytes 5242880 | tf_op jit(solution)/shard_map/reshape | solution.py:98
  37.8 2.5 %constant_dynamic-slice_fusion.8 = f32[16,4,1,4,1280]{4,3,2,1,0:T(4,128)} fusion(f32[16,4,2,4,1280]{4,3,2,1,0:T(4,128)} %reshape.250, s32[]{:T(128)S(6)} %select_n.83), kind=kLoop, calls=%fused_computation.96 | loop fusion | bytes 2621444 | tf_op jit(solution)/shard_map/jit(dynamic_index_in_dim)/dynamic_slice | solution.py:82
  40.3 2.1 collective-permute-start
  42.4 1.7 fusion.18
  44.1 1.0 copy.66
  45.1 1.5 fusion.29
  47.4 3.8 %fusion.5 = bf16[2048,512]{1,0:T(8,128)(2,1)} fusion(s32[512]{0:T(512)S(1)} %get-tuple-element.43, bf16[512,512]{0,1:T(8,128)(2,1)} %copy.66, f32[512]{0:T(512)S(1)} %negate_multiply_fusion, bf16[512,512]{0,1:T(8,128)(2,1)S(1)} %copy.56, f32[512,512]{0,1:T(8,128)S(1)} %copy-done.12, f32[512]{0:T(512)S(1)} %multiply_multiply_fusion, f32[512]{0:T(512)S(1)} %fusion.40, ...), kind=kOutput, calls=%fused_computation.12 | convolution fusion | flops 1078460416 | bytes 4204544 | tf_op jit(solution)/shard_map/dot_general | solution.py:149
  51.2 3.1 %reshape_reshape.9 = bf16[128,64,128]{2,1,0:T(8,128)(2,1)S(1)} reshape(bf16[2048,512]{1,0:T(8,128)(2,1)} %fusion.5) | data formatting | bytes 4194304 | tf_op jit(solution)/shard_map/reshape;reshape | solution.py:160
  54.4 1.7 fusion.6
  56.1 20.1 %all-to-all-start = ((bf16[128,65,128]{2,1,0:T(8,128)(2,1)}), bf16[128,65,128]{2,1,0:T(8,128)(2,1)S(1)}, u32[]{:S(2)}, u32[]{:S(2)}) async-start(bf16[128,65,128]{2,1,0:T(8,128)(2,1)} %fusion.6), calls=%async_computation | async-start | bytes 4718592 | tf_op jit(solution)/shard_map/all_to_all | solution.py:159
  76.2 3.1 %dynamic-slice_add_fusion = f32[16,4,1,4,1280]{4,3,2,1,0:T(4,128)} fusion(f32[16,4,1,4,1280]{4,3,2,1,0:T(4,128)} %collective-permute-done, f32[16,4,2,4,1280]{4,3,2,1,0:T(4,128)} %reshape.250, s32[]{:T(128)S(6)} %select_n.82), kind=kLoop, calls=%fused_computation.30 | loop fusion | flops 327680 | bytes 3932164 | tf_op jit(solution)/shard_map/add | solution.py:84
  79.4 3.1 %reshape_reshape_reshape.3 = f32[16,4,2,2,1,1280]{5,3,2,1,0,4:T(2,128)} reshape(f32[16,4,1,4,1280]{4,3,2,1,0:T(4,128)} %dynamic-slice_add_fusion) | data formatting | bytes 2621440 | tf_op jit(solution)/shard_map/reshape;reshape;reshape | solution.py:77
  82.5 2.8 %constant_dynamic-slice_fusion.7 = f32[16,4,2,1,1,1280]{5,3,2,1,0,4:T(1,128)} fusion(f32[16,4,2,2,1,1280]{5,3,2,1,0,4:T(2,128)} %reshape_reshape_reshape.3, s32[]{:T(128)S(6)} %select_n.85), kind=kLoop, calls=%fused_computation.95 | loop fusion | bytes 1310724 | tf_op jit(solution)/shard_map/jit(dynamic_index_in_dim)/dynamic_slice | solution.py:82
  85.3 2.7 %collective-permute-start.1 = (f32[16,4,2,1,1,1280]{5,3,2,1,0,4:T(1,128)}, f32[16,4,2,1,1,1280]{5,3,2,1,0,4:T(1,128)}, u32[]{:S(2)}, u32[]{:S(2)}) collective-permute-start(f32[16,4,2,1,1,1280]{5,3,2,1,0,4:T(1,128)} %constant_dynamic-slice_fusion.7), channel_id=1, source_target_pairs={{0,1},{1,0},{2,3},{3,2},{4,5},{5,4},{6,7},{7,6},{8,9},{9,8},{10,11... | collective-permute-start | bytes 1966088 | tf_op jit(solution)/shard_map/ppermute | solution.py:84
  88.0 15.7 %collective-permute-done.1 = f32[16,4,2,1,1,1280]{5,3,2,1,0,4:T(1,128)} collective-permute-done((f32[16,4,2,1,1,1280]{5,3,2,1,0,4:T(1,128)}, f32[16,4,2,1,1,1280]{5,3,2,1,0,4:T(1,128)}, u32[]{:S(2)}, u32[]{:S(2)}) %collective-permute-start.1) | collective-permute-done | bytes 655392 | tf_op jit(solution)/shard_map/ppermute | solution.py:84
  103.8 2.4 %dynamic-slice_add_fusion.1 = f32[16,4,2,1,1,1280]{5,3,2,1,0,4:T(1,128)S(1)} fusion(f32[16,4,2,1,1,1280]{5,3,2,1,0,4:T(1,128)} %collective-permute-done.1, f32[16,4,2,2,1,1280]{5,3,2,1,0,4:T(2,128)} %reshape_reshape_reshape.3, s32[]{:T(128)S(6)} %select_n.84), kind=kLoop, calls=%fused_computation.54 | loop fusion | flops 163840 | bytes 1966084 | tf_op jit(solution)/shard_map/add | solution.py:84
  106.2 0.8 copy-done.3
  107.0 0.8 constant_dynamic-slice_fusion.6
  107.8 3.3 %collective-permute-start.2 = (f32[16,4,1,1,1,1280]{5,3,2,1,0,4:T(1,128)}, f32[16,4,1,1,1,1280]{5,3,2,1,0,4:T(1,128)}, u32[]{:S(2)}, u32[]{:S(2)}) collective-permute-start(f32[16,4,1,1,1,1280]{5,3,2,1,0,4:T(1,128)} %constant_dynamic-slice_fusion.6), channel_id=1, source_target_pairs={{0,2},{1,3},{2,0},{3,1},{4,6},{5,7},{6,4},{7,5},{8,10},{9,11},{10,... | collective-permute-start | bytes 983048 | tf_op jit(solution)/shard_map/ppermute | solution.py:84
  111.1 8.7 %collective-permute-done.2 = f32[16,4,1,1,1,1280]{5,3,2,1,0,4:T(1,128)} collective-permute-done((f32[16,4,1,1,1,1280]{5,3,2,1,0,4:T(1,128)}, f32[16,4,1,1,1,1280]{5,3,2,1,0,4:T(1,128)}, u32[]{:S(2)}, u32[]{:S(2)}) %collective-permute-start.2) | collective-permute-done | bytes 327712 | tf_op jit(solution)/shard_map/ppermute | solution.py:84
  119.8 1.4 dynamic-slice_add_fusion.2
  121.3 0.7 copy-done.7
  122.6 4.2 %collective-permute-start.3 = (f32[16,2,1,1,1280]{4,3,2,1,0:T(1,128)}, f32[16,2,1,1,1280]{4,3,2,1,0:T(1,128)}, u32[]{:S(2)}, u32[]{:S(2)}) collective-permute-start(f32[16,2,1,1,1280]{4,3,2,1,0:T(1,128)} %constant_dynamic-slice_fusion.5), channel_id=1, source_target_pairs={{0,8},{8,0},{16,24},{24,16},{1,9},{9,1},{17,25},{25,17},{2,10},{10... | collective-permute-start | bytes 491528 | tf_op jit(solution)/shard_map/ppermute | solution.py:84
  126.8 4.0 %collective-permute-done.3 = f32[16,2,1,1,1280]{4,3,2,1,0:T(1,128)} collective-permute-done((f32[16,2,1,1,1280]{4,3,2,1,0:T(1,128)}, f32[16,2,1,1,1280]{4,3,2,1,0:T(1,128)}, u32[]{:S(2)}, u32[]{:S(2)}) %collective-permute-start.3) | collective-permute-done | bytes 163872 | tf_op jit(solution)/shard_map/ppermute | solution.py:84
  130.8 1.2 dynamic-slice_add_fusion.3
  132.6 5.4 %collective-permute-start.4 = (f32[16,1,1,1,1280]{4,3,2,1,0:T(1,128)S(1)}, f32[16,1,1,1,1280]{4,3,2,1,0:T(1,128)}, u32[]{:S(2)}, u32[]{:S(2)}) collective-permute-start(f32[16,1,1,1,1280]{4,3,2,1,0:T(1,128)S(1)} %constant_dynamic-slice_fusion.4), channel_id=1, source_target_pairs={{0,16},{8,24},{16,0},{24,8},{1,17},{9,25},{17,1},{25,9},{2,18},{10... | collective-permute-start | bytes 245768 | tf_op jit(solution)/shard_map/ppermute | solution.py:84
  138.1 2.6 %collective-permute-done.4 = f32[16,1,1,1,1280]{4,3,2,1,0:T(1,128)} collective-permute-done((f32[16,1,1,1,1280]{4,3,2,1,0:T(1,128)S(1)}, f32[16,1,1,1,1280]{4,3,2,1,0:T(1,128)}, u32[]{:S(2)}, u32[]{:S(2)}) %collective-permute-start.4) | collective-permute-done | bytes 81952 | tf_op jit(solution)/shard_map/ppermute | solution.py:84
  140.7 1.0 dynamic-slice_add_fusion.4
  141.7 4.4 %collective-permute-start.5 = (f32[2,2,2,1,1,1280]{5,4,3,2,1,0:T(1,128)S(1)}, f32[2,2,2,1,1,1280]{5,4,3,2,1,0:T(1,128)}, u32[]{:S(2)}, u32[]{:S(2)}) collective-permute-start(f32[2,2,2,1,1,1280]{5,4,3,2,1,0:T(1,128)S(1)} %constant_dynamic-slice_fusion.3), channel_id=1, source_target_pairs={{0,32},{32,0},{64,96},{96,64},{128,160},{160,128},{192,224},{224,1... | collective-permute-start | bytes 122888 | tf_op jit(solution)/shard_map/ppermute | solution.py:84
  146.2 32.5 %collective-permute-done.5 = f32[2,2,2,1,1,1280]{5,4,3,2,1,0:T(1,128)} collective-permute-done((f32[2,2,2,1,1,1280]{5,4,3,2,1,0:T(1,128)S(1)}, f32[2,2,2,1,1,1280]{5,4,3,2,1,0:T(1,128)}, u32[]{:S(2)}, u32[]{:S(2)}) %collective-permute-start.5) | collective-permute-done | bytes 40992 | tf_op jit(solution)/shard_map/ppermute | solution.py:84
  178.7 0.8 dynamic-slice_add_fusion.5
  179.5 3.9 %collective-permute-start.6 = (f32[2,2,1,1,1,1280]{5,4,3,2,1,0:T(1,128)S(1)}, f32[2,2,1,1,1,1280]{5,4,3,2,1,0:T(1,128)S(1)}, u32[]{:S(2)}, u32[]{:S(2)}) collective-permute-start(f32[2,2,1,1,1,1280]{5,4,3,2,1,0:T(1,128)S(1)} %constant_dynamic-slice_fusion.2), channel_id=1, source_target_pairs={{0,64},{32,96},{64,0},{96,32},{128,192},{160,224},{192,128},{224,1... | collective-permute-start | bytes 61448 | tf_op jit(solution)/shard_map/ppermute | solution.py:84
  183.5 2.8 %collective-permute-done.6 = f32[2,2,1,1,1,1280]{5,4,3,2,1,0:T(1,128)S(1)} collective-permute-done((f32[2,2,1,1,1,1280]{5,4,3,2,1,0:T(1,128)S(1)}, f32[2,2,1,1,1,1280]{5,4,3,2,1,0:T(1,128)S(1)}, u32[]{:S(2)}, u32[]{:S(2)}) %collective-permute-start.6) | collective-permute-done | bytes 20512 | tf_op jit(solution)/shard_map/ppermute | solution.py:84
  186.3 6.5 %collective-permute-start.7 = (f32[2,1,1,1,1,1280]{5,4,3,2,1,0:T(1,128)S(1)}, f32[2,1,1,1,1,1280]{5,4,3,2,1,0:T(1,128)S(1)}, u32[]{:S(2)}, u32[]{:S(2)}) collective-permute-start(f32[2,1,1,1,1,1280]{5,4,3,2,1,0:T(1,128)S(1)} %constant_dynamic-slice_fusion.1), channel_id=1, source_target_pairs={{0,128},{32,160},{64,192},{96,224},{128,0},{160,32},{192,64},{224,... | collective-permute-start | bytes 30728 | tf_op jit(solution)/shard_map/ppermute | solution.py:84
  192.9 2.9 %collective-permute-done.7 = f32[2,1,1,1,1,1280]{5,4,3,2,1,0:T(1,128)S(1)} collective-permute-done((f32[2,1,1,1,1,1280]{5,4,3,2,1,0:T(1,128)S(1)}, f32[2,1,1,1,1,1280]{5,4,3,2,1,0:T(1,128)S(1)}, u32[]{:S(2)}, u32[]{:S(2)}) %collective-permute-start.7) | collective-permute-done | bytes 10272 | tf_op jit(solution)/shard_map/ppermute | solution.py:84
  195.8 12.5 %collective-permute-start.8 = (f32[1,1,1,1,1,1280]{5,4,3,2,1,0:T(1,128)S(1)}, f32[1,1,1,1,1,1280]{5,4,3,2,1,0:T(1,128)S(1)}, u32[]{:S(2)}, u32[]{:S(2)}) collective-permute-start(f32[1,1,1,1,1,1280]{5,4,3,2,1,0:T(1,128)S(1)} %constant_dynamic-slice_fusion), channel_id=1, source_target_pairs={{0,256},{32,288},{64,320},{96,352},{128,384},{160,416},{192,448},{... | collective-permute-start | bytes 15368 | tf_op jit(solution)/shard_map/ppermute | solution.py:84
  208.3 1.7 collective-permute-done.8
  210.2 1.7 slice.45
  212.1 3.1 %reshape.252 = bf16[2048,512]{1,0:T(8,128)(2,1)S(1)} reshape(bf16[128,64,128]{2,1,0:T(8,128)(2,1)} %slice.45) | data formatting | bytes 4194304 | tf_op jit(solution)/shard_map/reshape | solution.py:167
  216.1 2.7 %collective-permute-start.9 = (f32[136,640]{1,0:T(8,128)S(1)}, f32[136,640]{1,0:T(8,128)S(1)}, u32[]{:S(2)}, u32[]{:S(2)}) collective-permute-start(f32[136,640]{1,0:T(8,128)S(1)} %pad_maximum_fusion.1), channel_id=1, source_target_pairs={{0,1},{1,0},{2,3},{3,2},{4,5},{5,4},{6,7},{7,6},{8,9},{9,8},{10,11... | collective-permute-start | bytes 1044488 | tf_op jit(solution)/shard_map/ppermute | solution.py:90
  218.8 7.1 %collective-permute-done.9 = f32[136,640]{1,0:T(8,128)S(1)} collective-permute-done((f32[136,640]{1,0:T(8,128)S(1)}, f32[136,640]{1,0:T(8,128)S(1)}, u32[]{:S(2)}, u32[]{:S(2)}) %collective-permute-start.9) | collective-permute-done | bytes 348192 | tf_op jit(solution)/shard_map/ppermute | solution.py:90
  225.9 2.7 %collective-permute-start.10 = (f32[136,640]{1,0:T(8,128)S(1)}, f32[136,640]{1,0:T(8,128)S(1)}, u32[]{:S(2)}, u32[]{:S(2)}) collective-permute-start(f32[136,640]{1,0:T(8,128)S(1)} %fusion.43), channel_id=1, source_target_pairs={{0,2},{1,3},{2,0},{3,1},{4,6},{5,7},{6,4},{7,5},{8,10},{9,11},{10,... | collective-permute-start | bytes 1044488 | tf_op jit(solution)/shard_map/ppermute | solution.py:90
  228.6 8.0 %collective-permute-done.10 = f32[136,640]{1,0:T(8,128)S(1)} collective-permute-done((f32[136,640]{1,0:T(8,128)S(1)}, f32[136,640]{1,0:T(8,128)S(1)}, u32[]{:S(2)}, u32[]{:S(2)}) %collective-permute-start.10) | collective-permute-done | bytes 348192 | tf_op jit(solution)/shard_map/ppermute | solution.py:90
  238.7 0.9 fusion.37
  (92 shorter events, 8.2 us)
Async XLA Ops:
  0.6 3.0 %copy-start = (bf16[512,1024]{1,0:T(8,128)(2,1)S(1)}, bf16[512,1024]{1,0:T(8,128)(2,1)}, u32[]{:S(2)}) copy-start(bf16[512,1024]{1,0:T(8,128)(2,1)} %param.17) | copy-start | bytes 3145732
  0.6 2.5 %copy-start.15 = (bf16[512,512]{1,0:T(8,128)(2,1)S(1)}, bf16[512,512]{1,0:T(8,128)(2,1)}, u32[]{:S(2)}) copy-start(bf16[512,512]{1,0:T(8,128)(2,1)} %param.12) | copy-start | bytes 1572868
  6.0 1.0 copy-start.4
  8.0 4.7 %copy-start.8 = (bf16[512,256]{0,1:T(8,128)(2,1)}, bf16[512,256]{0,1:T(8,128)(2,1)S(1)}, u32[]{:S(2)}) copy-start(bf16[512,256]{0,1:T(8,128)(2,1)S(1)} %copy.59) | copy-start | bytes 786436
  9.2 3.5 %copy-start.10 = (bf16[512,256]{0,1:T(8,128)(2,1)}, bf16[512,256]{0,1:T(8,128)(2,1)S(1)}, u32[]{:S(2)}) copy-start(bf16[512,256]{0,1:T(8,128)(2,1)S(1)} %copy.57) | copy-start | bytes 786436
  12.7 1.3 copy-start.1
  14.0 1.1 copy-start.2
  15.0 1.6 copy-start.5
  18.9 2.5 %copy-start.11 = (bf16[512,256]{0,1:T(8,128)(2,1)S(1)}, bf16[512,256]{0,1:T(8,128)(2,1)}, u32[]{:S(2)}) copy-start(bf16[512,256]{0,1:T(8,128)(2,1)} %copy-done.10) | copy-start | bytes 786436
  19.2 2.2 copy-start.13
  21.4 4.0 %copy-start.9 = (bf16[512,256]{0,1:T(8,128)(2,1)S(1)}, bf16[512,256]{0,1:T(8,128)(2,1)}, u32[]{:S(2)}) copy-start(bf16[512,256]{0,1:T(8,128)(2,1)} %copy-done.8) | copy-start | bytes 786436
  31.1 1.0 copy-start.6
  40.3 35.9 %collective-permute-start = (f32[16,4,1,4,1280]{4,3,2,1,0:T(4,128)}, f32[16,4,1,4,1280]{4,3,2,1,0:T(4,128)}, u32[]{:S(2)}, u32[]{:S(2)}) collective-permute-start(f32[16,4,1,4,1280]{4,3,2,1,0:T(4,128)} %constant_dynamic-slice_fusion.8), channel_id=1, source_target_pairs={{0,4},{4,0},{1,5},{5,1},{2,6},{6,2},{3,7},{7,3},{8,12},{12,8},{9,1... | collective-permute-start | bytes 3932168 | tf_op jit(solution)/shard_map/ppermute | solution.py:84
  44.1 2.5 %copy-start.18 = (s32[512,1]{0,1:T(1,128)S(1)}, s32[512,1]{0,1:T(1,128)}, u32[]{:S(2)}) copy-start(s32[512,1]{0,1:T(1,128)} %param.15) | copy-start | bytes 6148
  44.1 2.8 %copy-start.19 = (s32[512]{0:T(512)S(1)}, s32[512]{0:T(512)}, u32[]{:S(2)}) copy-start(s32[512]{0:T(512)} %param.16) | copy-start | bytes 6148
  44.1 3.3 %copy-start.12 = (f32[512,512]{0,1:T(8,128)S(1)}, f32[512,512]{0,1:T(8,128)}, u32[]{:S(2)}) copy-start(f32[512,512]{0,1:T(8,128)} %get-tuple-element.42) | copy-start | bytes 3145732
  56.1 154.1 %all-to-all-start = ((bf16[128,65,128]{2,1,0:T(8,128)(2,1)}), bf16[128,65,128]{2,1,0:T(8,128)(2,1)S(1)}, u32[]{:S(2)}, u32[]{:S(2)}) async-start(bf16[128,65,128]{2,1,0:T(8,128)(2,1)} %fusion.6), calls=%async_computation | async-start | bytes 4718592 | tf_op jit(solution)/shard_map/all_to_all | solution.py:159
  85.3 18.5 %collective-permute-start.1 = (f32[16,4,2,1,1,1280]{5,3,2,1,0,4:T(1,128)}, f32[16,4,2,1,1,1280]{5,3,2,1,0,4:T(1,128)}, u32[]{:S(2)}, u32[]{:S(2)}) collective-permute-start(f32[16,4,2,1,1,1280]{5,3,2,1,0,4:T(1,128)} %constant_dynamic-slice_fusion.7), channel_id=1, source_target_pairs={{0,1},{1,0},{2,3},{3,2},{4,5},{5,4},{6,7},{7,6},{8,9},{9,8},{10,11... | collective-permute-start | bytes 1966088 | tf_op jit(solution)/shard_map/ppermute | solution.py:84
  106.2 0.8 copy-start.3
  107.8 12.0 %collective-permute-start.2 = (f32[16,4,1,1,1,1280]{5,3,2,1,0,4:T(1,128)}, f32[16,4,1,1,1,1280]{5,3,2,1,0,4:T(1,128)}, u32[]{:S(2)}, u32[]{:S(2)}) collective-permute-start(f32[16,4,1,1,1,1280]{5,3,2,1,0,4:T(1,128)} %constant_dynamic-slice_fusion.6), channel_id=1, source_target_pairs={{0,2},{1,3},{2,0},{3,1},{4,6},{5,7},{6,4},{7,5},{8,10},{9,11},{10,... | collective-permute-start | bytes 983048 | tf_op jit(solution)/shard_map/ppermute | solution.py:84
  121.2 0.7 copy-start.7
  122.6 8.1 %collective-permute-start.3 = (f32[16,2,1,1,1280]{4,3,2,1,0:T(1,128)}, f32[16,2,1,1,1280]{4,3,2,1,0:T(1,128)}, u32[]{:S(2)}, u32[]{:S(2)}) collective-permute-start(f32[16,2,1,1,1280]{4,3,2,1,0:T(1,128)} %constant_dynamic-slice_fusion.5), channel_id=1, source_target_pairs={{0,8},{8,0},{16,24},{24,16},{1,9},{9,1},{17,25},{25,17},{2,10},{10... | collective-permute-start | bytes 491528 | tf_op jit(solution)/shard_map/ppermute | solution.py:84
  132.0 0.7 copy-start.14
  132.6 8.1 %collective-permute-start.4 = (f32[16,1,1,1,1280]{4,3,2,1,0:T(1,128)S(1)}, f32[16,1,1,1,1280]{4,3,2,1,0:T(1,128)}, u32[]{:S(2)}, u32[]{:S(2)}) collective-permute-start(f32[16,1,1,1,1280]{4,3,2,1,0:T(1,128)S(1)} %constant_dynamic-slice_fusion.4), channel_id=1, source_target_pairs={{0,16},{8,24},{16,0},{24,8},{1,17},{9,25},{17,1},{25,9},{2,18},{10... | collective-permute-start | bytes 245768 | tf_op jit(solution)/shard_map/ppermute | solution.py:84
  141.7 37.0 %collective-permute-start.5 = (f32[2,2,2,1,1,1280]{5,4,3,2,1,0:T(1,128)S(1)}, f32[2,2,2,1,1,1280]{5,4,3,2,1,0:T(1,128)}, u32[]{:S(2)}, u32[]{:S(2)}) collective-permute-start(f32[2,2,2,1,1,1280]{5,4,3,2,1,0:T(1,128)S(1)} %constant_dynamic-slice_fusion.3), channel_id=1, source_target_pairs={{0,32},{32,0},{64,96},{96,64},{128,160},{160,128},{192,224},{224,1... | collective-permute-start | bytes 122888 | tf_op jit(solution)/shard_map/ppermute | solution.py:84
  179.5 6.7 %collective-permute-start.6 = (f32[2,2,1,1,1,1280]{5,4,3,2,1,0:T(1,128)S(1)}, f32[2,2,1,1,1,1280]{5,4,3,2,1,0:T(1,128)S(1)}, u32[]{:S(2)}, u32[]{:S(2)}) collective-permute-start(f32[2,2,1,1,1,1280]{5,4,3,2,1,0:T(1,128)S(1)} %constant_dynamic-slice_fusion.2), channel_id=1, source_target_pairs={{0,64},{32,96},{64,0},{96,32},{128,192},{160,224},{192,128},{224,1... | collective-permute-start | bytes 61448 | tf_op jit(solution)/shard_map/ppermute | solution.py:84
  186.3 9.5 %collective-permute-start.7 = (f32[2,1,1,1,1,1280]{5,4,3,2,1,0:T(1,128)S(1)}, f32[2,1,1,1,1,1280]{5,4,3,2,1,0:T(1,128)S(1)}, u32[]{:S(2)}, u32[]{:S(2)}) collective-permute-start(f32[2,1,1,1,1,1280]{5,4,3,2,1,0:T(1,128)S(1)} %constant_dynamic-slice_fusion.1), channel_id=1, source_target_pairs={{0,128},{32,160},{64,192},{96,224},{128,0},{160,32},{192,64},{224,... | collective-permute-start | bytes 30728 | tf_op jit(solution)/shard_map/ppermute | solution.py:84
  195.8 14.2 %collective-permute-start.8 = (f32[1,1,1,1,1,1280]{5,4,3,2,1,0:T(1,128)S(1)}, f32[1,1,1,1,1,1280]{5,4,3,2,1,0:T(1,128)S(1)}, u32[]{:S(2)}, u32[]{:S(2)}) collective-permute-start(f32[1,1,1,1,1,1280]{5,4,3,2,1,0:T(1,128)S(1)} %constant_dynamic-slice_fusion), channel_id=1, source_target_pairs={{0,256},{32,288},{64,320},{96,352},{128,384},{160,416},{192,448},{... | collective-permute-start | bytes 15368 | tf_op jit(solution)/shard_map/ppermute | solution.py:84
  215.9 22.2 %copy-start.20 = (f32[128]{0:T(128)S(1)}, f32[128]{0:T(128)}, u32[]{:S(2)}) copy-start(f32[128]{0:T(128)} %param.21) | copy-start | bytes 1540
  215.9 22.7 %copy-start.16 = (f32[128,512]{1,0:T(8,128)S(1)}, f32[128,512]{1,0:T(8,128)}, u32[]{:S(2)}) copy-start(f32[128,512]{1,0:T(8,128)} %param.20) | copy-start | bytes 786436
  215.9 22.7 %copy-start.17 = (f32[128,512]{1,0:T(8,128)S(1)}, f32[128,512]{1,0:T(8,128)}, u32[]{:S(2)}) copy-start(f32[128,512]{1,0:T(8,128)} %param.19) | copy-start | bytes 786436
  216.1 9.8 %collective-permute-start.9 = (f32[136,640]{1,0:T(8,128)S(1)}, f32[136,640]{1,0:T(8,128)S(1)}, u32[]{:S(2)}, u32[]{:S(2)}) collective-permute-start(f32[136,640]{1,0:T(8,128)S(1)} %pad_maximum_fusion.1), channel_id=1, source_target_pairs={{0,1},{1,0},{2,3},{3,2},{4,5},{5,4},{6,7},{7,6},{8,9},{9,8},{10,11... | collective-permute-start | bytes 1044488 | tf_op jit(solution)/shard_map/ppermute | solution.py:90
  225.9 10.7 %collective-permute-start.10 = (f32[136,640]{1,0:T(8,128)S(1)}, f32[136,640]{1,0:T(8,128)S(1)}, u32[]{:S(2)}, u32[]{:S(2)}) collective-permute-start(f32[136,640]{1,0:T(8,128)S(1)} %fusion.43), channel_id=1, source_target_pairs={{0,2},{1,3},{2,0},{3,1},{4,6},{5,7},{6,4},{7,5},{8,10},{9,11},{10,... | collective-permute-start | bytes 1044488 | tf_op jit(solution)/shard_map/ppermute | solution.py:90

commit v10 on v9

--- a/solution.py
+++ b/solution.py
@@ -109,6 +109,26 @@
     tok_count = tokens.shape[0]
     width = tokens.shape[1]
     allowed = allowed_mask(seq_lengths[0], tok_count)
+    owner_count = 1
+    for a in ROW_AXES:
+        owner_count *= sizes[a]
+    capacity = max(2, 4 * tok_count // owner_count)
+    buffer_rows = owner_count * capacity
+    owner_of = owners[:, 0]
+    position = jnp.arange(tok_count, dtype=jnp.int32)
+    earlier = jnp.sum(
+        ((owner_of[:, None] == owner_of[None, :]) & (position[None, :] < position[:, None])).astype(
+            jnp.int32
+        ),
+        axis=1,
+    )
+    position_to = owner_of * capacity + earlier
+    chosen = position_to[None, :] == jnp.arange(buffer_rows, dtype=jnp.int32)[:, None]
+    out_slots = (jnp.sum(jnp.where(chosen, slots[None, :] + 1, 0), axis=1) - 1).reshape(
+        owner_count, capacity
+    )
+    got_slots = lax.all_to_all(out_slots, ROW_AXES, 0, 0, tiled=True).reshape(buffer_rows)
+    got_slots, tokens = lax.optimization_barrier((got_slots, tokens))
     normed_exact, norm_back = jax.vjp(layer_norm, tokens.astype(jnp.float32))
     normed = normed_exact.astype(jnp.bfloat16)
     pre = jnp.dot(normed, w_in, preferred_element_type=jnp.float32)
@@ -121,9 +141,6 @@
     emb_grad = (norm_back(normed_grad)[0] + out_grad.astype(jnp.float32)).astype(jnp.bfloat16)
     contract = (((0,), (0,)), ((), ()))
     in_cols = w_in.shape[1]
-    owner_count = 1
-    for a in ROW_AXES:
-        owner_count *= sizes[a]
     weight_share = reduce_weights(
         jnp.concatenate(
             [
@@ -134,38 +151,13 @@
         ),
         sizes,
     )
-    capacity = max(2, 4 * tok_count // owner_count)
-    buffer_rows = owner_count * capacity
-    owner_of = owners[:, 0]
-    position = jnp.arange(tok_count, dtype=jnp.int32)
-    earlier = jnp.sum(
-        ((owner_of[:, None] == owner_of[None, :]) & (position[None, :] < position[:, None])).astype(
-            jnp.int32
-        ),
-        axis=1,
-    )
-    position_to = owner_of * capacity + earlier
-    chosen = position_to[None, :] == jnp.arange(buffer_rows, dtype=jnp.int32)[:, None]
     outgoing = jnp.dot(
         chosen.astype(jnp.bfloat16), emb_grad, preferred_element_type=jnp.float32
     ).astype(jnp.bfloat16)
     outgoing = outgoing.reshape(owner_count, capacity, width)
-    out_slots = (jnp.sum(jnp.where(chosen, slots[None, :] + 1, 0), axis=1) - 1).reshape(
-        owner_count, capacity
-    )
-    block_rows = capacity * width // 128
-    slot_row = jnp.zeros((owner_count, 1, 128), jnp.bfloat16)
-    slot_row = slot_row.at[:, 0, :capacity].set(out_slots.astype(jnp.bfloat16))
-    arrived = lax.all_to_all(
-        jnp.concatenate([outgoing.reshape(owner_count, block_rows, 128), slot_row], axis=1),
-        ROW_AXES,
-        0,
-        0,
-        tiled=True,
-    )
+    arrived = lax.all_to_all(outgoing, ROW_AXES, 0, 0, tiled=True)
     arrived, weight_share = lax.optimization_barrier((arrived, weight_share))
-    received = arrived[:, :block_rows, :].reshape(buffer_rows, width)
-    got_slots = arrived[:, block_rows, :capacity].astype(jnp.int32).reshape(buffer_rows)
+    received = arrived.reshape(buffer_rows, width)
     slot_count = emb_rows.shape[0]
     matches = got_slots[None, :] == jnp.arange(slot_count, dtype=jnp.int32)[:, None]
     grad_part = jnp.dot(matches.astype(jnp.bfloat16), received, preferred_element_type=jnp.float32)

time: 241 us -> 246 us (1.021)
  starting transfers between devices: 70.5 us -> 77.2 us
  local copies, waits for them, and re-layouts: 33.8 us -> 29.4 us
  matrix products: 23.4 us -> 25.9 us
    ppermute x9, waiting for transfers between devices: 71 us -> 60.8 us  [halve_sum(): blocks = keep + lax.ppermute(send, axis, pairs)]
    all_to_all x1 -> x2, waiting for transfers between devices: 0.01 us -> 9.92 us  [the longest x1 9.92 us: local(): lax.all_to_all(out_slots, ROW_AXES, 0, 0, tiled=True).reshape(buffer_rows)]
    all_to_all x1 -> x2, starting transfers between devices: 20.1 us -> 26.3 us  [the longest x1 20.1 us: local(): lax.all_to_all(out_slots, ROW_AXES, 0, 0, tiled=True).reshape(buffer_rows)]
    split x4, local copies, waits for them, and re-layouts: 2.22 us -> 5.68 us  [core(): upart, vpart, qpart, kpart = jnp.split(proj, 4, axis=1)]
    another operation x1 -> x0, local copies, waits for them, and re-layouts: 3.1 us -> none  [local(): outgoing.reshape(owner_count, block_rows, 128)]
    reshape x1, local copies, waits for them, and re-layouts: 3.1 us -> 0.08 us  [local(): lax.all_to_all(out_slots, ROW_AXES, 0, 0, tiled=True).reshape(buffer_rows)]
    dot_general x3, matrix products: 4.73 us -> 7.5 us  [core(): jnp.einsum('thd,shd->hts', queries, keys_part, preferred_element_type=jnp...]
    unnamed x44 -> x33, local copies, waits for them, and re-layouts: 6.12 us -> 3.93 us
  transfers between devices with their start and end apart: 12 -> 13, of which waited for: 10 -> 11; matrix products, arithmetic and copies ran while one was open for 13% -> 10% of each run, Pallas kernels for 0% -> 0%
where the time goes in v10:
time: 246 us; the launch traced here: 245 us
  waiting for transfers between devices  85.7 us (35%)
  starting transfers between devices  77.2 us (31%)
  local copies, waits for them, and re-layouts  29.4 us (12%)
  matrix products  25.9 us (11%)
  other arithmetic  25.2 us (10%)
    ppermute x9, waiting for transfers between devices, halve_sum(): blocks = keep + lax.ppermute(send, axis, pairs)  60.8 us
    ppermute x9, starting transfers between devices, halve_sum(): blocks = keep + lax.ppermute(send, axis, pairs)  45.4 us
    all_to_all x1, starting transfers between devices, local(): lax.all_to_all(out_slots, ROW_AXES, 0, 0, tiled=True).reshape(buffer_rows)  20.1 us
    ppermute x2, waiting for transfers between devices, double_sum(): lax.ppermute(value, axis, [(i, i ^ 1 << bit) for i in range(size)])  15 us
    all_to_all x1, waiting for transfers between devices, local(): lax.all_to_all(out_slots, ROW_AXES, 0, 0, tiled=True).reshape(buffer_rows)  9.92 us
    add x8, other arithmetic, halve_sum(): blocks = keep + lax.ppermute(send, axis, pairs)  9.15 us
    dot_general x3, matrix products, core(): jnp.einsum('hts,shd->thd', weights, values_part, preferred_element_type=j...  7.62 us
    dot_general x3, matrix products, core(): jnp.einsum('thd,shd->hts', queries, keys_part, preferred_element_type=jnp...  7.5 us
  transfers between devices with their start and end apart: 13, of which 11 were waited for; matrix products, arithmetic and copies ran while one was open for 10% of the time, Pallas kernels for 0%

profile of v10, /device:TPU:6, one launch (start us, length us, event | category | flops | bytes accessed | tf_op | source)
XLA Modules:
  0.0 244.5 jit_solution(9442234881187718141)
XLA Ops:
  0.7 1.1 convert_reduce_fusion.2
  3.7 20.1 %all-to-all-start = ((s32[128,1,16]{2,1,0:T(1,128)}), s32[128,1,16]{2,1,0:T(1,128)S(1)}, u32[]{:S(2)}, u32[]{:S(2)}) async-start(s32[128,1,16]{2,1,0:T(1,128)} %bitcast.1), calls=%async_computation | async-start | bytes 131072 | tf_op jit(solution)/shard_map/all_to_all | solution.py:130
  23.8 0.8 reduce-window.8
  24.8 1.2 fusion.21
  26.0 1.2 fusion.20
  27.1 1.0 copy.66
  28.2 9.9 %all-to-all-done = s32[128,1,16]{2,1,0:T(1,128)S(1)} async-done(((s32[128,1,16]{2,1,0:T(1,128)}), s32[128,1,16]{2,1,0:T(1,128)S(1)}, u32[]{:S(2)}, u32[]{:S(2)}) %all-to-all-start) | async-done | bytes 8224 | tf_op jit(solution)/shard_map/all_to_all | solution.py:130
  38.6 0.8 reduce.8
  40.1 2.3 multiply_convert_fusion.1
  42.3 1.0 fusion.43
  43.3 1.1 copy.58
  44.4 1.8 copy.59
  46.2 1.8 copy.57
  48.0 4.8 %multiply_convert_fusion = (bf16[4,512,512]{2,1,0:T(8,128)(2,1)S(1)}, f32[4,512,512]{2,1,0:T(8,128)}) fusion(f32[512,512]{1,0:T(8,128)} %fusion.21, bf16[512,4,64]{0,2,1:T(8,128)(2,1)S(1)} %bitcast.60, bf16[512,4,64]{0,2,1:T(8,128)(2,1)} %bitcast.62), kind=kOutput, calls=%fused_computation.4 | convolution fusion | flops 142606336 | bytes 7864320 | tf_op jit(solution)/shard_map/jvp(thd,shd->hts)/dot_general | solution.py:46
  52.9 1.3 copy-done.1
  54.2 0.8 fusion.44
  55.3 1.4 multiply_reduce_fusion
  56.7 1.9 fusion.42
  58.7 0.8 broadcast_add_fusion
  59.5 1.1 copy.62
  60.6 2.8 %fusion.47 = bf16[4,64,512]{2,1,0:T(8,128)(2,1)} fusion(bf16[4,64,512]{2,1,0:T(8,128)(2,1)S(1)} %bitcast.69, bf16[4,512,512]{2,1,0:T(8,128)(2,1)} %copy-done.1), kind=kOutput, calls=%fused_computation.114 | convolution fusion | flops 134217728 | bytes 2621440 | tf_op jit(solution)/shard_map/transpose(jvp(hts,shd->thd))/dot_general | solution.py:50
  63.4 4.0 %fusion.2 = bf16[4,512,512]{2,1,0:T(8,128)(2,1)S(1)} fusion(f32[4,512,512]{2,1,0:T(8,128)} %get-tuple-element.28, f32[512,512]{1,0:T(8,128)S(1)} %copy-done.9, bf16[4,64,512]{2,1,0:T(8,128)(2,1)S(1)} %bitcast.70, bf16[512,4,64]{0,2,1:T(8,128)(2,1)} %bitcast.64), kind=kOutput, calls=%fused_computation.3 | convolution fusion | flops 148897792 | bytes 7864320 | tf_op jit(solution)/shard_map/transpose(jvp(hts,shd->thd))/dot_general | solution.py:50
  67.5 1.5 fusion.46
  68.9 1.2 fusion.45
  70.1 1.5 convolution_bitcast_fusion
  71.7 1.1 copy.63
  72.9 1.1 copy.65
  74.0 2.4 fusion.6
  77.2 1.7 fusion.16
  78.9 1.7 pad_maximum_fusion
  80.6 3.9 %reshape.219 = f32[16,4,2,4,1280]{4,3,2,1,0:T(4,128)} reshape(f32[512,1280]{1,0:T(8,128)} %pad_maximum_fusion) | data formatting | bytes 5242880 | tf_op jit(solution)/shard_map/reshape | solution.py:98
  84.5 2.6 %constant_dynamic-slice_fusion.8 = f32[16,4,1,4,1280]{4,3,2,1,0:T(4,128)} fusion(f32[16,4,2,4,1280]{4,3,2,1,0:T(4,128)} %reshape.219, s32[]{:T(128)S(6)} %select_n.83), kind=kLoop, calls=%fused_computation.91 | loop fusion | bytes 2621444 | tf_op jit(solution)/shard_map/jit(dynamic_index_in_dim)/dynamic_slice | solution.py:82
  87.2 2.1 collective-permute-start
  89.6 2.7 %fusion.4 = bf16[2048,512]{1,0:T(8,128)(2,1)} fusion(s32[512]{0:T(512)S(1)} %get-tuple-element.35, bf16[512,512]{0,1:T(8,128)(2,1)S(1)} %copy-done.12, f32[512]{0:T(512)S(1)} %negate_multiply_fusion, bf16[512,512]{0,1:T(8,128)(2,1)S(1)} %copy.56, f32[512,512]{0,1:T(8,128)S(1)} %copy-done.8, f32[512]{0:T(512)S(1)} %multiply_multiply_fusion, ...), kind=kOutput, calls=%fused_computation.10 | convolution fusion | flops 1078460416 | bytes 4204544 | tf_op jit(solution)/shard_map/dot_general | solution.py:154
  92.3 6.2 %all-to-all-start.1 = ((bf16[128,16,512]{2,1,0:T(8,128)(2,1)}), bf16[128,16,512]{2,1,0:T(8,128)(2,1)S(1)}, u32[]{:S(2)}, u32[]{:S(2)}) async-start(bf16[128,16,512]{2,1,0:T(8,128)(2,1)} %bitcast.57), calls=%async_computation.1 | async-start | bytes 4194304 | tf_op jit(solution)/shard_map/all_to_all | solution.py:158
  98.6 3.2 %dynamic-slice_add_fusion = f32[16,4,1,4,1280]{4,3,2,1,0:T(4,128)} fusion(f32[16,4,1,4,1280]{4,3,2,1,0:T(4,128)} %collective-permute-done, f32[16,4,2,4,1280]{4,3,2,1,0:T(4,128)} %reshape.219, s32[]{:T(128)S(6)} %select_n.82), kind=kLoop, calls=%fused_computation.27 | loop fusion | flops 327680 | bytes 3932164 | tf_op jit(solution)/shard_map/add | solution.py:84
  101.7 3.1 %reshape_reshape_reshape.3 = f32[16,4,2,2,1,1280]{5,3,2,1,0,4:T(2,128)} reshape(f32[16,4,1,4,1280]{4,3,2,1,0:T(4,128)} %dynamic-slice_add_fusion) | data formatting | bytes 2621440 | tf_op jit(solution)/shard_map/reshape;reshape;reshape | solution.py:77
  104.9 2.8 %constant_dynamic-slice_fusion.7 = f32[16,4,2,1,1,1280]{5,3,2,1,0,4:T(1,128)} fusion(f32[16,4,2,2,1,1280]{5,3,2,1,0,4:T(2,128)} %reshape_reshape_reshape.3, s32[]{:T(128)S(6)} %select_n.85), kind=kLoop, calls=%fused_computation.90 | loop fusion | bytes 1310724 | tf_op jit(solution)/shard_map/jit(dynamic_index_in_dim)/dynamic_slice | solution.py:82
  107.7 2.7 %collective-permute-start.1 = (f32[16,4,2,1,1,1280]{5,3,2,1,0,4:T(1,128)}, f32[16,4,2,1,1,1280]{5,3,2,1,0,4:T(1,128)}, u32[]{:S(2)}, u32[]{:S(2)}) collective-permute-start(f32[16,4,2,1,1,1280]{5,3,2,1,0,4:T(1,128)} %constant_dynamic-slice_fusion.7), channel_id=1, source_target_pairs={{0,1},{1,0},{2,3},{3,2},{4,5},{5,4},{6,7},{7,6},{8,9},{9,8},{10,11... | collective-permute-start | bytes 1966088 | tf_op jit(solution)/shard_map/ppermute | solution.py:84
  110.4 15.7 %collective-permute-done.1 = f32[16,4,2,1,1,1280]{5,3,2,1,0,4:T(1,128)} collective-permute-done((f32[16,4,2,1,1,1280]{5,3,2,1,0,4:T(1,128)}, f32[16,4,2,1,1,1280]{5,3,2,1,0,4:T(1,128)}, u32[]{:S(2)}, u32[]{:S(2)}) %collective-permute-start.1) | collective-permute-done | bytes 655392 | tf_op jit(solution)/shard_map/ppermute | solution.py:84
  126.1 2.4 dynamic-slice_add_fusion.1
  128.6 0.8 copy-done.3
  129.4 3.3 %collective-permute-start.2 = (f32[16,4,1,1,1,1280]{5,3,2,1,0,4:T(1,128)S(1)}, f32[16,4,1,1,1,1280]{5,3,2,1,0,4:T(1,128)}, u32[]{:S(2)}, u32[]{:S(2)}) collective-permute-start(f32[16,4,1,1,1,1280]{5,3,2,1,0,4:T(1,128)S(1)} %constant_dynamic-slice_fusion.6), channel_id=1, source_target_pairs={{0,2},{1,3},{2,0},{3,1},{4,6},{5,7},{6,4},{7,5},{8,10},{9,11},{10,... | collective-permute-start | bytes 983048 | tf_op jit(solution)/shard_map/ppermute | solution.py:84
  132.8 8.5 %collective-permute-done.2 = f32[16,4,1,1,1,1280]{5,3,2,1,0,4:T(1,128)} collective-permute-done((f32[16,4,1,1,1,1280]{5,3,2,1,0,4:T(1,128)S(1)}, f32[16,4,1,1,1,1280]{5,3,2,1,0,4:T(1,128)}, u32[]{:S(2)}, u32[]{:S(2)}) %collective-permute-start.2) | collective-permute-done | bytes 327712 | tf_op jit(solution)/shard_map/ppermute | solution.py:84
  141.3 1.4 dynamic-slice_add_fusion.2
  143.4 4.1 %collective-permute-start.3 = (f32[16,2,1,1,1280]{4,3,2,1,0:T(1,128)}, f32[16,2,1,1,1280]{4,3,2,1,0:T(1,128)}, u32[]{:S(2)}, u32[]{:S(2)}) collective-permute-start(f32[16,2,1,1,1280]{4,3,2,1,0:T(1,128)} %constant_dynamic-slice_fusion.5), channel_id=1, source_target_pairs={{0,8},{8,0},{16,24},{24,16},{1,9},{9,1},{17,25},{25,17},{2,10},{10... | collective-permute-start | bytes 491528 | tf_op jit(solution)/shard_map/ppermute | solution.py:84
  147.5 4.2 %collective-permute-done.3 = f32[16,2,1,1,1280]{4,3,2,1,0:T(1,128)} collective-permute-done((f32[16,2,1,1,1280]{4,3,2,1,0:T(1,128)}, f32[16,2,1,1,1280]{4,3,2,1,0:T(1,128)}, u32[]{:S(2)}, u32[]{:S(2)}) %collective-permute-start.3) | collective-permute-done | bytes 163872 | tf_op jit(solution)/shard_map/ppermute | solution.py:84
  151.7 1.1 dynamic-slice_add_fusion.3
  153.4 5.4 %collective-permute-start.4 = (f32[16,1,1,1,1280]{4,3,2,1,0:T(1,128)S(1)}, f32[16,1,1,1,1280]{4,3,2,1,0:T(1,128)S(1)}, u32[]{:S(2)}, u32[]{:S(2)}) collective-permute-start(f32[16,1,1,1,1280]{4,3,2,1,0:T(1,128)S(1)} %constant_dynamic-slice_fusion.4), channel_id=1, source_target_pairs={{0,16},{8,24},{16,0},{24,8},{1,17},{9,25},{17,1},{25,9},{2,18},{10... | collective-permute-start | bytes 245768 | tf_op jit(solution)/shard_map/ppermute | solution.py:84
  158.9 2.9 %collective-permute-done.4 = f32[16,1,1,1,1280]{4,3,2,1,0:T(1,128)S(1)} collective-permute-done((f32[16,1,1,1,1280]{4,3,2,1,0:T(1,128)S(1)}, f32[16,1,1,1,1280]{4,3,2,1,0:T(1,128)S(1)}, u32[]{:S(2)}, u32[]{:S(2)}) %collective-permute-start.4) | collective-permute-done | bytes 81952 | tf_op jit(solution)/shard_map/ppermute | solution.py:84
  161.8 1.0 dynamic-slice_add_fusion.4
  162.8 4.3 %collective-permute-start.5 = (f32[2,2,2,1,1,1280]{5,4,3,2,1,0:T(1,128)S(1)}, f32[2,2,2,1,1,1280]{5,4,3,2,1,0:T(1,128)S(1)}, u32[]{:S(2)}, u32[]{:S(2)}) collective-permute-start(f32[2,2,2,1,1,1280]{5,4,3,2,1,0:T(1,128)S(1)} %constant_dynamic-slice_fusion.3), channel_id=1, source_target_pairs={{0,32},{32,0},{64,96},{96,64},{128,160},{160,128},{192,224},{224,1... | collective-permute-start | bytes 122888 | tf_op jit(solution)/shard_map/ppermute | solution.py:84
  167.1 22.6 %collective-permute-done.5 = f32[2,2,2,1,1,1280]{5,4,3,2,1,0:T(1,128)S(1)} collective-permute-done((f32[2,2,2,1,1,1280]{5,4,3,2,1,0:T(1,128)S(1)}, f32[2,2,2,1,1,1280]{5,4,3,2,1,0:T(1,128)S(1)}, u32[]{:S(2)}, u32[]{:S(2)}) %collective-permute-start.5) | collective-permute-done | bytes 40992 | tf_op jit(solution)/shard_map/ppermute | solution.py:84
  189.8 3.9 %collective-permute-start.6 = (f32[2,2,1,1,1,1280]{5,4,3,2,1,0:T(1,128)S(1)}, f32[2,2,1,1,1,1280]{5,4,3,2,1,0:T(1,128)S(1)}, u32[]{:S(2)}, u32[]{:S(2)}) collective-permute-start(f32[2,2,1,1,1,1280]{5,4,3,2,1,0:T(1,128)S(1)} %constant_dynamic-slice_fusion.2), channel_id=1, source_target_pairs={{0,64},{32,96},{64,0},{96,32},{128,192},{160,224},{192,128},{224,1... | collective-permute-start | bytes 61448 | tf_op jit(solution)/shard_map/ppermute | solution.py:84
  193.6 2.8 %collective-permute-done.6 = f32[2,2,1,1,1,1280]{5,4,3,2,1,0:T(1,128)S(1)} collective-permute-done((f32[2,2,1,1,1,1280]{5,4,3,2,1,0:T(1,128)S(1)}, f32[2,2,1,1,1,1280]{5,4,3,2,1,0:T(1,128)S(1)}, u32[]{:S(2)}, u32[]{:S(2)}) %collective-permute-start.6) | collective-permute-done | bytes 20512 | tf_op jit(solution)/shard_map/ppermute | solution.py:84
  196.4 6.8 %collective-permute-start.7 = (f32[2,1,1,1,1,1280]{5,4,3,2,1,0:T(1,128)S(1)}, f32[2,1,1,1,1,1280]{5,4,3,2,1,0:T(1,128)S(1)}, u32[]{:S(2)}, u32[]{:S(2)}) collective-permute-start(f32[2,1,1,1,1,1280]{5,4,3,2,1,0:T(1,128)S(1)} %constant_dynamic-slice_fusion.1), channel_id=1, source_target_pairs={{0,128},{32,160},{64,192},{96,224},{128,0},{160,32},{192,64},{224,... | collective-permute-start | bytes 30728 | tf_op jit(solution)/shard_map/ppermute | solution.py:84
  203.2 2.7 %collective-permute-done.7 = f32[2,1,1,1,1,1280]{5,4,3,2,1,0:T(1,128)S(1)} collective-permute-done((f32[2,1,1,1,1,1280]{5,4,3,2,1,0:T(1,128)S(1)}, f32[2,1,1,1,1,1280]{5,4,3,2,1,0:T(1,128)S(1)}, u32[]{:S(2)}, u32[]{:S(2)}) %collective-permute-start.7) | collective-permute-done | bytes 10272 | tf_op jit(solution)/shard_map/ppermute | solution.py:84
  206.0 12.7 %collective-permute-start.8 = (f32[1,1,1,1,1,1280]{5,4,3,2,1,0:T(1,128)S(1)}, f32[1,1,1,1,1,1280]{5,4,3,2,1,0:T(1,128)S(1)}, u32[]{:S(2)}, u32[]{:S(2)}) collective-permute-start(f32[1,1,1,1,1,1280]{5,4,3,2,1,0:T(1,128)S(1)} %constant_dynamic-slice_fusion), channel_id=1, source_target_pairs={{0,256},{32,288},{64,320},{96,352},{128,384},{160,416},{192,448},{... | collective-permute-start | bytes 15368 | tf_op jit(solution)/shard_map/ppermute | solution.py:84
  218.9 1.4 collective-permute-done.8
  221.0 2.7 %collective-permute-start.9 = (f32[136,640]{1,0:T(8,128)S(1)}, f32[136,640]{1,0:T(8,128)S(1)}, u32[]{:S(2)}, u32[]{:S(2)}) collective-permute-start(f32[136,640]{1,0:T(8,128)S(1)} %pad_maximum_fusion.1), channel_id=1, source_target_pairs={{0,1},{1,0},{2,3},{3,2},{4,5},{5,4},{6,7},{7,6},{8,9},{9,8},{10,11... | collective-permute-start | bytes 1044488 | tf_op jit(solution)/shard_map/ppermute | solution.py:90
  223.8 7.0 %collective-permute-done.9 = f32[136,640]{1,0:T(8,128)S(1)} collective-permute-done((f32[136,640]{1,0:T(8,128)S(1)}, f32[136,640]{1,0:T(8,128)S(1)}, u32[]{:S(2)}, u32[]{:S(2)}) %collective-permute-start.9) | collective-permute-done | bytes 348192 | tf_op jit(solution)/shard_map/ppermute | solution.py:90
  230.9 2.7 %collective-permute-start.10 = (f32[136,640]{1,0:T(8,128)S(1)}, f32[136,640]{1,0:T(8,128)S(1)}, u32[]{:S(2)}, u32[]{:S(2)}) collective-permute-start(f32[136,640]{1,0:T(8,128)S(1)} %fusion.41), channel_id=1, source_target_pairs={{0,2},{1,3},{2,0},{3,1},{4,6},{5,7},{6,4},{7,5},{8,10},{9,11},{10,... | collective-permute-start | bytes 1044488 | tf_op jit(solution)/shard_map/ppermute | solution.py:90
  233.6 7.9 %collective-permute-done.10 = f32[136,640]{1,0:T(8,128)S(1)} collective-permute-done((f32[136,640]{1,0:T(8,128)S(1)}, f32[136,640]{1,0:T(8,128)S(1)}, u32[]{:S(2)}, u32[]{:S(2)}) %collective-permute-start.10) | collective-permute-done | bytes 348192 | tf_op jit(solution)/shard_map/ppermute | solution.py:90
  243.6 0.9 fusion.35
  (81 shorter events, 9.1 us)
Async XLA Ops:
  0.6 39.4 %copy-start = (bf16[512,1024]{1,0:T(8,128)(2,1)S(1)}, bf16[512,1024]{1,0:T(8,128)(2,1)}, u32[]{:S(2)}) copy-start(bf16[512,1024]{1,0:T(8,128)(2,1)} %param.15) | copy-start | bytes 3145732
  0.6 26.5 %copy-start.2 = (bf16[512,512]{1,0:T(8,128)(2,1)S(1)}, bf16[512,512]{1,0:T(8,128)(2,1)}, u32[]{:S(2)}) copy-start(bf16[512,512]{1,0:T(8,128)(2,1)} %param.11) | copy-start | bytes 1572868
  0.7 38.9 %copy-start.11 = (bf16[512,512]{1,0:T(8,128)(2,1)S(1)}, bf16[512,512]{1,0:T(8,128)(2,1)}, u32[]{:S(2)}) copy-start(bf16[512,512]{1,0:T(8,128)(2,1)} %param.10) | copy-start | bytes 1572868
  3.7 34.4 %all-to-all-start = ((s32[128,1,16]{2,1,0:T(1,128)}), s32[128,1,16]{2,1,0:T(1,128)S(1)}, u32[]{:S(2)}, u32[]{:S(2)}) async-start(s32[128,1,16]{2,1,0:T(1,128)} %bitcast.1), calls=%async_computation | async-start | bytes 131072 | tf_op jit(solution)/shard_map/all_to_all | solution.py:130
  42.3 10.5 %copy-start.4 = (bf16[512,1024]{1,0:T(8,128)(2,1)}, bf16[512,1024]{1,0:T(8,128)(2,1)S(1)}, u32[]{:S(2)}) copy-start(bf16[512,1024]{1,0:T(8,128)(2,1)S(1)} %get-tuple-element.25) | copy-start | bytes 3145732
  48.0 6.2 %copy-start.6 = (bf16[512,256]{0,1:T(8,128)(2,1)S(1)}, bf16[512,256]{0,1:T(8,128)(2,1)}, u32[]{:S(2)}) copy-start(bf16[512,256]{0,1:T(8,128)(2,1)} %copy.57) | copy-start | bytes 786436
  52.9 1.3 copy-start.1
  60.6 2.9 %copy-start.9 = (f32[512,512]{1,0:T(8,128)S(1)}, f32[512,512]{1,0:T(8,128)}, u32[]{:S(2)}) copy-start(f32[512,512]{1,0:T(8,128)} %fusion.20) | copy-start | bytes 3145732
  63.4 4.0 %copy-start.5 = (bf16[512,256]{0,1:T(8,128)(2,1)S(1)}, bf16[512,256]{0,1:T(8,128)(2,1)}, u32[]{:S(2)}) copy-start(bf16[512,256]{0,1:T(8,128)(2,1)} %copy.59) | copy-start | bytes 786436
  70.1 2.6 %copy-start.7 = (bf16[4,512,64]{1,2,0:T(8,128)(2,1)S(1)}, bf16[4,512,64]{1,2,0:T(8,128)(2,1)}, u32[]{:S(2)}) copy-start(bf16[4,512,64]{1,2,0:T(8,128)(2,1)} %fusion.46) | copy-start | bytes 786436
  84.5 4.8 %copy-start.8 = (f32[512,512]{0,1:T(8,128)S(1)}, f32[512,512]{0,1:T(8,128)}, u32[]{:S(2)}) copy-start(f32[512,512]{0,1:T(8,128)} %get-tuple-element.34) | copy-start | bytes 3145732
  84.5 5.1 %copy-start.12 = (bf16[512,512]{0,1:T(8,128)(2,1)S(1)}, bf16[512,512]{0,1:T(8,128)(2,1)}, u32[]{:S(2)}) copy-start(bf16[512,512]{0,1:T(8,128)(2,1)} %copy.66) | copy-start | bytes 1572868
  87.2 11.4 %collective-permute-start = (f32[16,4,1,4,1280]{4,3,2,1,0:T(4,128)}, f32[16,4,1,4,1280]{4,3,2,1,0:T(4,128)}, u32[]{:S(2)}, u32[]{:S(2)}) collective-permute-start(f32[16,4,1,4,1280]{4,3,2,1,0:T(4,128)} %constant_dynamic-slice_fusion.8), channel_id=1, source_target_pairs={{0,4},{4,0},{1,5},{5,1},{2,6},{6,2},{3,7},{7,3},{8,12},{12,8},{9,1... | collective-permute-start | bytes 3932168 | tf_op jit(solution)/shard_map/ppermute | solution.py:84
  92.3 128.1 %all-to-all-start.1 = ((bf16[128,16,512]{2,1,0:T(8,128)(2,1)}), bf16[128,16,512]{2,1,0:T(8,128)(2,1)S(1)}, u32[]{:S(2)}, u32[]{:S(2)}) async-start(bf16[128,16,512]{2,1,0:T(8,128)(2,1)} %bitcast.57), calls=%async_computation.1 | async-start | bytes 4194304 | tf_op jit(solution)/shard_map/all_to_all | solution.py:158
  107.7 18.5 %collective-permute-start.1 = (f32[16,4,2,1,1,1280]{5,3,2,1,0,4:T(1,128)}, f32[16,4,2,1,1,1280]{5,3,2,1,0,4:T(1,128)}, u32[]{:S(2)}, u32[]{:S(2)}) collective-permute-start(f32[16,4,2,1,1,1280]{5,3,2,1,0,4:T(1,128)} %constant_dynamic-slice_fusion.7), channel_id=1, source_target_pairs={{0,1},{1,0},{2,3},{3,2},{4,5},{5,4},{6,7},{7,6},{8,9},{9,8},{10,11... | collective-permute-start | bytes 1966088 | tf_op jit(solution)/shard_map/ppermute | solution.py:84
  128.6 0.8 copy-start.3
  129.4 11.8 %collective-permute-start.2 = (f32[16,4,1,1,1,1280]{5,3,2,1,0,4:T(1,128)S(1)}, f32[16,4,1,1,1,1280]{5,3,2,1,0,4:T(1,128)}, u32[]{:S(2)}, u32[]{:S(2)}) collective-permute-start(f32[16,4,1,1,1,1280]{5,3,2,1,0,4:T(1,128)S(1)} %constant_dynamic-slice_fusion.6), channel_id=1, source_target_pairs={{0,2},{1,3},{2,0},{3,1},{4,6},{5,7},{6,4},{7,5},{8,10},{9,11},{10,... | collective-permute-start | bytes 983048 | tf_op jit(solution)/shard_map/ppermute | solution.py:84
  143.4 8.3 %collective-permute-start.3 = (f32[16,2,1,1,1280]{4,3,2,1,0:T(1,128)}, f32[16,2,1,1,1280]{4,3,2,1,0:T(1,128)}, u32[]{:S(2)}, u32[]{:S(2)}) collective-permute-start(f32[16,2,1,1,1280]{4,3,2,1,0:T(1,128)} %constant_dynamic-slice_fusion.5), channel_id=1, source_target_pairs={{0,8},{8,0},{16,24},{24,16},{1,9},{9,1},{17,25},{25,17},{2,10},{10... | collective-permute-start | bytes 491528 | tf_op jit(solution)/shard_map/ppermute | solution.py:84
  152.8 0.7 copy-start.10
  153.4 8.3 %collective-permute-start.4 = (f32[16,1,1,1,1280]{4,3,2,1,0:T(1,128)S(1)}, f32[16,1,1,1,1280]{4,3,2,1,0:T(1,128)S(1)}, u32[]{:S(2)}, u32[]{:S(2)}) collective-permute-start(f32[16,1,1,1,1280]{4,3,2,1,0:T(1,128)S(1)} %constant_dynamic-slice_fusion.4), channel_id=1, source_target_pairs={{0,16},{8,24},{16,0},{24,8},{1,17},{9,25},{17,1},{25,9},{2,18},{10... | collective-permute-start | bytes 245768 | tf_op jit(solution)/shard_map/ppermute | solution.py:84
  162.8 26.9 %collective-permute-start.5 = (f32[2,2,2,1,1,1280]{5,4,3,2,1,0:T(1,128)S(1)}, f32[2,2,2,1,1,1280]{5,4,3,2,1,0:T(1,128)S(1)}, u32[]{:S(2)}, u32[]{:S(2)}) collective-permute-start(f32[2,2,2,1,1,1280]{5,4,3,2,1,0:T(1,128)S(1)} %constant_dynamic-slice_fusion.3), channel_id=1, source_target_pairs={{0,32},{32,0},{64,96},{96,64},{128,160},{160,128},{192,224},{224,1... | collective-permute-start | bytes 122888 | tf_op jit(solution)/shard_map/ppermute | solution.py:84
  189.8 6.6 %collective-permute-start.6 = (f32[2,2,1,1,1,1280]{5,4,3,2,1,0:T(1,128)S(1)}, f32[2,2,1,1,1,1280]{5,4,3,2,1,0:T(1,128)S(1)}, u32[]{:S(2)}, u32[]{:S(2)}) collective-permute-start(f32[2,2,1,1,1,1280]{5,4,3,2,1,0:T(1,128)S(1)} %constant_dynamic-slice_fusion.2), channel_id=1, source_target_pairs={{0,64},{32,96},{64,0},{96,32},{128,192},{160,224},{192,128},{224,1... | collective-permute-start | bytes 61448 | tf_op jit(solution)/shard_map/ppermute | solution.py:84
  196.4 9.5 %collective-permute-start.7 = (f32[2,1,1,1,1,1280]{5,4,3,2,1,0:T(1,128)S(1)}, f32[2,1,1,1,1,1280]{5,4,3,2,1,0:T(1,128)S(1)}, u32[]{:S(2)}, u32[]{:S(2)}) collective-permute-start(f32[2,1,1,1,1,1280]{5,4,3,2,1,0:T(1,128)S(1)} %constant_dynamic-slice_fusion.1), channel_id=1, source_target_pairs={{0,128},{32,160},{64,192},{96,224},{128,0},{160,32},{192,64},{224,... | collective-permute-start | bytes 30728 | tf_op jit(solution)/shard_map/ppermute | solution.py:84
  206.0 14.3 %collective-permute-start.8 = (f32[1,1,1,1,1,1280]{5,4,3,2,1,0:T(1,128)S(1)}, f32[1,1,1,1,1,1280]{5,4,3,2,1,0:T(1,128)S(1)}, u32[]{:S(2)}, u32[]{:S(2)}) collective-permute-start(f32[1,1,1,1,1,1280]{5,4,3,2,1,0:T(1,128)S(1)} %constant_dynamic-slice_fusion), channel_id=1, source_target_pairs={{0,256},{32,288},{64,320},{96,352},{128,384},{160,416},{192,448},{... | collective-permute-start | bytes 15368 | tf_op jit(solution)/shard_map/ppermute | solution.py:84
  220.9 22.2 %copy-start.15 = (f32[128]{0:T(128)S(1)}, f32[128]{0:T(128)}, u32[]{:S(2)}) copy-start(f32[128]{0:T(128)} %param.19) | copy-start | bytes 1540
  220.9 22.7 %copy-start.13 = (f32[128,512]{1,0:T(8,128)S(1)}, f32[128,512]{1,0:T(8,128)}, u32[]{:S(2)}) copy-start(f32[128,512]{1,0:T(8,128)} %param.18) | copy-start | bytes 786436
  220.9 22.7 %copy-start.14 = (f32[128,512]{1,0:T(8,128)S(1)}, f32[128,512]{1,0:T(8,128)}, u32[]{:S(2)}) copy-start(f32[128,512]{1,0:T(8,128)} %param.17) | copy-start | bytes 786436
  221.0 9.8 %collective-permute-start.9 = (f32[136,640]{1,0:T(8,128)S(1)}, f32[136,640]{1,0:T(8,128)S(1)}, u32[]{:S(2)}, u32[]{:S(2)}) collective-permute-start(f32[136,640]{1,0:T(8,128)S(1)} %pad_maximum_fusion.1), channel_id=1, source_target_pairs={{0,1},{1,0},{2,3},{3,2},{4,5},{5,4},{6,7},{7,6},{8,9},{9,8},{10,11... | collective-permute-start | bytes 1044488 | tf_op jit(solution)/shard_map/ppermute | solution.py:90
  230.9 10.7 %collective-permute-start.10 = (f32[136,640]{1,0:T(8,128)S(1)}, f32[136,640]{1,0:T(8,128)S(1)}, u32[]{:S(2)}, u32[]{:S(2)}) collective-permute-start(f32[136,640]{1,0:T(8,128)S(1)} %fusion.41), channel_id=1, source_target_pairs={{0,2},{1,3},{2,0},{3,1},{4,6},{5,7},{6,4},{7,5},{8,10},{9,11},{10,... | collective-permute-start | bytes 1044488 | tf_op jit(solution)/shard_map/ppermute | solution.py:90

commit v11 on v10

--- a/solution.py
+++ b/solution.py
@@ -99,6 +99,12 @@
     blocks = halve_sum(blocks, "core", n_c, 2)
     blocks = blocks.reshape(n_z, n_y, n_x, per_owner // n_x, width)
     blocks = halve_sum(blocks, "x", n_x, 2)
+    return blocks
+
+
+def finish_weights(blocks, sizes):
+    n_z, n_y, n_x = sizes["z"], sizes["y"], sizes["x"]
+    per_owner, width = blocks.shape[2] * n_x, blocks.shape[3]
     blocks = halve_sum(blocks, "y", n_y, 1)
     piece = halve_sum(blocks, "z", n_z, 0)
     mine = lax.axis_index("x") * (per_owner // n_x)
@@ -155,7 +161,9 @@
         chosen.astype(jnp.bfloat16), emb_grad, preferred_element_type=jnp.float32
     ).astype(jnp.bfloat16)
     outgoing = outgoing.reshape(owner_count, capacity, width)
+    outgoing, weight_share = lax.optimization_barrier((outgoing, weight_share))
     arrived = lax.all_to_all(outgoing, ROW_AXES, 0, 0, tiled=True)
+    weight_share = finish_weights(weight_share, sizes)
     arrived, weight_share = lax.optimization_barrier((arrived, weight_share))
     received = arrived.reshape(buffer_rows, width)
     slot_count = emb_rows.shape[0]

time: 246 us -> 280 us (1.14)
  waiting for transfers between devices: 85.7 us -> 133 us
  local copies, waits for them, and re-layouts: 29.4 us -> 24 us
  other arithmetic: 25.2 us -> 21.8 us
  starting transfers between devices: 77.2 us -> 74 us
    ppermute x9, waiting for transfers between devices: 60.8 us -> 106 us  [halve_sum(): blocks = keep + lax.ppermute(send, axis, pairs)]
    split x4, local copies, waits for them, and re-layouts: 5.68 us -> 2.22 us  [core(): upart, vpart, qpart, kpart = jnp.split(proj, 4, axis=1)]
    ppermute x9, starting transfers between devices: 45.4 us -> 42.2 us  [halve_sum(): blocks = keep + lax.ppermute(send, axis, pairs)]
    add x8 -> x7, other arithmetic: 9.15 us -> 6.17 us  [halve_sum(): blocks = keep + lax.ppermute(send, axis, pairs)]
  transfers between devices with their start and end apart: 13 -> 13, of which waited for: 11 -> 12; matrix products, arithmetic and copies ran while one was open for 10% -> 4% of each run, Pallas kernels for 0% -> 0%
where the time goes in v11:
time: 280 us; the launch traced here: 279 us
  waiting for transfers between devices  133 us (48%)
  starting transfers between devices  74 us (26%)
  matrix products  25.6 us (9%)
  local copies, waits for them, and re-layouts  24 us (9%)
  other arithmetic  21.8 us (8%)
    ppermute x9, waiting for transfers between devices, halve_sum(): blocks = keep + lax.ppermute(send, axis, pairs)  106 us
    ppermute x9, starting transfers between devices, halve_sum(): blocks = keep + lax.ppermute(send, axis, pairs)  42.2 us
    all_to_all x1, starting transfers between devices, local(): lax.all_to_all(out_slots, ROW_AXES, 0, 0, tiled=True).reshape(buffer_rows)  20.1 us
    ppermute x2, waiting for transfers between devices, double_sum(): lax.ppermute(value, axis, [(i, i ^ 1 << bit) for i in range(size)])  15 us
    all_to_all x1, waiting for transfers between devices, local(): lax.all_to_all(out_slots, ROW_AXES, 0, 0, tiled=True).reshape(buffer_rows)  12 us
    dot_general x3, matrix products, core(): jnp.einsum('hts,shd->thd', weights, values_part, preferred_element_type=j...  7.51 us
    all_to_all x1, starting transfers between devices, local(): arrived = lax.all_to_all(outgoing, ROW_AXES, 0, 0, tiled=True)  6.22 us
    add x7, other arithmetic, halve_sum(): blocks = keep + lax.ppermute(send, axis, pairs)  6.17 us
  transfers between devices with their start and end apart: 13, of which 12 were waited for; matrix products, arithmetic and copies ran while one was open for 4% of the time, Pallas kernels for 0%

profile of v11, /device:TPU:6, one launch (start us, length us, event | category | flops | bytes accessed | tf_op | source)
XLA Modules:
  0.0 279.3 jit_solution(15368172218407160164)
XLA Ops:
  0.7 1.1 convert_reduce_fusion.2
  1.7 0.7 multiply_add_fusion.3
  3.0 0.7 sub.66
  3.7 20.1 %all-to-all-start = ((s32[128,1,16]{2,1,0:T(1,128)}), s32[128,1,16]{2,1,0:T(1,128)S(1)}, u32[]{:S(2)}, u32[]{:S(2)}) async-start(s32[128,1,16]{2,1,0:T(1,128)} %bitcast.1), calls=%async_computation | async-start | bytes 131072 | tf_op jit(solution)/shard_map/all_to_all | solution.py:136
  23.8 0.8 reduce-window.8
  24.9 1.2 fusion.20
  26.1 12.0 %all-to-all-done = s32[128,1,16]{2,1,0:T(1,128)S(1)} async-done(((s32[128,1,16]{2,1,0:T(1,128)}), s32[128,1,16]{2,1,0:T(1,128)S(1)}, u32[]{:S(2)}, u32[]{:S(2)}) %all-to-all-start) | async-done | bytes 8224 | tf_op jit(solution)/shard_map/all_to_all | solution.py:136
  38.6 0.8 reduce.8
  40.0 2.3 multiply_convert_fusion.1
  42.3 1.1 copy-done.4
  43.4 0.8 fusion.43
  44.4 1.2 copy.57
  45.6 3.5 %multiply_convert_fusion = (bf16[4,512,512]{2,1,0:T(8,128)(2,1)S(1)}, f32[4,512,512]{2,1,0:T(8,128)}) fusion(f32[512,512]{1,0:T(8,128)S(1)} %fusion.21, bf16[512,4,64]{0,2,1:T(8,128)(2,1)S(1)} %bitcast.62, bf16[512,4,64]{0,2,1:T(8,128)(2,1)S(1)} %bitcast.64), kind=kOutput, calls=%fused_computation.4 | convolution fusion | flops 142606336 | bytes 7864320 | tf_op jit(solution)/shard_map/jvp(thd,shd->hts)/dot_general | solution.py:46
  49.1 1.3 copy-done.1
  50.5 0.8 fusion.44
  51.5 1.4 multiply_reduce_fusion
  53.0 1.9 fusion.42
  54.9 0.8 broadcast_add_fusion
  55.8 1.1 copy.62
  56.9 2.2 fusion.47
  59.1 4.6 %fusion.2 = bf16[4,512,512]{2,1,0:T(8,128)(2,1)S(1)} fusion(f32[4,512,512]{2,1,0:T(8,128)} %get-tuple-element.32, f32[512,512]{1,0:T(8,128)S(1)} %copy-done.12, bf16[4,64,512]{2,1,0:T(8,128)(2,1)} %bitcast.72, bf16[512,4,64]{0,2,1:T(8,128)(2,1)} %bitcast.67), kind=kOutput, calls=%fused_computation.3 | convolution fusion | flops 148897792 | bytes 7864320 | tf_op jit(solution)/shard_map/transpose(jvp(hts,shd->thd))/dot_general | solution.py:50
  63.7 1.5 fusion.46
  65.2 1.2 fusion.45
  66.3 2.3 convolution_bitcast_fusion
  68.7 0.8 copy.63
  69.5 0.8 copy.64
  70.3 0.8 copy.65
  71.2 2.7 fusion.6
  73.9 0.7 fusion.28
  75.3 1.7 pad_maximum_fusion
  77.0 3.9 %reshape.225 = f32[16,4,2,4,1280]{4,3,2,1,0:T(4,128)} reshape(f32[512,1280]{1,0:T(8,128)} %pad_maximum_fusion) | data formatting | bytes 5242880 | tf_op jit(solution)/shard_map/reshape | solution.py:98
  80.9 2.5 constant_dynamic-slice_fusion.8
  83.4 2.1 collective-permute-start
  85.5 1.0 copy.66
  86.6 2.1 collective-permute-done
  88.7 3.1 %dynamic-slice_add_fusion = f32[16,4,1,4,1280]{4,3,2,1,0:T(4,128)} fusion(f32[16,4,1,4,1280]{4,3,2,1,0:T(4,128)} %collective-permute-done, f32[16,4,2,4,1280]{4,3,2,1,0:T(4,128)} %reshape.225, s32[]{:T(128)S(6)} %select_n.82), kind=kLoop, calls=%fused_computation.27 | loop fusion | flops 327680 | bytes 3932164 | tf_op jit(solution)/shard_map/add | solution.py:84
  91.8 2.3 reshape_reshape_reshape.3
  94.8 2.7 collective-permute-start.1
  97.5 2.0 fusion.16
  99.8 13.6 %collective-permute-done.1 = f32[16,4,2,1,1,1280]{5,3,2,1,0,4:T(1,128)S(1)} collective-permute-done((f32[16,4,2,1,1,1280]{5,3,2,1,0,4:T(1,128)S(1)}, f32[16,4,2,1,1,1280]{5,3,2,1,0,4:T(1,128)S(1)}, u32[]{:S(2)}, u32[]{:S(2)}) %collective-permute-start.1) | collective-permute-done | bytes 655392 | tf_op jit(solution)/shard_map/ppermute | solution.py:84
  113.5 0.9 dynamic-slice_add_fusion.1
  114.4 3.3 %collective-permute-start.2 = (f32[16,4,1,1,1,1280]{5,3,2,1,0,4:T(1,128)S(1)}, f32[16,4,1,1,1,1280]{5,3,2,1,0,4:T(1,128)S(1)}, u32[]{:S(2)}, u32[]{:S(2)}) collective-permute-start(f32[16,4,1,1,1,1280]{5,3,2,1,0,4:T(1,128)S(1)} %constant_dynamic-slice_fusion.6), channel_id=1, source_target_pairs={{0,2},{1,3},{2,0},{3,1},{4,6},{5,7},{6,4},{7,5},{8,10},{9,11},{10,... | collective-permute-start | bytes 983048 | tf_op jit(solution)/shard_map/ppermute | solution.py:84
  117.7 2.8 fusion.4
  120.5 6.2 %collective-permute-done.2 = f32[16,4,1,1,1,1280]{5,3,2,1,0,4:T(1,128)S(1)} collective-permute-done((f32[16,4,1,1,1,1280]{5,3,2,1,0,4:T(1,128)S(1)}, f32[16,4,1,1,1,1280]{5,3,2,1,0,4:T(1,128)S(1)}, u32[]{:S(2)}, u32[]{:S(2)}) %collective-permute-start.2) | collective-permute-done | bytes 327712 | tf_op jit(solution)/shard_map/ppermute | solution.py:84
  127.1 6.2 %all-to-all-start.1 = ((bf16[128,16,512]{2,1,0:T(8,128)(2,1)}), bf16[128,16,512]{2,1,0:T(8,128)(2,1)S(1)}, u32[]{:S(2)}, u32[]{:S(2)}) async-start(bf16[128,16,512]{2,1,0:T(8,128)(2,1)} %bitcast.59), calls=%async_computation.1 | async-start | bytes 4194304 | tf_op jit(solution)/shard_map/all_to_all | solution.py:165
  134.0 2.9 %collective-permute-start.3 = (f32[16,2,1,1,1280]{4,3,2,1,0:T(1,128)}, f32[16,2,1,1,1280]{4,3,2,1,0:T(1,128)}, u32[]{:S(2)}, u32[]{:S(2)}) collective-permute-start(f32[16,2,1,1,1280]{4,3,2,1,0:T(1,128)} %constant_dynamic-slice_fusion.5), channel_id=1, source_target_pairs={{0,8},{8,0},{16,24},{24,16},{1,9},{9,1},{17,25},{25,17},{2,10},{10... | collective-permute-start | bytes 491528 | tf_op jit(solution)/shard_map/ppermute | solution.py:84
  137.0 6.5 %collective-permute-done.3 = f32[16,2,1,1,1280]{4,3,2,1,0:T(1,128)} collective-permute-done((f32[16,2,1,1,1280]{4,3,2,1,0:T(1,128)}, f32[16,2,1,1,1280]{4,3,2,1,0:T(1,128)}, u32[]{:S(2)}, u32[]{:S(2)}) %collective-permute-start.3) | collective-permute-done | bytes 163872 | tf_op jit(solution)/shard_map/ppermute | solution.py:84
  143.4 1.1 dynamic-slice_add_fusion.2
  145.2 5.0 %collective-permute-start.4 = (f32[16,1,1,1,1280]{4,3,2,1,0:T(1,128)S(1)}, f32[16,1,1,1,1280]{4,3,2,1,0:T(1,128)S(1)}, u32[]{:S(2)}, u32[]{:S(2)}) collective-permute-start(f32[16,1,1,1,1280]{4,3,2,1,0:T(1,128)S(1)} %constant_dynamic-slice_fusion.4), channel_id=1, source_target_pairs={{0,16},{8,24},{16,0},{24,8},{1,17},{9,25},{17,1},{25,9},{2,18},{10... | collective-permute-start | bytes 245768 | tf_op jit(solution)/shard_map/ppermute | solution.py:84
  150.2 3.3 %collective-permute-done.4 = f32[16,1,1,1,1280]{4,3,2,1,0:T(1,128)S(1)} collective-permute-done((f32[16,1,1,1,1280]{4,3,2,1,0:T(1,128)S(1)}, f32[16,1,1,1,1280]{4,3,2,1,0:T(1,128)S(1)}, u32[]{:S(2)}, u32[]{:S(2)}) %collective-permute-start.4) | collective-permute-done | bytes 81952 | tf_op jit(solution)/shard_map/ppermute | solution.py:84
  153.5 1.0 dynamic-slice_add_fusion.3
  154.5 2.8 collective-permute-start.5
  157.3 67.1 %collective-permute-done.5 = f32[2,2,2,1,1,1280]{5,4,3,2,1,0:T(1,128)S(1)} collective-permute-done((f32[2,2,2,1,1,1280]{5,4,3,2,1,0:T(1,128)S(1)}, f32[2,2,2,1,1,1280]{5,4,3,2,1,0:T(1,128)S(1)}, u32[]{:S(2)}, u32[]{:S(2)}) %collective-permute-start.5) | collective-permute-done | bytes 40992 | tf_op jit(solution)/shard_map/ppermute | solution.py:84
  224.5 3.9 %collective-permute-start.6 = (f32[2,2,1,1,1,1280]{5,4,3,2,1,0:T(1,128)S(1)}, f32[2,2,1,1,1,1280]{5,4,3,2,1,0:T(1,128)S(1)}, u32[]{:S(2)}, u32[]{:S(2)}) collective-permute-start(f32[2,2,1,1,1,1280]{5,4,3,2,1,0:T(1,128)S(1)} %constant_dynamic-slice_fusion.2), channel_id=1, source_target_pairs={{0,64},{32,96},{64,0},{96,32},{128,192},{160,224},{192,128},{224,1... | collective-permute-start | bytes 61448 | tf_op jit(solution)/shard_map/ppermute | solution.py:84
  228.4 2.8 collective-permute-done.6
  231.2 6.7 %collective-permute-start.7 = (f32[2,1,1,1,1,1280]{5,4,3,2,1,0:T(1,128)S(1)}, f32[2,1,1,1,1,1280]{5,4,3,2,1,0:T(1,128)S(1)}, u32[]{:S(2)}, u32[]{:S(2)}) collective-permute-start(f32[2,1,1,1,1,1280]{5,4,3,2,1,0:T(1,128)S(1)} %constant_dynamic-slice_fusion.1), channel_id=1, source_target_pairs={{0,128},{32,160},{64,192},{96,224},{128,0},{160,32},{192,64},{224,... | collective-permute-start | bytes 30728 | tf_op jit(solution)/shard_map/ppermute | solution.py:84
  237.9 2.8 %collective-permute-done.7 = f32[2,1,1,1,1,1280]{5,4,3,2,1,0:T(1,128)S(1)} collective-permute-done((f32[2,1,1,1,1,1280]{5,4,3,2,1,0:T(1,128)S(1)}, f32[2,1,1,1,1,1280]{5,4,3,2,1,0:T(1,128)S(1)}, u32[]{:S(2)}, u32[]{:S(2)}) %collective-permute-start.7) | collective-permute-done | bytes 10272 | tf_op jit(solution)/shard_map/ppermute | solution.py:84
  240.7 12.7 %collective-permute-start.8 = (f32[1,1,1,1,1,1280]{5,4,3,2,1,0:T(1,128)S(1)}, f32[1,1,1,1,1,1280]{5,4,3,2,1,0:T(1,128)S(1)}, u32[]{:S(2)}, u32[]{:S(2)}) collective-permute-start(f32[1,1,1,1,1,1280]{5,4,3,2,1,0:T(1,128)S(1)} %constant_dynamic-slice_fusion), channel_id=1, source_target_pairs={{0,256},{32,288},{64,320},{96,352},{128,384},{160,416},{192,448},{... | collective-permute-start | bytes 15368 | tf_op jit(solution)/shard_map/ppermute | solution.py:84
  253.7 1.4 collective-permute-done.8
  255.8 2.7 collective-permute-start.9
  258.6 7.0 %collective-permute-done.9 = f32[136,640]{1,0:T(8,128)S(1)} collective-permute-done((f32[136,640]{1,0:T(8,128)S(1)}, f32[136,640]{1,0:T(8,128)S(1)}, u32[]{:S(2)}, u32[]{:S(2)}) %collective-permute-start.9) | collective-permute-done | bytes 348192 | tf_op jit(solution)/shard_map/ppermute | solution.py:90
  265.6 2.7 collective-permute-start.10
  268.4 8.0 %collective-permute-done.10 = f32[136,640]{1,0:T(8,128)S(1)} collective-permute-done((f32[136,640]{1,0:T(8,128)S(1)}, f32[136,640]{1,0:T(8,128)S(1)}, u32[]{:S(2)}, u32[]{:S(2)}) %collective-permute-start.10) | collective-permute-done | bytes 348192 | tf_op jit(solution)/shard_map/ppermute | solution.py:90
  278.3 0.9 fusion.35
  (87 shorter events, 9.0 us)
Async XLA Ops:
  0.6 39.4 %copy-start = (bf16[512,1024]{1,0:T(8,128)(2,1)S(1)}, bf16[512,1024]{1,0:T(8,128)(2,1)}, u32[]{:S(2)}) copy-start(bf16[512,1024]{1,0:T(8,128)(2,1)} %param.15) | copy-start | bytes 3145732
  0.6 38.8 %copy-start.14 = (bf16[512,512]{1,0:T(8,128)(2,1)S(1)}, bf16[512,512]{1,0:T(8,128)(2,1)}, u32[]{:S(2)}) copy-start(bf16[512,512]{1,0:T(8,128)(2,1)} %param.10) | copy-start | bytes 1572868
  3.7 34.4 %all-to-all-start = ((s32[128,1,16]{2,1,0:T(1,128)}), s32[128,1,16]{2,1,0:T(1,128)S(1)}, u32[]{:S(2)}, u32[]{:S(2)}) async-start(s32[128,1,16]{2,1,0:T(1,128)} %bitcast.1), calls=%async_computation | async-start | bytes 131072 | tf_op jit(solution)/shard_map/all_to_all | solution.py:136
  42.3 1.1 copy-start.4
  44.4 4.7 %copy-start.6 = (bf16[512,256]{0,1:T(8,128)(2,1)}, bf16[512,256]{0,1:T(8,128)(2,1)S(1)}, u32[]{:S(2)}) copy-start(bf16[512,256]{0,1:T(8,128)(2,1)S(1)} %copy.59) | copy-start | bytes 786436
  45.6 3.5 %copy-start.8 = (bf16[512,256]{0,1:T(8,128)(2,1)}, bf16[512,256]{0,1:T(8,128)(2,1)S(1)}, u32[]{:S(2)}) copy-start(bf16[512,256]{0,1:T(8,128)(2,1)S(1)} %copy.57) | copy-start | bytes 786436
  49.1 1.3 copy-start.1
  50.5 1.1 copy-start.2
  56.8 2.2 copy-start.11
  56.9 2.2 copy-start.12
  59.1 4.6 %copy-start.7 = (bf16[512,256]{0,1:T(8,128)(2,1)S(1)}, bf16[512,256]{0,1:T(8,128)(2,1)}, u32[]{:S(2)}) copy-start(bf16[512,256]{0,1:T(8,128)(2,1)} %copy-done.6) | copy-start | bytes 786436
  65.2 4.3 %copy-start.9 = (bf16[4,512,64]{1,2,0:T(8,128)(2,1)S(1)}, bf16[4,512,64]{1,2,0:T(8,128)(2,1)}, u32[]{:S(2)}) copy-start(bf16[4,512,64]{1,2,0:T(8,128)(2,1)} %fusion.46) | copy-start | bytes 786436
  66.3 4.0 %copy-start.10 = (bf16[4,512,64]{1,2,0:T(8,128)(2,1)S(1)}, bf16[4,512,64]{1,2,0:T(8,128)(2,1)}, u32[]{:S(2)}) copy-start(bf16[4,512,64]{1,2,0:T(8,128)(2,1)} %fusion.45) | copy-start | bytes 786436
  73.8 3.2 %copy-start.3 = (bf16[512,1024]{1,0:T(8,128)(2,1)}, bf16[512,1024]{1,0:T(8,128)(2,1)S(1)}, u32[]{:S(2)}) copy-start(bf16[512,1024]{1,0:T(8,128)(2,1)S(1)} %fusion.6) | copy-start | bytes 3145732
  73.9 1.4 copy-start.5
  83.4 5.3 %collective-permute-start = (f32[16,4,1,4,1280]{4,3,2,1,0:T(4,128)}, f32[16,4,1,4,1280]{4,3,2,1,0:T(4,128)}, u32[]{:S(2)}, u32[]{:S(2)}) collective-permute-start(f32[16,4,1,4,1280]{4,3,2,1,0:T(4,128)} %constant_dynamic-slice_fusion.8), channel_id=1, source_target_pairs={{0,4},{4,0},{1,5},{5,1},{2,6},{6,2},{3,7},{7,3},{8,12},{12,8},{9,1... | collective-permute-start | bytes 3932168 | tf_op jit(solution)/shard_map/ppermute | solution.py:84
  94.8 18.7 %collective-permute-start.1 = (f32[16,4,2,1,1,1280]{5,3,2,1,0,4:T(1,128)S(1)}, f32[16,4,2,1,1,1280]{5,3,2,1,0,4:T(1,128)S(1)}, u32[]{:S(2)}, u32[]{:S(2)}) collective-permute-start(f32[16,4,2,1,1,1280]{5,3,2,1,0,4:T(1,128)S(1)} %constant_dynamic-slice_fusion.7), channel_id=1, source_target_pairs={{0,1},{1,0},{2,3},{3,2},{4,5},{5,4},{6,7},{7,6},{8,9},{9,8},{10,11... | collective-permute-start | bytes 1966088 | tf_op jit(solution)/shard_map/ppermute | solution.py:84
  99.5 18.2 %copy-start.15 = (bf16[512,512]{0,1:T(8,128)(2,1)S(1)}, bf16[512,512]{0,1:T(8,128)(2,1)}, u32[]{:S(2)}) copy-start(bf16[512,512]{0,1:T(8,128)(2,1)} %copy.66) | copy-start | bytes 1572868
  114.4 12.3 %collective-permute-start.2 = (f32[16,4,1,1,1,1280]{5,3,2,1,0,4:T(1,128)S(1)}, f32[16,4,1,1,1,1280]{5,3,2,1,0,4:T(1,128)S(1)}, u32[]{:S(2)}, u32[]{:S(2)}) collective-permute-start(f32[16,4,1,1,1,1280]{5,3,2,1,0,4:T(1,128)S(1)} %constant_dynamic-slice_fusion.6), channel_id=1, source_target_pairs={{0,2},{1,3},{2,0},{3,1},{4,6},{5,7},{6,4},{7,5},{8,10},{9,11},{10,... | collective-permute-start | bytes 983048 | tf_op jit(solution)/shard_map/ppermute | solution.py:84
  127.1 128.1 %all-to-all-start.1 = ((bf16[128,16,512]{2,1,0:T(8,128)(2,1)}), bf16[128,16,512]{2,1,0:T(8,128)(2,1)S(1)}, u32[]{:S(2)}, u32[]{:S(2)}) async-start(bf16[128,16,512]{2,1,0:T(8,128)(2,1)} %bitcast.59), calls=%async_computation.1 | async-start | bytes 4194304 | tf_op jit(solution)/shard_map/all_to_all | solution.py:165
  134.0 9.4 %collective-permute-start.3 = (f32[16,2,1,1,1280]{4,3,2,1,0:T(1,128)}, f32[16,2,1,1,1280]{4,3,2,1,0:T(1,128)}, u32[]{:S(2)}, u32[]{:S(2)}) collective-permute-start(f32[16,2,1,1,1280]{4,3,2,1,0:T(1,128)} %constant_dynamic-slice_fusion.5), channel_id=1, source_target_pairs={{0,8},{8,0},{16,24},{24,16},{1,9},{9,1},{17,25},{25,17},{2,10},{10... | collective-permute-start | bytes 491528 | tf_op jit(solution)/shard_map/ppermute | solution.py:84
  144.5 0.7 copy-start.13
  145.2 8.3 %collective-permute-start.4 = (f32[16,1,1,1,1280]{4,3,2,1,0:T(1,128)S(1)}, f32[16,1,1,1,1280]{4,3,2,1,0:T(1,128)S(1)}, u32[]{:S(2)}, u32[]{:S(2)}) collective-permute-start(f32[16,1,1,1,1280]{4,3,2,1,0:T(1,128)S(1)} %constant_dynamic-slice_fusion.4), channel_id=1, source_target_pairs={{0,16},{8,24},{16,0},{24,8},{1,17},{9,25},{17,1},{25,9},{2,18},{10... | collective-permute-start | bytes 245768 | tf_op jit(solution)/shard_map/ppermute | solution.py:84
  154.5 69.9 %collective-permute-start.5 = (f32[2,2,2,1,1,1280]{5,4,3,2,1,0:T(1,128)S(1)}, f32[2,2,2,1,1,1280]{5,4,3,2,1,0:T(1,128)S(1)}, u32[]{:S(2)}, u32[]{:S(2)}) collective-permute-start(f32[2,2,2,1,1,1280]{5,4,3,2,1,0:T(1,128)S(1)} %constant_dynamic-slice_fusion.3), channel_id=1, source_target_pairs={{0,32},{32,0},{64,96},{96,64},{128,160},{160,128},{192,224},{224,1... | collective-permute-start | bytes 122888 | tf_op jit(solution)/shard_map/ppermute | solution.py:84
  224.5 6.7 %collective-permute-start.6 = (f32[2,2,1,1,1,1280]{5,4,3,2,1,0:T(1,128)S(1)}, f32[2,2,1,1,1,1280]{5,4,3,2,1,0:T(1,128)S(1)}, u32[]{:S(2)}, u32[]{:S(2)}) collective-permute-start(f32[2,2,1,1,1,1280]{5,4,3,2,1,0:T(1,128)S(1)} %constant_dynamic-slice_fusion.2), channel_id=1, source_target_pairs={{0,64},{32,96},{64,0},{96,32},{128,192},{160,224},{192,128},{224,1... | collective-permute-start | bytes 61448 | tf_op jit(solution)/shard_map/ppermute | solution.py:84
  231.2 9.5 %collective-permute-start.7 = (f32[2,1,1,1,1,1280]{5,4,3,2,1,0:T(1,128)S(1)}, f32[2,1,1,1,1,1280]{5,4,3,2,1,0:T(1,128)S(1)}, u32[]{:S(2)}, u32[]{:S(2)}) collective-permute-start(f32[2,1,1,1,1,1280]{5,4,3,2,1,0:T(1,128)S(1)} %constant_dynamic-slice_fusion.1), channel_id=1, source_target_pairs={{0,128},{32,160},{64,192},{96,224},{128,0},{160,32},{192,64},{224,... | collective-permute-start | bytes 30728 | tf_op jit(solution)/shard_map/ppermute | solution.py:84
  240.7 14.3 %collective-permute-start.8 = (f32[1,1,1,1,1,1280]{5,4,3,2,1,0:T(1,128)S(1)}, f32[1,1,1,1,1,1280]{5,4,3,2,1,0:T(1,128)S(1)}, u32[]{:S(2)}, u32[]{:S(2)}) collective-permute-start(f32[1,1,1,1,1,1280]{5,4,3,2,1,0:T(1,128)S(1)} %constant_dynamic-slice_fusion), channel_id=1, source_target_pairs={{0,256},{32,288},{64,320},{96,352},{128,384},{160,416},{192,448},{... | collective-permute-start | bytes 15368 | tf_op jit(solution)/shard_map/ppermute | solution.py:84
  255.6 22.2 %copy-start.18 = (f32[128]{0:T(128)S(1)}, f32[128]{0:T(128)}, u32[]{:S(2)}) copy-start(f32[128]{0:T(128)} %param.19) | copy-start | bytes 1540
  255.7 22.7 %copy-start.16 = (f32[128,512]{1,0:T(8,128)S(1)}, f32[128,512]{1,0:T(8,128)}, u32[]{:S(2)}) copy-start(f32[128,512]{1,0:T(8,128)} %param.18) | copy-start | bytes 786436
  255.7 22.7 %copy-start.17 = (f32[128,512]{1,0:T(8,128)S(1)}, f32[128,512]{1,0:T(8,128)}, u32[]{:S(2)}) copy-start(f32[128,512]{1,0:T(8,128)} %param.17) | copy-start | bytes 786436
  255.8 9.8 %collective-permute-start.9 = (f32[136,640]{1,0:T(8,128)S(1)}, f32[136,640]{1,0:T(8,128)S(1)}, u32[]{:S(2)}, u32[]{:S(2)}) collective-permute-start(f32[136,640]{1,0:T(8,128)S(1)} %pad_maximum_fusion.1), channel_id=1, source_target_pairs={{0,1},{1,0},{2,3},{3,2},{4,5},{5,4},{6,7},{7,6},{8,9},{9,8},{10,11... | collective-permute-start | bytes 1044488 | tf_op jit(solution)/shard_map/ppermute | solution.py:90
  265.6 10.7 %collective-permute-start.10 = (f32[136,640]{1,0:T(8,128)S(1)}, f32[136,640]{1,0:T(8,128)S(1)}, u32[]{:S(2)}, u32[]{:S(2)}) collective-permute-start(f32[136,640]{1,0:T(8,128)S(1)} %fusion.41), channel_id=1, source_target_pairs={{0,2},{1,3},{2,0},{3,1},{4,6},{5,7},{6,4},{7,5},{8,10},{9,11},{10,... | collective-permute-start | bytes 1044488 | tf_op jit(solution)/shard_map/ppermute | solution.py:90

commit v12 on v9

--- a/solution.py
+++ b/solution.py
@@ -164,11 +164,22 @@
         tiled=True,
     )
     arrived, weight_share = lax.optimization_barrier((arrived, weight_share))
-    received = arrived[:, :block_rows, :].reshape(buffer_rows, width)
+    lane_blocks = width // 128
+    received = arrived[:, :block_rows, :].reshape(owner_count, capacity, lane_blocks, 128)
     got_slots = arrived[:, block_rows, :capacity].astype(jnp.int32).reshape(buffer_rows)
     slot_count = emb_rows.shape[0]
     matches = got_slots[None, :] == jnp.arange(slot_count, dtype=jnp.int32)[:, None]
-    grad_part = jnp.dot(matches.astype(jnp.bfloat16), received, preferred_element_type=jnp.float32)
+    grad_part = jnp.concatenate(
+        [
+            jnp.dot(
+                matches.astype(jnp.bfloat16),
+                received[:, :, j, :].reshape(buffer_rows, 128),
+                preferred_element_type=jnp.float32,
+            )
+            for j in range(lane_blocks)
+        ],
+        axis=1,
+    )
     count_part = jnp.sum(matches.astype(jnp.float32), axis=1)
     lanes = width + 128
     both = double_sum(

time: 241 us -> 238 us (0.988)
  waiting for transfers between devices: 86.1 us -> 91.1 us
  local copies, waits for them, and re-layouts: 33.8 us -> 29.4 us
  other arithmetic: 24.5 us -> 21 us
    ppermute x9, waiting for transfers between devices: 71 us -> 77.5 us  [halve_sum(): blocks = keep + lax.ppermute(send, axis, pairs)]
    reshape x1 -> x0, local copies, waits for them, and re-layouts: 3.1 us -> none  [local(): received = arrived[:, :block_rows, :].reshape(buffer_rows, width)]
    add x8, other arithmetic: 10 us -> 7.24 us  [halve_sum(): blocks = keep + lax.ppermute(send, axis, pairs)]
  transfers between devices with their start and end apart: 12 -> 12, of which waited for: 10 -> 10; matrix products, arithmetic and copies ran while one was open for 13% -> 11% of each run, Pallas kernels for 0% -> 0%
where the time goes in v12:
time: 238 us; the launch traced here: 237 us
  waiting for transfers between devices  91.1 us (38%)
  starting transfers between devices  71 us (30%)
  local copies, waits for them, and re-layouts  29.4 us (12%)
  matrix products  23.5 us (10%)
  other arithmetic  21 us (9%)
    ppermute x9, waiting for transfers between devices, halve_sum(): blocks = keep + lax.ppermute(send, axis, pairs)  77.5 us
    ppermute x9, starting transfers between devices, halve_sum(): blocks = keep + lax.ppermute(send, axis, pairs)  44.8 us
    all_to_all x1, starting transfers between devices, local(): lax.all_to_all(jnp.concatenate([outgoing.reshape(owner_count, block_rows,...  20.1 us
    ppermute x2, waiting for transfers between devices, double_sum(): lax.ppermute(value, axis, [(i, i ^ 1 << bit) for i in range(size)])  13.6 us
    add x8, other arithmetic, halve_sum(): blocks = keep + lax.ppermute(send, axis, pairs)  7.24 us
    dot_general x3, matrix products, core(): jnp.einsum('hts,shd->thd', weights, values_part, preferred_element_type=j...  6.92 us
    ppermute x2, starting transfers between devices, double_sum(): lax.ppermute(value, axis, [(i, i ^ 1 << bit) for i in range(size)])  6.14 us
    unnamed x44, local copies, waits for them, and re-layouts  5.05 us
  transfers between devices with their start and end apart: 12, of which 10 were waited for; matrix products, arithmetic and copies ran while one was open for 11% of the time, Pallas kernels for 0%

profile of v12, /device:TPU:6, one launch (start us, length us, event | category | flops | bytes accessed | tf_op | source)
XLA Modules:
  0.0 237.3 jit_solution(4926852492598987225)
XLA Ops:
  0.7 0.9 reduce-window.8
  1.9 1.3 fusion.21
  3.7 2.3 multiply_convert_fusion.1
  6.0 1.0 copy-done.4
  6.9 0.8 fusion.47
  8.0 1.2 copy.113
  9.2 3.5 %multiply_convert_fusion = (bf16[4,512,512]{2,1,0:T(8,128)(2,1)S(1)}, f32[4,512,512]{2,1,0:T(8,128)}) fusion(f32[512,512]{1,0:T(8,128)S(1)} %fusion.22, bf16[512,4,64]{0,2,1:T(8,128)(2,1)S(1)} %bitcast.68, bf16[512,4,64]{0,2,1:T(8,128)(2,1)S(1)} %bitcast.70), kind=kOutput, calls=%fused_computation.7 | convolution fusion | flops 142606336 | bytes 7864320 | tf_op jit(solution)/shard_map/jvp(thd,shd->hts)/dot_general | solution.py:46
  12.7 1.3 copy-done.2
  14.0 0.8 fusion.48
  15.1 1.5 multiply_reduce_fusion
  16.6 1.3 convolution_bitcast_fusion
  18.0 1.0 fusion.45
  19.2 2.1 fusion.51
  21.4 4.0 %fusion.3 = bf16[4,512,512]{2,1,0:T(8,128)(2,1)S(1)} fusion(f32[4,512,512]{2,1,0:T(8,128)} %get-tuple-element.65, f32[512,512]{1,0:T(8,128)S(1)} %copy-done.12, bf16[4,64,512]{2,1,0:T(8,128)(2,1)S(1)} %bitcast.76, bf16[512,4,64]{0,2,1:T(8,128)(2,1)S(1)} %bitcast.73), kind=kOutput, calls=%fused_computation.5 | convolution fusion | flops 148897792 | bytes 7864320 | tf_op jit(solution)/shard_map/transpose(jvp(hts,shd->thd))/dot_general | solution.py:50
  25.5 0.8 fusion.50
  26.2 0.5 fusion.49
  26.8 0.8 copy.120
  27.7 0.8 copy.121
  28.5 2.6 %fusion.8 = bf16[512,1024]{1,0:T(8,128)(2,1)S(1)} fusion(f32[512,1024]{1,0:T(8,128)} %get-tuple-element.63, bf16[512,256]{1,0:T(8,128)(2,1)} %copy.121, bf16[512,256]{1,0:T(8,128)(2,1)} %copy.120, bf16[512,256]{1,0:T(8,128)(2,1)S(1)} %copy.119, bf16[512,256]{1,0:T(8,128)(2,1)} %get-tuple-element.52), kind=kLoop, calls=%fused_computation.18 | loop fusion | flops 9437184 | bytes 4194304 | tf_op jit(solution)/shard_map/convert_element_type | solution.py:117
  31.1 0.7 fusion.32
  32.2 1.7 pad_maximum_fusion
  33.9 3.9 %reshape.250 = f32[16,4,2,4,1280]{4,3,2,1,0:T(4,128)} reshape(f32[512,1280]{1,0:T(8,128)} %pad_maximum_fusion) | data formatting | bytes 5242880 | tf_op jit(solution)/shard_map/reshape | solution.py:98
  37.8 2.5 %constant_dynamic-slice_fusion.8 = f32[16,4,1,4,1280]{4,3,2,1,0:T(4,128)} fusion(f32[16,4,2,4,1280]{4,3,2,1,0:T(4,128)} %reshape.250, s32[]{:T(128)S(6)} %select_n.83), kind=kLoop, calls=%fused_computation.101 | loop fusion | bytes 2621444 | tf_op jit(solution)/shard_map/jit(dynamic_index_in_dim)/dynamic_slice | solution.py:82
  40.3 2.1 collective-permute-start
  42.4 1.7 fusion.18
  44.4 1.6 fusion.31
  46.2 0.5 select_reduce_fusion
  46.8 2.7 %fusion.5 = bf16[2048,512]{1,0:T(8,128)(2,1)} fusion(s32[512]{0:T(512)S(1)} %get-tuple-element.72, bf16[512,512]{0,1:T(8,128)(2,1)S(1)} %copy.122, f32[512]{0:T(512)S(1)} %negate_multiply_fusion, bf16[512,512]{0,1:T(8,128)(2,1)S(1)} %copy.112, f32[512,512]{0,1:T(8,128)S(1)} %copy-done.11, f32[512]{0:T(512)S(1)} %multiply_multiply_fusion, ...), kind=kOutput, calls=%fused_computation.12 | convolution fusion | flops 1078460416 | bytes 4204544 | tf_op jit(solution)/shard_map/dot_general | solution.py:149
  49.5 3.1 %reshape_reshape.9 = bf16[128,64,128]{2,1,0:T(8,128)(2,1)S(1)} reshape(bf16[2048,512]{1,0:T(8,128)(2,1)} %fusion.5) | data formatting | bytes 4194304 | tf_op jit(solution)/shard_map/reshape;reshape | solution.py:160
  52.7 1.7 fusion.6
  54.4 20.1 %all-to-all-start = ((bf16[128,65,128]{2,1,0:T(8,128)(2,1)}), bf16[128,65,128]{2,1,0:T(8,128)(2,1)S(1)}, u32[]{:S(2)}, u32[]{:S(2)}) async-start(bf16[128,65,128]{2,1,0:T(8,128)(2,1)} %fusion.6), calls=%async_computation | async-start | bytes 4718592 | tf_op jit(solution)/shard_map/all_to_all | solution.py:159
  74.5 3.1 %dynamic-slice_add_fusion = f32[16,4,1,4,1280]{4,3,2,1,0:T(4,128)} fusion(f32[16,4,1,4,1280]{4,3,2,1,0:T(4,128)} %collective-permute-done, f32[16,4,2,4,1280]{4,3,2,1,0:T(4,128)} %reshape.250, s32[]{:T(128)S(6)} %select_n.82), kind=kLoop, calls=%fused_computation.30 | loop fusion | flops 327680 | bytes 3932164 | tf_op jit(solution)/shard_map/add | solution.py:84
  77.6 3.1 %reshape_reshape_reshape.3 = f32[16,4,2,2,1,1280]{5,3,2,1,0,4:T(2,128)} reshape(f32[16,4,1,4,1280]{4,3,2,1,0:T(4,128)} %dynamic-slice_add_fusion) | data formatting | bytes 2621440 | tf_op jit(solution)/shard_map/reshape;reshape;reshape | solution.py:77
  80.8 2.0 constant_dynamic-slice_fusion.7
  82.8 2.7 %collective-permute-start.1 = (f32[16,4,2,1,1,1280]{5,3,2,1,0,4:T(1,128)S(1)}, f32[16,4,2,1,1,1280]{5,3,2,1,0,4:T(1,128)}, u32[]{:S(2)}, u32[]{:S(2)}) collective-permute-start(f32[16,4,2,1,1,1280]{5,3,2,1,0,4:T(1,128)S(1)} %constant_dynamic-slice_fusion.7), channel_id=1, source_target_pairs={{0,1},{1,0},{2,3},{3,2},{4,5},{5,4},{6,7},{7,6},{8,9},{9,8},{10,11... | collective-permute-start | bytes 1966088 | tf_op jit(solution)/shard_map/ppermute | solution.py:84
  85.5 15.5 %collective-permute-done.1 = f32[16,4,2,1,1,1280]{5,3,2,1,0,4:T(1,128)} collective-permute-done((f32[16,4,2,1,1,1280]{5,3,2,1,0,4:T(1,128)S(1)}, f32[16,4,2,1,1,1280]{5,3,2,1,0,4:T(1,128)}, u32[]{:S(2)}, u32[]{:S(2)}) %collective-permute-start.1) | collective-permute-done | bytes 655392 | tf_op jit(solution)/shard_map/ppermute | solution.py:84
  101.0 2.4 %dynamic-slice_add_fusion.1 = f32[16,4,2,1,1,1280]{5,3,2,1,0,4:T(1,128)S(1)} fusion(f32[16,4,2,1,1,1280]{5,3,2,1,0,4:T(1,128)} %collective-permute-done.1, f32[16,4,2,2,1,1280]{5,3,2,1,0,4:T(2,128)} %reshape_reshape_reshape.3, s32[]{:T(128)S(6)} %select_n.84), kind=kLoop, calls=%fused_computation.58 | loop fusion | flops 163840 | bytes 1966084 | tf_op jit(solution)/shard_map/add | solution.py:84
  103.5 3.3 %collective-permute-start.2 = (f32[16,4,1,1,1,1280]{5,3,2,1,0,4:T(1,128)S(1)}, f32[16,4,1,1,1,1280]{5,3,2,1,0,4:T(1,128)}, u32[]{:S(2)}, u32[]{:S(2)}) collective-permute-start(f32[16,4,1,1,1,1280]{5,3,2,1,0,4:T(1,128)S(1)} %constant_dynamic-slice_fusion.6), channel_id=1, source_target_pairs={{0,2},{1,3},{2,0},{3,1},{4,6},{5,7},{6,4},{7,5},{8,10},{9,11},{10,... | collective-permute-start | bytes 983048 | tf_op jit(solution)/shard_map/ppermute | solution.py:84
  106.8 8.5 %collective-permute-done.2 = f32[16,4,1,1,1,1280]{5,3,2,1,0,4:T(1,128)} collective-permute-done((f32[16,4,1,1,1,1280]{5,3,2,1,0,4:T(1,128)S(1)}, f32[16,4,1,1,1,1280]{5,3,2,1,0,4:T(1,128)}, u32[]{:S(2)}, u32[]{:S(2)}) %collective-permute-start.2) | collective-permute-done | bytes 327712 | tf_op jit(solution)/shard_map/ppermute | solution.py:84
  115.3 1.3 dynamic-slice_add_fusion.2
  116.7 4.2 %collective-permute-start.3 = (f32[16,2,1,1,1280]{4,3,2,1,0:T(1,128)S(1)}, f32[16,2,1,1,1280]{4,3,2,1,0:T(1,128)S(1)}, u32[]{:S(2)}, u32[]{:S(2)}) collective-permute-start(f32[16,2,1,1,1280]{4,3,2,1,0:T(1,128)S(1)} %constant_dynamic-slice_fusion.5), channel_id=1, source_target_pairs={{0,8},{8,0},{16,24},{24,16},{1,9},{9,1},{17,25},{25,17},{2,10},{10... | collective-permute-start | bytes 491528 | tf_op jit(solution)/shard_map/ppermute | solution.py:84
  120.9 4.0 %collective-permute-done.3 = f32[16,2,1,1,1280]{4,3,2,1,0:T(1,128)S(1)} collective-permute-done((f32[16,2,1,1,1280]{4,3,2,1,0:T(1,128)S(1)}, f32[16,2,1,1,1280]{4,3,2,1,0:T(1,128)S(1)}, u32[]{:S(2)}, u32[]{:S(2)}) %collective-permute-start.3) | collective-permute-done | bytes 163872 | tf_op jit(solution)/shard_map/ppermute | solution.py:84
  125.1 5.2 %collective-permute-start.4 = (f32[16,1,1,1,1280]{4,3,2,1,0:T(1,128)S(1)}, f32[16,1,1,1,1280]{4,3,2,1,0:T(1,128)S(1)}, u32[]{:S(2)}, u32[]{:S(2)}) collective-permute-start(f32[16,1,1,1,1280]{4,3,2,1,0:T(1,128)S(1)} %constant_dynamic-slice_fusion.4), channel_id=1, source_target_pairs={{0,16},{8,24},{16,0},{24,8},{1,17},{9,25},{17,1},{25,9},{2,18},{10... | collective-permute-start | bytes 245768 | tf_op jit(solution)/shard_map/ppermute | solution.py:84
  130.3 3.1 %collective-permute-done.4 = f32[16,1,1,1,1280]{4,3,2,1,0:T(1,128)S(1)} collective-permute-done((f32[16,1,1,1,1280]{4,3,2,1,0:T(1,128)S(1)}, f32[16,1,1,1,1280]{4,3,2,1,0:T(1,128)S(1)}, u32[]{:S(2)}, u32[]{:S(2)}) %collective-permute-start.4) | collective-permute-done | bytes 81952 | tf_op jit(solution)/shard_map/ppermute | solution.py:84
  133.5 4.1 %collective-permute-start.5 = (f32[2,2,2,1,1,1280]{5,4,3,2,1,0:T(1,128)S(1)}, f32[2,2,2,1,1,1280]{5,4,3,2,1,0:T(1,128)S(1)}, u32[]{:S(2)}, u32[]{:S(2)}) collective-permute-start(f32[2,2,2,1,1,1280]{5,4,3,2,1,0:T(1,128)S(1)} %constant_dynamic-slice_fusion.3), channel_id=1, source_target_pairs={{0,32},{32,0},{64,96},{96,64},{128,160},{160,128},{192,224},{224,1... | collective-permute-start | bytes 122888 | tf_op jit(solution)/shard_map/ppermute | solution.py:84
  137.6 39.3 %collective-permute-done.5 = f32[2,2,2,1,1,1280]{5,4,3,2,1,0:T(1,128)S(1)} collective-permute-done((f32[2,2,2,1,1,1280]{5,4,3,2,1,0:T(1,128)S(1)}, f32[2,2,2,1,1,1280]{5,4,3,2,1,0:T(1,128)S(1)}, u32[]{:S(2)}, u32[]{:S(2)}) %collective-permute-start.5) | collective-permute-done | bytes 40992 | tf_op jit(solution)/shard_map/ppermute | solution.py:84
  176.9 3.9 %collective-permute-start.6 = (f32[2,2,1,1,1,1280]{5,4,3,2,1,0:T(1,128)S(1)}, f32[2,2,1,1,1,1280]{5,4,3,2,1,0:T(1,128)S(1)}, u32[]{:S(2)}, u32[]{:S(2)}) collective-permute-start(f32[2,2,1,1,1,1280]{5,4,3,2,1,0:T(1,128)S(1)} %constant_dynamic-slice_fusion.2), channel_id=1, source_target_pairs={{0,64},{32,96},{64,0},{96,32},{128,192},{160,224},{192,128},{224,1... | collective-permute-start | bytes 61448 | tf_op jit(solution)/shard_map/ppermute | solution.py:84
  180.9 2.7 %collective-permute-done.6 = f32[2,2,1,1,1,1280]{5,4,3,2,1,0:T(1,128)S(1)} collective-permute-done((f32[2,2,1,1,1,1280]{5,4,3,2,1,0:T(1,128)S(1)}, f32[2,2,1,1,1,1280]{5,4,3,2,1,0:T(1,128)S(1)}, u32[]{:S(2)}, u32[]{:S(2)}) %collective-permute-start.6) | collective-permute-done | bytes 20512 | tf_op jit(solution)/shard_map/ppermute | solution.py:84
  183.6 6.6 %collective-permute-start.7 = (f32[2,1,1,1,1,1280]{5,4,3,2,1,0:T(1,128)S(1)}, f32[2,1,1,1,1,1280]{5,4,3,2,1,0:T(1,128)S(1)}, u32[]{:S(2)}, u32[]{:S(2)}) collective-permute-start(f32[2,1,1,1,1,1280]{5,4,3,2,1,0:T(1,128)S(1)} %constant_dynamic-slice_fusion.1), channel_id=1, source_target_pairs={{0,128},{32,160},{64,192},{96,224},{128,0},{160,32},{192,64},{224,... | collective-permute-start | bytes 30728 | tf_op jit(solution)/shard_map/ppermute | solution.py:84
  190.3 2.8 %collective-permute-done.7 = f32[2,1,1,1,1,1280]{5,4,3,2,1,0:T(1,128)S(1)} collective-permute-done((f32[2,1,1,1,1,1280]{5,4,3,2,1,0:T(1,128)S(1)}, f32[2,1,1,1,1,1280]{5,4,3,2,1,0:T(1,128)S(1)}, u32[]{:S(2)}, u32[]{:S(2)}) %collective-permute-start.7) | collective-permute-done | bytes 10272 | tf_op jit(solution)/shard_map/ppermute | solution.py:84
  193.1 12.6 %collective-permute-start.8 = (f32[1,1,1,1,1,1280]{5,4,3,2,1,0:T(1,128)S(1)}, f32[1,1,1,1,1,1280]{5,4,3,2,1,0:T(1,128)S(1)}, u32[]{:S(2)}, u32[]{:S(2)}) collective-permute-start(f32[1,1,1,1,1,1280]{5,4,3,2,1,0:T(1,128)S(1)} %constant_dynamic-slice_fusion), channel_id=1, source_target_pairs={{0,256},{32,288},{64,320},{96,352},{128,384},{160,416},{192,448},{... | collective-permute-start | bytes 15368 | tf_op jit(solution)/shard_map/ppermute | solution.py:84
  205.7 1.6 collective-permute-done.8
  207.7 0.5 copy.125
  209.5 0.4 convolution_dynamic-update-slice_fusion.3
  211.1 0.4 convolution_dynamic-update-slice_fusion.2
  212.6 2.9 %collective-permute-start.9 = (f32[136,640]{1,0:T(8,128)S(1)}, f32[136,640]{1,0:T(8,128)S(1)}, u32[]{:S(2)}, u32[]{:S(2)}) collective-permute-start(f32[136,640]{1,0:T(8,128)S(1)} %copy.131), channel_id=1, source_target_pairs={{0,1},{1,0},{2,3},{3,2},{4,5},{5,4},{6,7},{7,6},{8,9},{9,8},{10,11... | collective-permute-start | bytes 1044488 | tf_op jit(solution)/shard_map/ppermute | solution.py:90
  215.5 6.5 %collective-permute-done.9 = f32[136,640]{1,0:T(8,128)S(1)} collective-permute-done((f32[136,640]{1,0:T(8,128)S(1)}, f32[136,640]{1,0:T(8,128)S(1)}, u32[]{:S(2)}, u32[]{:S(2)}) %collective-permute-start.9) | collective-permute-done | bytes 348192 | tf_op jit(solution)/shard_map/ppermute | solution.py:90
  222.5 3.3 %collective-permute-start.10 = (f32[136,640]{1,0:T(8,128)S(1)}, f32[136,640]{1,0:T(8,128)S(1)}, u32[]{:S(2)}, u32[]{:S(2)}) collective-permute-start(f32[136,640]{1,0:T(8,128)S(1)} %copy.133), channel_id=1, source_target_pairs={{0,2},{1,3},{2,0},{3,1},{4,6},{5,7},{6,4},{7,5},{8,10},{9,11},{10,... | collective-permute-start | bytes 1044488 | tf_op jit(solution)/shard_map/ppermute | solution.py:90
  226.0 7.1 %collective-permute-done.10 = f32[136,640]{1,0:T(8,128)S(1)} collective-permute-done((f32[136,640]{1,0:T(8,128)S(1)}, f32[136,640]{1,0:T(8,128)S(1)}, u32[]{:S(2)}, u32[]{:S(2)}) %collective-permute-start.10) | collective-permute-done | bytes 348192 | tf_op jit(solution)/shard_map/ppermute | solution.py:90
  233.8 0.6 slice.75
  234.4 0.6 slice.76
  235.0 0.5 fusion.43
  235.6 0.8 copy.140
  236.4 0.8 copy.141
  (106 shorter events, 8.4 us)
Async XLA Ops:
  0.6 3.0 %copy-start = (bf16[512,1024]{1,0:T(8,128)(2,1)S(1)}, bf16[512,1024]{1,0:T(8,128)(2,1)}, u32[]{:S(2)}) copy-start(bf16[512,1024]{1,0:T(8,128)(2,1)} %param.17) | copy-start | bytes 3145732
  0.6 2.5 %copy-start.13 = (bf16[512,512]{1,0:T(8,128)(2,1)S(1)}, bf16[512,512]{1,0:T(8,128)(2,1)}, u32[]{:S(2)}) copy-start(bf16[512,512]{1,0:T(8,128)(2,1)} %param.12) | copy-start | bytes 1572868
  6.0 1.0 copy-start.4
  8.0 4.7 %copy-start.7 = (bf16[512,256]{0,1:T(8,128)(2,1)}, bf16[512,256]{0,1:T(8,128)(2,1)S(1)}, u32[]{:S(2)}) copy-start(bf16[512,256]{0,1:T(8,128)(2,1)S(1)} %copy.115) | copy-start | bytes 786436
  9.2 3.5 %copy-start.9 = (bf16[512,256]{0,1:T(8,128)(2,1)}, bf16[512,256]{0,1:T(8,128)(2,1)S(1)}, u32[]{:S(2)}) copy-start(bf16[512,256]{0,1:T(8,128)(2,1)S(1)} %copy.113) | copy-start | bytes 786436
  12.7 1.3 copy-start.2
  14.0 1.1 copy-start.3
  15.0 1.6 copy-start.5
  18.9 2.5 %copy-start.10 = (bf16[512,256]{0,1:T(8,128)(2,1)S(1)}, bf16[512,256]{0,1:T(8,128)(2,1)}, u32[]{:S(2)}) copy-start(bf16[512,256]{0,1:T(8,128)(2,1)} %copy-done.9) | copy-start | bytes 786436
  19.2 2.2 copy-start.12
  21.4 4.0 %copy-start.8 = (bf16[512,256]{0,1:T(8,128)(2,1)S(1)}, bf16[512,256]{0,1:T(8,128)(2,1)}, u32[]{:S(2)}) copy-start(bf16[512,256]{0,1:T(8,128)(2,1)} %copy-done.7) | copy-start | bytes 786436
  31.1 1.0 copy-start.6
  40.3 34.2 %collective-permute-start = (f32[16,4,1,4,1280]{4,3,2,1,0:T(4,128)}, f32[16,4,1,4,1280]{4,3,2,1,0:T(4,128)}, u32[]{:S(2)}, u32[]{:S(2)}) collective-permute-start(f32[16,4,1,4,1280]{4,3,2,1,0:T(4,128)} %constant_dynamic-slice_fusion.8), channel_id=1, source_target_pairs={{0,4},{4,0},{1,5},{5,1},{2,6},{6,2},{3,7},{7,3},{8,12},{12,8},{9,1... | collective-permute-start | bytes 3932168 | tf_op jit(solution)/shard_map/ppermute | solution.py:84
  44.1 1.8 copy-start.16
  44.1 2.1 copy-start.17
  44.1 2.6 %copy-start.11 = (f32[512,512]{0,1:T(8,128)S(1)}, f32[512,512]{0,1:T(8,128)}, u32[]{:S(2)}) copy-start(f32[512,512]{0,1:T(8,128)} %get-tuple-element.71) | copy-start | bytes 3145732
  54.4 153.3 %all-to-all-start = ((bf16[128,65,128]{2,1,0:T(8,128)(2,1)}), bf16[128,65,128]{2,1,0:T(8,128)(2,1)S(1)}, u32[]{:S(2)}, u32[]{:S(2)}) async-start(bf16[128,65,128]{2,1,0:T(8,128)(2,1)} %fusion.6), calls=%async_computation | async-start | bytes 4718592 | tf_op jit(solution)/shard_map/all_to_all | solution.py:159
  82.8 18.3 %collective-permute-start.1 = (f32[16,4,2,1,1,1280]{5,3,2,1,0,4:T(1,128)S(1)}, f32[16,4,2,1,1,1280]{5,3,2,1,0,4:T(1,128)}, u32[]{:S(2)}, u32[]{:S(2)}) collective-permute-start(f32[16,4,2,1,1,1280]{5,3,2,1,0,4:T(1,128)S(1)} %constant_dynamic-slice_fusion.7), channel_id=1, source_target_pairs={{0,1},{1,0},{2,3},{3,2},{4,5},{5,4},{6,7},{7,6},{8,9},{9,8},{10,11... | collective-permute-start | bytes 1966088 | tf_op jit(solution)/shard_map/ppermute | solution.py:84
  103.5 11.8 %collective-permute-start.2 = (f32[16,4,1,1,1,1280]{5,3,2,1,0,4:T(1,128)S(1)}, f32[16,4,1,1,1,1280]{5,3,2,1,0,4:T(1,128)}, u32[]{:S(2)}, u32[]{:S(2)}) collective-permute-start(f32[16,4,1,1,1,1280]{5,3,2,1,0,4:T(1,128)S(1)} %constant_dynamic-slice_fusion.6), channel_id=1, source_target_pairs={{0,2},{1,3},{2,0},{3,1},{4,6},{5,7},{6,4},{7,5},{8,10},{9,11},{10,... | collective-permute-start | bytes 983048 | tf_op jit(solution)/shard_map/ppermute | solution.py:84
  116.7 8.1 %collective-permute-start.3 = (f32[16,2,1,1,1280]{4,3,2,1,0:T(1,128)S(1)}, f32[16,2,1,1,1280]{4,3,2,1,0:T(1,128)S(1)}, u32[]{:S(2)}, u32[]{:S(2)}) collective-permute-start(f32[16,2,1,1,1280]{4,3,2,1,0:T(1,128)S(1)} %constant_dynamic-slice_fusion.5), channel_id=1, source_target_pairs={{0,8},{8,0},{16,24},{24,16},{1,9},{9,1},{17,25},{25,17},{2,10},{10... | collective-permute-start | bytes 491528 | tf_op jit(solution)/shard_map/ppermute | solution.py:84
  125.1 8.3 %collective-permute-start.4 = (f32[16,1,1,1,1280]{4,3,2,1,0:T(1,128)S(1)}, f32[16,1,1,1,1280]{4,3,2,1,0:T(1,128)S(1)}, u32[]{:S(2)}, u32[]{:S(2)}) collective-permute-start(f32[16,1,1,1,1280]{4,3,2,1,0:T(1,128)S(1)} %constant_dynamic-slice_fusion.4), channel_id=1, source_target_pairs={{0,16},{8,24},{16,0},{24,8},{1,17},{9,25},{17,1},{25,9},{2,18},{10... | collective-permute-start | bytes 245768 | tf_op jit(solution)/shard_map/ppermute | solution.py:84
  133.5 43.3 %collective-permute-start.5 = (f32[2,2,2,1,1,1280]{5,4,3,2,1,0:T(1,128)S(1)}, f32[2,2,2,1,1,1280]{5,4,3,2,1,0:T(1,128)S(1)}, u32[]{:S(2)}, u32[]{:S(2)}) collective-permute-start(f32[2,2,2,1,1,1280]{5,4,3,2,1,0:T(1,128)S(1)} %constant_dynamic-slice_fusion.3), channel_id=1, source_target_pairs={{0,32},{32,0},{64,96},{96,64},{128,160},{160,128},{192,224},{224,1... | collective-permute-start | bytes 122888 | tf_op jit(solution)/shard_map/ppermute | solution.py:84
  176.9 6.6 %collective-permute-start.6 = (f32[2,2,1,1,1,1280]{5,4,3,2,1,0:T(1,128)S(1)}, f32[2,2,1,1,1,1280]{5,4,3,2,1,0:T(1,128)S(1)}, u32[]{:S(2)}, u32[]{:S(2)}) collective-permute-start(f32[2,2,1,1,1,1280]{5,4,3,2,1,0:T(1,128)S(1)} %constant_dynamic-slice_fusion.2), channel_id=1, source_target_pairs={{0,64},{32,96},{64,0},{96,32},{128,192},{160,224},{192,128},{224,1... | collective-permute-start | bytes 61448 | tf_op jit(solution)/shard_map/ppermute | solution.py:84
  183.6 9.5 %collective-permute-start.7 = (f32[2,1,1,1,1,1280]{5,4,3,2,1,0:T(1,128)S(1)}, f32[2,1,1,1,1,1280]{5,4,3,2,1,0:T(1,128)S(1)}, u32[]{:S(2)}, u32[]{:S(2)}) collective-permute-start(f32[2,1,1,1,1,1280]{5,4,3,2,1,0:T(1,128)S(1)} %constant_dynamic-slice_fusion.1), channel_id=1, source_target_pairs={{0,128},{32,160},{64,192},{96,224},{128,0},{160,32},{192,64},{224,... | collective-permute-start | bytes 30728 | tf_op jit(solution)/shard_map/ppermute | solution.py:84
  193.1 14.2 %collective-permute-start.8 = (f32[1,1,1,1,1,1280]{5,4,3,2,1,0:T(1,128)S(1)}, f32[1,1,1,1,1,1280]{5,4,3,2,1,0:T(1,128)S(1)}, u32[]{:S(2)}, u32[]{:S(2)}) collective-permute-start(f32[1,1,1,1,1,1280]{5,4,3,2,1,0:T(1,128)S(1)} %constant_dynamic-slice_fusion), channel_id=1, source_target_pairs={{0,256},{32,288},{64,320},{96,352},{128,384},{160,416},{192,448},{... | collective-permute-start | bytes 15368 | tf_op jit(solution)/shard_map/ppermute | solution.py:84
  212.6 13.1 %copy-start.14 = (f32[128,512]{1,0:T(8,128)S(1)}, f32[128,512]{1,0:T(8,128)}, u32[]{:S(2)}) copy-start(f32[128,512]{1,0:T(8,128)} %param.20) | copy-start | bytes 786436
  212.6 13.3 %copy-start.15 = (f32[128,512]{1,0:T(8,128)S(1)}, f32[128,512]{1,0:T(8,128)}, u32[]{:S(2)}) copy-start(f32[128,512]{1,0:T(8,128)} %param.19) | copy-start | bytes 786436
  212.6 9.4 %collective-permute-start.9 = (f32[136,640]{1,0:T(8,128)S(1)}, f32[136,640]{1,0:T(8,128)S(1)}, u32[]{:S(2)}, u32[]{:S(2)}) collective-permute-start(f32[136,640]{1,0:T(8,128)S(1)} %copy.131), channel_id=1, source_target_pairs={{0,1},{1,0},{2,3},{3,2},{4,5},{5,4},{6,7},{7,6},{8,9},{9,8},{10,11... | collective-permute-start | bytes 1044488 | tf_op jit(solution)/shard_map/ppermute | solution.py:90
  222.5 10.7 %collective-permute-start.10 = (f32[136,640]{1,0:T(8,128)S(1)}, f32[136,640]{1,0:T(8,128)S(1)}, u32[]{:S(2)}, u32[]{:S(2)}) collective-permute-start(f32[136,640]{1,0:T(8,128)S(1)} %copy.133), channel_id=1, source_target_pairs={{0,2},{1,3},{2,0},{3,1},{4,6},{5,7},{6,4},{7,5},{8,10},{9,11},{10,... | collective-permute-start | bytes 1044488 | tf_op jit(solution)/shard_map/ppermute | solution.py:90
  226.0 9.0 %copy-start.18 = (f32[128]{0:T(128)S(1)}, f32[128]{0:T(128)}, u32[]{:S(2)}) copy-start(f32[128]{0:T(128)} %param.21) | copy-start | bytes 1540
  233.4 3.9 %copy-start.1 = (bf16[512,1024]{1,0:T(8,128)(2,1)S(1)}, bf16[512,1024]{1,0:T(8,128)(2,1)}, u32[]{:S(2)}) copy-start(bf16[512,1024]{1,0:T(8,128)(2,1)} %param.17) | copy-start | bytes 3145732

commit v13 on v12

--- a/solution.py
+++ b/solution.py
@@ -181,22 +181,20 @@
         axis=1,
     )
     count_part = jnp.sum(matches.astype(jnp.float32), axis=1)
-    lanes = width + 128
+    weight_rows = weight_share.size // width
+    count_rows = slot_count // width + 1
+    counts = jnp.zeros((count_rows * width,), jnp.float32).at[:slot_count].set(count_part)
     both = double_sum(
         jnp.concatenate(
-            [
-                jnp.concatenate(
-                    [grad_part, jnp.broadcast_to(count_part[:, None], (slot_count, 128))], axis=1
-                ),
-                weight_share.reshape(-1, lanes),
-            ],
+            [grad_part, weight_share.reshape(weight_rows, width), counts.reshape(count_rows, width)],
             axis=0,
         ),
         "x",
         sizes["x"],
     )
-    grad_all, count_all = both[:slot_count, :width], both[:slot_count, width]
-    weight_share = both[slot_count:].reshape(weight_share.shape)
+    grad_all = both[:slot_count]
+    weight_share = both[slot_count : slot_count + weight_rows].reshape(weight_share.shape)
+    count_all = both[slot_count + weight_rows :].reshape(-1)[:slot_count]
     w_in_grad = weight_share[:, :in_cols]
     w_out_grad = weight_share[:, in_cols:]
     new_rows, new_mom, new_var = row_adam(emb_rows, emb_mom, emb_var, grad_all, count_all)

time: 238 us -> 246 us (1.034)
  local copies, waits for them, and re-layouts: 29.4 us -> 33.8 us
  other arithmetic: 21 us -> 23.9 us
    ppermute x9, waiting for transfers between devices: 77.5 us -> 71 us  [halve_sum(): blocks = keep + lax.ppermute(send, axis, pairs)]
    ppermute x2, waiting for transfers between devices: 13.6 us -> 19.3 us  [double_sum(): lax.ppermute(value, axis, [(i, i ^ 1 << bit) for i in range(size)])]
    unnamed x44 -> x48, local copies, waits for them, and re-layouts: 5.05 us -> 8.03 us
    add x8, other arithmetic: 7.24 us -> 10 us  [halve_sum(): blocks = keep + lax.ppermute(send, axis, pairs)]
  transfers between devices with their start and end apart: 12 -> 12, of which waited for: 10 -> 10; matrix products, arithmetic and copies ran while one was open for 11% -> 13% of each run, Pallas kernels for 0% -> 0%
where the time goes in v13:
time: 246 us; the launch traced here: 245 us
  waiting for transfers between devices  90.3 us (37%)
  starting transfers between devices  70.8 us (29%)
  local copies, waits for them, and re-layouts  33.8 us (14%)
  matrix products  24.5 us (10%)
  other arithmetic  23.9 us (10%)
    ppermute x9, waiting for transfers between devices, halve_sum(): blocks = keep + lax.ppermute(send, axis, pairs)  71 us
    ppermute x9, starting transfers between devices, halve_sum(): blocks = keep + lax.ppermute(send, axis, pairs)  45.1 us
    all_to_all x1, starting transfers between devices, local(): lax.all_to_all(jnp.concatenate([outgoing.reshape(owner_count, block_rows,...  20.1 us
    ppermute x2, waiting for transfers between devices, double_sum(): lax.ppermute(value, axis, [(i, i ^ 1 << bit) for i in range(size)])  19.3 us
    add x8, other arithmetic, halve_sum(): blocks = keep + lax.ppermute(send, axis, pairs)  10 us
    unnamed x48, local copies, waits for them, and re-layouts  8.03 us
    dot_general x3, matrix products, core(): jnp.einsum('hts,shd->thd', weights, values_part, preferred_element_type=j...  6.92 us
    dynamic_slice x9, local copies, waits for them, and re-layouts, halve_sum(): send = lax.dynamic_index_in_dim(blocks, 1 - mine, at, keepdims=True)  6.86 us
  transfers between devices with their start and end apart: 12, of which 10 were waited for; matrix products, arithmetic and copies ran while one was open for 13% of the time, Pallas kernels for 0%

profile of v13, /device:TPU:6, one launch (start us, length us, event | category | flops | bytes accessed | tf_op | source)
XLA Modules:
  0.0 244.7 jit_solution(15043741516351542374)
XLA Ops:
  0.7 0.9 reduce-window.8
  1.9 1.3 fusion.25
  3.7 2.3 multiply_convert_fusion.1
  6.0 1.0 copy-done.4
  6.9 0.8 fusion.51
  8.0 1.2 copy.113
  9.2 3.5 %multiply_convert_fusion = (bf16[4,512,512]{2,1,0:T(8,128)(2,1)S(1)}, f32[4,512,512]{2,1,0:T(8,128)}) fusion(f32[512,512]{1,0:T(8,128)S(1)} %fusion.26, bf16[512,4,64]{0,2,1:T(8,128)(2,1)S(1)} %bitcast.65, bf16[512,4,64]{0,2,1:T(8,128)(2,1)S(1)} %bitcast.67), kind=kOutput, calls=%fused_computation.7 | convolution fusion | flops 142606336 | bytes 7864320 | tf_op jit(solution)/shard_map/jvp(thd,shd->hts)/dot_general | solution.py:46
  12.7 1.3 copy-done.1
  14.0 0.8 fusion.52
  15.1 1.5 multiply_reduce_fusion
  16.6 1.3 convolution_bitcast_fusion
  18.0 1.0 fusion.49
  19.2 2.1 fusion.55
  21.4 4.0 %fusion.3 = bf16[4,512,512]{2,1,0:T(8,128)(2,1)S(1)} fusion(f32[4,512,512]{2,1,0:T(8,128)} %get-tuple-element.77, f32[512,512]{1,0:T(8,128)S(1)} %copy-done.13, bf16[4,64,512]{2,1,0:T(8,128)(2,1)S(1)} %bitcast.73, bf16[512,4,64]{0,2,1:T(8,128)(2,1)S(1)} %bitcast.70), kind=kOutput, calls=%fused_computation.5 | convolution fusion | flops 148897792 | bytes 7864320 | tf_op jit(solution)/shard_map/transpose(jvp(hts,shd->thd))/dot_general | solution.py:50
  25.5 0.8 fusion.54
  26.8 0.8 copy.120
  27.7 0.8 copy.121
  28.5 2.6 %fusion.8 = bf16[512,1024]{1,0:T(8,128)(2,1)S(1)} fusion(f32[512,1024]{1,0:T(8,128)} %get-tuple-element.75, bf16[512,256]{1,0:T(8,128)(2,1)} %copy.121, bf16[512,256]{1,0:T(8,128)(2,1)} %copy.120, bf16[512,256]{1,0:T(8,128)(2,1)S(1)} %copy.119, bf16[512,256]{1,0:T(8,128)(2,1)} %get-tuple-element.64), kind=kLoop, calls=%fused_computation.18 | loop fusion | flops 9437184 | bytes 4194304 | tf_op jit(solution)/shard_map/convert_element_type | solution.py:117
  31.1 0.7 fusion.36
  32.1 1.7 pad_maximum_fusion
  33.9 3.9 %reshape.282 = f32[16,4,2,4,1280]{4,3,2,1,0:T(4,128)} reshape(f32[512,1280]{1,0:T(8,128)} %pad_maximum_fusion) | data formatting | bytes 5242880 | tf_op jit(solution)/shard_map/reshape | solution.py:98
  37.8 2.5 %constant_dynamic-slice_fusion.8 = f32[16,4,1,4,1280]{4,3,2,1,0:T(4,128)} fusion(f32[16,4,2,4,1280]{4,3,2,1,0:T(4,128)} %reshape.282, s32[]{:T(128)S(6)} %select_n.83), kind=kLoop, calls=%fused_computation.103 | loop fusion | bytes 2621444 | tf_op jit(solution)/shard_map/jit(dynamic_index_in_dim)/dynamic_slice | solution.py:82
  40.3 2.1 collective-permute-start
  42.4 1.7 fusion.18
  44.1 1.0 copy.122
  45.1 1.5 fusion.35
  47.4 3.8 %fusion.5 = bf16[2048,512]{1,0:T(8,128)(2,1)} fusion(s32[512]{0:T(512)S(1)} %get-tuple-element.84, bf16[512,512]{0,1:T(8,128)(2,1)} %copy.122, f32[512]{0:T(512)S(1)} %negate_multiply_fusion, bf16[512,512]{0,1:T(8,128)(2,1)S(1)} %copy.112, f32[512,512]{0,1:T(8,128)S(1)} %copy-done.12, f32[512]{0:T(512)S(1)} %multiply_multiply_fusion, f32[512]{0:T(512)S(1)} %fusion.46, ...), kind=kOutput, calls=%fused_computation.12 | convolution fusion | flops 1078460416 | bytes 4204544 | tf_op jit(solution)/shard_map/dot_general | solution.py:149
  51.2 3.1 %reshape_reshape.9 = bf16[128,64,128]{2,1,0:T(8,128)(2,1)S(1)} reshape(bf16[2048,512]{1,0:T(8,128)(2,1)} %fusion.5) | data formatting | bytes 4194304 | tf_op jit(solution)/shard_map/reshape;reshape | solution.py:160
  54.4 1.7 fusion.6
  56.1 20.1 %all-to-all-start = ((bf16[128,65,128]{2,1,0:T(8,128)(2,1)}), bf16[128,65,128]{2,1,0:T(8,128)(2,1)S(1)}, u32[]{:S(2)}, u32[]{:S(2)}) async-start(bf16[128,65,128]{2,1,0:T(8,128)(2,1)} %fusion.6), calls=%async_computation | async-start | bytes 4718592 | tf_op jit(solution)/shard_map/all_to_all | solution.py:159
  76.2 3.1 %dynamic-slice_add_fusion = f32[16,4,1,4,1280]{4,3,2,1,0:T(4,128)} fusion(f32[16,4,1,4,1280]{4,3,2,1,0:T(4,128)} %collective-permute-done, f32[16,4,2,4,1280]{4,3,2,1,0:T(4,128)} %reshape.282, s32[]{:T(128)S(6)} %select_n.82), kind=kLoop, calls=%fused_computation.30 | loop fusion | flops 327680 | bytes 3932164 | tf_op jit(solution)/shard_map/add | solution.py:84
  79.4 3.1 %reshape_reshape_reshape.3 = f32[16,4,2,2,1,1280]{5,3,2,1,0,4:T(2,128)} reshape(f32[16,4,1,4,1280]{4,3,2,1,0:T(4,128)} %dynamic-slice_add_fusion) | data formatting | bytes 2621440 | tf_op jit(solution)/shard_map/reshape;reshape;reshape | solution.py:77
  82.5 2.8 %constant_dynamic-slice_fusion.7 = f32[16,4,2,1,1,1280]{5,3,2,1,0,4:T(1,128)} fusion(f32[16,4,2,2,1,1280]{5,3,2,1,0,4:T(2,128)} %reshape_reshape_reshape.3, s32[]{:T(128)S(6)} %select_n.85), kind=kLoop, calls=%fused_computation.102 | loop fusion | bytes 1310724 | tf_op jit(solution)/shard_map/jit(dynamic_index_in_dim)/dynamic_slice | solution.py:82
  85.3 2.7 %collective-permute-start.1 = (f32[16,4,2,1,1,1280]{5,3,2,1,0,4:T(1,128)}, f32[16,4,2,1,1,1280]{5,3,2,1,0,4:T(1,128)}, u32[]{:S(2)}, u32[]{:S(2)}) collective-permute-start(f32[16,4,2,1,1,1280]{5,3,2,1,0,4:T(1,128)} %constant_dynamic-slice_fusion.7), channel_id=1, source_target_pairs={{0,1},{1,0},{2,3},{3,2},{4,5},{5,4},{6,7},{7,6},{8,9},{9,8},{10,11... | collective-permute-start | bytes 1966088 | tf_op jit(solution)/shard_map/ppermute | solution.py:84
  88.0 15.7 %collective-permute-done.1 = f32[16,4,2,1,1,1280]{5,3,2,1,0,4:T(1,128)} collective-permute-done((f32[16,4,2,1,1,1280]{5,3,2,1,0,4:T(1,128)}, f32[16,4,2,1,1,1280]{5,3,2,1,0,4:T(1,128)}, u32[]{:S(2)}, u32[]{:S(2)}) %collective-permute-start.1) | collective-permute-done | bytes 655392 | tf_op jit(solution)/shard_map/ppermute | solution.py:84
  103.8 2.4 dynamic-slice_add_fusion.1
  106.2 0.8 copy-done.3
  107.0 0.8 constant_dynamic-slice_fusion.6
  107.8 3.3 %collective-permute-start.2 = (f32[16,4,1,1,1,1280]{5,3,2,1,0,4:T(1,128)}, f32[16,4,1,1,1,1280]{5,3,2,1,0,4:T(1,128)}, u32[]{:S(2)}, u32[]{:S(2)}) collective-permute-start(f32[16,4,1,1,1,1280]{5,3,2,1,0,4:T(1,128)} %constant_dynamic-slice_fusion.6), channel_id=1, source_target_pairs={{0,2},{1,3},{2,0},{3,1},{4,6},{5,7},{6,4},{7,5},{8,10},{9,11},{10,... | collective-permute-start | bytes 983048 | tf_op jit(solution)/shard_map/ppermute | solution.py:84
  111.1 8.7 %collective-permute-done.2 = f32[16,4,1,1,1,1280]{5,3,2,1,0,4:T(1,128)} collective-permute-done((f32[16,4,1,1,1,1280]{5,3,2,1,0,4:T(1,128)}, f32[16,4,1,1,1,1280]{5,3,2,1,0,4:T(1,128)}, u32[]{:S(2)}, u32[]{:S(2)}) %collective-permute-start.2) | collective-permute-done | bytes 327712 | tf_op jit(solution)/shard_map/ppermute | solution.py:84
  119.8 1.4 dynamic-slice_add_fusion.2
  121.3 0.7 copy-done.7
  122.0 0.7 constant_dynamic-slice_fusion.5
  122.6 4.2 %collective-permute-start.3 = (f32[16,2,1,1,1280]{4,3,2,1,0:T(1,128)}, f32[16,2,1,1,1280]{4,3,2,1,0:T(1,128)}, u32[]{:S(2)}, u32[]{:S(2)}) collective-permute-start(f32[16,2,1,1,1280]{4,3,2,1,0:T(1,128)} %constant_dynamic-slice_fusion.5), channel_id=1, source_target_pairs={{0,8},{8,0},{16,24},{24,16},{1,9},{9,1},{17,25},{25,17},{2,10},{10... | collective-permute-start | bytes 491528 | tf_op jit(solution)/shard_map/ppermute | solution.py:84
  126.8 4.0 %collective-permute-done.3 = f32[16,2,1,1,1280]{4,3,2,1,0:T(1,128)} collective-permute-done((f32[16,2,1,1,1280]{4,3,2,1,0:T(1,128)}, f32[16,2,1,1,1280]{4,3,2,1,0:T(1,128)}, u32[]{:S(2)}, u32[]{:S(2)}) %collective-permute-start.3) | collective-permute-done | bytes 163872 | tf_op jit(solution)/shard_map/ppermute | solution.py:84
  130.8 1.2 dynamic-slice_add_fusion.3
  132.6 5.4 %collective-permute-start.4 = (f32[16,1,1,1,1280]{4,3,2,1,0:T(1,128)S(1)}, f32[16,1,1,1,1280]{4,3,2,1,0:T(1,128)}, u32[]{:S(2)}, u32[]{:S(2)}) collective-permute-start(f32[16,1,1,1,1280]{4,3,2,1,0:T(1,128)S(1)} %constant_dynamic-slice_fusion.4), channel_id=1, source_target_pairs={{0,16},{8,24},{16,0},{24,8},{1,17},{9,25},{17,1},{25,9},{2,18},{10... | collective-permute-start | bytes 245768 | tf_op jit(solution)/shard_map/ppermute | solution.py:84
  138.1 2.6 %collective-permute-done.4 = f32[16,1,1,1,1280]{4,3,2,1,0:T(1,128)} collective-permute-done((f32[16,1,1,1,1280]{4,3,2,1,0:T(1,128)S(1)}, f32[16,1,1,1,1280]{4,3,2,1,0:T(1,128)}, u32[]{:S(2)}, u32[]{:S(2)}) %collective-permute-start.4) | collective-permute-done | bytes 81952 | tf_op jit(solution)/shard_map/ppermute | solution.py:84
  140.7 1.0 dynamic-slice_add_fusion.4
  141.7 4.4 %collective-permute-start.5 = (f32[2,2,2,1,1,1280]{5,4,3,2,1,0:T(1,128)S(1)}, f32[2,2,2,1,1,1280]{5,4,3,2,1,0:T(1,128)}, u32[]{:S(2)}, u32[]{:S(2)}) collective-permute-start(f32[2,2,2,1,1,1280]{5,4,3,2,1,0:T(1,128)S(1)} %constant_dynamic-slice_fusion.3), channel_id=1, source_target_pairs={{0,32},{32,0},{64,96},{96,64},{128,160},{160,128},{192,224},{224,1... | collective-permute-start | bytes 122888 | tf_op jit(solution)/shard_map/ppermute | solution.py:84
  146.2 32.5 %collective-permute-done.5 = f32[2,2,2,1,1,1280]{5,4,3,2,1,0:T(1,128)} collective-permute-done((f32[2,2,2,1,1,1280]{5,4,3,2,1,0:T(1,128)S(1)}, f32[2,2,2,1,1,1280]{5,4,3,2,1,0:T(1,128)}, u32[]{:S(2)}, u32[]{:S(2)}) %collective-permute-start.5) | collective-permute-done | bytes 40992 | tf_op jit(solution)/shard_map/ppermute | solution.py:84
  178.7 0.8 dynamic-slice_add_fusion.5
  179.5 3.9 %collective-permute-start.6 = (f32[2,2,1,1,1,1280]{5,4,3,2,1,0:T(1,128)S(1)}, f32[2,2,1,1,1,1280]{5,4,3,2,1,0:T(1,128)S(1)}, u32[]{:S(2)}, u32[]{:S(2)}) collective-permute-start(f32[2,2,1,1,1,1280]{5,4,3,2,1,0:T(1,128)S(1)} %constant_dynamic-slice_fusion.2), channel_id=1, source_target_pairs={{0,64},{32,96},{64,0},{96,32},{128,192},{160,224},{192,128},{224,1... | collective-permute-start | bytes 61448 | tf_op jit(solution)/shard_map/ppermute | solution.py:84
  183.5 2.8 %collective-permute-done.6 = f32[2,2,1,1,1,1280]{5,4,3,2,1,0:T(1,128)S(1)} collective-permute-done((f32[2,2,1,1,1,1280]{5,4,3,2,1,0:T(1,128)S(1)}, f32[2,2,1,1,1,1280]{5,4,3,2,1,0:T(1,128)S(1)}, u32[]{:S(2)}, u32[]{:S(2)}) %collective-permute-start.6) | collective-permute-done | bytes 20512 | tf_op jit(solution)/shard_map/ppermute | solution.py:84
  186.3 6.5 %collective-permute-start.7 = (f32[2,1,1,1,1,1280]{5,4,3,2,1,0:T(1,128)S(1)}, f32[2,1,1,1,1,1280]{5,4,3,2,1,0:T(1,128)S(1)}, u32[]{:S(2)}, u32[]{:S(2)}) collective-permute-start(f32[2,1,1,1,1,1280]{5,4,3,2,1,0:T(1,128)S(1)} %constant_dynamic-slice_fusion.1), channel_id=1, source_target_pairs={{0,128},{32,160},{64,192},{96,224},{128,0},{160,32},{192,64},{224,... | collective-permute-start | bytes 30728 | tf_op jit(solution)/shard_map/ppermute | solution.py:84
  192.9 2.9 %collective-permute-done.7 = f32[2,1,1,1,1,1280]{5,4,3,2,1,0:T(1,128)S(1)} collective-permute-done((f32[2,1,1,1,1,1280]{5,4,3,2,1,0:T(1,128)S(1)}, f32[2,1,1,1,1,1280]{5,4,3,2,1,0:T(1,128)S(1)}, u32[]{:S(2)}, u32[]{:S(2)}) %collective-permute-start.7) | collective-permute-done | bytes 10272 | tf_op jit(solution)/shard_map/ppermute | solution.py:84
  195.8 12.5 %collective-permute-start.8 = (f32[1,1,1,1,1,1280]{5,4,3,2,1,0:T(1,128)S(1)}, f32[1,1,1,1,1,1280]{5,4,3,2,1,0:T(1,128)S(1)}, u32[]{:S(2)}, u32[]{:S(2)}) collective-permute-start(f32[1,1,1,1,1,1280]{5,4,3,2,1,0:T(1,128)S(1)} %constant_dynamic-slice_fusion), channel_id=1, source_target_pairs={{0,256},{32,288},{64,320},{96,352},{128,384},{160,416},{192,448},{... | collective-permute-start | bytes 15368 | tf_op jit(solution)/shard_map/ppermute | solution.py:84
  208.3 1.7 collective-permute-done.8
  215.3 2.7 %collective-permute-start.9 = (f32[139,512]{0,1:T(8,128)S(1)}, f32[139,512]{0,1:T(8,128)S(1)}, u32[]{:S(2)}, u32[]{:S(2)}) collective-permute-start(f32[139,512]{0,1:T(8,128)S(1)} %select_maximum_fusion), channel_id=1, source_target_pairs={{0,1},{1,0},{2,3},{3,2},{4,5},{5,4},{6,7},{7,6},{8,9},{9,8},{10,11... | collective-permute-start | bytes 854024 | tf_op jit(solution)/shard_map/ppermute | solution.py:90
  218.0 10.0 %collective-permute-done.9 = f32[139,512]{0,1:T(8,128)S(1)} collective-permute-done((f32[139,512]{0,1:T(8,128)S(1)}, f32[139,512]{0,1:T(8,128)S(1)}, u32[]{:S(2)}, u32[]{:S(2)}) %collective-permute-start.9) | collective-permute-done | bytes 284704 | tf_op jit(solution)/shard_map/ppermute | solution.py:90
  228.1 3.0 %collective-permute-start.10 = (f32[139,512]{0,1:T(8,128)S(1)}, f32[139,512]{0,1:T(8,128)S(1)}, u32[]{:S(2)}, u32[]{:S(2)}) collective-permute-start(f32[139,512]{0,1:T(8,128)S(1)} %fusion.79), channel_id=1, source_target_pairs={{0,2},{1,3},{2,0},{3,1},{4,6},{5,7},{6,4},{7,5},{8,10},{9,11},{10,... | collective-permute-start | bytes 854024 | tf_op jit(solution)/shard_map/ppermute | solution.py:90
  231.3 9.3 %collective-permute-done.10 = f32[139,512]{0,1:T(8,128)S(1)} collective-permute-done((f32[139,512]{0,1:T(8,128)S(1)}, f32[139,512]{0,1:T(8,128)S(1)}, u32[]{:S(2)}, u32[]{:S(2)}) %collective-permute-start.10) | collective-permute-done | bytes 284704 | tf_op jit(solution)/shard_map/ppermute | solution.py:90
  243.0 0.8 copy.137
  243.8 0.8 copy.138
  (106 shorter events, 12.0 us)
Async XLA Ops:
  0.6 3.0 %copy-start = (bf16[512,1024]{1,0:T(8,128)(2,1)S(1)}, bf16[512,1024]{1,0:T(8,128)(2,1)}, u32[]{:S(2)}) copy-start(bf16[512,1024]{1,0:T(8,128)(2,1)} %param.19) | copy-start | bytes 3145732
  0.6 2.5 %copy-start.15 = (bf16[512,512]{1,0:T(8,128)(2,1)S(1)}, bf16[512,512]{1,0:T(8,128)(2,1)}, u32[]{:S(2)}) copy-start(bf16[512,512]{1,0:T(8,128)(2,1)} %param.14) | copy-start | bytes 1572868
  6.0 1.0 copy-start.4
  8.0 4.7 %copy-start.8 = (bf16[512,256]{0,1:T(8,128)(2,1)}, bf16[512,256]{0,1:T(8,128)(2,1)S(1)}, u32[]{:S(2)}) copy-start(bf16[512,256]{0,1:T(8,128)(2,1)S(1)} %copy.115) | copy-start | bytes 786436
  9.2 3.5 %copy-start.10 = (bf16[512,256]{0,1:T(8,128)(2,1)}, bf16[512,256]{0,1:T(8,128)(2,1)S(1)}, u32[]{:S(2)}) copy-start(bf16[512,256]{0,1:T(8,128)(2,1)S(1)} %copy.113) | copy-start | bytes 786436
  12.7 1.3 copy-start.1
  14.0 1.1 copy-start.2
  15.0 1.6 copy-start.5
  18.9 2.5 %copy-start.11 = (bf16[512,256]{0,1:T(8,128)(2,1)S(1)}, bf16[512,256]{0,1:T(8,128)(2,1)}, u32[]{:S(2)}) copy-start(bf16[512,256]{0,1:T(8,128)(2,1)} %copy-done.10) | copy-start | bytes 786436
  19.2 2.2 copy-start.13
  21.4 4.0 %copy-start.9 = (bf16[512,256]{0,1:T(8,128)(2,1)S(1)}, bf16[512,256]{0,1:T(8,128)(2,1)}, u32[]{:S(2)}) copy-start(bf16[512,256]{0,1:T(8,128)(2,1)} %copy-done.8) | copy-start | bytes 786436
  31.1 1.0 copy-start.6
  40.3 35.9 %collective-permute-start = (f32[16,4,1,4,1280]{4,3,2,1,0:T(4,128)}, f32[16,4,1,4,1280]{4,3,2,1,0:T(4,128)}, u32[]{:S(2)}, u32[]{:S(2)}) collective-permute-start(f32[16,4,1,4,1280]{4,3,2,1,0:T(4,128)} %constant_dynamic-slice_fusion.8), channel_id=1, source_target_pairs={{0,4},{4,0},{1,5},{5,1},{2,6},{6,2},{3,7},{7,3},{8,12},{12,8},{9,1... | collective-permute-start | bytes 3932168 | tf_op jit(solution)/shard_map/ppermute | solution.py:84
  44.1 2.5 %copy-start.18 = (s32[512,1]{0,1:T(1,128)S(1)}, s32[512,1]{0,1:T(1,128)}, u32[]{:S(2)}) copy-start(s32[512,1]{0,1:T(1,128)} %param.17) | copy-start | bytes 6148
  44.1 2.8 %copy-start.19 = (s32[512]{0:T(512)S(1)}, s32[512]{0:T(512)}, u32[]{:S(2)}) copy-start(s32[512]{0:T(512)} %param.18) | copy-start | bytes 6148
  44.1 3.3 %copy-start.12 = (f32[512,512]{0,1:T(8,128)S(1)}, f32[512,512]{0,1:T(8,128)}, u32[]{:S(2)}) copy-start(f32[512,512]{0,1:T(8,128)} %get-tuple-element.83) | copy-start | bytes 3145732
  56.1 154.3 %all-to-all-start = ((bf16[128,65,128]{2,1,0:T(8,128)(2,1)}), bf16[128,65,128]{2,1,0:T(8,128)(2,1)S(1)}, u32[]{:S(2)}, u32[]{:S(2)}) async-start(bf16[128,65,128]{2,1,0:T(8,128)(2,1)} %fusion.6), calls=%async_computation | async-start | bytes 4718592 | tf_op jit(solution)/shard_map/all_to_all | solution.py:159
  85.3 18.5 %collective-permute-start.1 = (f32[16,4,2,1,1,1280]{5,3,2,1,0,4:T(1,128)}, f32[16,4,2,1,1,1280]{5,3,2,1,0,4:T(1,128)}, u32[]{:S(2)}, u32[]{:S(2)}) collective-permute-start(f32[16,4,2,1,1,1280]{5,3,2,1,0,4:T(1,128)} %constant_dynamic-slice_fusion.7), channel_id=1, source_target_pairs={{0,1},{1,0},{2,3},{3,2},{4,5},{5,4},{6,7},{7,6},{8,9},{9,8},{10,11... | collective-permute-start | bytes 1966088 | tf_op jit(solution)/shard_map/ppermute | solution.py:84
  106.2 0.8 copy-start.3
  107.8 12.0 %collective-permute-start.2 = (f32[16,4,1,1,1,1280]{5,3,2,1,0,4:T(1,128)}, f32[16,4,1,1,1,1280]{5,3,2,1,0,4:T(1,128)}, u32[]{:S(2)}, u32[]{:S(2)}) collective-permute-start(f32[16,4,1,1,1,1280]{5,3,2,1,0,4:T(1,128)} %constant_dynamic-slice_fusion.6), channel_id=1, source_target_pairs={{0,2},{1,3},{2,0},{3,1},{4,6},{5,7},{6,4},{7,5},{8,10},{9,11},{10,... | collective-permute-start | bytes 983048 | tf_op jit(solution)/shard_map/ppermute | solution.py:84
  121.2 0.7 copy-start.7
  122.6 8.1 %collective-permute-start.3 = (f32[16,2,1,1,1280]{4,3,2,1,0:T(1,128)}, f32[16,2,1,1,1280]{4,3,2,1,0:T(1,128)}, u32[]{:S(2)}, u32[]{:S(2)}) collective-permute-start(f32[16,2,1,1,1280]{4,3,2,1,0:T(1,128)} %constant_dynamic-slice_fusion.5), channel_id=1, source_target_pairs={{0,8},{8,0},{16,24},{24,16},{1,9},{9,1},{17,25},{25,17},{2,10},{10... | collective-permute-start | bytes 491528 | tf_op jit(solution)/shard_map/ppermute | solution.py:84
  132.0 0.7 copy-start.14
  132.6 8.1 %collective-permute-start.4 = (f32[16,1,1,1,1280]{4,3,2,1,0:T(1,128)S(1)}, f32[16,1,1,1,1280]{4,3,2,1,0:T(1,128)}, u32[]{:S(2)}, u32[]{:S(2)}) collective-permute-start(f32[16,1,1,1,1280]{4,3,2,1,0:T(1,128)S(1)} %constant_dynamic-slice_fusion.4), channel_id=1, source_target_pairs={{0,16},{8,24},{16,0},{24,8},{1,17},{9,25},{17,1},{25,9},{2,18},{10... | collective-permute-start | bytes 245768 | tf_op jit(solution)/shard_map/ppermute | solution.py:84
  141.7 37.0 %collective-permute-start.5 = (f32[2,2,2,1,1,1280]{5,4,3,2,1,0:T(1,128)S(1)}, f32[2,2,2,1,1,1280]{5,4,3,2,1,0:T(1,128)}, u32[]{:S(2)}, u32[]{:S(2)}) collective-permute-start(f32[2,2,2,1,1,1280]{5,4,3,2,1,0:T(1,128)S(1)} %constant_dynamic-slice_fusion.3), channel_id=1, source_target_pairs={{0,32},{32,0},{64,96},{96,64},{128,160},{160,128},{192,224},{224,1... | collective-permute-start | bytes 122888 | tf_op jit(solution)/shard_map/ppermute | solution.py:84
  179.5 6.7 %collective-permute-start.6 = (f32[2,2,1,1,1,1280]{5,4,3,2,1,0:T(1,128)S(1)}, f32[2,2,1,1,1,1280]{5,4,3,2,1,0:T(1,128)S(1)}, u32[]{:S(2)}, u32[]{:S(2)}) collective-permute-start(f32[2,2,1,1,1,1280]{5,4,3,2,1,0:T(1,128)S(1)} %constant_dynamic-slice_fusion.2), channel_id=1, source_target_pairs={{0,64},{32,96},{64,0},{96,32},{128,192},{160,224},{192,128},{224,1... | collective-permute-start | bytes 61448 | tf_op jit(solution)/shard_map/ppermute | solution.py:84
  186.3 9.5 %collective-permute-start.7 = (f32[2,1,1,1,1,1280]{5,4,3,2,1,0:T(1,128)S(1)}, f32[2,1,1,1,1,1280]{5,4,3,2,1,0:T(1,128)S(1)}, u32[]{:S(2)}, u32[]{:S(2)}) collective-permute-start(f32[2,1,1,1,1,1280]{5,4,3,2,1,0:T(1,128)S(1)} %constant_dynamic-slice_fusion.1), channel_id=1, source_target_pairs={{0,128},{32,160},{64,192},{96,224},{128,0},{160,32},{192,64},{224,... | collective-permute-start | bytes 30728 | tf_op jit(solution)/shard_map/ppermute | solution.py:84
  195.8 14.2 %collective-permute-start.8 = (f32[1,1,1,1,1,1280]{5,4,3,2,1,0:T(1,128)S(1)}, f32[1,1,1,1,1,1280]{5,4,3,2,1,0:T(1,128)S(1)}, u32[]{:S(2)}, u32[]{:S(2)}) collective-permute-start(f32[1,1,1,1,1,1280]{5,4,3,2,1,0:T(1,128)S(1)} %constant_dynamic-slice_fusion), channel_id=1, source_target_pairs={{0,256},{32,288},{64,320},{96,352},{128,384},{160,416},{192,448},{... | collective-permute-start | bytes 15368 | tf_op jit(solution)/shard_map/ppermute | solution.py:84
  214.5 16.6 %copy-start.16 = (f32[128,512]{1,0:T(8,128)S(1)}, f32[128,512]{1,0:T(8,128)}, u32[]{:S(2)}) copy-start(f32[128,512]{1,0:T(8,128)} %param.22) | copy-start | bytes 786436
  214.5 16.7 %copy-start.17 = (f32[128,512]{1,0:T(8,128)S(1)}, f32[128,512]{1,0:T(8,128)}, u32[]{:S(2)}) copy-start(f32[128,512]{1,0:T(8,128)} %param.21) | copy-start | bytes 786436
  215.3 12.7 %collective-permute-start.9 = (f32[139,512]{0,1:T(8,128)S(1)}, f32[139,512]{0,1:T(8,128)S(1)}, u32[]{:S(2)}, u32[]{:S(2)}) collective-permute-start(f32[139,512]{0,1:T(8,128)S(1)} %select_maximum_fusion), channel_id=1, source_target_pairs={{0,1},{1,0},{2,3},{3,2},{4,5},{5,4},{6,7},{7,6},{8,9},{9,8},{10,11... | collective-permute-start | bytes 854024 | tf_op jit(solution)/shard_map/ppermute | solution.py:90
  228.1 14.3 %copy-start.20 = (f32[128]{0:T(128)S(1)}, f32[128]{0:T(128)}, u32[]{:S(2)}) copy-start(f32[128]{0:T(128)} %param.23) | copy-start | bytes 1540
  228.1 12.6 %collective-permute-start.10 = (f32[139,512]{0,1:T(8,128)S(1)}, f32[139,512]{0,1:T(8,128)S(1)}, u32[]{:S(2)}, u32[]{:S(2)}) collective-permute-start(f32[139,512]{0,1:T(8,128)S(1)} %fusion.79), channel_id=1, source_target_pairs={{0,2},{1,3},{2,0},{3,1},{4,6},{5,7},{6,4},{7,5},{8,10},{9,11},{10,... | collective-permute-start | bytes 854024 | tf_op jit(solution)/shard_map/ppermute | solution.py:90

commit v14 on v12

--- a/solution.py
+++ b/solution.py
@@ -146,10 +146,19 @@
     )
     position_to = owner_of * capacity + earlier
     chosen = position_to[None, :] == jnp.arange(buffer_rows, dtype=jnp.int32)[:, None]
-    outgoing = jnp.dot(
-        chosen.astype(jnp.bfloat16), emb_grad, preferred_element_type=jnp.float32
-    ).astype(jnp.bfloat16)
-    outgoing = outgoing.reshape(owner_count, capacity, width)
+    outgoing = jnp.stack(
+        [
+            jnp.dot(
+                chosen.astype(jnp.bfloat16),
+                emb_grad[:, j * 128 : (j + 1) * 128],
+                preferred_element_type=jnp.float32,
+            )
+            .astype(jnp.bfloat16)
+            .reshape(owner_count, capacity, 128)
+            for j in range(width // 128)
+        ],
+        axis=2,
+    )
     out_slots = (jnp.sum(jnp.where(chosen, slots[None, :] + 1, 0), axis=1) - 1).reshape(
         owner_count, capacity
     )

time: 238 us -> 236 us (level)
    concatenate x0 -> x1, local copies, waits for them, and re-layouts: none -> 2.82 us  [local(): jnp.concatenate([outgoing.reshape(owner_count, block_rows, 128), slot_row...]
    another operation x1 -> x4, local copies, waits for them, and re-layouts: 3.1 us -> 0.55 us  [local(): jnp.stack([jnp.dot(chosen.astype(jnp.bfloat16), emb_grad[:, j * 128:(j +...]
    unnamed x44 -> x46, local copies, waits for them, and re-layouts: 5.05 us -> 5.58 us
  transfers between devices with their start and end apart: 12 -> 12, of which waited for: 10 -> 10; matrix products, arithmetic and copies ran while one was open for 11% -> 10% of each run, Pallas kernels for 0% -> 0%
where the time goes in v14:
time: 236 us; the launch traced here: 235 us
  waiting for transfers between devices  90.9 us (39%)
  starting transfers between devices  71.2 us (30%)
  local copies, waits for them, and re-layouts  30.1 us (13%)
  matrix products  23 us (10%)
  other arithmetic  18.8 us (8%)
    ppermute x9, waiting for transfers between devices, halve_sum(): blocks = keep + lax.ppermute(send, axis, pairs)  77.3 us
    ppermute x9, starting transfers between devices, halve_sum(): blocks = keep + lax.ppermute(send, axis, pairs)  45 us
    all_to_all x1, starting transfers between devices, local(): lax.all_to_all(jnp.concatenate([outgoing.reshape(owner_count, block_rows,...  20.1 us
    ppermute x2, waiting for transfers between devices, double_sum(): lax.ppermute(value, axis, [(i, i ^ 1 << bit) for i in range(size)])  13.6 us
    add x8, other arithmetic, halve_sum(): blocks = keep + lax.ppermute(send, axis, pairs)  7.24 us
    dot_general x3, matrix products, core(): jnp.einsum('hts,shd->thd', weights, values_part, preferred_element_type=j...  6.92 us
    ppermute x2, starting transfers between devices, double_sum(): lax.ppermute(value, axis, [(i, i ^ 1 << bit) for i in range(size)])  6.13 us
    unnamed x46, local copies, waits for them, and re-layouts  5.58 us
  transfers between devices with their start and end apart: 12, of which 10 were waited for; matrix products, arithmetic and copies ran while one was open for 10% of the time, Pallas kernels for 0%

profile of v14, /device:TPU:6, one launch (start us, length us, event | category | flops | bytes accessed | tf_op | source)
XLA Modules:
  0.0 235.3 jit_solution(12850430598038752004)
XLA Ops:
  0.7 0.9 reduce-window.8
  1.9 1.3 fusion.30
  3.7 2.3 multiply_convert_fusion.1
  6.0 1.0 copy-done.6
  6.9 0.8 fusion.59
  8.0 1.2 copy.128
  9.2 3.5 %multiply_convert_fusion = (bf16[4,512,512]{2,1,0:T(8,128)(2,1)S(1)}, f32[4,512,512]{2,1,0:T(8,128)}) fusion(f32[512,512]{1,0:T(8,128)S(1)} %fusion.31, bf16[512,4,64]{0,2,1:T(8,128)(2,1)S(1)} %bitcast.74, bf16[512,4,64]{0,2,1:T(8,128)(2,1)S(1)} %bitcast.76), kind=kOutput, calls=%fused_computation.7 | convolution fusion | flops 142606336 | bytes 7864320 | tf_op jit(solution)/shard_map/jvp(thd,shd->hts)/dot_general | solution.py:46
  12.7 1.3 copy-done.2
  14.0 0.8 fusion.60
  15.1 1.5 multiply_reduce_fusion
  16.6 1.3 convolution_bitcast_fusion
  18.0 1.0 fusion.57
  19.3 2.1 fusion.63
  21.4 4.0 %fusion.3 = bf16[4,512,512]{2,1,0:T(8,128)(2,1)S(1)} fusion(f32[4,512,512]{2,1,0:T(8,128)} %get-tuple-element.65, f32[512,512]{1,0:T(8,128)S(1)} %copy-done.13, bf16[4,64,512]{2,1,0:T(8,128)(2,1)S(1)} %bitcast.82, bf16[512,4,64]{0,2,1:T(8,128)(2,1)S(1)} %bitcast.79), kind=kOutput, calls=%fused_computation.5 | convolution fusion | flops 148897792 | bytes 7864320 | tf_op jit(solution)/shard_map/transpose(jvp(hts,shd->thd))/dot_general | solution.py:50
  25.5 0.8 fusion.62
  26.2 0.5 fusion.61
  26.8 0.9 copy.135
  27.7 0.8 copy.136
  28.5 2.6 %fusion.14 = bf16[512,1024]{1,0:T(8,128)(2,1)S(1)} fusion(f32[512,1024]{1,0:T(8,128)} %get-tuple-element.63, bf16[512,256]{1,0:T(8,128)(2,1)} %copy.136, bf16[512,256]{1,0:T(8,128)(2,1)} %copy.135, bf16[512,256]{1,0:T(8,128)(2,1)S(1)} %copy.134, bf16[512,256]{1,0:T(8,128)(2,1)} %get-tuple-element.52), kind=kLoop, calls=%fused_computation.24 | loop fusion | flops 9437184 | bytes 4194304 | tf_op jit(solution)/shard_map/convert_element_type | solution.py:117
  31.1 0.7 fusion.40
  31.9 0.7 copy-done.8
  32.6 1.7 pad_maximum_fusion
  34.3 3.9 %reshape.254 = f32[16,4,2,4,1280]{4,3,2,1,0:T(4,128)} reshape(f32[512,1280]{1,0:T(8,128)} %pad_maximum_fusion) | data formatting | bytes 5242880 | tf_op jit(solution)/shard_map/reshape | solution.py:98
  38.2 2.6 %constant_dynamic-slice_fusion.8 = f32[16,4,1,4,1280]{4,3,2,1,0:T(4,128)} fusion(f32[16,4,2,4,1280]{4,3,2,1,0:T(4,128)} %reshape.254, s32[]{:T(128)S(6)} %select_n.83), kind=kLoop, calls=%fused_computation.114 | loop fusion | bytes 2621444 | tf_op jit(solution)/shard_map/jit(dynamic_index_in_dim)/dynamic_slice | solution.py:82
  40.8 2.1 collective-permute-start
  42.9 0.8 fusion.27
  45.0 0.8 fusion.8
  45.8 0.8 fusion.9
  46.6 0.8 fusion.10
  47.4 0.8 fusion.11
  48.7 0.5 select_reduce_fusion
  49.9 2.8 %copy.142 = bf16[128,65,128]{2,1,0:T(8,128)(2,1)} copy(bf16[128,65,128]{2,0,1:T(8,128)(2,1)S(1)} %fusion.12) | data formatting | bytes 4259840 | tf_op jit(solution)/shard_map/concatenate | solution.py:169
  52.7 20.1 %all-to-all-start = ((bf16[128,65,128]{2,1,0:T(8,128)(2,1)}), bf16[128,65,128]{2,1,0:T(8,128)(2,1)S(1)}, u32[]{:S(2)}, u32[]{:S(2)}) async-start(bf16[128,65,128]{2,1,0:T(8,128)(2,1)} %copy.142), calls=%async_computation | async-start | bytes 4718592 | tf_op jit(solution)/shard_map/all_to_all | solution.py:168
  72.8 3.1 %dynamic-slice_add_fusion = f32[16,4,1,4,1280]{4,3,2,1,0:T(4,128)} fusion(f32[16,4,1,4,1280]{4,3,2,1,0:T(4,128)} %collective-permute-done, f32[16,4,2,4,1280]{4,3,2,1,0:T(4,128)} %reshape.254, s32[]{:T(128)S(6)} %select_n.82), kind=kLoop, calls=%fused_computation.40 | loop fusion | flops 327680 | bytes 3932164 | tf_op jit(solution)/shard_map/add | solution.py:84
  75.9 3.1 %reshape_reshape_reshape.3 = f32[16,4,2,2,1,1280]{5,3,2,1,0,4:T(2,128)} reshape(f32[16,4,1,4,1280]{4,3,2,1,0:T(4,128)} %dynamic-slice_add_fusion) | data formatting | bytes 2621440 | tf_op jit(solution)/shard_map/reshape;reshape;reshape | solution.py:77
  79.1 2.0 constant_dynamic-slice_fusion.7
  81.1 3.0 %collective-permute-start.1 = (f32[16,4,2,1,1,1280]{5,3,2,1,0,4:T(1,128)S(1)}, f32[16,4,2,1,1,1280]{5,3,2,1,0,4:T(1,128)}, u32[]{:S(2)}, u32[]{:S(2)}) collective-permute-start(f32[16,4,2,1,1,1280]{5,3,2,1,0,4:T(1,128)S(1)} %constant_dynamic-slice_fusion.7), channel_id=1, source_target_pairs={{0,1},{1,0},{2,3},{3,2},{4,5},{5,4},{6,7},{7,6},{8,9},{9,8},{10,11... | collective-permute-start | bytes 1966088 | tf_op jit(solution)/shard_map/ppermute | solution.py:84
  84.0 15.3 %collective-permute-done.1 = f32[16,4,2,1,1,1280]{5,3,2,1,0,4:T(1,128)} collective-permute-done((f32[16,4,2,1,1,1280]{5,3,2,1,0,4:T(1,128)S(1)}, f32[16,4,2,1,1,1280]{5,3,2,1,0,4:T(1,128)}, u32[]{:S(2)}, u32[]{:S(2)}) %collective-permute-start.1) | collective-permute-done | bytes 655392 | tf_op jit(solution)/shard_map/ppermute | solution.py:84
  99.3 2.4 %dynamic-slice_add_fusion.1 = f32[16,4,2,1,1,1280]{5,3,2,1,0,4:T(1,128)S(1)} fusion(f32[16,4,2,1,1,1280]{5,3,2,1,0,4:T(1,128)} %collective-permute-done.1, f32[16,4,2,2,1,1280]{5,3,2,1,0,4:T(2,128)} %reshape_reshape_reshape.3, s32[]{:T(128)S(6)} %select_n.84), kind=kLoop, calls=%fused_computation.68 | loop fusion | flops 163840 | bytes 1966084 | tf_op jit(solution)/shard_map/add | solution.py:84
  101.8 3.3 %collective-permute-start.2 = (f32[16,4,1,1,1,1280]{5,3,2,1,0,4:T(1,128)S(1)}, f32[16,4,1,1,1,1280]{5,3,2,1,0,4:T(1,128)}, u32[]{:S(2)}, u32[]{:S(2)}) collective-permute-start(f32[16,4,1,1,1,1280]{5,3,2,1,0,4:T(1,128)S(1)} %constant_dynamic-slice_fusion.6), channel_id=1, source_target_pairs={{0,2},{1,3},{2,0},{3,1},{4,6},{5,7},{6,4},{7,5},{8,10},{9,11},{10,... | collective-permute-start | bytes 983048 | tf_op jit(solution)/shard_map/ppermute | solution.py:84
  105.1 8.5 %collective-permute-done.2 = f32[16,4,1,1,1,1280]{5,3,2,1,0,4:T(1,128)} collective-permute-done((f32[16,4,1,1,1,1280]{5,3,2,1,0,4:T(1,128)S(1)}, f32[16,4,1,1,1,1280]{5,3,2,1,0,4:T(1,128)}, u32[]{:S(2)}, u32[]{:S(2)}) %collective-permute-start.2) | collective-permute-done | bytes 327712 | tf_op jit(solution)/shard_map/ppermute | solution.py:84
  113.6 1.3 dynamic-slice_add_fusion.2
  115.0 4.2 %collective-permute-start.3 = (f32[16,2,1,1,1280]{4,3,2,1,0:T(1,128)S(1)}, f32[16,2,1,1,1280]{4,3,2,1,0:T(1,128)S(1)}, u32[]{:S(2)}, u32[]{:S(2)}) collective-permute-start(f32[16,2,1,1,1280]{4,3,2,1,0:T(1,128)S(1)} %constant_dynamic-slice_fusion.5), channel_id=1, source_target_pairs={{0,8},{8,0},{16,24},{24,16},{1,9},{9,1},{17,25},{25,17},{2,10},{10... | collective-permute-start | bytes 491528 | tf_op jit(solution)/shard_map/ppermute | solution.py:84
  119.2 4.0 %collective-permute-done.3 = f32[16,2,1,1,1280]{4,3,2,1,0:T(1,128)S(1)} collective-permute-done((f32[16,2,1,1,1280]{4,3,2,1,0:T(1,128)S(1)}, f32[16,2,1,1,1280]{4,3,2,1,0:T(1,128)S(1)}, u32[]{:S(2)}, u32[]{:S(2)}) %collective-permute-start.3) | collective-permute-done | bytes 163872 | tf_op jit(solution)/shard_map/ppermute | solution.py:84
  123.4 5.2 %collective-permute-start.4 = (f32[16,1,1,1,1280]{4,3,2,1,0:T(1,128)S(1)}, f32[16,1,1,1,1280]{4,3,2,1,0:T(1,128)S(1)}, u32[]{:S(2)}, u32[]{:S(2)}) collective-permute-start(f32[16,1,1,1,1280]{4,3,2,1,0:T(1,128)S(1)} %constant_dynamic-slice_fusion.4), channel_id=1, source_target_pairs={{0,16},{8,24},{16,0},{24,8},{1,17},{9,25},{17,1},{25,9},{2,18},{10... | collective-permute-start | bytes 245768 | tf_op jit(solution)/shard_map/ppermute | solution.py:84
  128.6 3.1 %collective-permute-done.4 = f32[16,1,1,1,1280]{4,3,2,1,0:T(1,128)S(1)} collective-permute-done((f32[16,1,1,1,1280]{4,3,2,1,0:T(1,128)S(1)}, f32[16,1,1,1,1280]{4,3,2,1,0:T(1,128)S(1)}, u32[]{:S(2)}, u32[]{:S(2)}) %collective-permute-start.4) | collective-permute-done | bytes 81952 | tf_op jit(solution)/shard_map/ppermute | solution.py:84
  131.8 4.1 %collective-permute-start.5 = (f32[2,2,2,1,1,1280]{5,4,3,2,1,0:T(1,128)S(1)}, f32[2,2,2,1,1,1280]{5,4,3,2,1,0:T(1,128)S(1)}, u32[]{:S(2)}, u32[]{:S(2)}) collective-permute-start(f32[2,2,2,1,1,1280]{5,4,3,2,1,0:T(1,128)S(1)} %constant_dynamic-slice_fusion.3), channel_id=1, source_target_pairs={{0,32},{32,0},{64,96},{96,64},{128,160},{160,128},{192,224},{224,1... | collective-permute-start | bytes 122888 | tf_op jit(solution)/shard_map/ppermute | solution.py:84
  135.9 39.3 %collective-permute-done.5 = f32[2,2,2,1,1,1280]{5,4,3,2,1,0:T(1,128)S(1)} collective-permute-done((f32[2,2,2,1,1,1280]{5,4,3,2,1,0:T(1,128)S(1)}, f32[2,2,2,1,1,1280]{5,4,3,2,1,0:T(1,128)S(1)}, u32[]{:S(2)}, u32[]{:S(2)}) %collective-permute-start.5) | collective-permute-done | bytes 40992 | tf_op jit(solution)/shard_map/ppermute | solution.py:84
  175.2 3.9 %collective-permute-start.6 = (f32[2,2,1,1,1,1280]{5,4,3,2,1,0:T(1,128)S(1)}, f32[2,2,1,1,1,1280]{5,4,3,2,1,0:T(1,128)S(1)}, u32[]{:S(2)}, u32[]{:S(2)}) collective-permute-start(f32[2,2,1,1,1,1280]{5,4,3,2,1,0:T(1,128)S(1)} %constant_dynamic-slice_fusion.2), channel_id=1, source_target_pairs={{0,64},{32,96},{64,0},{96,32},{128,192},{160,224},{192,128},{224,1... | collective-permute-start | bytes 61448 | tf_op jit(solution)/shard_map/ppermute | solution.py:84
  179.2 2.7 %collective-permute-done.6 = f32[2,2,1,1,1,1280]{5,4,3,2,1,0:T(1,128)S(1)} collective-permute-done((f32[2,2,1,1,1,1280]{5,4,3,2,1,0:T(1,128)S(1)}, f32[2,2,1,1,1,1280]{5,4,3,2,1,0:T(1,128)S(1)}, u32[]{:S(2)}, u32[]{:S(2)}) %collective-permute-start.6) | collective-permute-done | bytes 20512 | tf_op jit(solution)/shard_map/ppermute | solution.py:84
  181.9 6.6 %collective-permute-start.7 = (f32[2,1,1,1,1,1280]{5,4,3,2,1,0:T(1,128)S(1)}, f32[2,1,1,1,1,1280]{5,4,3,2,1,0:T(1,128)S(1)}, u32[]{:S(2)}, u32[]{:S(2)}) collective-permute-start(f32[2,1,1,1,1,1280]{5,4,3,2,1,0:T(1,128)S(1)} %constant_dynamic-slice_fusion.1), channel_id=1, source_target_pairs={{0,128},{32,160},{64,192},{96,224},{128,0},{160,32},{192,64},{224,... | collective-permute-start | bytes 30728 | tf_op jit(solution)/shard_map/ppermute | solution.py:84
  188.6 2.8 %collective-permute-done.7 = f32[2,1,1,1,1,1280]{5,4,3,2,1,0:T(1,128)S(1)} collective-permute-done((f32[2,1,1,1,1,1280]{5,4,3,2,1,0:T(1,128)S(1)}, f32[2,1,1,1,1,1280]{5,4,3,2,1,0:T(1,128)S(1)}, u32[]{:S(2)}, u32[]{:S(2)}) %collective-permute-start.7) | collective-permute-done | bytes 10272 | tf_op jit(solution)/shard_map/ppermute | solution.py:84
  191.4 12.6 %collective-permute-start.8 = (f32[1,1,1,1,1,1280]{5,4,3,2,1,0:T(1,128)S(1)}, f32[1,1,1,1,1,1280]{5,4,3,2,1,0:T(1,128)S(1)}, u32[]{:S(2)}, u32[]{:S(2)}) collective-permute-start(f32[1,1,1,1,1,1280]{5,4,3,2,1,0:T(1,128)S(1)} %constant_dynamic-slice_fusion), channel_id=1, source_target_pairs={{0,256},{32,288},{64,320},{96,352},{128,384},{160,416},{192,448},{... | collective-permute-start | bytes 15368 | tf_op jit(solution)/shard_map/ppermute | solution.py:84
  204.0 1.6 collective-permute-done.8
  205.8 0.5 copy.144
  210.7 2.9 %collective-permute-start.9 = (f32[136,640]{1,0:T(8,128)S(1)}, f32[136,640]{1,0:T(8,128)S(1)}, u32[]{:S(2)}, u32[]{:S(2)}) collective-permute-start(f32[136,640]{1,0:T(8,128)S(1)} %copy.150), channel_id=1, source_target_pairs={{0,1},{1,0},{2,3},{3,2},{4,5},{5,4},{6,7},{7,6},{8,9},{9,8},{10,11... | collective-permute-start | bytes 1044488 | tf_op jit(solution)/shard_map/ppermute | solution.py:90
  213.5 6.5 %collective-permute-done.9 = f32[136,640]{1,0:T(8,128)S(1)} collective-permute-done((f32[136,640]{1,0:T(8,128)S(1)}, f32[136,640]{1,0:T(8,128)S(1)}, u32[]{:S(2)}, u32[]{:S(2)}) %collective-permute-start.9) | collective-permute-done | bytes 348192 | tf_op jit(solution)/shard_map/ppermute | solution.py:90
  220.5 3.3 %collective-permute-start.10 = (f32[136,640]{1,0:T(8,128)S(1)}, f32[136,640]{1,0:T(8,128)S(1)}, u32[]{:S(2)}, u32[]{:S(2)}) collective-permute-start(f32[136,640]{1,0:T(8,128)S(1)} %copy.152), channel_id=1, source_target_pairs={{0,2},{1,3},{2,0},{3,1},{4,6},{5,7},{6,4},{7,5},{8,10},{9,11},{10,... | collective-permute-start | bytes 1044488 | tf_op jit(solution)/shard_map/ppermute | solution.py:90
  224.1 7.1 %collective-permute-done.10 = f32[136,640]{1,0:T(8,128)S(1)} collective-permute-done((f32[136,640]{1,0:T(8,128)S(1)}, f32[136,640]{1,0:T(8,128)S(1)}, u32[]{:S(2)}, u32[]{:S(2)}) %collective-permute-start.10) | collective-permute-done | bytes 348192 | tf_op jit(solution)/shard_map/ppermute | solution.py:90
  231.8 0.6 slice.95
  232.5 0.6 slice.96
  233.1 0.5 fusion.55
  233.7 0.8 copy.159
  234.5 0.8 copy.160
  (117 shorter events, 10.5 us)
Async XLA Ops:
  0.6 3.0 %copy-start = (bf16[512,1024]{1,0:T(8,128)(2,1)S(1)}, bf16[512,1024]{1,0:T(8,128)(2,1)}, u32[]{:S(2)}) copy-start(bf16[512,1024]{1,0:T(8,128)(2,1)} %param.17) | copy-start | bytes 3145732
  0.6 2.5 %copy-start.14 = (bf16[512,512]{1,0:T(8,128)(2,1)S(1)}, bf16[512,512]{1,0:T(8,128)(2,1)}, u32[]{:S(2)}) copy-start(bf16[512,512]{1,0:T(8,128)(2,1)} %param.12) | copy-start | bytes 1572868
  5.9 1.0 copy-start.6
  8.0 4.7 %copy-start.9 = (bf16[512,256]{0,1:T(8,128)(2,1)}, bf16[512,256]{0,1:T(8,128)(2,1)S(1)}, u32[]{:S(2)}) copy-start(bf16[512,256]{0,1:T(8,128)(2,1)S(1)} %copy.130) | copy-start | bytes 786436
  9.2 3.5 %copy-start.11 = (bf16[512,256]{0,1:T(8,128)(2,1)}, bf16[512,256]{0,1:T(8,128)(2,1)S(1)}, u32[]{:S(2)}) copy-start(bf16[512,256]{0,1:T(8,128)(2,1)S(1)} %copy.128) | copy-start | bytes 786436
  12.7 1.3 copy-start.2
  14.0 1.1 copy-start.3
  15.0 1.6 copy-start.7
  18.9 2.5 %copy-start.12 = (bf16[512,256]{0,1:T(8,128)(2,1)S(1)}, bf16[512,256]{0,1:T(8,128)(2,1)}, u32[]{:S(2)}) copy-start(bf16[512,256]{0,1:T(8,128)(2,1)} %copy-done.11) | copy-start | bytes 786436
  19.2 2.2 copy-start.13
  21.4 4.0 %copy-start.10 = (bf16[512,256]{0,1:T(8,128)(2,1)S(1)}, bf16[512,256]{0,1:T(8,128)(2,1)}, u32[]{:S(2)}) copy-start(bf16[512,256]{0,1:T(8,128)(2,1)} %copy-done.9) | copy-start | bytes 786436
  31.1 3.2 %copy-start.4 = (bf16[512,1024]{1,0:T(8,128)(2,1)}, bf16[512,1024]{1,0:T(8,128)(2,1)S(1)}, u32[]{:S(2)}) copy-start(bf16[512,1024]{1,0:T(8,128)(2,1)S(1)} %fusion.14) | copy-start | bytes 3145732
  31.1 1.4 copy-start.8
  38.2 4.7 %copy-start.5 = (bf16[512,1024]{1,0:T(8,128)(2,1)S(1)}, bf16[512,1024]{1,0:T(8,128)(2,1)}, u32[]{:S(2)}) copy-start(bf16[512,1024]{1,0:T(8,128)(2,1)} %copy-done.4) | copy-start | bytes 3145732
  40.8 32.0 %collective-permute-start = (f32[16,4,1,4,1280]{4,3,2,1,0:T(4,128)}, f32[16,4,1,4,1280]{4,3,2,1,0:T(4,128)}, u32[]{:S(2)}, u32[]{:S(2)}) collective-permute-start(f32[16,4,1,4,1280]{4,3,2,1,0:T(4,128)} %constant_dynamic-slice_fusion.8), channel_id=1, source_target_pairs={{0,4},{4,0},{1,5},{5,1},{2,6},{6,2},{3,7},{7,3},{8,12},{12,8},{9,1... | collective-permute-start | bytes 3932168 | tf_op jit(solution)/shard_map/ppermute | solution.py:84
  43.7 0.7 copy-start.17
  43.9 1.0 copy-start.18
  52.7 153.1 %all-to-all-start = ((bf16[128,65,128]{2,1,0:T(8,128)(2,1)}), bf16[128,65,128]{2,1,0:T(8,128)(2,1)S(1)}, u32[]{:S(2)}, u32[]{:S(2)}) async-start(bf16[128,65,128]{2,1,0:T(8,128)(2,1)} %copy.142), calls=%async_computation | async-start | bytes 4718592 | tf_op jit(solution)/shard_map/all_to_all | solution.py:168
  81.1 18.3 %collective-permute-start.1 = (f32[16,4,2,1,1,1280]{5,3,2,1,0,4:T(1,128)S(1)}, f32[16,4,2,1,1,1280]{5,3,2,1,0,4:T(1,128)}, u32[]{:S(2)}, u32[]{:S(2)}) collective-permute-start(f32[16,4,2,1,1,1280]{5,3,2,1,0,4:T(1,128)S(1)} %constant_dynamic-slice_fusion.7), channel_id=1, source_target_pairs={{0,1},{1,0},{2,3},{3,2},{4,5},{5,4},{6,7},{7,6},{8,9},{9,8},{10,11... | collective-permute-start | bytes 1966088 | tf_op jit(solution)/shard_map/ppermute | solution.py:84
  101.8 11.8 %collective-permute-start.2 = (f32[16,4,1,1,1,1280]{5,3,2,1,0,4:T(1,128)S(1)}, f32[16,4,1,1,1,1280]{5,3,2,1,0,4:T(1,128)}, u32[]{:S(2)}, u32[]{:S(2)}) collective-permute-start(f32[16,4,1,1,1,1280]{5,3,2,1,0,4:T(1,128)S(1)} %constant_dynamic-slice_fusion.6), channel_id=1, source_target_pairs={{0,2},{1,3},{2,0},{3,1},{4,6},{5,7},{6,4},{7,5},{8,10},{9,11},{10,... | collective-permute-start | bytes 983048 | tf_op jit(solution)/shard_map/ppermute | solution.py:84
  115.0 8.2 %collective-permute-start.3 = (f32[16,2,1,1,1280]{4,3,2,1,0:T(1,128)S(1)}, f32[16,2,1,1,1280]{4,3,2,1,0:T(1,128)S(1)}, u32[]{:S(2)}, u32[]{:S(2)}) collective-permute-start(f32[16,2,1,1,1280]{4,3,2,1,0:T(1,128)S(1)} %constant_dynamic-slice_fusion.5), channel_id=1, source_target_pairs={{0,8},{8,0},{16,24},{24,16},{1,9},{9,1},{17,25},{25,17},{2,10},{10... | collective-permute-start | bytes 491528 | tf_op jit(solution)/shard_map/ppermute | solution.py:84
  123.4 8.3 %collective-permute-start.4 = (f32[16,1,1,1,1280]{4,3,2,1,0:T(1,128)S(1)}, f32[16,1,1,1,1280]{4,3,2,1,0:T(1,128)S(1)}, u32[]{:S(2)}, u32[]{:S(2)}) collective-permute-start(f32[16,1,1,1,1280]{4,3,2,1,0:T(1,128)S(1)} %constant_dynamic-slice_fusion.4), channel_id=1, source_target_pairs={{0,16},{8,24},{16,0},{24,8},{1,17},{9,25},{17,1},{25,9},{2,18},{10... | collective-permute-start | bytes 245768 | tf_op jit(solution)/shard_map/ppermute | solution.py:84
  131.8 43.3 %collective-permute-start.5 = (f32[2,2,2,1,1,1280]{5,4,3,2,1,0:T(1,128)S(1)}, f32[2,2,2,1,1,1280]{5,4,3,2,1,0:T(1,128)S(1)}, u32[]{:S(2)}, u32[]{:S(2)}) collective-permute-start(f32[2,2,2,1,1,1280]{5,4,3,2,1,0:T(1,128)S(1)} %constant_dynamic-slice_fusion.3), channel_id=1, source_target_pairs={{0,32},{32,0},{64,96},{96,64},{128,160},{160,128},{192,224},{224,1... | collective-permute-start | bytes 122888 | tf_op jit(solution)/shard_map/ppermute | solution.py:84
  175.2 6.6 %collective-permute-start.6 = (f32[2,2,1,1,1,1280]{5,4,3,2,1,0:T(1,128)S(1)}, f32[2,2,1,1,1,1280]{5,4,3,2,1,0:T(1,128)S(1)}, u32[]{:S(2)}, u32[]{:S(2)}) collective-permute-start(f32[2,2,1,1,1,1280]{5,4,3,2,1,0:T(1,128)S(1)} %constant_dynamic-slice_fusion.2), channel_id=1, source_target_pairs={{0,64},{32,96},{64,0},{96,32},{128,192},{160,224},{192,128},{224,1... | collective-permute-start | bytes 61448 | tf_op jit(solution)/shard_map/ppermute | solution.py:84
  181.9 9.5 %collective-permute-start.7 = (f32[2,1,1,1,1,1280]{5,4,3,2,1,0:T(1,128)S(1)}, f32[2,1,1,1,1,1280]{5,4,3,2,1,0:T(1,128)S(1)}, u32[]{:S(2)}, u32[]{:S(2)}) collective-permute-start(f32[2,1,1,1,1,1280]{5,4,3,2,1,0:T(1,128)S(1)} %constant_dynamic-slice_fusion.1), channel_id=1, source_target_pairs={{0,128},{32,160},{64,192},{96,224},{128,0},{160,32},{192,64},{224,... | collective-permute-start | bytes 30728 | tf_op jit(solution)/shard_map/ppermute | solution.py:84
  191.4 14.2 %collective-permute-start.8 = (f32[1,1,1,1,1,1280]{5,4,3,2,1,0:T(1,128)S(1)}, f32[1,1,1,1,1,1280]{5,4,3,2,1,0:T(1,128)S(1)}, u32[]{:S(2)}, u32[]{:S(2)}) collective-permute-start(f32[1,1,1,1,1,1280]{5,4,3,2,1,0:T(1,128)S(1)} %constant_dynamic-slice_fusion), channel_id=1, source_target_pairs={{0,256},{32,288},{64,320},{96,352},{128,384},{160,416},{192,448},{... | collective-permute-start | bytes 15368 | tf_op jit(solution)/shard_map/ppermute | solution.py:84
  210.7 13.2 %copy-start.15 = (f32[128,512]{1,0:T(8,128)S(1)}, f32[128,512]{1,0:T(8,128)}, u32[]{:S(2)}) copy-start(f32[128,512]{1,0:T(8,128)} %param.20) | copy-start | bytes 786436
  210.7 13.3 %copy-start.16 = (f32[128,512]{1,0:T(8,128)S(1)}, f32[128,512]{1,0:T(8,128)}, u32[]{:S(2)}) copy-start(f32[128,512]{1,0:T(8,128)} %param.19) | copy-start | bytes 786436
  210.7 9.4 %collective-permute-start.9 = (f32[136,640]{1,0:T(8,128)S(1)}, f32[136,640]{1,0:T(8,128)S(1)}, u32[]{:S(2)}, u32[]{:S(2)}) collective-permute-start(f32[136,640]{1,0:T(8,128)S(1)} %copy.150), channel_id=1, source_target_pairs={{0,1},{1,0},{2,3},{3,2},{4,5},{5,4},{6,7},{7,6},{8,9},{9,8},{10,11... | collective-permute-start | bytes 1044488 | tf_op jit(solution)/shard_map/ppermute | solution.py:90
  220.5 10.7 %collective-permute-start.10 = (f32[136,640]{1,0:T(8,128)S(1)}, f32[136,640]{1,0:T(8,128)S(1)}, u32[]{:S(2)}, u32[]{:S(2)}) collective-permute-start(f32[136,640]{1,0:T(8,128)S(1)} %copy.152), channel_id=1, source_target_pairs={{0,2},{1,3},{2,0},{3,1},{4,6},{5,7},{6,4},{7,5},{8,10},{9,11},{10,... | collective-permute-start | bytes 1044488 | tf_op jit(solution)/shard_map/ppermute | solution.py:90
  224.1 8.9 %copy-start.19 = (f32[128]{0:T(128)S(1)}, f32[128]{0:T(128)}, u32[]{:S(2)}) copy-start(f32[128]{0:T(128)} %param.21) | copy-start | bytes 1540
  231.5 3.9 %copy-start.1 = (bf16[512,1024]{1,0:T(8,128)(2,1)S(1)}, bf16[512,1024]{1,0:T(8,128)(2,1)}, u32[]{:S(2)}) copy-start(bf16[512,1024]{1,0:T(8,128)(2,1)} %param.17) | copy-start | bytes 3145732

commit v15 on v14

--- a/solution.py
+++ b/solution.py
@@ -97,12 +97,8 @@
     per_owner = partial.shape[0] // (n_z * n_y * n_c)
     blocks = partial.reshape(n_z, n_y, n_c, per_owner, width)
     blocks = halve_sum(blocks, "core", n_c, 2)
-    blocks = blocks.reshape(n_z, n_y, n_x, per_owner // n_x, width)
-    blocks = halve_sum(blocks, "x", n_x, 2)
     blocks = halve_sum(blocks, "y", n_y, 1)
-    piece = halve_sum(blocks, "z", n_z, 0)
-    mine = lax.axis_index("x") * (per_owner // n_x)
-    return lax.dynamic_update_slice_in_dim(jnp.zeros((per_owner, width), piece.dtype), piece, mine, 0)
+    return halve_sum(blocks, "z", n_z, 0).reshape(per_owner, width)
 
 
 def local(sizes, tokens, out_grad, seq_lengths, owners, slots, w_in, w_out, emb_rows, emb_mom, emb_var):

time: 236 us -> 244 us (1.034)
  waiting for transfers between devices: 90.9 us -> 108 us
  starting transfers between devices: 71.2 us -> 61.6 us
  matrix products: 23 us -> 27.9 us
  local copies, waits for them, and re-layouts: 30.1 us -> 26.8 us
    ppermute x9 -> x7, waiting for transfers between devices: 77.3 us -> 93.7 us  [halve_sum(): blocks = keep + lax.ppermute(send, axis, pairs)]
    ppermute x9 -> x7, starting transfers between devices: 45 us -> 34.8 us  [halve_sum(): blocks = keep + lax.ppermute(send, axis, pairs)]
    add x8 -> x6, other arithmetic: 7.24 us -> 2.01 us  [halve_sum(): blocks = keep + lax.ppermute(send, axis, pairs)]
    dynamic_slice x9 -> x6, local copies, waits for them, and re-layouts: 4.72 us -> 1.28 us  [halve_sum(): send = lax.dynamic_index_in_dim(blocks, 1 - mine, at, keepdims=True)]
    another operation x1 -> x0, local copies, waits for them, and re-layouts: 3.14 us -> none  [halve_sum(): blocks = blocks.reshape(lead + (2,) * bits + blocks.shape[dim + 1:])]
    unnamed x46 -> x37, local copies, waits for them, and re-layouts: 5.58 us -> 2.65 us
  transfers between devices with their start and end apart: 12 -> 10, of which waited for: 10 -> 9; matrix products, arithmetic and copies ran while one was open for 10% -> 4% of each run, Pallas kernels for 0% -> 0%
where the time goes in v15:
time: 244 us; the launch traced here: 242 us
  waiting for transfers between devices  108 us (44%)
  starting transfers between devices  61.6 us (25%)
  matrix products  27.9 us (11%)
  local copies, waits for them, and re-layouts  26.8 us (11%)
  other arithmetic  17.1 us (7%)
    ppermute x7, waiting for transfers between devices, halve_sum(): blocks = keep + lax.ppermute(send, axis, pairs)  93.7 us
    ppermute x7, starting transfers between devices, halve_sum(): blocks = keep + lax.ppermute(send, axis, pairs)  34.8 us
    all_to_all x1, starting transfers between devices, local(): lax.all_to_all(jnp.concatenate([outgoing.reshape(owner_count, block_rows,...  20.5 us
    ppermute x2, waiting for transfers between devices, double_sum(): lax.ppermute(value, axis, [(i, i ^ 1 << bit) for i in range(size)])  13.9 us
    dot_general x3, matrix products, core(): jnp.einsum('hts,shd->thd', weights, values_part, preferred_element_type=j...  9.31 us
    dot_general x3, matrix products, core(): jnp.einsum('thd,shd->hts', queries, keys_part, preferred_element_type=jnp...  6.81 us
    ppermute x2, starting transfers between devices, double_sum(): lax.ppermute(value, axis, [(i, i ^ 1 << bit) for i in range(size)])  6.22 us
  transfers between devices with their start and end apart: 10, of which 9 were waited for; matrix products, arithmetic and copies ran while one was open for 4% of the time, Pallas kernels for 0%

profile of v15, /device:TPU:6, one launch (start us, length us, event | category | flops | bytes accessed | tf_op | source)
XLA Modules:
  0.0 242.4 jit_solution(7878741302932365562)
XLA Ops:
  0.7 0.9 reduce-window.8
  1.9 1.2 fusion.30
  3.6 2.7 %multiply_convert_fusion.1 = (bf16[512,1024]{1,0:T(8,128)(2,1)}, f32[512,1024]{1,0:T(8,128)}) fusion(bf16[512,1024]{1,0:T(8,128)(2,1)S(1)} %copy-done, bf16[512,512]{0,1:T(8,128)(2,1)S(1)} %copy.133, f32[512]{0:T(512)S(1)} %fusion.53, f32[512]{0:T(512)S(1)} %broadcast_multiply_fusion.1), kind=kOutput, calls=%fused_computation.27 | convolution fusion | flops 540540928 | bytes 4722688 | tf_op jit(solution)/shard_map/dot_general | solution.py:110
  6.3 1.9 fusion.59
  8.5 1.2 copy.134
  9.7 4.2 %multiply_convert_fusion = (bf16[4,512,512]{2,1,0:T(8,128)(2,1)}, f32[4,512,512]{2,1,0:T(8,128)}) fusion(f32[512,512]{1,0:T(8,128)S(1)} %fusion.31, bf16[512,4,64]{0,2,1:T(8,128)(2,1)S(1)} %bitcast.75, bf16[512,4,64]{0,2,1:T(8,128)(2,1)S(1)} %bitcast.77), kind=kOutput, calls=%fused_computation.7 | convolution fusion | flops 142606336 | bytes 7864320 | tf_op jit(solution)/shard_map/jvp(thd,shd->hts)/dot_general | solution.py:46
  13.9 2.4 fusion.60
  16.6 1.4 multiply_reduce_fusion
  18.0 1.9 fusion.57
  20.0 0.8 broadcast_add_fusion
  20.8 1.1 copy.139
  21.9 2.9 %fusion.63 = bf16[4,64,512]{2,1,0:T(8,128)(2,1)} fusion(bf16[4,64,512]{2,1,0:T(8,128)(2,1)S(1)} %bitcast.82, bf16[4,512,512]{2,1,0:T(8,128)(2,1)} %get-tuple-element.66), kind=kOutput, calls=%fused_computation.135 | convolution fusion | flops 134217728 | bytes 2621440 | tf_op jit(solution)/shard_map/transpose(jvp(hts,shd->thd))/dot_general | solution.py:50
  24.8 4.0 %fusion.3 = bf16[4,512,512]{2,1,0:T(8,128)(2,1)S(1)} fusion(f32[4,512,512]{2,1,0:T(8,128)} %get-tuple-element.67, f32[512,512]{1,0:T(8,128)S(1)} %copy-done.8, bf16[4,64,512]{2,1,0:T(8,128)(2,1)S(1)} %bitcast.83, bf16[512,4,64]{0,2,1:T(8,128)(2,1)} %bitcast.80), kind=kOutput, calls=%fused_computation.5 | convolution fusion | flops 148897792 | bytes 7864320 | tf_op jit(solution)/shard_map/transpose(jvp(hts,shd->thd))/dot_general | solution.py:50
  28.8 1.5 fusion.62
  30.3 1.2 fusion.61
  31.7 1.1 copy.140
  32.8 1.8 copy.141
  34.6 1.8 copy.142
  36.4 2.6 %fusion.14 = bf16[512,1024]{1,0:T(8,128)(2,1)S(1)} fusion(f32[512,1024]{1,0:T(8,128)} %get-tuple-element.65, bf16[512,256]{1,0:T(8,128)(2,1)} %copy.142, bf16[512,256]{1,0:T(8,128)(2,1)} %copy.141, bf16[512,256]{1,0:T(8,128)(2,1)S(1)} %copy.140, bf16[512,256]{1,0:T(8,128)(2,1)} %get-tuple-element.54), kind=kLoop, calls=%fused_computation.24 | loop fusion | flops 9437184 | bytes 4194304 | tf_op jit(solution)/shard_map/convert_element_type | solution.py:113
  39.0 0.8 fusion.27
  40.9 0.8 fusion.8
  41.7 0.8 fusion.9
  42.5 0.8 fusion.10
  43.3 0.8 fusion.11
  44.5 0.9 copy.147
  45.4 0.5 select_reduce_fusion
  46.0 1.3 pad_maximum_fusion.1
  47.6 2.8 %copy.148 = bf16[128,65,128]{2,1,0:T(8,128)(2,1)} copy(bf16[128,65,128]{2,0,1:T(8,128)(2,1)S(1)} %fusion.12) | data formatting | bytes 4259840 | tf_op jit(solution)/shard_map/concatenate | solution.py:165
  50.5 20.5 %all-to-all-start = ((bf16[128,65,128]{2,1,0:T(8,128)(2,1)}), bf16[128,65,128]{2,1,0:T(8,128)(2,1)}, u32[]{:S(2)}, u32[]{:S(2)}) async-start(bf16[128,65,128]{2,1,0:T(8,128)(2,1)} %copy.148), calls=%async_computation | async-start | bytes 4718592 | tf_op jit(solution)/shard_map/all_to_all | solution.py:164
  71.0 1.5 convolution_bitcast_fusion
  72.5 0.7 fusion.40
  73.2 1.7 pad_maximum_fusion
  74.9 2.8 %reshape.254 = f32[16,4,2,4,1280]{4,3,2,1,0:T(4,128)S(1)} reshape(f32[512,1280]{1,0:T(8,128)} %pad_maximum_fusion) | data formatting | bytes 5242880 | tf_op jit(solution)/shard_map/reshape | solution.py:98
  77.7 1.2 constant_dynamic-slice_fusion.7
  78.9 1.9 collective-permute-start
  80.8 3.3 %collective-permute-done = f32[16,4,1,4,1280]{4,3,2,1,0:T(4,128)} collective-permute-done((f32[16,4,1,4,1280]{4,3,2,1,0:T(4,128)}, f32[16,4,1,4,1280]{4,3,2,1,0:T(4,128)}, u32[]{:S(2)}, u32[]{:S(2)}) %collective-permute-start) | collective-permute-done | bytes 1310752 | tf_op jit(solution)/shard_map/ppermute | solution.py:84
  84.1 1.7 dynamic-slice_add_fusion
  86.0 3.0 %collective-permute-start.1 = (f32[16,2,1,4,1280]{4,3,0,2,1:T(4,128)S(1)}, f32[16,2,1,4,1280]{4,3,0,2,1:T(4,128)S(1)}, u32[]{:S(2)}, u32[]{:S(2)}) collective-permute-start(f32[16,2,1,4,1280]{4,3,0,2,1:T(4,128)S(1)} %copy.172), channel_id=1, source_target_pairs={{0,8},{8,0},{16,24},{24,16},{1,9},{9,1},{17,25},{25,17},{2,10},{10... | collective-permute-start | bytes 1966088 | tf_op jit(solution)/shard_map/ppermute | solution.py:84
  89.0 20.2 %collective-permute-done.1 = f32[16,2,1,4,1280]{4,3,0,2,1:T(4,128)S(1)} collective-permute-done((f32[16,2,1,4,1280]{4,3,0,2,1:T(4,128)S(1)}, f32[16,2,1,4,1280]{4,3,0,2,1:T(4,128)S(1)}, u32[]{:S(2)}, u32[]{:S(2)}) %collective-permute-start.1) | collective-permute-done | bytes 655392 | tf_op jit(solution)/shard_map/ppermute | solution.py:84
  109.4 4.1 %collective-permute-start.2 = (f32[16,1,1,4,1280]{4,3,0,2,1:T(4,128)S(1)}, f32[16,1,1,4,1280]{4,3,0,2,1:T(4,128)S(1)}, u32[]{:S(2)}, u32[]{:S(2)}) collective-permute-start(f32[16,1,1,4,1280]{4,3,0,2,1:T(4,128)S(1)} %constant_dynamic-slice_fusion.4), channel_id=1, source_target_pairs={{0,16},{8,24},{16,0},{24,8},{1,17},{9,25},{17,1},{25,9},{2,18},{10... | collective-permute-start | bytes 983048 | tf_op jit(solution)/shard_map/ppermute | solution.py:84
  113.4 12.0 %collective-permute-done.2 = f32[16,1,1,4,1280]{4,3,0,2,1:T(4,128)S(1)} collective-permute-done((f32[16,1,1,4,1280]{4,3,0,2,1:T(4,128)S(1)}, f32[16,1,1,4,1280]{4,3,0,2,1:T(4,128)S(1)}, u32[]{:S(2)}, u32[]{:S(2)}) %collective-permute-start.2) | collective-permute-done | bytes 327712 | tf_op jit(solution)/shard_map/ppermute | solution.py:84
  125.5 2.8 %collective-permute-start.3 = (f32[2,2,2,1,4,1280]{5,4,3,2,1,0:T(4,128)S(1)}, f32[2,2,2,1,4,1280]{5,4,3,2,1,0:T(4,128)S(1)}, u32[]{:S(2)}, u32[]{:S(2)}) collective-permute-start(f32[2,2,2,1,4,1280]{5,4,3,2,1,0:T(4,128)S(1)} %constant_dynamic-slice_fusion.3), channel_id=1, source_target_pairs={{0,32},{32,0},{64,96},{96,64},{128,160},{160,128},{192,224},{224,1... | collective-permute-start | bytes 491528 | tf_op jit(solution)/shard_map/ppermute | solution.py:84
  128.4 48.2 %collective-permute-done.3 = f32[2,2,2,1,4,1280]{5,4,3,2,1,0:T(4,128)S(1)} collective-permute-done((f32[2,2,2,1,4,1280]{5,4,3,2,1,0:T(4,128)S(1)}, f32[2,2,2,1,4,1280]{5,4,3,2,1,0:T(4,128)S(1)}, u32[]{:S(2)}, u32[]{:S(2)}) %collective-permute-start.3) | collective-permute-done | bytes 163872 | tf_op jit(solution)/shard_map/ppermute | solution.py:84
  176.6 3.7 %collective-permute-start.4 = (f32[2,2,1,1,4,1280]{5,4,3,2,1,0:T(4,128)S(1)}, f32[2,2,1,1,4,1280]{5,4,3,2,1,0:T(4,128)S(1)}, u32[]{:S(2)}, u32[]{:S(2)}) collective-permute-start(f32[2,2,1,1,4,1280]{5,4,3,2,1,0:T(4,128)S(1)} %constant_dynamic-slice_fusion.2), channel_id=1, source_target_pairs={{0,64},{32,96},{64,0},{96,32},{128,192},{160,224},{192,128},{224,1... | collective-permute-start | bytes 245768 | tf_op jit(solution)/shard_map/ppermute | solution.py:84
  180.3 4.7 %collective-permute-done.4 = f32[2,2,1,1,4,1280]{5,4,3,2,1,0:T(4,128)S(1)} collective-permute-done((f32[2,2,1,1,4,1280]{5,4,3,2,1,0:T(4,128)S(1)}, f32[2,2,1,1,4,1280]{5,4,3,2,1,0:T(4,128)S(1)}, u32[]{:S(2)}, u32[]{:S(2)}) %collective-permute-start.4) | collective-permute-done | bytes 81952 | tf_op jit(solution)/shard_map/ppermute | solution.py:84
  185.1 7.4 %collective-permute-start.5 = (f32[2,1,1,1,4,1280]{5,4,3,2,1,0:T(4,128)S(1)}, f32[2,1,1,1,4,1280]{5,4,3,2,1,0:T(4,128)S(1)}, u32[]{:S(2)}, u32[]{:S(2)}) collective-permute-start(f32[2,1,1,1,4,1280]{5,4,3,2,1,0:T(4,128)S(1)} %constant_dynamic-slice_fusion.1), channel_id=1, source_target_pairs={{0,128},{32,160},{64,192},{96,224},{128,0},{160,32},{192,64},{224,... | collective-permute-start | bytes 122888 | tf_op jit(solution)/shard_map/ppermute | solution.py:84
  192.6 2.8 %collective-permute-done.5 = f32[2,1,1,1,4,1280]{5,4,3,2,1,0:T(4,128)S(1)} collective-permute-done((f32[2,1,1,1,4,1280]{5,4,3,2,1,0:T(4,128)S(1)}, f32[2,1,1,1,4,1280]{5,4,3,2,1,0:T(4,128)S(1)}, u32[]{:S(2)}, u32[]{:S(2)}) %collective-permute-start.5) | collective-permute-done | bytes 40992 | tf_op jit(solution)/shard_map/ppermute | solution.py:84
  195.4 11.9 %collective-permute-start.6 = (f32[1,1,1,1,4,1280]{5,4,3,2,1,0:T(4,128)S(1)}, f32[1,1,1,1,4,1280]{5,4,3,2,1,0:T(4,128)S(1)}, u32[]{:S(2)}, u32[]{:S(2)}) collective-permute-start(f32[1,1,1,1,4,1280]{5,4,3,2,1,0:T(4,128)S(1)} %constant_dynamic-slice_fusion), channel_id=1, source_target_pairs={{0,256},{32,288},{64,320},{96,352},{128,384},{160,416},{192,448},{... | collective-permute-start | bytes 61448 | tf_op jit(solution)/shard_map/ppermute | solution.py:84
  207.3 2.5 %collective-permute-done.6 = f32[1,1,1,1,4,1280]{5,4,3,2,1,0:T(4,128)S(1)} collective-permute-done((f32[1,1,1,1,4,1280]{5,4,3,2,1,0:T(4,128)S(1)}, f32[1,1,1,1,4,1280]{5,4,3,2,1,0:T(4,128)S(1)}, u32[]{:S(2)}, u32[]{:S(2)}) %collective-permute-start.6) | collective-permute-done | bytes 20512 | tf_op jit(solution)/shard_map/ppermute | solution.py:84
  209.8 2.2 copy.152
  212.0 1.2 convert_reduce_fusion.3
  214.3 0.4 convolution_dynamic-update-slice_fusion.3
  215.9 0.4 convolution_dynamic-update-slice_fusion.2
  216.3 0.4 convolution_dynamic-update-slice_fusion.1
  216.7 0.4 convolution_dynamic-update-slice_fusion
  217.4 2.9 %collective-permute-start.7 = (f32[136,640]{1,0:T(8,128)S(1)}, f32[136,640]{1,0:T(8,128)S(1)}, u32[]{:S(2)}, u32[]{:S(2)}) collective-permute-start(f32[136,640]{1,0:T(8,128)S(1)} %copy.158), channel_id=1, source_target_pairs={{0,1},{1,0},{2,3},{3,2},{4,5},{5,4},{6,7},{7,6},{8,9},{9,8},{10,11... | collective-permute-start | bytes 1044488 | tf_op jit(solution)/shard_map/ppermute | solution.py:90
  220.3 6.8 %collective-permute-done.7 = f32[136,640]{1,0:T(8,128)S(1)} collective-permute-done((f32[136,640]{1,0:T(8,128)S(1)}, f32[136,640]{1,0:T(8,128)S(1)}, u32[]{:S(2)}, u32[]{:S(2)}) %collective-permute-start.7) | collective-permute-done | bytes 348192 | tf_op jit(solution)/shard_map/ppermute | solution.py:90
  227.6 3.3 %collective-permute-start.8 = (f32[136,640]{1,0:T(8,128)S(1)}, f32[136,640]{1,0:T(8,128)S(1)}, u32[]{:S(2)}, u32[]{:S(2)}) collective-permute-start(f32[136,640]{1,0:T(8,128)S(1)} %copy.160), channel_id=1, source_target_pairs={{0,2},{1,3},{2,0},{3,1},{4,6},{5,7},{6,4},{7,5},{8,10},{9,11},{10,... | collective-permute-start | bytes 1044488 | tf_op jit(solution)/shard_map/ppermute | solution.py:90
  231.3 7.1 %collective-permute-done.8 = f32[136,640]{1,0:T(8,128)S(1)} collective-permute-done((f32[136,640]{1,0:T(8,128)S(1)}, f32[136,640]{1,0:T(8,128)S(1)}, u32[]{:S(2)}, u32[]{:S(2)}) %collective-permute-start.8) | collective-permute-done | bytes 348192 | tf_op jit(solution)/shard_map/ppermute | solution.py:90
  238.9 0.6 slice.95
  239.5 0.6 slice.96
  240.1 0.5 fusion.55
  240.7 0.8 copy.167
  241.6 0.8 copy.168
  (97 shorter events, 8.0 us)
Async XLA Ops:
  0.6 3.0 %copy-start = (bf16[512,1024]{1,0:T(8,128)(2,1)S(1)}, bf16[512,1024]{1,0:T(8,128)(2,1)}, u32[]{:S(2)}) copy-start(bf16[512,1024]{1,0:T(8,128)(2,1)} %param.17) | copy-start | bytes 3145732
  0.6 2.4 copy-start.9
  8.5 5.4 %copy-start.5 = (bf16[512,256]{0,1:T(8,128)(2,1)}, bf16[512,256]{0,1:T(8,128)(2,1)S(1)}, u32[]{:S(2)}) copy-start(bf16[512,256]{0,1:T(8,128)(2,1)S(1)} %copy.136) | copy-start | bytes 786436
  9.7 4.2 %copy-start.7 = (bf16[512,256]{0,1:T(8,128)(2,1)}, bf16[512,256]{0,1:T(8,128)(2,1)S(1)}, u32[]{:S(2)}) copy-start(bf16[512,256]{0,1:T(8,128)(2,1)S(1)} %copy.134) | copy-start | bytes 786436
  13.9 2.7 %copy-start.2 = (bf16[512,512]{1,0:T(8,128)(2,1)S(1)}, bf16[512,512]{1,0:T(8,128)(2,1)}, u32[]{:S(2)}) copy-start(bf16[512,512]{1,0:T(8,128)(2,1)} %param.13) | copy-start | bytes 1572868
  21.9 2.9 %copy-start.8 = (f32[512,512]{1,0:T(8,128)S(1)}, f32[512,512]{1,0:T(8,128)}, u32[]{:S(2)}) copy-start(f32[512,512]{1,0:T(8,128)} %fusion.30) | copy-start | bytes 3145732
  24.8 4.0 %copy-start.6 = (bf16[512,256]{0,1:T(8,128)(2,1)S(1)}, bf16[512,256]{0,1:T(8,128)(2,1)}, u32[]{:S(2)}) copy-start(bf16[512,256]{0,1:T(8,128)(2,1)} %copy-done.5) | copy-start | bytes 786436
  38.9 1.0 copy-start.3
  39.0 1.3 copy-start.12
  39.9 0.9 copy-start.13
  50.5 22.0 %copy-start.4 = (bf16[512,1024]{1,0:T(8,128)(2,1)S(1)}, bf16[512,1024]{1,0:T(8,128)(2,1)}, u32[]{:S(2)}) copy-start(bf16[512,1024]{1,0:T(8,128)(2,1)} %copy-done.3) | copy-start | bytes 3145732
  50.5 159.3 %all-to-all-start = ((bf16[128,65,128]{2,1,0:T(8,128)(2,1)}), bf16[128,65,128]{2,1,0:T(8,128)(2,1)}, u32[]{:S(2)}, u32[]{:S(2)}) async-start(bf16[128,65,128]{2,1,0:T(8,128)(2,1)} %copy.148), calls=%async_computation | async-start | bytes 4718592 | tf_op jit(solution)/shard_map/all_to_all | solution.py:164
  78.9 5.3 %collective-permute-start = (f32[16,4,1,4,1280]{4,3,2,1,0:T(4,128)}, f32[16,4,1,4,1280]{4,3,2,1,0:T(4,128)}, u32[]{:S(2)}, u32[]{:S(2)}) collective-permute-start(f32[16,4,1,4,1280]{4,3,2,1,0:T(4,128)} %constant_dynamic-slice_fusion.7), channel_id=1, source_target_pairs={{0,4},{4,0},{1,5},{5,1},{2,6},{6,2},{3,7},{7,3},{8,12},{12,8},{9,1... | collective-permute-start | bytes 3932168 | tf_op jit(solution)/shard_map/ppermute | solution.py:84
  86.0 23.2 %collective-permute-start.1 = (f32[16,2,1,4,1280]{4,3,0,2,1:T(4,128)S(1)}, f32[16,2,1,4,1280]{4,3,0,2,1:T(4,128)S(1)}, u32[]{:S(2)}, u32[]{:S(2)}) collective-permute-start(f32[16,2,1,4,1280]{4,3,0,2,1:T(4,128)S(1)} %copy.172), channel_id=1, source_target_pairs={{0,8},{8,0},{16,24},{24,16},{1,9},{9,1},{17,25},{25,17},{2,10},{10... | collective-permute-start | bytes 1966088 | tf_op jit(solution)/shard_map/ppermute | solution.py:84
  109.4 16.0 %collective-permute-start.2 = (f32[16,1,1,4,1280]{4,3,0,2,1:T(4,128)S(1)}, f32[16,1,1,4,1280]{4,3,0,2,1:T(4,128)S(1)}, u32[]{:S(2)}, u32[]{:S(2)}) collective-permute-start(f32[16,1,1,4,1280]{4,3,0,2,1:T(4,128)S(1)} %constant_dynamic-slice_fusion.4), channel_id=1, source_target_pairs={{0,16},{8,24},{16,0},{24,8},{1,17},{9,25},{17,1},{25,9},{2,18},{10... | collective-permute-start | bytes 983048 | tf_op jit(solution)/shard_map/ppermute | solution.py:84
  125.5 51.0 %collective-permute-start.3 = (f32[2,2,2,1,4,1280]{5,4,3,2,1,0:T(4,128)S(1)}, f32[2,2,2,1,4,1280]{5,4,3,2,1,0:T(4,128)S(1)}, u32[]{:S(2)}, u32[]{:S(2)}) collective-permute-start(f32[2,2,2,1,4,1280]{5,4,3,2,1,0:T(4,128)S(1)} %constant_dynamic-slice_fusion.3), channel_id=1, source_target_pairs={{0,32},{32,0},{64,96},{96,64},{128,160},{160,128},{192,224},{224,1... | collective-permute-start | bytes 491528 | tf_op jit(solution)/shard_map/ppermute | solution.py:84
  176.6 8.4 %collective-permute-start.4 = (f32[2,2,1,1,4,1280]{5,4,3,2,1,0:T(4,128)S(1)}, f32[2,2,1,1,4,1280]{5,4,3,2,1,0:T(4,128)S(1)}, u32[]{:S(2)}, u32[]{:S(2)}) collective-permute-start(f32[2,2,1,1,4,1280]{5,4,3,2,1,0:T(4,128)S(1)} %constant_dynamic-slice_fusion.2), channel_id=1, source_target_pairs={{0,64},{32,96},{64,0},{96,32},{128,192},{160,224},{192,128},{224,1... | collective-permute-start | bytes 245768 | tf_op jit(solution)/shard_map/ppermute | solution.py:84
  185.1 10.2 %collective-permute-start.5 = (f32[2,1,1,1,4,1280]{5,4,3,2,1,0:T(4,128)S(1)}, f32[2,1,1,1,4,1280]{5,4,3,2,1,0:T(4,128)S(1)}, u32[]{:S(2)}, u32[]{:S(2)}) collective-permute-start(f32[2,1,1,1,4,1280]{5,4,3,2,1,0:T(4,128)S(1)} %constant_dynamic-slice_fusion.1), channel_id=1, source_target_pairs={{0,128},{32,160},{64,192},{96,224},{128,0},{160,32},{192,64},{224,... | collective-permute-start | bytes 122888 | tf_op jit(solution)/shard_map/ppermute | solution.py:84
  195.4 14.4 %collective-permute-start.6 = (f32[1,1,1,1,4,1280]{5,4,3,2,1,0:T(4,128)S(1)}, f32[1,1,1,1,4,1280]{5,4,3,2,1,0:T(4,128)S(1)}, u32[]{:S(2)}, u32[]{:S(2)}) collective-permute-start(f32[1,1,1,1,4,1280]{5,4,3,2,1,0:T(4,128)S(1)} %constant_dynamic-slice_fusion), channel_id=1, source_target_pairs={{0,256},{32,288},{64,320},{96,352},{128,384},{160,416},{192,448},{... | collective-permute-start | bytes 61448 | tf_op jit(solution)/shard_map/ppermute | solution.py:84
  217.4 13.6 %copy-start.10 = (f32[128,512]{1,0:T(8,128)S(1)}, f32[128,512]{1,0:T(8,128)}, u32[]{:S(2)}) copy-start(f32[128,512]{1,0:T(8,128)} %param.20) | copy-start | bytes 786436
  217.4 13.7 %copy-start.11 = (f32[128,512]{1,0:T(8,128)S(1)}, f32[128,512]{1,0:T(8,128)}, u32[]{:S(2)}) copy-start(f32[128,512]{1,0:T(8,128)} %param.19) | copy-start | bytes 786436
  217.4 9.7 %collective-permute-start.7 = (f32[136,640]{1,0:T(8,128)S(1)}, f32[136,640]{1,0:T(8,128)S(1)}, u32[]{:S(2)}, u32[]{:S(2)}) collective-permute-start(f32[136,640]{1,0:T(8,128)S(1)} %copy.158), channel_id=1, source_target_pairs={{0,1},{1,0},{2,3},{3,2},{4,5},{5,4},{6,7},{7,6},{8,9},{9,8},{10,11... | collective-permute-start | bytes 1044488 | tf_op jit(solution)/shard_map/ppermute | solution.py:90
  227.6 10.7 %collective-permute-start.8 = (f32[136,640]{1,0:T(8,128)S(1)}, f32[136,640]{1,0:T(8,128)S(1)}, u32[]{:S(2)}, u32[]{:S(2)}) collective-permute-start(f32[136,640]{1,0:T(8,128)S(1)} %copy.160), channel_id=1, source_target_pairs={{0,2},{1,3},{2,0},{3,1},{4,6},{5,7},{6,4},{7,5},{8,10},{9,11},{10,... | collective-permute-start | bytes 1044488 | tf_op jit(solution)/shard_map/ppermute | solution.py:90
  231.3 8.9 %copy-start.14 = (f32[128]{0:T(128)S(1)}, f32[128]{0:T(128)}, u32[]{:S(2)}) copy-start(f32[128]{0:T(128)} %param.21) | copy-start | bytes 1540
  238.6 3.9 %copy-start.1 = (bf16[512,1024]{1,0:T(8,128)(2,1)S(1)}, bf16[512,1024]{1,0:T(8,128)(2,1)}, u32[]{:S(2)}) copy-start(bf16[512,1024]{1,0:T(8,128)(2,1)} %param.17) | copy-start | bytes 3145732
